TPU v7x, 256 devices: a whole 4x4x8 slice. The times are simulated.
256 devices in a mesh: head: 8 (over z), ctx: 32 (over x, y, core).
Axes of the slice: x: 4, y: 4, z: 8, core: 2. Of those that a mesh axis runs over, the one named last changes fastest.
Arguments:
- queries: bfloat16 [16384, 4096], P('ctx', 'head'), may hold values from -100 to 100
- keys: bfloat16 [16384, 4096], P('ctx', 'head'), may hold values from -100 to 100
- values: bfloat16 [16384, 4096], P('ctx', 'head'), may hold values from -4 to 4
- out_grad: bfloat16 [16384, 4096], P('ctx', 'head'), may hold values from -6 to 6
- q_gain: float32 [4096], P('head'), may hold values from 0.1 to 1.9
- k_gain: float32 [4096], P('head'), may hold values from 0.1 to 1.9
- signs: int32 [2, 128, 16], replicated, may hold values from 0 to 1
Outputs:
- attended: bfloat16 [16384, 4096], P('ctx', 'head')
- q_grad: bfloat16 [16384, 4096], P('ctx', 'head')
- k_grad: bfloat16 [16384, 4096], P('ctx', 'head')
- v_grad: bfloat16 [16384, 4096], P('ctx', 'head')
All inputs are finite; a program needn't handle non-finite values.
Results may differ from a plain program's by a relative error of at most 0.012.
The roundings to bfloat16 on the way count: a program that leaves them out, or rounds other values in their place, can miss the bound.
Values sent between devices are 32-bit elements; how exact they have to be, the bound alone decides.
No kernel may reach another device: no remote copies, remote signals or barrier semaphores. Data moves between devices by JAX's collectives and lax.ppermute only.
A program may use at most 128 MiB of HBM per device.

v0:
```python
import jax
import jax.numpy as jnp
from jax import lax
from jax.sharding import PartitionSpec as P

HEADS = 32
DH = 128
RS = 16
BLOCK = 256


EPSILON = 1e-06
HIGHEST_PREC = lax.Precision.HIGHEST


def carried_in(part, axis, reverse):
    count = lax.axis_size(axis)
    leaves = jax.tree.leaves(part)
    flat = jnp.concatenate([leaf.reshape(-1) for leaf in leaves])
    total = flat.shape[0]
    chunk = -(-total // (count * 128)) * 128
    rows = jnp.pad(flat, (0, chunk * count - total)).reshape(count, chunk)
    mine = lax.all_to_all(rows, axis, 0, 0, tiled=True)
    dest = lax.broadcasted_iota(jnp.int32, (count, count), 0)
    source = lax.broadcasted_iota(jnp.int32, (count, count), 1)
    taken = (source > dest) if reverse else (source < dest)
    shifted = jnp.einsum(
        "ij,jc->ic", taken.astype(jnp.float32), mine, precision=HIGHEST_PREC
    )
    back = lax.all_to_all(shifted, axis, 0, 0, tiled=True).reshape(-1)[:total]
    pieces = []
    offset = 0
    for leaf in leaves:
        pieces.append(back[offset : offset + leaf.size].reshape(leaf.shape))
        offset += leaf.size
    return jax.tree.unflatten(jax.tree.structure(part), pieces)


def product_of(spec, lhs, rhs):
    return jnp.einsum(spec, lhs, rhs, preferred_element_type=jnp.float32)


def precise_product(spec, lhs, rhs):
    return jnp.einsum(
        spec, lhs.astype(jnp.float32), rhs.astype(jnp.float32), precision=HIGHEST_PREC
    )


def causal_mask():
    row_ids = lax.broadcasted_iota(jnp.int32, (BLOCK, BLOCK), 0)
    col_ids = lax.broadcasted_iota(jnp.int32, (BLOCK, BLOCK), 1)
    return row_ids >= col_ids


def sketch(inputs, sign_pair):
    projected = product_of("...d,dr->...r", inputs, sign_pair)
    left_part = projected[..., :RS]
    right_part = projected[..., RS:]
    sketched = left_part * right_part * (RS * DH) ** (-0.5)
    outer_prod = sketched[..., :, None] * sketched[..., None, :]
    sketch_feats = outer_prod.reshape(sketched.shape[:-1] + (RS * RS,)).astype(jnp.bfloat16)
    return (sketch_feats, sketched, left_part, right_part)


def sketch_back(feat_grad, sketched, left_part, right_part, sign_pair):
    grid = feat_grad.reshape(feat_grad.shape[:-1] + (RS, RS))
    symmetric = grid + jnp.swapaxes(grid, -1, -2)
    sketch_grad = jnp.sum(symmetric * sketched[..., None, :], axis=-1)
    both_grad = jnp.concatenate([sketch_grad * right_part, sketch_grad * left_part], axis=-1) * (
        RS * DH
    ) ** (-0.5)
    return precise_product("...r,dr->...d", both_grad, sign_pair)


def forward_blocks(q_normed, k_normed, values, sign_pair):
    scores = product_of("...id,...jd->...ij", q_normed, k_normed) * DH ** (-0.5)
    weights = jnp.where(causal_mask(), scores**4, 0.0).astype(jnp.bfloat16)
    q_parts = sketch(q_normed, sign_pair)
    k_parts = sketch(k_normed, sign_pair)
    block_kv = product_of("...jr,...jd->...rd", k_parts[0], values)
    block_keys = jnp.sum(k_parts[0].astype(jnp.float32), axis=-2)
    return (scores, weights, q_parts, k_parts, block_kv, block_keys)


def before_blocks(block_kv, block_keys, prior_kv, prior_keys):
    key_state = prior_kv[..., None, :, :] + jnp.cumsum(block_kv, axis=-3) - block_kv
    key_total = prior_keys[..., None, :] + jnp.cumsum(block_keys, axis=-2) - block_keys
    return (key_state, key_total)


def after_blocks(block_u, block_w, later_u, later_w):
    rev_u = jnp.flip(jnp.cumsum(jnp.flip(block_u, -3), axis=-3), -3)
    rev_w = jnp.flip(jnp.cumsum(jnp.flip(block_w, -2), axis=-2), -2)
    return (later_u[..., None, :, :] + rev_u - block_u, later_w[..., None, :] + rev_w - block_w)


def finish_forward(weights, values, q_feats, key_state, key_total):
    state_half = key_state.astype(jnp.bfloat16)
    numerator = product_of("...ij,...jd->...id", weights, values) + product_of(
        "...ir,...rd->...id", q_feats, state_half
    )
    denominator = (
        1.0
        + jnp.sum(weights.astype(jnp.float32), axis=-1)
        + precise_product("...ir,...r->...i", q_feats, key_total)
    )
    attended = (numerator / denominator[..., None]).astype(jnp.bfloat16)
    return (state_half, numerator, denominator, attended)


def backward_blocks(
    grad_in,
    numerator,
    denominator,
    scores,
    weights,
    values,
    q_normed,
    k_normed,
    q_feats,
    state_half,
    key_total,
):
    grad_float = grad_in.astype(jnp.float32)
    scaled_grad = (grad_float / denominator[..., None]).astype(jnp.bfloat16)
    den_grad = -jnp.sum(grad_float * numerator, axis=-1) / (denominator * denominator)
    weight_grad = product_of("...id,...jd->...ij", scaled_grad, values) + den_grad[..., None]
    score_grad = jnp.where(
        causal_mask(), 4.0 * scores**3 * weight_grad * DH ** (-0.5), 0.0
    ).astype(jnp.bfloat16)
    q_diag = product_of("...ij,...jd->...id", score_grad, k_normed)
    k_diag = product_of("...ij,...id->...jd", score_grad, q_normed)
    v_diag = product_of("...ij,...id->...jd", weights, scaled_grad)
    qf_grad = (
        product_of("...id,...rd->...ir", scaled_grad, state_half)
        + den_grad[..., None] * key_total[..., None, :]
    )
    block_u = product_of("...ir,...id->...rd", q_feats, scaled_grad)
    block_w = precise_product("...ir,...i->...r", q_feats, den_grad)
    return (q_diag, k_diag, v_diag, qf_grad, block_u, block_w)


def finish_backward(values, k_feats, later_state, later_total, v_diag):
    later_half = later_state.astype(jnp.bfloat16)
    kf_grad = product_of("...jd,...rd->...jr", values, later_half) + later_total[..., None, :]
    v_grad = v_diag + product_of("...jr,...rd->...jd", k_feats, later_half)
    return (kf_grad, v_grad)


def normalize(raw, gain, total):
    scale = lax.rsqrt(total / (HEADS * DH) + EPSILON)[:, None]
    return (scale, (raw.astype(jnp.float32) * scale * gain).astype(jnp.bfloat16))


def norm_back(raw, gain, scale, normed_grad, dot_total):
    raw_float = raw.astype(jnp.float32)
    return (
        scale * gain * normed_grad - raw_float * scale**3 * dot_total[:, None] / (HEADS * DH)
    ).astype(jnp.bfloat16)


def on_device(queries, keys, values, out_grad, q_gain, k_gain, signs):
    tok_rows = queries.shape[0]
    heads_here = queries.shape[1] // DH
    block_count = tok_rows // BLOCK
    sign_pair = jnp.concatenate([2 * signs[0] - 1, 2 * signs[1] - 1], axis=1).astype(jnp.bfloat16)
    q_float = queries.astype(jnp.float32)
    k_float = keys.astype(jnp.float32)
    q_total, k_total = lax.psum(
        (jnp.sum(q_float * q_float, axis=-1), jnp.sum(k_float * k_float, axis=-1)), "head"
    )
    q_scale, q_normed = normalize(queries, q_gain, q_total)
    k_scale, k_normed = normalize(keys, k_gain, k_total)

    def split_heads(array):
        return (
            array.reshape(tok_rows, heads_here, DH)
            .transpose(1, 0, 2)
            .reshape(heads_here, block_count, BLOCK, DH)
        )

    def join_heads(array):
        return (
            array.reshape(heads_here, tok_rows, DH)
            .transpose(1, 0, 2)
            .reshape(tok_rows, heads_here * DH)
        )

    q_heads = split_heads(q_normed)
    k_heads = split_heads(k_normed)
    v_heads = split_heads(values)
    g_heads = split_heads(out_grad)
    scores, weights, q_parts, k_parts, block_kv, block_keys = forward_blocks(
        q_heads, k_heads, v_heads, sign_pair
    )
    sum_kv = jnp.sum(block_kv, axis=1)
    sum_keys = jnp.sum(block_keys, axis=1)
    prior_kv, prior_keys = carried_in((sum_kv, sum_keys), "ctx", False)
    key_state, key_total = before_blocks(block_kv, block_keys, prior_kv, prior_keys)
    state_half, numerator, denominator, attended = finish_forward(
        weights, v_heads, q_parts[0], key_state, key_total
    )
    q_diag, k_diag, v_diag, qf_grad, block_u, block_w = backward_blocks(
        g_heads,
        numerator,
        denominator,
        scores,
        weights,
        v_heads,
        q_heads,
        k_heads,
        q_parts[0],
        state_half,
        key_total,
    )
    later_u, later_w = carried_in(
        (jnp.sum(block_u, axis=1), jnp.sum(block_w, axis=1)),
        "ctx",
        True,
    )
    later_state, later_total = after_blocks(block_u, block_w, later_u, later_w)
    kf_grad, v_grad = finish_backward(v_heads, k_parts[0], later_state, later_total, v_diag)
    qn_grad = join_heads(
        q_diag + sketch_back(qf_grad, q_parts[1], q_parts[2], q_parts[3], sign_pair)
    )
    kn_grad = join_heads(
        k_diag + sketch_back(kf_grad, k_parts[1], k_parts[2], k_parts[3], sign_pair)
    )
    q_dot, k_dot = lax.psum(
        (
            jnp.sum(q_float * q_gain * qn_grad, axis=-1),
            jnp.sum(k_float * k_gain * kn_grad, axis=-1),
        ),
        "head",
    )
    q_grad = norm_back(queries, q_gain, q_scale, qn_grad, q_dot)
    k_grad = norm_back(keys, k_gain, k_scale, kn_grad, k_dot)
    return (join_heads(attended), q_grad, k_grad, join_heads(v_grad).astype(jnp.bfloat16))


def solution(mesh):
    in_specs = (
        P("ctx", "head"),
        P("ctx", "head"),
        P("ctx", "head"),
        P("ctx", "head"),
        P("head"),
        P("head"),
        P(),
    )
    out_specs = (P("ctx", "head"), P("ctx", "head"), P("ctx", "head"), P("ctx", "head"))
    return jax.shard_map(
        on_device, mesh=mesh, in_specs=in_specs, out_specs=out_specs, check_vma=False
    )
```

profile of v0, /device:TPU:1, one launch (start us, length us, event | category | flops | bytes accessed | tf_op | source)
XLA Modules:
  0.0 156.2 jit_solution(7403571390134981156)
XLA Ops:
  0.6 1.2 fusion.14
  1.8 1.2 fusion.23
  3.1 0.7 fusion.48
  3.8 17.3 %all-reduce.3 = (f32[512]{0:T(512)S(1)}, f32[512]{0:T(512)S(1)}) all-reduce(f32[512]{0:T(512)S(1)} %fusion.14, f32[512]{0:T(512)S(1)} %fusion.23), channel_id=1, replica_groups=mesh['head'=8,'ctx'=32] {'head'}, use_global_device_ids=true, to_apply=%region_1.0 | all-reduce | flops 1024 | bytes 8192 | tf_op jit(solution)/shard_map/psum | solution.py:169
  21.1 0.6 multiply_multiply_fusion.4
  21.7 1.3 fusion.25
  23.2 0.8 copy-done.12
  24.5 0.5 convert_reduce_fusion
  25.6 0.9 select_maximum_fusion.1
  26.5 11.3 %all-to-all-start = ((f32[32,1,4224]{2,1,0:T(1,128)}), f32[32,1,4224]{2,1,0:T(1,128)}, u32[]{:S(2)}, u32[]{:S(2)}) async-start(f32[32,1,4224]{2,1,0:T(1,128)} %bitcast.171), calls=%async_computation | async-start | bytes 1081344 | tf_op jit(solution)/shard_map/all_to_all | solution.py:23
  37.8 0.6 iota_compare_fusion.1
  38.7 0.9 reshape.149
  39.6 1.2 copy.42
  40.8 1.0 fusion.55
  41.8 2.1 %copy_bitcast_fusion = f32[512,4,128]{2,0,1:T(8,128)} fusion(bf16[512,512]{1,0:T(8,128)(2,1)} %param.10), kind=kLoop, calls=%fused_computation.60 | loop fusion | flops 262144 | bytes 1572864 | tf_op jit(solution)/shard_map/convert_element_type | solution.py:124
  44.0 0.6 copy-done.26
  44.6 0.6 reduce_window_sum.35
  45.2 1.0 multiply_multiply_fusion.3
  46.2 3.6 %convert_reduce_fusion.2 = (f32[4,2,256]{2,1,0:T(2,128)}, bf16[4,2,256,256]{2,3,1,0:T(8,128)(2,1)}, f32[4,2,256,256]{2,3,1,0:T(8,128)}) fusion(pred[256,256]{0,1:T(8,128)(4,1)} %iota_compare_fusion.1, bf16[4,2,256,128]{3,2,1,0:T(8,128)(2,1)S(1)} %bitcast.165, bf16[4,2,256,128]{3,2,1,0:T(8,128)(2,1)S(1)} %bitcast.169), kind=kOutput, calls=%fused_computation.20 | convolution fusion | flops 137885696 | bytes 4268032 | tf_op jit(solution)/shard_map/...id,...jd->...ij/dot_general | solution.py:40
  49.8 1.4 convolution_bitcast_fusion.1
  51.2 1.4 copy.46
  52.6 7.4 %all-to-all-start.1 = ((f32[32,1,4224]{2,1,0:T(1,128)}), f32[32,1,4224]{2,1,0:T(1,128)}, u32[]{:S(2)}, u32[]{:S(2)}) async-start(f32[32,1,4224]{2,1,0:T(1,128)} %copy.46), calls=%async_computation.1 | async-start | bytes 1081344 | tf_op jit(solution)/shard_map/all_to_all | solution.py:30
  60.3 2.8 %fusion.61 = f32[4,2,256,128]{3,2,1,0:T(8,128)} fusion(bf16[4,2,256,256]{2,3,1,0:T(8,128)(2,1)} %get-tuple-element.13, bf16[4,2,256,128]{3,2,1,0:T(8,128)(2,1)} %bitcast.161), kind=kOutput, calls=%fused_computation.124 | convolution fusion | flops 134217728 | bytes 2621440 | tf_op jit(solution)/shard_map/...ij,...jd->...id/dot_general | solution.py:40
  63.1 8.7 %all-to-all-done.1 = f32[32,1,4224]{2,1,0:T(1,128)} async-done(((f32[32,1,4224]{2,1,0:T(1,128)}), f32[32,1,4224]{2,1,0:T(1,128)}, u32[]{:S(2)}, u32[]{:S(2)}) %all-to-all-start.1) | async-done | bytes 540704 | tf_op jit(solution)/shard_map/all_to_all | solution.py:30
  71.8 1.9 %slice.58 = f32[131072]{0:T(1024)} slice(f32[135168]{0:T(1024)} %bitcast.16), slice={[0:131072]} | slice | bytes 1048576 | tf_op jit(solution)/shard_map/slice | solution.py:34
  73.7 3.1 %reduce.3 = f32[32,4224]{1,0:T(8,128)} reduce(f32[32,1,4224]{2,1,0:T(1,128)} %all-to-all-done.1, f32[]{:T(128)} %constant.40), dimensions={1}, to_apply=%all_to_all.32.reduce_sub_computation | reduce | bytes 1081348 | tf_op jit(solution)/shard_map/all_to_all | solution.py:30
  76.8 2.0 %slice.49 = f32[528,1,256]{2,0,1:T(8,128)} reshape(f32[32,4224]{1,0:T(8,128)} %reduce.3) | data formatting | bytes 1081344 | tf_op jit(solution)/shard_map/slice | solution.py:34
  78.8 0.7 slice_bitcast_fusion.1
  79.6 1.3 fusion.12
  80.9 0.5 fusion.46
  81.5 0.7 multiply_reduce_fusion
  82.5 1.2 divide_convert_fusion
  84.2 1.8 %multiply_add_fusion = f32[4,2,256,256]{2,3,1,0:T(8,128)} fusion(bf16[4,2,256,128]{3,2,1,0:T(8,128)(2,1)S(1)} %get-tuple-element.21, bf16[4,2,256,128]{3,2,1,0:T(8,128)(2,1)S(1)} %fusion.12, f32[4,2,256]{2,1,0:T(2,128)S(1)} %add_subtract_fusion.1, f32[4,2,256]{2,1,0:T(2,128)S(1)} %get-tuple-element.10), kind=kOutput, calls=%fused_computation.19 | convolution fusion | flops 135266304 | bytes 3162112 | tf_op jit(solution)/shard_map/...id,...rd->...ir/dot_general | solution.py:40
  85.9 0.7 copy-done.21
  86.6 1.7 %fusion.6 = bf16[4,2,256,256]{2,3,1,0:T(8,128)(2,1)} fusion(f32[4,2,256,256]{2,3,1,0:T(8,128)S(1)} %copy-done.21, bf16[4,2,256,128]{3,2,1,0:T(8,128)(2,1)S(1)} %get-tuple-element.21, bf16[4,2,256,128]{3,2,1,0:T(8,128)(2,1)S(1)} %bitcast.162, f32[4,2,256]{2,1,0:T(2,128)S(1)} %get-tuple-element.10, pred[256,256]{0,1:T(8,128)(4,1)S(1)} %copy-done.25), kind=kOutput, calls=%fused_computation.12 | convolution fusion | flops 138936320 | bytes 4268032 | tf_op jit(solution)/shard_map/...id,...jd->...ij/dot_general | solution.py:40
  88.4 0.9 fusion.44
  89.3 0.9 select_maximum_fusion
  90.2 4.6 %all-to-all-start.2 = ((f32[32,1,4224]{2,1,0:T(1,128)}), f32[32,1,4224]{2,1,0:T(1,128)}, u32[]{:S(2)}, u32[]{:S(2)}) async-start(f32[32,1,4224]{2,1,0:T(1,128)} %bitcast.33), calls=%async_computation.2 | async-start | bytes 1081344 | tf_op jit(solution)/shard_map/all_to_all | solution.py:23
  94.8 3.9 %fusion.10 = f32[4,2,256,16]{2,3,1,0:T(8,128)S(1)} fusion(f32[4,2,256,16,16]{2,4,3,1,0:T(8,128)} %bitcast.158, f32[4,2,256,16]{2,3,1,0:T(8,128)S(1)} %multiply_multiply_fusion.3), kind=kLoop, calls=%fused_computation.18 | loop fusion | flops 1540096 | bytes 2359296 | tf_op jit(solution)/shard_map/reduce_sum | solution.py:68
  98.8 2.0 %fusion.36 = f32[4,2,256,128]{3,2,1,0:T(8,128)} fusion(f32[4,2,256,16]{2,3,1,0:T(8,128)S(1)} %get-tuple-element.17, f32[4,2,256,16]{2,3,1,0:T(8,128)S(1)} %get-tuple-element.16, bf16[128,16]{0,1:T(8,128)(2,1)S(1)} %get-tuple-element.20, bf16[128,16]{0,1:T(8,128)(2,1)S(1)} %get-tuple-element.19), kind=kOutput, calls=%fused_computation.76 | convolution fusion | flops 100810752 | bytes 1318912 | tf_op jit(solution)/shard_map/...r,dr->...d/dot_general | solution.py:44
  100.8 0.9 copy.108
  101.9 1.1 rev.14
  102.9 2.2 %convolution_add_fusion.3 = f32[4,2,256,128]{3,2,1,0:T(8,128)S(1)} fusion(f32[4,2,256,128]{3,2,1,0:T(8,128)} %fusion.36, bf16[4,2,256,256]{2,3,1,0:T(8,128)(2,1)} %fusion.6, bf16[4,2,256,128]{3,2,1,0:T(8,128)(2,1)} %bitcast.168), kind=kOutput, calls=%fused_computation.36 | convolution fusion | flops 134479872 | bytes 3670016 | tf_op jit(solution)/shard_map/...ij,...jd->...id/dot_general | solution.py:40
  105.4 0.7 all-to-all-done.2
  106.2 1.4 convolution_bitcast_fusion
  107.6 1.4 copy.54
  109.0 6.3 %all-to-all-start.3 = ((f32[32,1,4224]{2,1,0:T(1,128)}), f32[32,1,4224]{2,1,0:T(1,128)}, u32[]{:S(2)}, u32[]{:S(2)}) async-start(f32[32,1,4224]{2,1,0:T(1,128)} %copy.54), calls=%async_computation.3 | async-start | bytes 1081344 | tf_op jit(solution)/shard_map/all_to_all | solution.py:30
  115.3 2.4 %fusion.60 = f32[4,2,256,128]{3,2,1,0:T(8,128)} fusion(f32[4,2,256,128]{3,2,1,0:T(8,128)} %rev.14), kind=kOutput, calls=%fused_computation.123 | output fusion | flops 262144 | bytes 2097152 | tf_op jit(solution)/shard_map/jit(cumsum)/reduce_window_sum | solution.py:92
  117.7 1.4 fusion.62
  119.1 8.0 %all-to-all-done.3 = f32[32,1,4224]{2,1,0:T(1,128)} async-done(((f32[32,1,4224]{2,1,0:T(1,128)}), f32[32,1,4224]{2,1,0:T(1,128)}, u32[]{:S(2)}, u32[]{:S(2)}) %all-to-all-start.3) | async-done | bytes 540704 | tf_op jit(solution)/shard_map/all_to_all | solution.py:30
  127.1 1.9 %slice.60 = f32[131072]{0:T(1024)} slice(f32[135168]{0:T(1024)} %bitcast.35), slice={[0:131072]} | slice | bytes 1048576 | tf_op jit(solution)/shard_map/slice | solution.py:34
  129.0 3.1 %reduce.4 = f32[32,4224]{1,0:T(8,128)} reduce(f32[32,1,4224]{2,1,0:T(1,128)} %all-to-all-done.3, f32[]{:T(128)} %constant.40), dimensions={1}, to_apply=%all_to_all.37.reduce_sub_computation | reduce | bytes 1081348 | tf_op jit(solution)/shard_map/all_to_all | solution.py:30
  132.1 2.0 %slice.52 = f32[528,1,256]{2,0,1:T(8,128)} reshape(f32[32,4224]{1,0:T(8,128)} %reduce.4) | data formatting | bytes 1081344 | tf_op jit(solution)/shard_map/slice | solution.py:34
  134.1 0.8 slice_bitcast_fusion
  134.9 1.5 subtract_convert_fusion
  136.4 0.5 fusion.13
  136.9 0.9 copy.107
  137.8 0.4 convolution_add_fusion
  138.3 2.3 %fusion.8 = f32[4,2,256,16]{2,3,1,0:T(8,128)S(1)} fusion(f32[4,2,256,16,16]{2,4,3,1,0:T(8,128)S(1)} %bitcast.159, f32[4,2,256,16]{2,3,1,0:T(8,128)S(1)} %copy-done.23), kind=kLoop, calls=%fused_computation.15 | loop fusion | flops 1540096 | bytes 2359296 | tf_op jit(solution)/shard_map/reduce_sum | solution.py:68
  140.7 1.0 fusion.39
  142.2 0.5 copy-done.1
  143.0 11.0 %all-reduce.2 = (f32[512]{0:T(512)S(1)}, f32[512]{0:T(512)S(1)}) all-reduce(f32[512]{0:T(512)S(1)} %fusion.22, f32[512]{0:T(512)S(1)} %fusion.31), channel_id=1, replica_groups=mesh['head'=8,'ctx'=32] {'head'}, use_global_device_ids=true, to_apply=%region_13.14 | all-reduce | flops 1024 | bytes 8192 | tf_op jit(solution)/shard_map/psum | solution.py:229
  154.0 1.1 fusion.29
  155.1 1.1 fusion.20
  (101 shorter events, 3.8 us)
Async XLA Ops:
  21.7 2.6 %copy-start.35 = (f32[512]{0:T(512)}, f32[512]{0:T(512)S(1)}, u32[]{:S(2)}) copy-start(f32[512]{0:T(512)S(1)} %get-tuple-element.24) | copy-start | bytes 6148
  21.7 16.8 %copy-start.33 = (f32[512]{0:T(512)}, f32[512]{0:T(512)S(1)}, u32[]{:S(2)}) copy-start(f32[512]{0:T(512)S(1)} %get-tuple-element.34) | copy-start | bytes 6148
  21.7 2.6 %copy-start.24 = (bf16[512,512]{1,0:T(8,128)(2,1)S(1)}, bf16[512,512]{1,0:T(8,128)(2,1)}, u32[]{:S(2)}) copy-start(bf16[512,512]{1,0:T(8,128)(2,1)} %param.9) | copy-start | bytes 1572868
  23.2 0.8 copy-start.12
  24.3 0.8 copy-start.22
  24.5 1.1 copy-start.5
  25.2 13.3 %copy-start.2 = (bf16[512,512]{1,0:T(8,128)(2,1)S(1)}, bf16[512,512]{1,0:T(8,128)(2,1)}, u32[]{:S(2)}) copy-start(bf16[512,512]{1,0:T(8,128)(2,1)} %param.7) | copy-start | bytes 1572868
  25.2 13.3 %copy-start.31 = (f32[512]{0:T(512)S(1)}, f32[512]{0:T(512)}, u32[]{:S(2)}) copy-start(f32[512]{0:T(512)} %param.11) | copy-start | bytes 6148
  26.5 23.3 %all-to-all-start = ((f32[32,1,4224]{2,1,0:T(1,128)}), f32[32,1,4224]{2,1,0:T(1,128)}, u32[]{:S(2)}, u32[]{:S(2)}) async-start(f32[32,1,4224]{2,1,0:T(1,128)} %bitcast.171), calls=%async_computation | async-start | bytes 1081344 | tf_op jit(solution)/shard_map/all_to_all | solution.py:23
  39.6 6.6 %copy-start.13 = (bf16[4,512,128]{2,1,0:T(8,128)(2,1)S(1)}, bf16[4,512,128]{2,1,0:T(8,128)(2,1)}, u32[]{:S(2)}) copy-start(bf16[4,512,128]{2,1,0:T(8,128)(2,1)} %copy-done.12) | copy-start | bytes 1572868
  40.8 9.0 %copy-start.10 = (bf16[4,512,128]{2,1,0:T(8,128)(2,1)}, bf16[4,512,128]{2,1,0:T(8,128)(2,1)S(1)}, u32[]{:S(2)}) copy-start(bf16[4,512,128]{2,1,0:T(8,128)(2,1)S(1)} %copy.42) | copy-start | bytes 1572868
  44.0 0.6 copy-start.26
  52.6 19.2 %all-to-all-start.1 = ((f32[32,1,4224]{2,1,0:T(1,128)}), f32[32,1,4224]{2,1,0:T(1,128)}, u32[]{:S(2)}, u32[]{:S(2)}) async-start(f32[32,1,4224]{2,1,0:T(1,128)} %copy.46), calls=%async_computation.1 | async-start | bytes 1081344 | tf_op jit(solution)/shard_map/all_to_all | solution.py:30
  78.8 2.1 %copy-start.27 = (f32[4,2,256]{2,1,0:T(2,128)S(1)}, f32[4,2,256]{2,1,0:T(2,128)}, u32[]{:S(2)}) copy-start(f32[4,2,256]{2,1,0:T(2,128)} %copy-done.26) | copy-start | bytes 24580
  78.8 2.1 %copy-start.29 = (f32[4,2,256]{2,1,0:T(2,128)S(1)}, f32[4,2,256]{2,1,0:T(2,128)}, u32[]{:S(2)}) copy-start(f32[4,2,256]{2,1,0:T(2,128)} %reduce_window_sum.35) | copy-start | bytes 24580
  79.6 1.9 %copy-start.16 = (f32[512,4,128]{2,0,1:T(8,128)S(1)}, f32[512,4,128]{2,0,1:T(8,128)}, u32[]{:S(2)}) copy-start(f32[512,4,128]{2,0,1:T(8,128)} %copy_bitcast_fusion) | copy-start | bytes 3145732
  79.6 1.9 %copy-start.17 = (f32[4,2,256,128]{3,2,1,0:T(8,128)S(1)}, f32[4,2,256,128]{3,2,1,0:T(8,128)}, u32[]{:S(2)}) copy-start(f32[4,2,256,128]{3,2,1,0:T(8,128)} %fusion.61) | copy-start | bytes 3145732
  81.5 0.7 copy-start.28
  81.5 1.1 copy-start.19
  83.7 2.3 %copy-start.8 = (bf16[4,2,256,128]{3,2,1,0:T(8,128)(2,1)}, bf16[4,2,256,128]{3,2,1,0:T(8,128)(2,1)S(1)}, u32[]{:S(2)}) copy-start(bf16[4,2,256,128]{3,2,1,0:T(8,128)(2,1)S(1)} %get-tuple-element.21) | copy-start | bytes 1572868
  84.1 1.8 %copy-start.6 = (bf16[4,512,128]{2,1,0:T(8,128)(2,1)S(1)}, bf16[4,512,128]{2,1,0:T(8,128)(2,1)}, u32[]{:S(2)}) copy-start(bf16[4,512,128]{2,1,0:T(8,128)(2,1)} %copy-done.5) | copy-start | bytes 1572868
  84.1 2.5 %copy-start.21 = (f32[4,2,256,256]{2,3,1,0:T(8,128)S(1)}, f32[4,2,256,256]{2,3,1,0:T(8,128)}, u32[]{:S(2)}) copy-start(f32[4,2,256,256]{2,3,1,0:T(8,128)} %get-tuple-element.27) | copy-start | bytes 6291460
  84.1 2.5 %copy-start.25 = (pred[256,256]{0,1:T(8,128)(4,1)S(1)}, pred[256,256]{0,1:T(8,128)(4,1)}, u32[]{:S(2)}) copy-start(pred[256,256]{0,1:T(8,128)(4,1)} %iota_compare_fusion.1) | copy-start | bytes 196612
  89.3 9.4 %copy-start.18 = (f32[4,2,256,32]{2,3,1,0:T(8,128)S(1)}, f32[4,2,256,32]{2,3,1,0:T(8,128)}, u32[]{:S(2)}) copy-start(f32[4,2,256,32]{2,3,1,0:T(8,128)} %fusion.55) | copy-start | bytes 786436
  90.2 16.0 %all-to-all-start.2 = ((f32[32,1,4224]{2,1,0:T(1,128)}), f32[32,1,4224]{2,1,0:T(1,128)}, u32[]{:S(2)}, u32[]{:S(2)}) async-start(f32[32,1,4224]{2,1,0:T(1,128)} %bitcast.33), calls=%async_computation.2 | async-start | bytes 1081344 | tf_op jit(solution)/shard_map/all_to_all | solution.py:23
  94.8 6.0 %copy-start.20 = (bf16[4,2,256,128]{3,2,1,0:T(8,128)(2,1)S(1)}, bf16[4,2,256,128]{3,2,1,0:T(8,128)(2,1)}, u32[]{:S(2)}) copy-start(bf16[4,2,256,128]{3,2,1,0:T(8,128)(2,1)} %get-tuple-element.22) | copy-start | bytes 1572868
  102.9 2.3 %copy-start.3 = (bf16[512,512]{1,0:T(8,128)(2,1)S(1)}, bf16[512,512]{1,0:T(8,128)(2,1)}, u32[]{:S(2)}) copy-start(bf16[512,512]{1,0:T(8,128)(2,1)} %param.7) | copy-start | bytes 1572868
  102.9 2.3 %copy-start.32 = (f32[512]{0:T(512)S(1)}, f32[512]{0:T(512)}, u32[]{:S(2)}) copy-start(f32[512]{0:T(512)} %param.11) | copy-start | bytes 6148
  109.0 18.1 %all-to-all-start.3 = ((f32[32,1,4224]{2,1,0:T(1,128)}), f32[32,1,4224]{2,1,0:T(1,128)}, u32[]{:S(2)}, u32[]{:S(2)}) async-start(f32[32,1,4224]{2,1,0:T(1,128)} %copy.54), calls=%async_computation.3 | async-start | bytes 1081344 | tf_op jit(solution)/shard_map/all_to_all | solution.py:30
  115.3 2.4 %copy-start = (bf16[4,2,256,256]{2,3,1,0:T(8,128)(2,1)S(1)}, bf16[4,2,256,256]{2,3,1,0:T(8,128)(2,1)}, u32[]{:S(2)}) copy-start(bf16[4,2,256,256]{2,3,1,0:T(8,128)(2,1)} %get-tuple-element.13) | copy-start | bytes 3145732
  115.3 2.4 %copy-start.9 = (bf16[4,2,256,128]{3,2,1,0:T(8,128)(2,1)S(1)}, bf16[4,2,256,128]{3,2,1,0:T(8,128)(2,1)}, u32[]{:S(2)}) copy-start(bf16[4,2,256,128]{3,2,1,0:T(8,128)(2,1)} %copy-done.8) | copy-start | bytes 1572868
  134.1 2.3 %copy-start.15 = (f32[4,2,256,128]{3,2,1,0:T(8,128)S(1)}, f32[4,2,256,128]{3,2,1,0:T(8,128)}, u32[]{:S(2)}) copy-start(f32[4,2,256,128]{3,2,1,0:T(8,128)} %fusion.62) | copy-start | bytes 3145732
  136.4 1.4 copy-start.7
  136.9 1.4 copy-start.23
  138.3 3.4 %copy-start.11 = (bf16[4,512,128]{2,1,0:T(8,128)(2,1)S(1)}, bf16[4,512,128]{2,1,0:T(8,128)(2,1)}, u32[]{:S(2)}) copy-start(bf16[4,512,128]{2,1,0:T(8,128)(2,1)} %copy-done.10) | copy-start | bytes 1572868
  138.3 3.4 %copy-start.14 = (bf16[4,2,256,256]{2,3,1,0:T(8,128)(2,1)S(1)}, bf16[4,2,256,256]{2,3,1,0:T(8,128)(2,1)}, u32[]{:S(2)}) copy-start(bf16[4,2,256,256]{2,3,1,0:T(8,128)(2,1)} %fusion.6) | copy-start | bytes 3145732
  141.7 1.0 copy-start.1
  141.7 1.0 copy-start.30
  141.7 12.2 %copy-start.36 = (f32[512]{0:T(512)S(1)}, f32[512]{0:T(512)}, u32[]{:S(2)}) copy-start(f32[512]{0:T(512)} %copy-done.35) | copy-start | bytes 6148
  141.7 12.2 %copy-start.38 = (f32[512]{0:T(512)S(1)}, f32[512]{0:T(512)}, u32[]{:S(2)}) copy-start(f32[512]{0:T(512)} %get-tuple-element.23) | copy-start | bytes 6148
  142.2 12.9 %copy-start.4 = (bf16[512,512]{1,0:T(8,128)(2,1)S(1)}, bf16[512,512]{1,0:T(8,128)(2,1)}, u32[]{:S(2)}) copy-start(bf16[512,512]{1,0:T(8,128)(2,1)} %param.7) | copy-start | bytes 1572868
  142.2 12.9 %copy-start.34 = (f32[512]{0:T(512)S(1)}, f32[512]{0:T(512)}, u32[]{:S(2)}) copy-start(f32[512]{0:T(512)} %copy-done.33) | copy-start | bytes 6148
  142.2 12.9 %copy-start.37 = (f32[512]{0:T(512)S(1)}, f32[512]{0:T(512)}, u32[]{:S(2)}) copy-start(f32[512]{0:T(512)} %get-tuple-element.35) | copy-start | bytes 6148
where the time goes:
time: 159 us; the launch traced here: 156 us
  other arithmetic  33.9 us (21%)
  starting transfers between devices  29.6 us (19%)
  blocking collectives  28.3 us (18%)
  matrix products  25 us (16%)
  local copies, waits for them, and re-layouts  20.7 us (13%)
  waiting for transfers between devices  17.4 us (11%)
    dot_general x14, matrix products, product_of(): return jnp.einsum(spec, lhs, rhs, preferred_element_type=jnp.float32)  17.8 us
    psum x1, blocking collectives, on_device(): lax.psum((jnp.sum(q_float * q_float, axis=-1), jnp.sum(k_float * k_float,...  17.3 us
    all_to_all x2, waiting for transfers between devices, carried_in(): back = lax.all_to_all(shifted, axis, 0, 0, tiled=True).reshape(-1)[:total]  16.7 us
    all_to_all x2, starting transfers between devices, carried_in(): mine = lax.all_to_all(rows, axis, 0, 0, tiled=True)  15.9 us
    all_to_all x2, starting transfers between devices, carried_in(): back = lax.all_to_all(shifted, axis, 0, 0, tiled=True).reshape(-1)[:total]  13.7 us
    psum x1, blocking collectives, on_device(): lax.psum((jnp.sum(q_float * q_gain * qn_grad, axis=-1), jnp.sum(k_float *...  11 us
    slice x4, local copies, waits for them, and re-layouts, carried_in(): pieces.append(back[offset:offset + leaf.size].reshape(leaf.shape))  7.74 us
    reduce_sum x2, other arithmetic, sketch_back(): sketch_grad = jnp.sum(symmetric * sketched[..., None, :], axis=-1)  6.27 us
  transfers between devices with their start and end apart: 4, of which 3 were waited for; matrix products, arithmetic and copies ran while one was open for 18% of the time, Pallas kernels for 0%

commit v1 on v0

--- a/solution.py
+++ b/solution.py
@@ -13,27 +13,38 @@
 HIGHEST_PREC = lax.Precision.HIGHEST
 
 
-def carried_in(part, axis, reverse):
+def carried_in(state, totals, axis, reverse):
     count = lax.axis_size(axis)
-    leaves = jax.tree.leaves(part)
-    flat = jnp.concatenate([leaf.reshape(-1) for leaf in leaves])
-    total = flat.shape[0]
-    chunk = -(-total // (count * 128)) * 128
-    rows = jnp.pad(flat, (0, chunk * count - total)).reshape(count, chunk)
-    mine = lax.all_to_all(rows, axis, 0, 0, tiled=True)
+    heads_here, rows, lanes = state.shape
+    total_rows = totals.shape[1] // lanes
+    room = -(-(rows + total_rows) * heads_here // (count * 8)) * 8
+    padded = room * count // heads_here
+    stacked = jnp.concatenate(
+        [
+            state,
+            totals.reshape(heads_here, total_rows, lanes),
+            jnp.zeros((heads_here, padded - rows - total_rows, lanes), state.dtype),
+        ],
+        axis=1,
+    ).reshape(count, room, lanes)
+    mine = lax.all_to_all(stacked, axis, 0, 0, tiled=True)
     dest = lax.broadcasted_iota(jnp.int32, (count, count), 0)
     source = lax.broadcasted_iota(jnp.int32, (count, count), 1)
     taken = (source > dest) if reverse else (source < dest)
     shifted = jnp.einsum(
-        "ij,jc->ic", taken.astype(jnp.float32), mine, precision=HIGHEST_PREC
-    )
-    back = lax.all_to_all(shifted, axis, 0, 0, tiled=True).reshape(-1)[:total]
-    pieces = []
-    offset = 0
-    for leaf in leaves:
-        pieces.append(back[offset : offset + leaf.size].reshape(leaf.shape))
-        offset += leaf.size
-    return jax.tree.unflatten(jax.tree.structure(part), pieces)
+        "ij,jrc->irc", taken.astype(jnp.float32), mine, precision=HIGHEST_PREC
+    )
+    back = lax.all_to_all(shifted, axis, 0, 0, tiled=True).reshape(heads_here, padded, lanes)
+    return (back[:, :rows], back[:, rows : rows + total_rows].reshape(totals.shape))
+
+
+def head_sum(parts, axis):
+    count = lax.axis_size(axis)
+    stacked = jnp.stack(parts)
+    spread = jnp.broadcast_to(stacked[None], (count,) + stacked.shape)
+    gathered = lax.all_to_all(spread, axis, 0, 0, tiled=True)
+    summed = jnp.sum(gathered, axis=0)
+    return tuple(summed[i] for i in range(len(parts)))
 
 
 def product_of(spec, lhs, rhs):
@@ -166,7 +177,7 @@
     sign_pair = jnp.concatenate([2 * signs[0] - 1, 2 * signs[1] - 1], axis=1).astype(jnp.bfloat16)
     q_float = queries.astype(jnp.float32)
     k_float = keys.astype(jnp.float32)
-    q_total, k_total = lax.psum(
+    q_total, k_total = head_sum(
         (jnp.sum(q_float * q_float, axis=-1), jnp.sum(k_float * k_float, axis=-1)), "head"
     )
     q_scale, q_normed = normalize(queries, q_gain, q_total)
@@ -195,7 +206,7 @@
     )
     sum_kv = jnp.sum(block_kv, axis=1)
     sum_keys = jnp.sum(block_keys, axis=1)
-    prior_kv, prior_keys = carried_in((sum_kv, sum_keys), "ctx", False)
+    prior_kv, prior_keys = carried_in(sum_kv, sum_keys, "ctx", False)
     key_state, key_total = before_blocks(block_kv, block_keys, prior_kv, prior_keys)
     state_half, numerator, denominator, attended = finish_forward(
         weights, v_heads, q_parts[0], key_state, key_total
@@ -214,9 +225,7 @@
         key_total,
     )
     later_u, later_w = carried_in(
-        (jnp.sum(block_u, axis=1), jnp.sum(block_w, axis=1)),
-        "ctx",
-        True,
+        jnp.sum(block_u, axis=1), jnp.sum(block_w, axis=1), "ctx", True
     )
     later_state, later_total = after_blocks(block_u, block_w, later_u, later_w)
     kf_grad, v_grad = finish_backward(v_heads, k_parts[0], later_state, later_total, v_diag)
@@ -226,7 +235,7 @@
     kn_grad = join_heads(
         k_diag + sketch_back(kf_grad, k_parts[1], k_parts[2], k_parts[3], sign_pair)
     )
-    q_dot, k_dot = lax.psum(
+    q_dot, k_dot = head_sum(
         (
             jnp.sum(q_float * q_gain * qn_grad, axis=-1),
             jnp.sum(k_float * k_gain * kn_grad, axis=-1),

time: 159 us -> 139 us (0.87)
  blocking collectives: 28.3 us -> 0 us
  waiting for transfers between devices: 17.4 us -> 35.4 us
  other arithmetic: 33.9 us -> 26.2 us
  starting transfers between devices: 29.6 us -> 35.1 us
  matrix products: 25 us -> 21.2 us
  local copies, waits for them, and re-layouts: 20.7 us -> 18.3 us
    psum x2 -> x0, blocking collectives: 28.3 us -> none  [the longest x1 17.3 us: on_device(): lax.psum((jnp.sum(q_float * q_float, axis=-1), jnp.sum(k_float * k_float,...]
    all_to_all x4 -> x6, waiting for transfers between devices: 17.4 us -> 35.4 us  [the longest x2 17.2 us: carried_in(): mine = lax.all_to_all(stacked, axis, 0, 0, tiled=True)]
    all_to_all x2 -> x0, other arithmetic: 6.26 us -> none  [carried_in(): back = lax.all_to_all(shifted, axis, 0, 0, tiled=True).reshape(-1)[:total]]
    slice x4 -> x3, local copies, waits for them, and re-layouts: 7.74 us -> 2.28 us  [the longest x2 2.27 us: carried_in(): back[:, :rows]]
    all_to_all x4 -> x6, starting transfers between devices: 29.6 us -> 35.1 us  [the longest x2 13.9 us: carried_in(): mine = lax.all_to_all(stacked, axis, 0, 0, tiled=True)]
    dot_general x14, matrix products: 17.8 us -> 14.7 us  [product_of(): return jnp.einsum(spec, lhs, rhs, preferred_element_type=jnp.float32)]
    unnamed x79 -> x98, local copies, waits for them, and re-layouts: 3.11 us -> 6 us
    all_to_all x2 -> x0, local copies, waits for them, and re-layouts: 2.74 us -> none  [carried_in(): back = lax.all_to_all(shifted, axis, 0, 0, tiled=True).reshape(-1)[:total]]
  transfers between devices with their start and end apart: 4 -> 6, of which waited for: 3 -> 6; matrix products, arithmetic and copies ran while one was open for 18% -> 19% of each run, Pallas kernels for 0% -> 0%
where the time goes in v1:
time: 139 us; the launch traced here: 138 us
  waiting for transfers between devices  35.4 us (25%)
  starting transfers between devices  35.1 us (25%)
  other arithmetic  26.2 us (19%)
  matrix products  21.2 us (15%)
  local copies, waits for them, and re-layouts  18.3 us (13%)
  between operations  1.43 us (1%)
    all_to_all x2, waiting for transfers between devices, carried_in(): mine = lax.all_to_all(stacked, axis, 0, 0, tiled=True)  17.2 us
    dot_general x14, matrix products, product_of(): return jnp.einsum(spec, lhs, rhs, preferred_element_type=jnp.float32)  14.7 us
    all_to_all x2, starting transfers between devices, carried_in(): mine = lax.all_to_all(stacked, axis, 0, 0, tiled=True)  13.9 us
    all_to_all x2, starting transfers between devices, head_sum(): gathered = lax.all_to_all(spread, axis, 0, 0, tiled=True)  12.3 us
    all_to_all x2, waiting for transfers between devices, carried_in(): lax.all_to_all(shifted, axis, 0, 0, tiled=True)  10.7 us
    all_to_all x2, starting transfers between devices, carried_in(): lax.all_to_all(shifted, axis, 0, 0, tiled=True)  8.8 us
    all_to_all x2, waiting for transfers between devices, head_sum(): gathered = lax.all_to_all(spread, axis, 0, 0, tiled=True)  7.54 us
    reduce_sum x2, other arithmetic, sketch_back(): sketch_grad = jnp.sum(symmetric * sketched[..., None, :], axis=-1)  6.36 us
  transfers between devices with their start and end apart: 6, of which 6 were waited for; matrix products, arithmetic and copies ran while one was open for 19% of the time, Pallas kernels for 0%

profile of v1, /device:TPU:1, one launch (start us, length us, event | category | flops | bytes accessed | tf_op | source)
XLA Modules:
  0.0 137.7 jit_solution(1483807497236478155)
XLA Ops:
  0.6 1.3 fusion.14
  1.9 1.3 fusion.23
  3.2 0.6 broadcast_in_dim.17
  3.9 9.0 %all-to-all-start = ((f32[8,2,512]{2,1,0:T(2,128)}), f32[8,2,512]{2,1,0:T(2,128)S(1)}, u32[]{:S(2)}, u32[]{:S(2)}) async-start(f32[8,2,512]{2,1,0:T(2,128)} %broadcast_in_dim.17), calls=%async_computation | async-start | bytes 65536 | tf_op jit(solution)/shard_map/all_to_all | solution.py:45
  12.9 0.7 fusion.52
  13.6 1.2 reshape.169
  14.9 1.0 copy_bitcast_fusion
  16.0 0.6 iota_compare_fusion
  16.6 3.1 %all-to-all-done = f32[8,2,512]{2,1,0:T(2,128)S(1)} async-done(((f32[8,2,512]{2,1,0:T(2,128)}), f32[8,2,512]{2,1,0:T(2,128)S(1)}, u32[]{:S(2)}, u32[]{:S(2)}) %all-to-all-start) | async-done | bytes 32800 | tf_op jit(solution)/shard_map/all_to_all | solution.py:45
  21.5 1.0 convert_reduce_fusion
  22.6 0.4 fusion.67
  23.1 1.0 maximum_maximum_fusion
  24.0 9.2 %all-to-all-start.1 = ((f32[32,40,128]{2,1,0:T(8,128)}), f32[32,40,128]{2,1,0:T(8,128)}, u32[]{:S(2)}, u32[]{:S(2)}) async-start(f32[32,40,128]{2,1,0:T(8,128)} %bitcast.18), calls=%async_computation.1 | async-start | bytes 1310720 | tf_op jit(solution)/shard_map/all_to_all | solution.py:30
  33.3 0.6 multiply_multiply_fusion.5
  34.1 12.1 %all-to-all-done.1 = f32[32,40,128]{2,1,0:T(8,128)} async-done(((f32[32,40,128]{2,1,0:T(8,128)}), f32[32,40,128]{2,1,0:T(8,128)}, u32[]{:S(2)}, u32[]{:S(2)}) %all-to-all-start.1) | async-done | bytes 655392 | tf_op jit(solution)/shard_map/all_to_all | solution.py:30
  46.2 1.6 %fusion.34 = f32[32,40,128]{2,0,1:T(8,128)S(1)} fusion(f32[32,40,128]{2,1,0:T(8,128)} %all-to-all-done.1), kind=kOutput, calls=%fused_computation.68 | convolution fusion | flops 62915584 | bytes 1310720 | tf_op jit(solution)/shard_map/ij,jrc->irc/dot_general | solution.py:34
  47.8 1.2 copy.90
  49.1 4.4 %all-to-all-start.2 = ((f32[32,40,128]{2,1,0:T(8,128)}), f32[32,40,128]{2,1,0:T(8,128)}, u32[]{:S(2)}, u32[]{:S(2)}) async-start(f32[32,40,128]{2,1,0:T(8,128)} %copy.90), calls=%async_computation.2 | async-start | bytes 1310720 | tf_op jit(solution)/shard_map/all_to_all | solution.py:37
  53.5 0.6 multiply_multiply_fusion.4
  54.1 0.9 reduce_sum.144
  55.0 0.6 reduce_window_sum.35
  55.6 3.7 %convert_reduce_fusion.2 = (f32[4,2,256]{2,1,0:T(2,128)}, bf16[4,2,256,256]{2,3,1,0:T(8,128)(2,1)S(1)}, f32[4,2,256,256]{2,3,1,0:T(8,128)}) fusion(pred[256,256]{0,1:T(8,128)(4,1)} %iota_compare_fusion, bf16[4,2,256,128]{3,2,1,0:T(8,128)(2,1)} %bitcast.167, bf16[4,2,256,128]{3,2,1,0:T(8,128)(2,1)} %bitcast.170), kind=kOutput, calls=%fused_computation.18 | convolution fusion | flops 137885696 | bytes 4268032 | tf_op jit(solution)/shard_map/...id,...jd->...ij/dot_general | solution.py:51
  59.3 1.0 copy-done
  60.3 1.5 %fusion.70 = f32[4,2,256,128]{3,2,1,0:T(8,128)} fusion(bf16[4,2,256,256]{2,3,1,0:T(8,128)(2,1)S(1)} %get-tuple-element.9, bf16[4,2,256,128]{3,2,1,0:T(8,128)(2,1)S(1)} %bitcast.163), kind=kOutput, calls=%fused_computation.132 | convolution fusion | flops 134217728 | bytes 2621440 | tf_op jit(solution)/shard_map/...ij,...jd->...id/dot_general | solution.py:51
  61.8 4.4 %all-to-all-done.2 = f32[32,40,128]{2,1,0:T(8,128)} async-done(((f32[32,40,128]{2,1,0:T(8,128)}), f32[32,40,128]{2,1,0:T(8,128)}, u32[]{:S(2)}, u32[]{:S(2)}) %all-to-all-start.2) | async-done | bytes 655392 | tf_op jit(solution)/shard_map/all_to_all | solution.py:37
  66.2 0.7 slice_bitcast_fusion.1
  66.9 1.1 slice.62
  68.3 0.5 fusion.50
  68.8 0.5 copy-done.20
  69.6 0.6 multiply_reduce_fusion
  70.6 1.2 divide_convert_fusion
  71.8 1.2 fusion.68
  73.1 1.8 %multiply_add_fusion = f32[4,2,256,256]{2,3,1,0:T(8,128)} fusion(bf16[4,2,256,128]{3,2,1,0:T(8,128)(2,1)S(1)} %get-tuple-element.17, bf16[4,2,256,128]{3,2,1,0:T(8,128)(2,1)S(1)} %fusion.12, f32[4,2,256]{2,1,0:T(2,128)S(1)} %add_subtract_fusion.1, f32[4,2,256]{2,1,0:T(2,128)S(1)} %get-tuple-element.6), kind=kOutput, calls=%fused_computation.17 | convolution fusion | flops 135266304 | bytes 3162112 | tf_op jit(solution)/shard_map/...id,...rd->...ir/dot_general | solution.py:51
  74.9 0.9 fusion.48
  75.8 2.0 %maximum_maximum_fusion.1 = f32[4,320,128]{2,1,0:T(8,128)} fusion(f32[4,2,128]{2,1,0:T(2,128)S(1)} %reshape.179, f32[4,256,128]{2,1,0:T(8,128)} %get-tuple-element.28, f32[320]{0:T(512)} %copy-done.44), kind=kLoop, calls=%fused_computation.65 | loop fusion | flops 327680 | bytes 1185024 | tf_op jit(solution)/shard_map/concatenate | solution.py:22
  77.9 4.7 %all-to-all-start.3 = ((f32[32,40,128]{2,1,0:T(8,128)}), f32[32,40,128]{2,1,0:T(8,128)}, u32[]{:S(2)}, u32[]{:S(2)}) async-start(f32[32,40,128]{2,1,0:T(8,128)} %bitcast.35), calls=%async_computation.3 | async-start | bytes 1310720 | tf_op jit(solution)/shard_map/all_to_all | solution.py:30
  82.6 4.0 %fusion.10 = f32[4,2,256,16]{2,3,1,0:T(8,128)S(1)} fusion(f32[4,2,256,16,16]{2,4,3,1,0:T(8,128)} %bitcast.160, f32[4,2,256,16]{2,3,1,0:T(8,128)S(1)} %multiply_multiply_fusion.3), kind=kLoop, calls=%fused_computation.16 | loop fusion | flops 1540096 | bytes 2359296 | tf_op jit(solution)/shard_map/reduce_sum | solution.py:79
  86.7 1.0 fusion.36
  87.8 0.8 fusion.6
  88.6 1.0 copy-done.17
  89.6 0.5 convolution_add_fusion.3
  90.1 5.0 %all-to-all-done.3 = f32[32,40,128]{2,1,0:T(8,128)} async-done(((f32[32,40,128]{2,1,0:T(8,128)}), f32[32,40,128]{2,1,0:T(8,128)}, u32[]{:S(2)}, u32[]{:S(2)}) %all-to-all-start.3) | async-done | bytes 655392 | tf_op jit(solution)/shard_map/all_to_all | solution.py:30
  95.1 1.6 %fusion.32 = f32[32,40,128]{2,0,1:T(8,128)S(1)} fusion(f32[32,40,128]{2,1,0:T(8,128)} %all-to-all-done.3), kind=kOutput, calls=%fused_computation.66 | convolution fusion | flops 62915584 | bytes 1310720 | tf_op jit(solution)/shard_map/ij,jrc->irc/dot_general | solution.py:34
  96.7 1.3 copy.99
  98.0 4.4 %all-to-all-start.4 = ((f32[32,40,128]{2,1,0:T(8,128)}), f32[32,40,128]{2,1,0:T(8,128)}, u32[]{:S(2)}, u32[]{:S(2)}) async-start(f32[32,40,128]{2,1,0:T(8,128)} %copy.99), calls=%async_computation.4 | async-start | bytes 1310720 | tf_op jit(solution)/shard_map/all_to_all | solution.py:37
  102.4 1.3 fusion.22
  103.9 1.0 rev.14
  104.9 2.4 %fusion.69 = f32[4,2,256,128]{3,2,1,0:T(8,128)} fusion(f32[4,2,256,128]{3,2,1,0:T(8,128)} %rev.14), kind=kOutput, calls=%fused_computation.131 | output fusion | flops 262144 | bytes 2097152 | tf_op jit(solution)/shard_map/jit(cumsum)/reduce_window_sum | solution.py:103
  107.3 1.4 %fusion.71 = f32[4,2,256,128]{3,2,1,0:T(8,128)} fusion(bf16[4,2,256,256]{2,3,1,0:T(8,128)(2,1)S(1)} %copy-done.1, bf16[4,2,256,128]{3,2,1,0:T(8,128)(2,1)S(1)} %copy-done.8), kind=kOutput, calls=%fused_computation.133 | convolution fusion | flops 134217728 | bytes 2621440 | tf_op jit(solution)/shard_map/...ij,...id->...jd/dot_general | solution.py:51
  108.7 6.3 %all-to-all-done.4 = f32[32,40,128]{2,1,0:T(8,128)} async-done(((f32[32,40,128]{2,1,0:T(8,128)}), f32[32,40,128]{2,1,0:T(8,128)}, u32[]{:S(2)}, u32[]{:S(2)}) %all-to-all-start.4) | async-done | bytes 655392 | tf_op jit(solution)/shard_map/all_to_all | solution.py:37
  115.1 0.7 slice_bitcast_fusion
  115.8 1.2 slice.64
  117.0 1.4 %subtract_convert_fusion = bf16[4,2,256,128]{3,2,1,0:T(8,128)(2,1)S(1)} fusion(f32[4,2,256,128]{3,2,1,0:T(8,128)S(1)} %get-tuple-element.29, f32[4,2,256,128]{3,2,1,0:T(8,128)} %fusion.69, f32[4,256,128]{2,1,0:T(8,128)S(1)} %slice.64), kind=kLoop, calls=%fused_computation.60 | loop fusion | flops 786432 | bytes 3145728 | tf_op jit(solution)/shard_map/convert_element_type | solution.py:155
  118.4 1.3 fusion.13
  119.7 0.4 convolution_add_fusion
  120.2 0.4 copy-done.28
  120.6 2.3 %fusion.8 = f32[4,2,256,16]{2,3,1,0:T(8,128)S(1)} fusion(f32[4,2,256,16,16]{2,4,3,1,0:T(8,128)S(1)} %bitcast.161, f32[4,2,256,16]{2,3,1,0:T(8,128)S(1)} %copy-done.28), kind=kLoop, calls=%fused_computation.13 | loop fusion | flops 1540096 | bytes 2359296 | tf_op jit(solution)/shard_map/reduce_sum | solution.py:79
  123.0 1.0 fusion.39
  124.5 0.5 copy-done.12
  125.3 0.6 broadcast_in_dim.19
  125.9 3.3 %all-to-all-start.5 = ((f32[8,2,512]{2,1,0:T(2,128)}), f32[8,2,512]{2,1,0:T(2,128)S(1)}, u32[]{:S(2)}, u32[]{:S(2)}) async-start(f32[8,2,512]{2,1,0:T(2,128)} %broadcast_in_dim.19), calls=%async_computation.5 | async-start | bytes 65536 | tf_op jit(solution)/shard_map/all_to_all | solution.py:45
  129.3 2.3 %copy_bitcast_fusion.1 = (bf16[512,512]{1,0:T(8,128)(2,1)}, bf16[512,512]{1,0:T(8,128)(2,1)}) fusion(bf16[4,64,8,128]{3,2,1,0:T(8,128)(2,1)} %bitcast.177, bf16[4,64,8,128]{3,2,1,0:T(8,128)(2,1)} %bitcast.173), kind=kLoop, calls=%fused_computation.70 | loop fusion | bytes 2097152 | tf_op jit(solution)/shard_map/convert_element_type | solution.py:247
  131.6 4.4 %all-to-all-done.5 = f32[8,2,512]{2,1,0:T(2,128)S(1)} async-done(((f32[8,2,512]{2,1,0:T(2,128)}), f32[8,2,512]{2,1,0:T(2,128)S(1)}, u32[]{:S(2)}, u32[]{:S(2)}) %all-to-all-start.5) | async-done | bytes 32800 | tf_op jit(solution)/shard_map/all_to_all | solution.py:45
  136.1 1.6 %fusion.20 = (bf16[512,512]{1,0:T(8,128)(2,1)}, bf16[512,512]{1,0:T(8,128)(2,1)}) fusion(bf16[512,512]{1,0:T(8,128)(2,1)S(1)} %copy-done.10, f32[4,64,8,128]{3,2,1,0:T(8,128)S(1)} %bitcast.157, f32[512]{0:T(512)S(1)} %bitcast.191, f32[512]{0:T(512)S(1)} %copy-done.45, f32[512]{0:T(512)S(1)} %copy-done.41, f32[512]{0:T(512)S(1)} %bitcast.185, ...), kind=kLoop, calls=%fused_computation.44 | loop fusion | flops 4194304 | bytes 4210688 | tf_op jit(solution)/shard_map/convert_element_type | solution.py:170
  (126 shorter events, 4.2 us)
Async XLA Ops:
  0.6 14.2 %copy-start.24 = (bf16[512,512]{1,0:T(8,128)(2,1)S(1)}, bf16[512,512]{1,0:T(8,128)(2,1)}, u32[]{:S(2)}) copy-start(bf16[512,512]{1,0:T(8,128)(2,1)} %param.10) | copy-start | bytes 1572868
  1.9 17.9 %copy-start.9 = (bf16[512,512]{1,0:T(8,128)(2,1)S(1)}, bf16[512,512]{1,0:T(8,128)(2,1)}, u32[]{:S(2)}) copy-start(bf16[512,512]{1,0:T(8,128)(2,1)} %param.7) | copy-start | bytes 1572868
  1.9 17.9 %copy-start.40 = (f32[512]{0:T(512)S(1)}, f32[512]{0:T(512)}, u32[]{:S(2)}) copy-start(f32[512]{0:T(512)} %param.11) | copy-start | bytes 6148
  3.9 15.9 %all-to-all-start = ((f32[8,2,512]{2,1,0:T(2,128)}), f32[8,2,512]{2,1,0:T(2,128)S(1)}, u32[]{:S(2)}, u32[]{:S(2)}) async-start(f32[8,2,512]{2,1,0:T(2,128)} %broadcast_in_dim.17), calls=%async_computation | async-start | bytes 65536 | tf_op jit(solution)/shard_map/all_to_all | solution.py:45
  14.8 7.8 %copy-start.2 = (bf16[4,512,128]{2,1,0:T(8,128)(2,1)}, bf16[4,512,128]{2,1,0:T(8,128)(2,1)S(1)}, u32[]{:S(2)}) copy-start(bf16[4,512,128]{2,1,0:T(8,128)(2,1)S(1)} %copy.87) | copy-start | bytes 1572868
  14.8 5.4 %copy-start.11 = (bf16[512,512]{1,0:T(8,128)(2,1)S(1)}, bf16[512,512]{1,0:T(8,128)(2,1)}, u32[]{:S(2)}) copy-start(bf16[512,512]{1,0:T(8,128)(2,1)} %param.8) | copy-start | bytes 1572868
  14.9 5.4 %copy-start.42 = (f32[512]{0:T(512)S(1)}, f32[512]{0:T(512)}, u32[]{:S(2)}) copy-start(f32[512]{0:T(512)} %param.12) | copy-start | bytes 6148
  16.0 7.1 %copy-start.44 = (f32[320]{0:T(512)}, f32[320]{0:T(512)S(1)}, u32[]{:S(2)}) copy-start(f32[320]{0:T(512)S(1)} %pad.11.clone) | copy-start | bytes 3844
  19.8 13.5 %copy-start.37 = (f32[1,512]{1,0:T(1,128)}, f32[1,512]{1,0:T(1,128)S(1)}, u32[]{:S(2)}) copy-start(f32[1,512]{1,0:T(1,128)S(1)} %get-tuple-element.22) | copy-start | bytes 6148
  19.8 33.7 %copy-start.35 = (f32[1,512]{1,0:T(1,128)}, f32[1,512]{1,0:T(1,128)S(1)}, u32[]{:S(2)}) copy-start(f32[1,512]{1,0:T(1,128)S(1)} %get-tuple-element.21) | copy-start | bytes 6148
  20.2 1.0 copy-start.13
  20.7 0.8 copy-start.15
  20.9 12.9 %copy-start.22 = (f32[4,2,256,32]{2,3,1,0:T(8,128)}, f32[4,2,256,32]{2,3,1,0:T(8,128)S(1)}, u32[]{:S(2)}) copy-start(f32[4,2,256,32]{2,3,1,0:T(8,128)S(1)} %fusion.63) | copy-start | bytes 786436
  21.5 1.6 %copy-start.27 = (f32[4,2,256,16]{2,3,1,0:T(8,128)}, f32[4,2,256,16]{2,3,1,0:T(8,128)S(1)}, u32[]{:S(2)}) copy-start(f32[4,2,256,16]{2,3,1,0:T(8,128)S(1)} %multiply_multiply_fusion.2) | copy-start | bytes 393220
  24.0 22.2 %all-to-all-start.1 = ((f32[32,40,128]{2,1,0:T(8,128)}), f32[32,40,128]{2,1,0:T(8,128)}, u32[]{:S(2)}, u32[]{:S(2)}) async-start(f32[32,40,128]{2,1,0:T(8,128)} %bitcast.18), calls=%async_computation.1 | async-start | bytes 1310720 | tf_op jit(solution)/shard_map/all_to_all | solution.py:30
  49.1 17.1 %all-to-all-start.2 = ((f32[32,40,128]{2,1,0:T(8,128)}), f32[32,40,128]{2,1,0:T(8,128)}, u32[]{:S(2)}, u32[]{:S(2)}) async-start(f32[32,40,128]{2,1,0:T(8,128)} %copy.90), calls=%async_computation.2 | async-start | bytes 1310720 | tf_op jit(solution)/shard_map/all_to_all | solution.py:37
  55.0 4.4 %copy-start.32 = (f32[4,2,256]{2,1,0:T(2,128)}, f32[4,2,256]{2,1,0:T(2,128)S(1)}, u32[]{:S(2)}) copy-start(f32[4,2,256]{2,1,0:T(2,128)S(1)} %reduce_sum.144) | copy-start | bytes 24580
  55.6 4.7 %copy-start.3 = (bf16[4,512,128]{2,1,0:T(8,128)(2,1)S(1)}, bf16[4,512,128]{2,1,0:T(8,128)(2,1)}, u32[]{:S(2)}) copy-start(bf16[4,512,128]{2,1,0:T(8,128)(2,1)} %copy-done.2) | copy-start | bytes 1572868
  59.3 1.0 copy-start
  66.9 1.3 copy-start.33
  66.9 1.3 copy-start.39
  68.0 1.2 copy-start.20
  68.1 1.5 %copy-start.21 = (f32[4,2,256,128]{3,2,1,0:T(8,128)S(1)}, f32[4,2,256,128]{3,2,1,0:T(8,128)}, u32[]{:S(2)}) copy-start(f32[4,2,256,128]{3,2,1,0:T(8,128)} %fusion.70) | copy-start | bytes 3145732
  69.6 0.7 copy-start.34
  69.6 1.1 copy-start.25
  70.3 4.5 %copy-start.30 = (f32[4,2,256]{2,1,0:T(2,128)}, f32[4,2,256]{2,1,0:T(2,128)S(1)}, u32[]{:S(2)}) copy-start(f32[4,2,256]{2,1,0:T(2,128)S(1)} %get-tuple-element.6) | copy-start | bytes 24580
  71.8 3.0 %copy-start.6 = (bf16[4,2,256,128]{3,2,1,0:T(8,128)(2,1)}, bf16[4,2,256,128]{3,2,1,0:T(8,128)(2,1)S(1)}, u32[]{:S(2)}) copy-start(bf16[4,2,256,128]{3,2,1,0:T(8,128)(2,1)S(1)} %get-tuple-element.17) | copy-start | bytes 1572868
  77.9 8.8 %copy-start.23 = (f32[4,2,256,32]{2,3,1,0:T(8,128)S(1)}, f32[4,2,256,32]{2,3,1,0:T(8,128)}, u32[]{:S(2)}) copy-start(f32[4,2,256,32]{2,3,1,0:T(8,128)} %copy-done.22) | copy-start | bytes 786436
  77.9 17.3 %all-to-all-start.3 = ((f32[32,40,128]{2,1,0:T(8,128)}), f32[32,40,128]{2,1,0:T(8,128)}, u32[]{:S(2)}, u32[]{:S(2)}) async-start(f32[32,40,128]{2,1,0:T(8,128)} %bitcast.35), calls=%async_computation.3 | async-start | bytes 1310720 | tf_op jit(solution)/shard_map/all_to_all | solution.py:30
  82.6 5.2 %copy-start.4 = (bf16[4,512,128]{2,1,0:T(8,128)(2,1)S(1)}, bf16[4,512,128]{2,1,0:T(8,128)(2,1)}, u32[]{:S(2)}) copy-start(bf16[4,512,128]{2,1,0:T(8,128)(2,1)} %copy-done.2) | copy-start | bytes 1572868
  82.6 5.2 %copy-start.7 = (bf16[4,2,256,128]{3,2,1,0:T(8,128)(2,1)S(1)}, bf16[4,2,256,128]{3,2,1,0:T(8,128)(2,1)}, u32[]{:S(2)}) copy-start(bf16[4,2,256,128]{3,2,1,0:T(8,128)(2,1)} %copy-done.6) | copy-start | bytes 1572868
  82.6 5.2 %copy-start.26 = (f32[4,2,256,256]{2,3,1,0:T(8,128)S(1)}, f32[4,2,256,256]{2,3,1,0:T(8,128)}, u32[]{:S(2)}) copy-start(f32[4,2,256,256]{2,3,1,0:T(8,128)} %get-tuple-element.23) | copy-start | bytes 6291460
  82.6 5.2 %copy-start.29 = (pred[256,256]{0,1:T(8,128)(4,1)S(1)}, pred[256,256]{0,1:T(8,128)(4,1)}, u32[]{:S(2)}) copy-start(pred[256,256]{0,1:T(8,128)(4,1)} %iota_compare_fusion) | copy-start | bytes 196612
  82.6 5.2 %copy-start.31 = (f32[4,2,256]{2,1,0:T(2,128)S(1)}, f32[4,2,256]{2,1,0:T(2,128)}, u32[]{:S(2)}) copy-start(f32[4,2,256]{2,1,0:T(2,128)} %copy-done.30) | copy-start | bytes 24580
  87.8 1.8 %copy-start.16 = (bf16[4,512,128]{2,1,0:T(8,128)(2,1)S(1)}, bf16[4,512,128]{2,1,0:T(8,128)(2,1)}, u32[]{:S(2)}) copy-start(bf16[4,512,128]{2,1,0:T(8,128)(2,1)} %copy-done.15) | copy-start | bytes 1572868
  88.6 1.0 copy-start.17
  90.1 12.3 %copy-start.41 = (f32[512]{0:T(512)S(1)}, f32[512]{0:T(512)}, u32[]{:S(2)}) copy-start(f32[512]{0:T(512)} %param.11) | copy-start | bytes 6148
  98.0 17.1 %all-to-all-start.4 = ((f32[32,40,128]{2,1,0:T(8,128)}), f32[32,40,128]{2,1,0:T(8,128)}, u32[]{:S(2)}, u32[]{:S(2)}) async-start(f32[32,40,128]{2,1,0:T(8,128)} %copy.99), calls=%async_computation.4 | async-start | bytes 1310720 | tf_op jit(solution)/shard_map/all_to_all | solution.py:37
  104.9 2.4 %copy-start.1 = (bf16[4,2,256,256]{2,3,1,0:T(8,128)(2,1)S(1)}, bf16[4,2,256,256]{2,3,1,0:T(8,128)(2,1)}, u32[]{:S(2)}) copy-start(bf16[4,2,256,256]{2,3,1,0:T(8,128)(2,1)} %copy-done) | copy-start | bytes 3145732
  104.9 2.4 %copy-start.8 = (bf16[4,2,256,128]{3,2,1,0:T(8,128)(2,1)S(1)}, bf16[4,2,256,128]{3,2,1,0:T(8,128)(2,1)}, u32[]{:S(2)}) copy-start(bf16[4,2,256,128]{3,2,1,0:T(8,128)(2,1)} %copy-done.6) | copy-start | bytes 1572868
  115.8 2.6 %copy-start.19 = (f32[4,2,256,128]{3,2,1,0:T(8,128)S(1)}, f32[4,2,256,128]{3,2,1,0:T(8,128)}, u32[]{:S(2)}) copy-start(f32[4,2,256,128]{3,2,1,0:T(8,128)} %fusion.71) | copy-start | bytes 3145732
  118.4 1.3 copy-start.5
  119.7 0.9 copy-start.28
  120.6 3.4 %copy-start.14 = (bf16[4,512,128]{2,1,0:T(8,128)(2,1)S(1)}, bf16[4,512,128]{2,1,0:T(8,128)(2,1)}, u32[]{:S(2)}) copy-start(bf16[4,512,128]{2,1,0:T(8,128)(2,1)} %copy-done.13) | copy-start | bytes 1572868
  120.6 3.4 %copy-start.18 = (bf16[4,2,256,256]{2,3,1,0:T(8,128)(2,1)S(1)}, bf16[4,2,256,256]{2,3,1,0:T(8,128)(2,1)}, u32[]{:S(2)}) copy-start(bf16[4,2,256,256]{2,3,1,0:T(8,128)(2,1)} %copy-done.17) | copy-start | bytes 3145732
  124.0 1.0 copy-start.12
  124.0 1.0 copy-start.43
  124.5 11.6 %copy-start.10 = (bf16[512,512]{1,0:T(8,128)(2,1)S(1)}, bf16[512,512]{1,0:T(8,128)(2,1)}, u32[]{:S(2)}) copy-start(bf16[512,512]{1,0:T(8,128)(2,1)} %param.7) | copy-start | bytes 1572868
  124.5 11.6 %copy-start.36 = (f32[1,512]{1,0:T(1,128)S(1)}, f32[1,512]{1,0:T(1,128)}, u32[]{:S(2)}) copy-start(f32[1,512]{1,0:T(1,128)} %copy-done.35) | copy-start | bytes 6148
  124.5 11.6 %copy-start.38 = (f32[1,512]{1,0:T(1,128)S(1)}, f32[1,512]{1,0:T(1,128)}, u32[]{:S(2)}) copy-start(f32[1,512]{1,0:T(1,128)} %copy-done.37) | copy-start | bytes 6148
  124.5 11.6 %copy-start.45 = (f32[512]{0:T(512)S(1)}, f32[512]{0:T(512)}, u32[]{:S(2)}) copy-start(f32[512]{0:T(512)} %multiply_multiply_fusion.5) | copy-start | bytes 6148
  124.5 11.6 %copy-start.46 = (f32[512]{0:T(512)S(1)}, f32[512]{0:T(512)}, u32[]{:S(2)}) copy-start(f32[512]{0:T(512)} %multiply_multiply_fusion.4) | copy-start | bytes 6148
  125.9 10.1 %all-to-all-start.5 = ((f32[8,2,512]{2,1,0:T(2,128)}), f32[8,2,512]{2,1,0:T(2,128)S(1)}, u32[]{:S(2)}, u32[]{:S(2)}) async-start(f32[8,2,512]{2,1,0:T(2,128)} %broadcast_in_dim.19), calls=%async_computation.5 | async-start | bytes 65536 | tf_op jit(solution)/shard_map/all_to_all | solution.py:45

commit v2 on v1

--- a/solution.py
+++ b/solution.py
@@ -1,3 +1,4 @@
+import numpy as np
 import jax
 import jax.numpy as jnp
 from jax import lax
@@ -11,6 +12,15 @@
 
 EPSILON = 1e-06
 HIGHEST_PREC = lax.Precision.HIGHEST
+
+
+def shift_rows(rows, step, reverse):
+    widths = [(0, 0)] * rows.ndim
+    if reverse:
+        widths[0] = (0, step)
+        return jnp.pad(rows[step:], widths)
+    widths[0] = (step, 0)
+    return jnp.pad(rows[:-step], widths)
 
 
 def carried_in(state, totals, axis, reverse):
@@ -28,12 +38,11 @@
         axis=1,
     ).reshape(count, room, lanes)
     mine = lax.all_to_all(stacked, axis, 0, 0, tiled=True)
-    dest = lax.broadcasted_iota(jnp.int32, (count, count), 0)
-    source = lax.broadcasted_iota(jnp.int32, (count, count), 1)
-    taken = (source > dest) if reverse else (source < dest)
-    shifted = jnp.einsum(
-        "ij,jrc->irc", taken.astype(jnp.float32), mine, precision=HIGHEST_PREC
-    )
+    shifted = shift_rows(mine, 1, reverse)
+    step = 1
+    while step < count:
+        shifted = shifted + shift_rows(shifted, step, reverse)
+        step *= 2
     back = lax.all_to_all(shifted, axis, 0, 0, tiled=True).reshape(heads_here, padded, lanes)
     return (back[:, :rows], back[:, rows : rows + total_rows].reshape(totals.shape))
 
@@ -73,10 +82,21 @@
     return (sketch_feats, sketched, left_part, right_part)
 
 
+def lane_select(rule):
+    lanes = np.arange(RS * RS)
+    return jnp.asarray((rule(lanes)[:, None] == np.arange(RS)[None, :]).astype(np.float32))
+
+
 def sketch_back(feat_grad, sketched, left_part, right_part, sign_pair):
-    grid = feat_grad.reshape(feat_grad.shape[:-1] + (RS, RS))
-    symmetric = grid + jnp.swapaxes(grid, -1, -2)
-    sketch_grad = jnp.sum(symmetric * sketched[..., None, :], axis=-1)
+    by_row = lane_select(lambda f: f // RS)
+    by_col = lane_select(lambda f: f % RS)
+    row_copy = precise_product("...r,fr->...f", sketched, by_row)
+    col_copy = precise_product("...s,fs->...f", sketched, by_col)
+    sketch_grad = precise_product(
+        "...f,fr->...r",
+        jnp.concatenate([feat_grad * col_copy, feat_grad * row_copy], axis=-1),
+        jnp.concatenate([by_row, by_col], axis=0),
+    )
     both_grad = jnp.concatenate([sketch_grad * right_part, sketch_grad * left_part], axis=-1) * (
         RS * DH
     ) ** (-0.5)
@@ -93,16 +113,27 @@
     return (scores, weights, q_parts, k_parts, block_kv, block_keys)
 
 
+def exclusive_blocks(blocks, prior, axis, reverse):
+    count = blocks.shape[axis]
+    running = prior
+    outs = [None] * count
+    for b in reversed(range(count)) if reverse else range(count):
+        outs[b] = running
+        running = running + lax.index_in_dim(blocks, b, axis, keepdims=False)
+    return jnp.stack(outs, axis=axis)
+
+
 def before_blocks(block_kv, block_keys, prior_kv, prior_keys):
-    key_state = prior_kv[..., None, :, :] + jnp.cumsum(block_kv, axis=-3) - block_kv
-    key_total = prior_keys[..., None, :] + jnp.cumsum(block_keys, axis=-2) - block_keys
+    key_state = exclusive_blocks(block_kv, prior_kv, -3, False)
+    key_total = exclusive_blocks(block_keys, prior_keys, -2, False)
     return (key_state, key_total)
 
 
 def after_blocks(block_u, block_w, later_u, later_w):
-    rev_u = jnp.flip(jnp.cumsum(jnp.flip(block_u, -3), axis=-3), -3)
-    rev_w = jnp.flip(jnp.cumsum(jnp.flip(block_w, -2), axis=-2), -2)
-    return (later_u[..., None, :, :] + rev_u - block_u, later_w[..., None, :] + rev_w - block_w)
+    return (
+        exclusive_blocks(block_u, later_u, -3, True),
+        exclusive_blocks(block_w, later_w, -2, True),
+    )
 
 
 def finish_forward(weights, values, q_feats, key_state, key_total):

time: 139 us -> 142 us (1.022)
  matrix products: 21.2 us -> 35.9 us
  other arithmetic: 26.2 us -> 18.5 us
  local copies, waits for them, and re-layouts: 18.3 us -> 11.2 us
  waiting for transfers between devices: 35.4 us -> 38.8 us
    dot_general x4 -> x10, matrix products: 3.43 us -> 17.4 us  [precise_product(): jnp.einsum(spec, lhs.astype(jnp.float32), rhs.astype(jnp.float32), precis...]
    reduce_sum x2 -> x0, other arithmetic: 6.36 us -> none  [sketch_back(): sketch_grad = jnp.sum(symmetric * sketched[..., None, :], axis=-1)]
    all_to_all x2, waiting for transfers between devices: 10.7 us -> 16.4 us  [carried_in(): lax.all_to_all(shifted, axis, 0, 0, tiled=True)]
    unnamed x98 -> x84, local copies, waits for them, and re-layouts: 6 us -> 1.04 us
    dot_general x14, matrix products: 14.7 us -> 18.5 us  [product_of(): return jnp.einsum(spec, lhs, rhs, preferred_element_type=jnp.float32)]
    dot_general x2 -> x0, matrix products: 3.12 us -> none  [carried_in(): jnp.einsum('ij,jrc->irc', taken.astype(jnp.float32), mine, precision=HIGH...]
    all_to_all x2, waiting for transfers between devices: 17.2 us -> 14.2 us  [carried_in(): mine = lax.all_to_all(stacked, axis, 0, 0, tiled=True)]
    dot_general x2 -> x0, local copies, waits for them, and re-layouts: 2.5 us -> none  [carried_in(): jnp.einsum('ij,jrc->irc', taken.astype(jnp.float32), mine, precision=HIGH...]
  transfers between devices with their start and end apart: 6 -> 6, of which waited for: 6 -> 6; matrix products, arithmetic and copies ran while one was open for 19% -> 18% of each run, Pallas kernels for 0% -> 0%
where the time goes in v2:
time: 142 us; the launch traced here: 141 us
  waiting for transfers between devices  38.8 us (27%)
  matrix products  35.9 us (25%)
  starting transfers between devices  35.3 us (25%)
  other arithmetic  18.5 us (13%)
  local copies, waits for them, and re-layouts  11.2 us (8%)
  between operations  1.47 us (1%)
    dot_general x14, matrix products, product_of(): return jnp.einsum(spec, lhs, rhs, preferred_element_type=jnp.float32)  18.5 us
    dot_general x10, matrix products, precise_product(): jnp.einsum(spec, lhs.astype(jnp.float32), rhs.astype(jnp.float32), precis...  17.4 us
    all_to_all x2, waiting for transfers between devices, carried_in(): lax.all_to_all(shifted, axis, 0, 0, tiled=True)  16.4 us
    all_to_all x2, waiting for transfers between devices, carried_in(): mine = lax.all_to_all(stacked, axis, 0, 0, tiled=True)  14.2 us
    all_to_all x2, starting transfers between devices, carried_in(): mine = lax.all_to_all(stacked, axis, 0, 0, tiled=True)  13.8 us
    all_to_all x2, starting transfers between devices, head_sum(): gathered = lax.all_to_all(spread, axis, 0, 0, tiled=True)  12.3 us
    all_to_all x2, starting transfers between devices, carried_in(): lax.all_to_all(shifted, axis, 0, 0, tiled=True)  9.24 us
    all_to_all x2, waiting for transfers between devices, head_sum(): gathered = lax.all_to_all(spread, axis, 0, 0, tiled=True)  8.2 us
  transfers between devices with their start and end apart: 6, of which 6 were waited for; matrix products, arithmetic and copies ran while one was open for 18% of the time, Pallas kernels for 0%

profile of v2, /device:TPU:1, one launch (start us, length us, event | category | flops | bytes accessed | tf_op | source)
XLA Modules:
  0.0 141.2 jit_solution(16201255698097342458)
XLA Ops:
  0.6 1.3 fusion.18
  1.9 1.3 fusion.27
  3.2 0.6 broadcast_in_dim.17
  3.9 9.0 %all-to-all-start = ((f32[8,2,512]{2,1,0:T(2,128)}), f32[8,2,512]{2,1,0:T(2,128)S(1)}, u32[]{:S(2)}, u32[]{:S(2)}) async-start(f32[8,2,512]{2,1,0:T(2,128)} %broadcast_in_dim.17), calls=%async_computation | async-start | bytes 65536 | tf_op jit(solution)/shard_map/all_to_all | solution.py:54
  12.9 0.7 fusion.64
  13.6 1.2 reshape.157
  14.9 1.0 copy_bitcast_fusion
  16.0 3.7 %all-to-all-done = f32[8,2,512]{2,1,0:T(2,128)S(1)} async-done(((f32[8,2,512]{2,1,0:T(2,128)}), f32[8,2,512]{2,1,0:T(2,128)S(1)}, u32[]{:S(2)}, u32[]{:S(2)}) %all-to-all-start) | async-done | bytes 32800 | tf_op jit(solution)/shard_map/all_to_all | solution.py:54
  20.7 0.3 fusion.77
  20.9 0.3 fusion.76
  21.2 0.2 copy-done.16
  21.5 0.5 convert_reduce_fusion
  22.2 1.5 %fusion.82 = (f32[4,256,128]{2,1,0:T(8,128)S(1)}, f32[4,2,256,128]{3,2,1,0:T(8,128)}) fusion(bf16[4,2,256,256]{2,3,1,0:T(8,128)(2,1)S(1)} %bitcast.163, bf16[4,2,256,128]{3,2,1,0:T(8,128)(2,1)S(1)} %bitcast.169), kind=kOutput, calls=%fused_computation.157 | convolution fusion | flops 134348800 | bytes 3145728 | tf_op jit(solution)/shard_map/...jr,...jd->...rd/dot_general | solution.py:60
  23.6 1.0 maximum_maximum_fusion
  24.6 9.2 %all-to-all-start.1 = ((f32[32,40,128]{2,1,0:T(8,128)}), f32[32,40,128]{2,1,0:T(8,128)S(1)}, u32[]{:S(2)}, u32[]{:S(2)}) async-start(f32[32,40,128]{2,1,0:T(8,128)} %bitcast.17), calls=%async_computation.1 | async-start | bytes 1310720 | tf_op jit(solution)/shard_map/all_to_all | solution.py:40
  33.8 0.6 multiply_multiply_fusion.5
  34.4 0.2 multiply_convert_fusion.1
  34.6 12.1 %all-to-all-done.1 = f32[32,40,128]{2,1,0:T(8,128)S(1)} async-done(((f32[32,40,128]{2,1,0:T(8,128)}), f32[32,40,128]{2,1,0:T(8,128)S(1)}, u32[]{:S(2)}, u32[]{:S(2)}) %all-to-all-start.1) | async-done | bytes 655392 | tf_op jit(solution)/shard_map/all_to_all | solution.py:40
  47.3 0.9 pad_add_fusion.4
  48.2 4.4 %all-to-all-start.2 = ((f32[32,40,128]{2,1,0:T(8,128)}), f32[32,40,128]{2,1,0:T(8,128)}, u32[]{:S(2)}, u32[]{:S(2)}) async-start(f32[32,40,128]{2,1,0:T(8,128)} %pad_add_fusion.4), calls=%async_computation.2 | async-start | bytes 1310720 | tf_op jit(solution)/shard_map/all_to_all | solution.py:46
  52.6 0.6 multiply_multiply_fusion.4
  53.3 3.1 %convert_reduce_fusion.2 = (f32[4,2,256]{2,1,0:T(2,128)S(1)}, bf16[4,2,256,256]{2,3,1,0:T(8,128)(2,1)S(1)}, f32[4,2,256,256]{2,3,1,0:T(8,128)}) fusion(pred[256,256]{0,1:T(8,128)(4,1)S(1)} %iota_compare_fusion, bf16[4,2,256,128]{3,2,1,0:T(8,128)(2,1)} %bitcast.174, bf16[4,2,256,128]{3,2,1,0:T(8,128)(2,1)} %bitcast.177), kind=kOutput, calls=%fused_computation.22 | convolution fusion | flops 137885696 | bytes 4268032 | tf_op jit(solution)/shard_map/...id,...jd->...ij/dot_general | solution.py:60
  56.4 1.5 %fusion.84 = f32[4,2,256,128]{3,2,1,0:T(8,128)} fusion(bf16[4,2,256,256]{2,3,1,0:T(8,128)(2,1)S(1)} %get-tuple-element.9, bf16[4,2,256,128]{3,2,1,0:T(8,128)(2,1)S(1)} %bitcast.170), kind=kOutput, calls=%fused_computation.159 | convolution fusion | flops 134217728 | bytes 2621440 | tf_op jit(solution)/shard_map/...ij,...jd->...id/dot_general | solution.py:60
  57.9 7.4 %all-to-all-done.2 = f32[32,40,128]{2,1,0:T(8,128)} async-done(((f32[32,40,128]{2,1,0:T(8,128)}), f32[32,40,128]{2,1,0:T(8,128)}, u32[]{:S(2)}, u32[]{:S(2)}) %all-to-all-start.2) | async-done | bytes 655392 | tf_op jit(solution)/shard_map/all_to_all | solution.py:46
  65.3 0.9 slice.134
  66.2 1.1 fusion.48
  67.3 1.3 fusion.50
  68.6 0.5 fusion.62
  69.1 0.6 multiply_reduce_fusion
  69.8 0.9 fusion.60
  70.7 0.6 copy.161
  71.3 1.2 divide_convert_fusion
  72.5 2.2 %fusion.83 = (f32[4,256,128]{2,1,0:T(8,128)}, f32[4,2,256,128]{3,2,1,0:T(8,128)}) fusion(bf16[4,2,256,256]{2,3,1,0:T(8,128)(2,1)S(1)} %bitcast.162, bf16[4,2,256,128]{3,2,1,0:T(8,128)(2,1)S(1)} %get-tuple-element.19), kind=kOutput, calls=%fused_computation.158 | convolution fusion | flops 134348800 | bytes 3145728 | tf_op jit(solution)/shard_map/...ir,...id->...rd/dot_general | solution.py:60
  74.7 0.4 fusion.45
  75.2 2.0 %maximum_maximum_fusion.1 = f32[4,320,128]{2,1,0:T(8,128)} fusion(f32[4,2,128]{2,1,0:T(2,128)S(1)} %reshape.166, f32[4,256,128]{2,1,0:T(8,128)} %get-tuple-element.30, f32[320]{0:T(512)S(1)} %pad.81.clone), kind=kLoop, calls=%fused_computation.66 | loop fusion | flops 327680 | bytes 1185024 | tf_op jit(solution)/shard_map/concatenate | solution.py:32
  77.2 4.6 %all-to-all-start.3 = ((f32[32,40,128]{2,1,0:T(8,128)}), f32[32,40,128]{2,1,0:T(8,128)}, u32[]{:S(2)}, u32[]{:S(2)}) async-start(f32[32,40,128]{2,1,0:T(8,128)} %bitcast.183), calls=%async_computation.3 | async-start | bytes 1310720 | tf_op jit(solution)/shard_map/all_to_all | solution.py:40
  81.8 2.1 %fusion.15 = f32[4,2,256,256]{2,3,1,0:T(8,128)S(1)} fusion(f32[4,2,256,256]{2,3,1,0:T(8,128)S(1)} %fusion.45, f32[4,2,256,16]{2,3,1,0:T(8,128)S(1)} %multiply_multiply_fusion.3, f32[256,16,1,1]{0,1,3,2:T(8,128)S(1)} %copy-done.33, f32[4,2,256]{2,1,0:T(2,128)S(1)} %get-tuple-element.17, f32[4,2,256]{2,1,0:T(2,128)S(1)} %get-tuple-element.6), kind=kOutput, calls=%fused_computation.25 | convolution fusion | flops 102236160 | bytes 4358144 | tf_op jit(solution)/shard_map/...r,fr->...f/dot_general | solution.py:64
  83.9 2.1 %fusion.16 = f32[4,2,256,256]{2,3,1,0:T(8,128)S(1)} fusion(f32[4,2,256,256]{2,3,1,0:T(8,128)S(1)} %fusion.45, f32[4,2,256,16]{2,3,1,0:T(8,128)S(1)} %multiply_multiply_fusion.3, f32[256,16,1,1]{0,1,3,2:T(8,128)S(1)} %copy-done.32, f32[4,2,256]{2,1,0:T(2,128)S(1)} %get-tuple-element.17, f32[4,2,256]{2,1,0:T(2,128)S(1)} %get-tuple-element.6), kind=kOutput, calls=%fused_computation.26 | convolution fusion | flops 102236160 | bytes 4358144 | tf_op jit(solution)/shard_map/...s,fs->...f/dot_general | solution.py:64
  86.1 2.3 %slice_multiply_fusion.2 = (f32[4,2,256,16]{2,3,1,0:T(8,128)S(1)}, f32[4,2,256,16]{2,3,1,0:T(8,128)S(1)}) fusion(f32[4,2,256,32]{2,3,1,0:T(8,128)S(1)} %copy-done.30, f32[512,16,1,1]{0,1,3,2:T(8,128)S(1)} %copy-done.31, f32[4,2,256,256]{2,3,1,0:T(8,128)S(1)} %fusion.15, f32[4,2,256,256]{2,3,1,0:T(8,128)S(1)} %fusion.16), kind=kOutput, calls=%fused_computation.118 | convolution fusion | flops 202440704 | bytes 4751360 | tf_op jit(solution)/shard_map/...f,fr->...r/dot_general | solution.py:64
  88.4 2.0 %fusion.52 = f32[4,2,256,128]{3,2,1,0:T(8,128)} fusion(f32[4,2,256,16]{2,3,1,0:T(8,128)S(1)} %get-tuple-element.13, f32[4,2,256,16]{2,3,1,0:T(8,128)S(1)} %get-tuple-element.12, bf16[128,16]{0,1:T(8,128)(2,1)S(1)} %get-tuple-element.16, bf16[128,16]{0,1:T(8,128)(2,1)S(1)} %get-tuple-element.15), kind=kOutput, calls=%fused_computation.104 | convolution fusion | flops 100810752 | bytes 1318912 | tf_op jit(solution)/shard_map/...r,dr->...d/dot_general | solution.py:64
  90.4 1.8 %fusion.14 = bf16[4,2,256,256]{2,3,1,0:T(8,128)(2,1)} fusion(f32[4,2,256,256]{2,3,1,0:T(8,128)S(1)} %copy-done.26, bf16[4,2,256,128]{3,2,1,0:T(8,128)(2,1)S(1)} %copy-done.7, bf16[4,2,256,128]{3,2,1,0:T(8,128)(2,1)S(1)} %bitcast.171, f32[4,2,256]{2,1,0:T(2,128)S(1)} %get-tuple-element.6, pred[256,256]{0,1:T(8,128)(4,1)S(1)} %iota_compare_fusion), kind=kOutput, calls=%fused_computation.18 | convolution fusion | flops 138936320 | bytes 4268032 | tf_op jit(solution)/shard_map/...id,...jd->...ij/dot_general | solution.py:60
  92.2 2.1 %all-to-all-done.3 = f32[32,40,128]{2,1,0:T(8,128)} async-done(((f32[32,40,128]{2,1,0:T(8,128)}), f32[32,40,128]{2,1,0:T(8,128)}, u32[]{:S(2)}, u32[]{:S(2)}) %all-to-all-start.3) | async-done | bytes 655392 | tf_op jit(solution)/shard_map/all_to_all | solution.py:40
  94.3 1.1 slice.136
  96.0 0.9 pad_add_fusion
  96.9 4.8 %all-to-all-start.4 = ((f32[32,40,128]{2,1,0:T(8,128)}), f32[32,40,128]{2,1,0:T(8,128)S(1)}, u32[]{:S(2)}, u32[]{:S(2)}) async-start(f32[32,40,128]{2,1,0:T(8,128)} %pad_add_fusion), calls=%async_computation.4 | async-start | bytes 1310720 | tf_op jit(solution)/shard_map/all_to_all | solution.py:46
  101.8 2.2 %convolution_add_fusion.2 = f32[4,2,256,128]{3,2,1,0:T(8,128)S(1)} fusion(f32[4,2,256,128]{3,2,1,0:T(8,128)} %fusion.52, bf16[4,2,256,256]{2,3,1,0:T(8,128)(2,1)} %fusion.14, bf16[4,2,256,128]{3,2,1,0:T(8,128)(2,1)S(1)} %bitcast.178), kind=kOutput, calls=%fused_computation.37 | convolution fusion | flops 134479872 | bytes 3670016 | tf_op jit(solution)/shard_map/...ij,...jd->...id/dot_general | solution.py:60
  104.0 0.2 fusion.26
  104.2 1.4 fusion.85
  105.6 9.0 %all-to-all-done.4 = f32[32,40,128]{2,1,0:T(8,128)S(1)} async-done(((f32[32,40,128]{2,1,0:T(8,128)}), f32[32,40,128]{2,1,0:T(8,128)S(1)}, u32[]{:S(2)}, u32[]{:S(2)}) %all-to-all-start.4) | async-done | bytes 655392 | tf_op jit(solution)/shard_map/all_to_all | solution.py:46
  114.6 0.7 fusion.49
  115.3 1.8 %fusion.51 = bf16[4,1,256,128]{3,2,0,1:T(8,128)(2,1)} fusion(f32[4,2,256,128]{3,2,1,0:T(8,128)} %get-tuple-element.31, f32[4,320,128]{2,1,0:T(8,128)S(1)} %bitcast.182), kind=kLoop, calls=%fused_computation.102 | loop fusion | flops 262144 | bytes 1310720 | tf_op jit(solution)/shard_map/stack | solution.py:123
  117.2 1.5 %fusion.43 = f32[4,2,256,256]{3,2,1,0:T(8,128)S(1)} fusion(bf16[4,2,256,128]{3,2,1,0:T(8,128)(2,1)S(1)} %bitcast.172, bf16[4,1,256,128]{3,2,0,1:T(8,128)(2,1)} %fusion.49, bf16[4,1,256,128]{3,2,0,1:T(8,128)(2,1)} %fusion.51), kind=kOutput, calls=%fused_computation.94 | convolution fusion | flops 134479872 | bytes 3145728 | tf_op jit(solution)/shard_map/...jd,...rd->...jr/dot_general | solution.py:60
  118.7 2.1 %bitcast_multiply_fusion = f32[4,2,256,256]{2,3,1,0:T(8,128)S(1)} fusion(f32[4,2,256,256]{3,2,1,0:T(8,128)S(1)} %fusion.43, f32[4,2,256,16]{2,3,1,0:T(8,128)S(1)} %multiply_multiply_fusion.2, f32[256,16,1,1]{0,1,3,2:T(8,128)S(1)} %copy-done.34, f32[4,2,256]{2,1,0:T(2,128)S(1)} %copy.100), kind=kOutput, calls=%fused_computation.19 | convolution fusion | flops 101711872 | bytes 4349952 | tf_op jit(solution)/shard_map/...r,fr->...f/dot_general | solution.py:64
  120.8 2.1 %bitcast_multiply_fusion.1 = f32[4,2,256,256]{2,3,1,0:T(8,128)S(1)} fusion(f32[4,2,256,256]{3,2,1,0:T(8,128)S(1)} %fusion.43, f32[4,2,256,16]{2,3,1,0:T(8,128)S(1)} %multiply_multiply_fusion.2, f32[256,16,1,1]{0,1,3,2:T(8,128)S(1)} %copy-done.32, f32[4,2,256]{2,1,0:T(2,128)S(1)} %copy.100), kind=kOutput, calls=%fused_computation.20 | convolution fusion | flops 101711872 | bytes 4349952 | tf_op jit(solution)/shard_map/...s,fs->...f/dot_general | solution.py:64
  122.9 1.3 fusion.17
  124.2 2.3 %slice_multiply_fusion = (f32[4,2,256,16]{2,3,1,0:T(8,128)S(1)}, f32[4,2,256,16]{2,3,1,0:T(8,128)S(1)}) fusion(f32[4,2,256,32]{2,3,1,0:T(8,128)S(1)} %copy-done.28, f32[512,16,1,1]{0,1,3,2:T(8,128)S(1)} %copy-done.31, f32[4,2,256,256]{2,3,1,0:T(8,128)S(1)} %bitcast_multiply_fusion, f32[4,2,256,256]{2,3,1,0:T(8,128)S(1)} %bitcast_multiply_fusion.1), kind=kOutput, calls=%fused_computation.116 | convolution fusion | flops 202440704 | bytes 4751360 | tf_op jit(solution)/shard_map/...f,fr->...r/dot_general | solution.py:64
  126.5 1.0 fusion.55
  127.6 0.5 convolution_add_fusion.1
  128.1 0.5 copy-done.13
  128.8 0.6 broadcast_in_dim.19
  129.5 3.3 %all-to-all-start.5 = ((f32[8,2,512]{2,1,0:T(2,128)}), f32[8,2,512]{2,1,0:T(2,128)S(1)}, u32[]{:S(2)}, u32[]{:S(2)}) async-start(f32[8,2,512]{2,1,0:T(2,128)} %broadcast_in_dim.19), calls=%async_computation.5 | async-start | bytes 65536 | tf_op jit(solution)/shard_map/all_to_all | solution.py:54
  132.8 2.3 %copy_bitcast_fusion.1 = (bf16[512,512]{1,0:T(8,128)(2,1)}, bf16[512,512]{1,0:T(8,128)(2,1)}) fusion(bf16[4,64,8,128]{3,2,1,0:T(8,128)(2,1)} %bitcast.188, bf16[4,64,8,128]{3,2,1,0:T(8,128)(2,1)} %bitcast.184), kind=kLoop, calls=%fused_computation.81 | loop fusion | bytes 2097152 | tf_op jit(solution)/shard_map/convert_element_type | solution.py:278
  135.1 4.5 %all-to-all-done.5 = f32[8,2,512]{2,1,0:T(2,128)S(1)} async-done(((f32[8,2,512]{2,1,0:T(2,128)}), f32[8,2,512]{2,1,0:T(2,128)S(1)}, u32[]{:S(2)}, u32[]{:S(2)}) %all-to-all-start.5) | async-done | bytes 32800 | tf_op jit(solution)/shard_map/all_to_all | solution.py:54
  139.6 1.6 %fusion.24 = (bf16[512,512]{1,0:T(8,128)(2,1)}, bf16[512,512]{1,0:T(8,128)(2,1)}) fusion(bf16[512,512]{1,0:T(8,128)(2,1)S(1)} %copy-done.11, f32[4,64,8,128]{3,2,1,0:T(8,128)S(1)} %bitcast.166, f32[512]{0:T(512)S(1)} %bitcast.201, f32[512]{0:T(512)S(1)} %copy-done.40, f32[512]{0:T(512)S(1)} %copy-done.36, f32[512]{0:T(512)S(1)} %bitcast.197, ...), kind=kLoop, calls=%fused_computation.46 | loop fusion | flops 4194304 | bytes 4210688 | tf_op jit(solution)/shard_map/convert_element_type | solution.py:201
  (130 shorter events, 2.8 us)
Async XLA Ops:
  0.6 14.2 %copy-start.24 = (bf16[512,512]{1,0:T(8,128)(2,1)S(1)}, bf16[512,512]{1,0:T(8,128)(2,1)}, u32[]{:S(2)}) copy-start(bf16[512,512]{1,0:T(8,128)(2,1)} %param.14) | copy-start | bytes 1572868
  1.9 17.9 %copy-start.9 = (bf16[512,512]{1,0:T(8,128)(2,1)S(1)}, bf16[512,512]{1,0:T(8,128)(2,1)}, u32[]{:S(2)}) copy-start(bf16[512,512]{1,0:T(8,128)(2,1)} %param.11) | copy-start | bytes 1572868
  1.9 17.9 %copy-start.35 = (f32[512]{0:T(512)S(1)}, f32[512]{0:T(512)}, u32[]{:S(2)}) copy-start(f32[512]{0:T(512)} %param.15) | copy-start | bytes 6148
  3.9 15.9 %all-to-all-start = ((f32[8,2,512]{2,1,0:T(2,128)}), f32[8,2,512]{2,1,0:T(2,128)S(1)}, u32[]{:S(2)}, u32[]{:S(2)}) async-start(f32[8,2,512]{2,1,0:T(2,128)} %broadcast_in_dim.17), calls=%async_computation | async-start | bytes 65536 | tf_op jit(solution)/shard_map/all_to_all | solution.py:54
  14.8 7.3 %copy-start.2 = (bf16[4,512,128]{2,1,0:T(8,128)(2,1)}, bf16[4,512,128]{2,1,0:T(8,128)(2,1)S(1)}, u32[]{:S(2)}) copy-start(bf16[4,512,128]{2,1,0:T(8,128)(2,1)S(1)} %copy.86) | copy-start | bytes 1572868
  14.8 5.4 %copy-start.12 = (bf16[512,512]{1,0:T(8,128)(2,1)S(1)}, bf16[512,512]{1,0:T(8,128)(2,1)}, u32[]{:S(2)}) copy-start(bf16[512,512]{1,0:T(8,128)(2,1)} %param.12) | copy-start | bytes 1572868
  14.9 5.4 %copy-start.37 = (f32[512]{0:T(512)S(1)}, f32[512]{0:T(512)}, u32[]{:S(2)}) copy-start(f32[512]{0:T(512)} %param.16) | copy-start | bytes 6148
  20.2 1.0 copy-start.14
  20.6 0.8 copy-start.16
  20.9 13.4 %copy-start.29 = (f32[4,2,256,32]{2,3,1,0:T(8,128)}, f32[4,2,256,32]{2,3,1,0:T(8,128)S(1)}, u32[]{:S(2)}) copy-start(f32[4,2,256,32]{2,3,1,0:T(8,128)S(1)} %fusion.77) | copy-start | bytes 786436
  21.4 0.7 copy-start.27
  24.6 22.1 %all-to-all-start.1 = ((f32[32,40,128]{2,1,0:T(8,128)}), f32[32,40,128]{2,1,0:T(8,128)S(1)}, u32[]{:S(2)}, u32[]{:S(2)}) async-start(f32[32,40,128]{2,1,0:T(8,128)} %bitcast.17), calls=%async_computation.1 | async-start | bytes 1310720 | tf_op jit(solution)/shard_map/all_to_all | solution.py:40
  48.2 17.2 %all-to-all-start.2 = ((f32[32,40,128]{2,1,0:T(8,128)}), f32[32,40,128]{2,1,0:T(8,128)}, u32[]{:S(2)}, u32[]{:S(2)}) async-start(f32[32,40,128]{2,1,0:T(8,128)} %pad_add_fusion.4), calls=%async_computation.2 | async-start | bytes 1310720 | tf_op jit(solution)/shard_map/all_to_all | solution.py:46
  53.3 3.2 %copy-start.3 = (bf16[4,512,128]{2,1,0:T(8,128)(2,1)S(1)}, bf16[4,512,128]{2,1,0:T(8,128)(2,1)}, u32[]{:S(2)}) copy-start(bf16[4,512,128]{2,1,0:T(8,128)(2,1)} %copy-done.2) | copy-start | bytes 1572868
  56.4 12.1 %copy-start = (bf16[4,2,256,256]{2,3,1,0:T(8,128)(2,1)}, bf16[4,2,256,256]{2,3,1,0:T(8,128)(2,1)S(1)}, u32[]{:S(2)}) copy-start(bf16[4,2,256,256]{2,3,1,0:T(8,128)(2,1)S(1)} %get-tuple-element.9) | copy-start | bytes 3145732
  65.3 3.8 %copy-start.20 = (f32[512,4,128]{2,0,1:T(8,128)S(1)}, f32[512,4,128]{2,0,1:T(8,128)}, u32[]{:S(2)}) copy-start(f32[512,4,128]{2,0,1:T(8,128)} %copy_bitcast_fusion) | copy-start | bytes 3145732
  65.3 3.8 %copy-start.21 = (f32[4,2,256,128]{3,2,1,0:T(8,128)S(1)}, f32[4,2,256,128]{3,2,1,0:T(8,128)}, u32[]{:S(2)}) copy-start(f32[4,2,256,128]{3,2,1,0:T(8,128)} %fusion.84) | copy-start | bytes 3145732
  69.1 2.2 %copy-start.25 = (bf16[512,512]{1,0:T(8,128)(2,1)S(1)}, bf16[512,512]{1,0:T(8,128)(2,1)}, u32[]{:S(2)}) copy-start(bf16[512,512]{1,0:T(8,128)(2,1)} %param.14) | copy-start | bytes 1572868
  72.5 2.3 %copy-start.6 = (bf16[4,2,256,128]{3,2,1,0:T(8,128)(2,1)}, bf16[4,2,256,128]{3,2,1,0:T(8,128)(2,1)S(1)}, u32[]{:S(2)}) copy-start(bf16[4,2,256,128]{3,2,1,0:T(8,128)(2,1)S(1)} %get-tuple-element.19) | copy-start | bytes 1572868
  74.7 7.0 %copy-start.33 = (f32[256,16,1,1]{0,1,3,2:T(8,128)S(1)}, f32[256,16,1,1]{0,1,3,2:T(8,128)}, u32[]{:S(2)}) copy-start(f32[256,16,1,1]{0,1,3,2:T(8,128)} %constant.61) | copy-start | bytes 49156
  77.2 17.1 %all-to-all-start.3 = ((f32[32,40,128]{2,1,0:T(8,128)}), f32[32,40,128]{2,1,0:T(8,128)}, u32[]{:S(2)}, u32[]{:S(2)}) async-start(f32[32,40,128]{2,1,0:T(8,128)} %bitcast.183), calls=%async_computation.3 | async-start | bytes 1310720 | tf_op jit(solution)/shard_map/all_to_all | solution.py:40
  81.8 2.1 %copy-start.32 = (f32[256,16,1,1]{0,1,3,2:T(8,128)S(1)}, f32[256,16,1,1]{0,1,3,2:T(8,128)}, u32[]{:S(2)}) copy-start(f32[256,16,1,1]{0,1,3,2:T(8,128)} %constant.60) | copy-start | bytes 49156
  83.9 2.1 %copy-start.30 = (f32[4,2,256,32]{2,3,1,0:T(8,128)S(1)}, f32[4,2,256,32]{2,3,1,0:T(8,128)}, u32[]{:S(2)}) copy-start(f32[4,2,256,32]{2,3,1,0:T(8,128)} %copy-done.29) | copy-start | bytes 786436
  83.9 2.1 %copy-start.31 = (f32[512,16,1,1]{0,1,3,2:T(8,128)S(1)}, f32[512,16,1,1]{0,1,3,2:T(8,128)}, u32[]{:S(2)}) copy-start(f32[512,16,1,1]{0,1,3,2:T(8,128)} %constant.62) | copy-start | bytes 98308
  86.1 4.4 %copy-start.4 = (bf16[4,512,128]{2,1,0:T(8,128)(2,1)S(1)}, bf16[4,512,128]{2,1,0:T(8,128)(2,1)}, u32[]{:S(2)}) copy-start(bf16[4,512,128]{2,1,0:T(8,128)(2,1)} %copy-done.2) | copy-start | bytes 1572868
  86.1 4.3 %copy-start.7 = (bf16[4,2,256,128]{3,2,1,0:T(8,128)(2,1)S(1)}, bf16[4,2,256,128]{3,2,1,0:T(8,128)(2,1)}, u32[]{:S(2)}) copy-start(bf16[4,2,256,128]{3,2,1,0:T(8,128)(2,1)} %copy-done.6) | copy-start | bytes 1572868
  86.1 4.3 %copy-start.26 = (f32[4,2,256,256]{2,3,1,0:T(8,128)S(1)}, f32[4,2,256,256]{2,3,1,0:T(8,128)}, u32[]{:S(2)}) copy-start(f32[4,2,256,256]{2,3,1,0:T(8,128)} %get-tuple-element.25) | copy-start | bytes 6291460
  95.9 5.8 %copy-start.17 = (bf16[4,512,128]{2,1,0:T(8,128)(2,1)S(1)}, bf16[4,512,128]{2,1,0:T(8,128)(2,1)}, u32[]{:S(2)}) copy-start(bf16[4,512,128]{2,1,0:T(8,128)(2,1)} %copy-done.16) | copy-start | bytes 1572868
  96.9 17.8 %all-to-all-start.4 = ((f32[32,40,128]{2,1,0:T(8,128)}), f32[32,40,128]{2,1,0:T(8,128)S(1)}, u32[]{:S(2)}, u32[]{:S(2)}) async-start(f32[32,40,128]{2,1,0:T(8,128)} %pad_add_fusion), calls=%async_computation.4 | async-start | bytes 1310720 | tf_op jit(solution)/shard_map/all_to_all | solution.py:46
  101.7 2.2 %copy-start.10 = (bf16[512,512]{1,0:T(8,128)(2,1)S(1)}, bf16[512,512]{1,0:T(8,128)(2,1)}, u32[]{:S(2)}) copy-start(bf16[512,512]{1,0:T(8,128)(2,1)} %param.11) | copy-start | bytes 1572868
  101.7 2.2 %copy-start.36 = (f32[512]{0:T(512)S(1)}, f32[512]{0:T(512)}, u32[]{:S(2)}) copy-start(f32[512]{0:T(512)} %param.15) | copy-start | bytes 6148
  101.7 2.5 %copy-start.1 = (bf16[4,2,256,256]{2,3,1,0:T(8,128)(2,1)S(1)}, bf16[4,2,256,256]{2,3,1,0:T(8,128)(2,1)}, u32[]{:S(2)}) copy-start(bf16[4,2,256,256]{2,3,1,0:T(8,128)(2,1)} %copy-done) | copy-start | bytes 3145732
  101.7 2.5 %copy-start.8 = (bf16[4,2,256,128]{3,2,1,0:T(8,128)(2,1)S(1)}, bf16[4,2,256,128]{3,2,1,0:T(8,128)(2,1)}, u32[]{:S(2)}) copy-start(bf16[4,2,256,128]{3,2,1,0:T(8,128)(2,1)} %copy-done.6) | copy-start | bytes 1572868
  104.2 13.0 %copy-start.39 = (f32[4,2,1,256]{3,0,1,2:T(4,128)S(1)}, f32[4,2,1,256]{3,0,1,2:T(4,128)}, u32[]{:S(2)}) copy-start(f32[4,2,1,256]{3,0,1,2:T(4,128)} %copy.161) | copy-start | bytes 24580
  105.6 11.6 %copy-start.5 = (bf16[4,512,128]{2,1,0:T(8,128)(2,1)S(1)}, bf16[4,512,128]{2,1,0:T(8,128)(2,1)}, u32[]{:S(2)}) copy-start(bf16[4,512,128]{2,1,0:T(8,128)(2,1)} %copy-done.2) | copy-start | bytes 1572868
  115.3 3.3 %copy-start.34 = (f32[256,16,1,1]{0,1,3,2:T(8,128)S(1)}, f32[256,16,1,1]{0,1,3,2:T(8,128)}, u32[]{:S(2)}) copy-start(f32[256,16,1,1]{0,1,3,2:T(8,128)} %constant.61) | copy-start | bytes 49156
  120.8 2.1 %copy-start.19 = (f32[4,2,256,128]{3,2,1,0:T(8,128)S(1)}, f32[4,2,256,128]{3,2,1,0:T(8,128)}, u32[]{:S(2)}) copy-start(f32[4,2,256,128]{3,2,1,0:T(8,128)} %fusion.85) | copy-start | bytes 3145732
  120.8 2.1 %copy-start.22 = (bf16[4,1,256,128]{3,2,0,1:T(8,128)(2,1)S(1)}, bf16[4,1,256,128]{3,2,0,1:T(8,128)(2,1)}, u32[]{:S(2)}) copy-start(bf16[4,1,256,128]{3,2,0,1:T(8,128)(2,1)} %fusion.51) | copy-start | bytes 786436
  120.8 2.1 %copy-start.23 = (bf16[4,1,256,128]{3,2,0,1:T(8,128)(2,1)S(1)}, bf16[4,1,256,128]{3,2,0,1:T(8,128)(2,1)}, u32[]{:S(2)}) copy-start(bf16[4,1,256,128]{3,2,0,1:T(8,128)(2,1)} %fusion.49) | copy-start | bytes 786436
  122.9 1.3 copy-start.28
  124.2 3.3 %copy-start.15 = (bf16[4,512,128]{2,1,0:T(8,128)(2,1)S(1)}, bf16[4,512,128]{2,1,0:T(8,128)(2,1)}, u32[]{:S(2)}) copy-start(bf16[4,512,128]{2,1,0:T(8,128)(2,1)} %copy-done.14) | copy-start | bytes 1572868
  124.2 3.3 %copy-start.18 = (bf16[4,2,256,256]{2,3,1,0:T(8,128)(2,1)S(1)}, bf16[4,2,256,256]{2,3,1,0:T(8,128)(2,1)}, u32[]{:S(2)}) copy-start(bf16[4,2,256,256]{2,3,1,0:T(8,128)(2,1)} %fusion.14) | copy-start | bytes 3145732
  127.6 1.0 copy-start.13
  127.6 1.0 copy-start.38
  128.1 11.6 %copy-start.11 = (bf16[512,512]{1,0:T(8,128)(2,1)S(1)}, bf16[512,512]{1,0:T(8,128)(2,1)}, u32[]{:S(2)}) copy-start(bf16[512,512]{1,0:T(8,128)(2,1)} %param.11) | copy-start | bytes 1572868
  128.1 11.6 %copy-start.40 = (f32[512]{0:T(512)S(1)}, f32[512]{0:T(512)}, u32[]{:S(2)}) copy-start(f32[512]{0:T(512)} %multiply_multiply_fusion.5) | copy-start | bytes 6148
  128.1 11.6 %copy-start.41 = (f32[512]{0:T(512)S(1)}, f32[512]{0:T(512)}, u32[]{:S(2)}) copy-start(f32[512]{0:T(512)} %multiply_multiply_fusion.4) | copy-start | bytes 6148
  129.5 10.1 %all-to-all-start.5 = ((f32[8,2,512]{2,1,0:T(2,128)}), f32[8,2,512]{2,1,0:T(2,128)S(1)}, u32[]{:S(2)}, u32[]{:S(2)}) async-start(f32[8,2,512]{2,1,0:T(2,128)} %broadcast_in_dim.19), calls=%async_computation.5 | async-start | bytes 65536 | tf_op jit(solution)/shard_map/all_to_all | solution.py:54

commit v3 on v2

--- a/solution.py
+++ b/solution.py
@@ -82,21 +82,10 @@
     return (sketch_feats, sketched, left_part, right_part)
 
 
-def lane_select(rule):
-    lanes = np.arange(RS * RS)
-    return jnp.asarray((rule(lanes)[:, None] == np.arange(RS)[None, :]).astype(np.float32))
-
-
 def sketch_back(feat_grad, sketched, left_part, right_part, sign_pair):
-    by_row = lane_select(lambda f: f // RS)
-    by_col = lane_select(lambda f: f % RS)
-    row_copy = precise_product("...r,fr->...f", sketched, by_row)
-    col_copy = precise_product("...s,fs->...f", sketched, by_col)
-    sketch_grad = precise_product(
-        "...f,fr->...r",
-        jnp.concatenate([feat_grad * col_copy, feat_grad * row_copy], axis=-1),
-        jnp.concatenate([by_row, by_col], axis=0),
-    )
+    grid = feat_grad.reshape(feat_grad.shape[:-1] + (RS, RS))
+    symmetric = grid + jnp.swapaxes(grid, -1, -2)
+    sketch_grad = jnp.sum(symmetric * sketched[..., None, :], axis=-1)
     both_grad = jnp.concatenate([sketch_grad * right_part, sketch_grad * left_part], axis=-1) * (
         RS * DH
     ) ** (-0.5)

time: 142 us -> 143 us (level)
  matrix products: 35.9 us -> 25.2 us
  other arithmetic: 18.5 us -> 24.9 us
  local copies, waits for them, and re-layouts: 11.2 us -> 15 us
  waiting for transfers between devices: 38.8 us -> 40.8 us
    dot_general x10 -> x4, matrix products: 17.4 us -> 4.39 us  [precise_product(): jnp.einsum(spec, lhs.astype(jnp.float32), rhs.astype(jnp.float32), precis...]
    reduce_sum x0 -> x2, other arithmetic: none -> 4.62 us  [sketch_back(): sketch_grad = jnp.sum(symmetric * sketched[..., None, :], axis=-1)]
    all_to_all x2, waiting for transfers between devices: 14.2 us -> 17.1 us  [carried_in(): mine = lax.all_to_all(stacked, axis, 0, 0, tiled=True)]
    dot_general x14, matrix products: 18.5 us -> 20.8 us  [product_of(): return jnp.einsum(spec, lhs, rhs, preferred_element_type=jnp.float32)]
    unnamed x84 -> x92, local copies, waits for them, and re-layouts: 1.04 us -> 2.54 us
  transfers between devices with their start and end apart: 6 -> 6, of which waited for: 6 -> 6; matrix products, arithmetic and copies ran while one was open for 18% -> 17% of each run, Pallas kernels for 0% -> 0%
where the time goes in v3:
time: 143 us; the launch traced here: 142 us
  waiting for transfers between devices  40.8 us (29%)
  starting transfers between devices  34.2 us (24%)
  matrix products  25.2 us (18%)
  other arithmetic  24.9 us (17%)
  local copies, waits for them, and re-layouts  15 us (10%)
  between operations  1.48 us (1%)
    dot_general x14, matrix products, product_of(): return jnp.einsum(spec, lhs, rhs, preferred_element_type=jnp.float32)  20.8 us
    all_to_all x2, waiting for transfers between devices, carried_in(): mine = lax.all_to_all(stacked, axis, 0, 0, tiled=True)  17.1 us
    all_to_all x2, waiting for transfers between devices, carried_in(): lax.all_to_all(shifted, axis, 0, 0, tiled=True)  15.6 us
    all_to_all x2, starting transfers between devices, carried_in(): mine = lax.all_to_all(stacked, axis, 0, 0, tiled=True)  13.1 us
    all_to_all x2, starting transfers between devices, head_sum(): gathered = lax.all_to_all(spread, axis, 0, 0, tiled=True)  12.3 us
    all_to_all x2, starting transfers between devices, carried_in(): lax.all_to_all(shifted, axis, 0, 0, tiled=True)  8.8 us
    all_to_all x2, waiting for transfers between devices, head_sum(): gathered = lax.all_to_all(spread, axis, 0, 0, tiled=True)  8.13 us
    reduce_sum x2, other arithmetic, sketch_back(): sketch_grad = jnp.sum(symmetric * sketched[..., None, :], axis=-1)  4.62 us
  transfers between devices with their start and end apart: 6, of which 6 were waited for; matrix products, arithmetic and copies ran while one was open for 17% of the time, Pallas kernels for 0%

profile of v3, /device:TPU:1, one launch (start us, length us, event | category | flops | bytes accessed | tf_op | source)
XLA Modules:
  0.0 141.7 jit_solution(13198183676659065070)
XLA Ops:
  0.6 1.3 fusion.12
  1.9 1.3 fusion.21
  3.2 0.6 broadcast_in_dim.17
  3.9 9.0 %all-to-all-start = ((f32[8,2,512]{2,1,0:T(2,128)}), f32[8,2,512]{2,1,0:T(2,128)S(1)}, u32[]{:S(2)}, u32[]{:S(2)}) async-start(f32[8,2,512]{2,1,0:T(2,128)} %broadcast_in_dim.17), calls=%async_computation | async-start | bytes 65536 | tf_op jit(solution)/shard_map/all_to_all | solution.py:54
  12.9 0.7 fusion.56
  13.6 1.2 reshape.163
  14.9 1.1 copy_bitcast_fusion
  16.1 3.7 %all-to-all-done = f32[8,2,512]{2,1,0:T(2,128)S(1)} async-done(((f32[8,2,512]{2,1,0:T(2,128)}), f32[8,2,512]{2,1,0:T(2,128)S(1)}, u32[]{:S(2)}, u32[]{:S(2)}) %all-to-all-start) | async-done | bytes 32800 | tf_op jit(solution)/shard_map/all_to_all | solution.py:54
  20.7 0.3 fusion.67
  20.9 0.3 fusion.66
  21.5 0.7 copy-done.20
  22.2 0.6 copy-done.26
  22.8 0.5 convert_reduce_fusion
  23.5 1.4 %fusion.72 = (f32[4,256,128]{2,1,0:T(8,128)S(1)}, f32[4,2,256,128]{3,2,1,0:T(8,128)}) fusion(bf16[4,2,256,256]{2,3,1,0:T(8,128)(2,1)S(1)} %bitcast.157, bf16[4,2,256,128]{3,2,1,0:T(8,128)(2,1)S(1)} %bitcast.165), kind=kOutput, calls=%fused_computation.148 | convolution fusion | flops 134348800 | bytes 3145728 | tf_op jit(solution)/shard_map/...jr,...jd->...rd/dot_general | solution.py:60
  24.9 1.0 maximum_maximum_fusion
  25.9 9.2 %all-to-all-start.1 = ((f32[32,40,128]{2,1,0:T(8,128)}), f32[32,40,128]{2,1,0:T(8,128)}, u32[]{:S(2)}, u32[]{:S(2)}) async-start(f32[32,40,128]{2,1,0:T(8,128)} %bitcast.17), calls=%async_computation.1 | async-start | bytes 1310720 | tf_op jit(solution)/shard_map/all_to_all | solution.py:40
  35.1 0.6 multiply_multiply_fusion.5
  36.0 12.1 %all-to-all-done.1 = f32[32,40,128]{2,1,0:T(8,128)} async-done(((f32[32,40,128]{2,1,0:T(8,128)}), f32[32,40,128]{2,1,0:T(8,128)}, u32[]{:S(2)}, u32[]{:S(2)}) %all-to-all-start.1) | async-done | bytes 655392 | tf_op jit(solution)/shard_map/all_to_all | solution.py:40
  48.1 1.1 slice.126
  49.7 0.9 pad_add_fusion.4
  50.6 4.4 %all-to-all-start.2 = ((f32[32,40,128]{2,1,0:T(8,128)}), f32[32,40,128]{2,1,0:T(8,128)}, u32[]{:S(2)}, u32[]{:S(2)}) async-start(f32[32,40,128]{2,1,0:T(8,128)} %pad_add_fusion.4), calls=%async_computation.2 | async-start | bytes 1310720 | tf_op jit(solution)/shard_map/all_to_all | solution.py:46
  55.0 0.6 multiply_multiply_fusion.4
  55.7 3.7 %convert_reduce_fusion.2 = (f32[4,2,256]{2,1,0:T(2,128)}, bf16[4,2,256,256]{2,3,1,0:T(8,128)(2,1)S(1)}, f32[4,2,256,256]{2,3,1,0:T(8,128)}) fusion(pred[256,256]{0,1:T(8,128)(4,1)S(1)} %iota_compare_fusion, bf16[4,2,256,128]{3,2,1,0:T(8,128)(2,1)} %bitcast.170, bf16[4,2,256,128]{3,2,1,0:T(8,128)(2,1)} %bitcast.173), kind=kOutput, calls=%fused_computation.18 | convolution fusion | flops 137885696 | bytes 4268032 | tf_op jit(solution)/shard_map/...id,...jd->...ij/dot_general | solution.py:60
  59.4 1.5 %fusion.74 = f32[4,2,256,128]{3,2,1,0:T(8,128)} fusion(bf16[4,2,256,256]{2,3,1,0:T(8,128)(2,1)S(1)} %get-tuple-element.9, bf16[4,2,256,128]{3,2,1,0:T(8,128)(2,1)S(1)} %bitcast.166), kind=kOutput, calls=%fused_computation.150 | convolution fusion | flops 134217728 | bytes 2621440 | tf_op jit(solution)/shard_map/...ij,...jd->...id/dot_general | solution.py:60
  61.0 6.8 %all-to-all-done.2 = f32[32,40,128]{2,1,0:T(8,128)} async-done(((f32[32,40,128]{2,1,0:T(8,128)}), f32[32,40,128]{2,1,0:T(8,128)}, u32[]{:S(2)}, u32[]{:S(2)}) %all-to-all-start.2) | async-done | bytes 655392 | tf_op jit(solution)/shard_map/all_to_all | solution.py:46
  67.8 0.9 slice.134
  68.6 1.1 fusion.40
  69.7 1.4 fusion.42
  71.1 0.6 pad_maximum_fusion.2
  71.7 0.5 fusion.54
  72.2 1.6 %multiply_reduce_fusion = (f32[4,2,256]{2,1,0:T(2,128)S(1)}, f32[4,2,256,128]{3,2,1,0:T(8,128)}) fusion(f32[4,2,256,128]{3,2,1,0:T(8,128)S(1)} %bitcast.175, f32[4,2,256,128]{3,2,1,0:T(8,128)S(1)} %copy-done.17, bf16[4,2,256,256]{2,3,1,0:T(8,128)(2,1)S(1)} %bitcast.154, bf16[4,1,256,128]{3,2,0,1:T(8,128)(2,1)S(1)} %fusion.42, ...), kind=kOutput, calls=%fused_computation.57 | convolution fusion | flops 135264256 | bytes 4726784 | tf_op jit(solution)/shard_map/...ir,...rd->...id/dot_general | solution.py:60
  73.8 0.6 multiply_divide_fusion
  74.4 0.9 fusion.52
  75.3 0.6 fusion.68
  75.9 0.6 copy.153
  76.5 1.3 reshape.173
  77.8 2.5 %divide_convert_fusion = (bf16[4,2,256,128]{3,2,1,0:T(8,128)(2,1)S(1)}, bf16[4,2,256,128]{3,2,1,0:T(8,128)(2,1)}) fusion(f32[4,2,256]{2,1,0:T(2,128)} %get-tuple-element.7, f32[4,2,256,128]{3,2,1,0:T(8,128)} %get-tuple-element.29, bf16[512,512]{1,0:T(8,128)(2,1)} %param.10), kind=kLoop, calls=%fused_computation.58 | loop fusion | flops 1310720 | bytes 2629632 | tf_op jit(solution)/shard_map/convert_element_type | solution.py:156
  80.3 1.5 %fusion.73 = (f32[4,256,128]{2,1,0:T(8,128)S(1)}, f32[4,2,256,128]{3,2,1,0:T(8,128)}) fusion(bf16[4,2,256,256]{2,3,1,0:T(8,128)(2,1)S(1)} %bitcast.156, bf16[4,2,256,128]{3,2,1,0:T(8,128)(2,1)S(1)} %get-tuple-element.19), kind=kOutput, calls=%fused_computation.149 | convolution fusion | flops 134348800 | bytes 3145728 | tf_op jit(solution)/shard_map/...ir,...id->...rd/dot_general | solution.py:60
  81.8 1.0 maximum_maximum_fusion.1
  82.8 3.9 %all-to-all-start.3 = ((f32[32,40,128]{2,1,0:T(8,128)}), f32[32,40,128]{2,1,0:T(8,128)S(1)}, u32[]{:S(2)}, u32[]{:S(2)}) async-start(f32[32,40,128]{2,1,0:T(8,128)} %bitcast.38), calls=%async_computation.3 | async-start | bytes 1310720 | tf_op jit(solution)/shard_map/all_to_all | solution.py:40
  86.7 1.5 %multiply_add_fusion = f32[4,2,256,256]{2,3,1,0:T(8,128)S(1)} fusion(bf16[4,2,256,128]{3,2,1,0:T(8,128)(2,1)} %copy-done.4, f32[4,2,256]{2,1,0:T(2,128)S(1)} %copy-done.30, f32[4,2,256]{2,1,0:T(2,128)S(1)} %get-tuple-element.6, bf16[4,1,256,128]{3,2,0,1:T(8,128)(2,1)S(1)} %fusion.42, bf16[4,1,256,128]{3,2,0,1:T(8,128)(2,1)S(1)} %copy-done.19), kind=kOutput, calls=%fused_computation.17 | convolution fusion | flops 135528448 | bytes 3162112 | tf_op jit(solution)/shard_map/...id,...rd->...ir/dot_general | solution.py:60
  88.3 2.3 %fusion.10 = f32[4,2,256,16]{2,3,1,0:T(8,128)S(1)} fusion(f32[4,2,256,16,16]{2,4,3,1,0:T(8,128)S(1)} %bitcast.164, f32[4,2,256,16]{2,3,1,0:T(8,128)S(1)} %multiply_multiply_fusion.3), kind=kLoop, calls=%fused_computation.16 | loop fusion | flops 1540096 | bytes 2359296 | tf_op jit(solution)/shard_map/reduce_sum | solution.py:88
  90.6 2.0 %fusion.44 = f32[4,2,256,128]{3,2,1,0:T(8,128)} fusion(f32[4,2,256,16]{2,3,1,0:T(8,128)S(1)} %get-tuple-element.13, f32[4,2,256,16]{2,3,1,0:T(8,128)S(1)} %get-tuple-element.12, bf16[128,16]{0,1:T(8,128)(2,1)S(1)} %get-tuple-element.16, bf16[128,16]{0,1:T(8,128)(2,1)S(1)} %get-tuple-element.15), kind=kOutput, calls=%fused_computation.97 | convolution fusion | flops 100810752 | bytes 1318912 | tf_op jit(solution)/shard_map/...r,dr->...d/dot_general | solution.py:64
  92.6 1.8 %fusion.6 = bf16[4,2,256,256]{2,3,1,0:T(8,128)(2,1)} fusion(f32[4,2,256,256]{2,3,1,0:T(8,128)S(1)} %copy-done.25, bf16[4,2,256,128]{3,2,1,0:T(8,128)(2,1)S(1)} %copy-done.5, bf16[4,2,256,128]{3,2,1,0:T(8,128)(2,1)S(1)} %bitcast.167, f32[4,2,256]{2,1,0:T(2,128)S(1)} %get-tuple-element.6, pred[256,256]{0,1:T(8,128)(4,1)S(1)} %copy-done.29), kind=kOutput, calls=%fused_computation.10 | convolution fusion | flops 138936320 | bytes 4268032 | tf_op jit(solution)/shard_map/...id,...jd->...ij/dot_general | solution.py:60
  94.4 5.0 %all-to-all-done.3 = f32[32,40,128]{2,1,0:T(8,128)S(1)} async-done(((f32[32,40,128]{2,1,0:T(8,128)}), f32[32,40,128]{2,1,0:T(8,128)S(1)}, u32[]{:S(2)}, u32[]{:S(2)}) %all-to-all-start.3) | async-done | bytes 655392 | tf_op jit(solution)/shard_map/all_to_all | solution.py:40
  99.9 0.9 pad_add_fusion
  100.9 4.4 %all-to-all-start.4 = ((f32[32,40,128]{2,1,0:T(8,128)}), f32[32,40,128]{2,1,0:T(8,128)}, u32[]{:S(2)}, u32[]{:S(2)}) async-start(f32[32,40,128]{2,1,0:T(8,128)} %pad_add_fusion), calls=%async_computation.4 | async-start | bytes 1310720 | tf_op jit(solution)/shard_map/all_to_all | solution.py:46
  105.3 2.3 %convolution_add_fusion.3 = f32[4,2,256,128]{3,2,1,0:T(8,128)S(1)} fusion(f32[4,2,256,128]{3,2,1,0:T(8,128)} %fusion.44, bf16[4,2,256,256]{2,3,1,0:T(8,128)(2,1)} %fusion.6, bf16[4,2,256,128]{3,2,1,0:T(8,128)(2,1)} %bitcast.174), kind=kOutput, calls=%fused_computation.32 | convolution fusion | flops 134479872 | bytes 3670016 | tf_op jit(solution)/shard_map/...ij,...jd->...id/dot_general | solution.py:60
  107.9 1.4 fusion.75
  109.3 8.8 %all-to-all-done.4 = f32[32,40,128]{2,1,0:T(8,128)} async-done(((f32[32,40,128]{2,1,0:T(8,128)}), f32[32,40,128]{2,1,0:T(8,128)}, u32[]{:S(2)}, u32[]{:S(2)}) %all-to-all-start.4) | async-done | bytes 655392 | tf_op jit(solution)/shard_map/all_to_all | solution.py:46
  118.0 0.7 slice.144
  118.8 1.1 fusion.41
  119.8 1.3 fusion.43
  121.2 2.5 %fusion.11 = bf16[4,2,256,128]{3,2,1,0:T(8,128)(2,1)} fusion(f32[4,2,256,128]{3,2,1,0:T(8,128)} %fusion.75, bf16[4,2,256,256]{2,3,1,0:T(8,128)(2,1)S(1)} %bitcast.158, bf16[4,1,256,128]{3,2,0,1:T(8,128)(2,1)S(1)} %fusion.41, bf16[4,1,256,128]{3,2,0,1:T(8,128)(2,1)S(1)} %fusion.43), kind=kOutput, calls=%fused_computation.34 | convolution fusion | flops 135004160 | bytes 3145728 | tf_op jit(solution)/shard_map/...jr,...rd->...jd/dot_general | solution.py:60
  123.7 0.6 convolution_add_fusion
  124.7 2.3 %fusion.8 = f32[4,2,256,16]{2,3,1,0:T(8,128)S(1)} fusion(f32[4,2,256,16,16]{2,4,3,1,0:T(8,128)S(1)} %bitcast.163, f32[4,2,256,16]{2,3,1,0:T(8,128)S(1)} %copy-done.27), kind=kLoop, calls=%fused_computation.13 | loop fusion | flops 1540096 | bytes 2359296 | tf_op jit(solution)/shard_map/reduce_sum | solution.py:88
  127.0 1.0 fusion.47
  128.1 0.5 convolution_add_fusion.2
  128.6 0.5 copy-done.11
  129.3 0.6 broadcast_in_dim.19
  129.9 3.3 %all-to-all-start.5 = ((f32[8,2,512]{2,1,0:T(2,128)}), f32[8,2,512]{2,1,0:T(2,128)S(1)}, u32[]{:S(2)}, u32[]{:S(2)}) async-start(f32[8,2,512]{2,1,0:T(2,128)} %broadcast_in_dim.19), calls=%async_computation.5 | async-start | bytes 65536 | tf_op jit(solution)/shard_map/all_to_all | solution.py:54
  133.3 2.3 %copy_bitcast_fusion.1 = (bf16[512,512]{1,0:T(8,128)(2,1)}, bf16[512,512]{1,0:T(8,128)(2,1)}) fusion(bf16[4,64,8,128]{3,2,1,0:T(8,128)(2,1)} %bitcast.180, bf16[4,64,8,128]{3,2,1,0:T(8,128)(2,1)} %bitcast.176), kind=kLoop, calls=%fused_computation.76 | loop fusion | bytes 2097152 | tf_op jit(solution)/shard_map/convert_element_type | solution.py:267
  135.6 4.4 %all-to-all-done.5 = f32[8,2,512]{2,1,0:T(2,128)S(1)} async-done(((f32[8,2,512]{2,1,0:T(2,128)}), f32[8,2,512]{2,1,0:T(2,128)S(1)}, u32[]{:S(2)}, u32[]{:S(2)}) %all-to-all-start.5) | async-done | bytes 32800 | tf_op jit(solution)/shard_map/all_to_all | solution.py:54
  140.1 1.6 %fusion.18 = (bf16[512,512]{1,0:T(8,128)(2,1)}, bf16[512,512]{1,0:T(8,128)(2,1)}) fusion(bf16[512,512]{1,0:T(8,128)(2,1)S(1)} %copy-done.9, f32[4,64,8,128]{3,2,1,0:T(8,128)S(1)} %bitcast.160, f32[512]{0:T(512)S(1)} %bitcast.193, f32[512]{0:T(512)S(1)} %copy-done.44, f32[512]{0:T(512)S(1)} %copy-done.37, f32[512]{0:T(512)S(1)} %bitcast.189, ...), kind=kLoop, calls=%fused_computation.41 | loop fusion | flops 4194304 | bytes 4210688 | tf_op jit(solution)/shard_map/convert_element_type | solution.py:190
  (136 shorter events, 3.6 us)
Async XLA Ops:
  0.6 14.2 %copy-start.24 = (bf16[512,512]{1,0:T(8,128)(2,1)S(1)}, bf16[512,512]{1,0:T(8,128)(2,1)}, u32[]{:S(2)}) copy-start(bf16[512,512]{1,0:T(8,128)(2,1)} %param.10) | copy-start | bytes 1572868
  1.9 17.9 %copy-start.7 = (bf16[512,512]{1,0:T(8,128)(2,1)S(1)}, bf16[512,512]{1,0:T(8,128)(2,1)}, u32[]{:S(2)}) copy-start(bf16[512,512]{1,0:T(8,128)(2,1)} %param.7) | copy-start | bytes 1572868
  1.9 17.9 %copy-start.36 = (f32[512]{0:T(512)S(1)}, f32[512]{0:T(512)}, u32[]{:S(2)}) copy-start(f32[512]{0:T(512)} %param.11) | copy-start | bytes 6148
  3.9 15.9 %all-to-all-start = ((f32[8,2,512]{2,1,0:T(2,128)}), f32[8,2,512]{2,1,0:T(2,128)S(1)}, u32[]{:S(2)}, u32[]{:S(2)}) async-start(f32[8,2,512]{2,1,0:T(2,128)} %broadcast_in_dim.17), calls=%async_computation | async-start | bytes 65536 | tf_op jit(solution)/shard_map/all_to_all | solution.py:54
  14.8 8.6 %copy-start = (bf16[4,512,128]{2,1,0:T(8,128)(2,1)}, bf16[4,512,128]{2,1,0:T(8,128)(2,1)S(1)}, u32[]{:S(2)}) copy-start(bf16[4,512,128]{2,1,0:T(8,128)(2,1)S(1)} %copy.81) | copy-start | bytes 1572868
  14.8 5.4 %copy-start.10 = (bf16[512,512]{1,0:T(8,128)(2,1)S(1)}, bf16[512,512]{1,0:T(8,128)(2,1)}, u32[]{:S(2)}) copy-start(bf16[512,512]{1,0:T(8,128)(2,1)} %param.8) | copy-start | bytes 1572868
  14.9 5.4 %copy-start.38 = (f32[512]{0:T(512)S(1)}, f32[512]{0:T(512)}, u32[]{:S(2)}) copy-start(f32[512]{0:T(512)} %param.12) | copy-start | bytes 6148
  16.0 8.9 %copy-start.40 = (f32[320]{0:T(512)}, f32[320]{0:T(512)S(1)}, u32[]{:S(2)}) copy-start(f32[320]{0:T(512)S(1)} %pad.77.clone) | copy-start | bytes 3844
  16.0 39.7 %copy-start.28 = (pred[256,256]{0,1:T(8,128)(4,1)}, pred[256,256]{0,1:T(8,128)(4,1)S(1)}, u32[]{:S(2)}) copy-start(pred[256,256]{0,1:T(8,128)(4,1)S(1)} %iota_compare_fusion) | copy-start | bytes 196612
  19.8 15.3 %copy-start.34 = (f32[1,512]{1,0:T(1,128)}, f32[1,512]{1,0:T(1,128)S(1)}, u32[]{:S(2)}) copy-start(f32[1,512]{1,0:T(1,128)S(1)} %get-tuple-element.24) | copy-start | bytes 6148
  19.8 35.2 %copy-start.32 = (f32[1,512]{1,0:T(1,128)}, f32[1,512]{1,0:T(1,128)S(1)}, u32[]{:S(2)}) copy-start(f32[1,512]{1,0:T(1,128)S(1)} %get-tuple-element.23) | copy-start | bytes 6148
  20.2 1.0 copy-start.12
  20.7 0.8 copy-start.14
  20.9 14.8 %copy-start.22 = (f32[4,2,256,32]{2,3,1,0:T(8,128)}, f32[4,2,256,32]{2,3,1,0:T(8,128)S(1)}, u32[]{:S(2)}) copy-start(f32[4,2,256,32]{2,3,1,0:T(8,128)S(1)} %fusion.67) | copy-start | bytes 786436
  21.5 0.7 copy-start.20
  22.2 0.7 copy-start.26
  25.9 22.2 %all-to-all-start.1 = ((f32[32,40,128]{2,1,0:T(8,128)}), f32[32,40,128]{2,1,0:T(8,128)}, u32[]{:S(2)}, u32[]{:S(2)}) async-start(f32[32,40,128]{2,1,0:T(8,128)} %bitcast.17), calls=%async_computation.1 | async-start | bytes 1310720 | tf_op jit(solution)/shard_map/all_to_all | solution.py:40
  50.6 17.1 %all-to-all-start.2 = ((f32[32,40,128]{2,1,0:T(8,128)}), f32[32,40,128]{2,1,0:T(8,128)}, u32[]{:S(2)}, u32[]{:S(2)}) async-start(f32[32,40,128]{2,1,0:T(8,128)} %pad_add_fusion.4), calls=%async_computation.2 | async-start | bytes 1310720 | tf_op jit(solution)/shard_map/all_to_all | solution.py:46
  55.7 3.7 %copy-start.1 = (bf16[4,512,128]{2,1,0:T(8,128)(2,1)S(1)}, bf16[4,512,128]{2,1,0:T(8,128)(2,1)}, u32[]{:S(2)}) copy-start(bf16[4,512,128]{2,1,0:T(8,128)(2,1)} %copy-done) | copy-start | bytes 1572868
  67.7 4.5 %copy-start.16 = (f32[512,4,128]{2,0,1:T(8,128)S(1)}, f32[512,4,128]{2,0,1:T(8,128)}, u32[]{:S(2)}) copy-start(f32[512,4,128]{2,0,1:T(8,128)} %copy_bitcast_fusion) | copy-start | bytes 3145732
  67.8 4.5 %copy-start.17 = (f32[4,2,256,128]{3,2,1,0:T(8,128)S(1)}, f32[4,2,256,128]{3,2,1,0:T(8,128)}, u32[]{:S(2)}) copy-start(f32[4,2,256,128]{3,2,1,0:T(8,128)} %fusion.74) | copy-start | bytes 3145732
  69.7 4.1 %copy-start.18 = (bf16[4,1,256,128]{3,2,0,1:T(8,128)(2,1)}, bf16[4,1,256,128]{3,2,0,1:T(8,128)(2,1)S(1)}, u32[]{:S(2)}) copy-start(bf16[4,1,256,128]{3,2,0,1:T(8,128)(2,1)S(1)} %fusion.40) | copy-start | bytes 786436
  72.2 1.6 %copy-start.31 = (f32[4,2,256]{2,1,0:T(2,128)S(1)}, f32[4,2,256]{2,1,0:T(2,128)}, u32[]{:S(2)}) copy-start(f32[4,2,256]{2,1,0:T(2,128)} %get-tuple-element.8) | copy-start | bytes 24580
  80.3 2.4 %copy-start.4 = (bf16[4,2,256,128]{3,2,1,0:T(8,128)(2,1)}, bf16[4,2,256,128]{3,2,1,0:T(8,128)(2,1)S(1)}, u32[]{:S(2)}) copy-start(bf16[4,2,256,128]{3,2,1,0:T(8,128)(2,1)S(1)} %get-tuple-element.19) | copy-start | bytes 1572868
  80.3 1.5 %copy-start.41 = (f32[320]{0:T(512)S(1)}, f32[320]{0:T(512)}, u32[]{:S(2)}) copy-start(f32[320]{0:T(512)} %copy-done.40) | copy-start | bytes 3844
  80.3 1.5 %copy-start.43 = (f32[4,2,128]{2,1,0:T(2,128)S(1)}, f32[4,2,128]{2,1,0:T(2,128)}, u32[]{:S(2)}) copy-start(f32[4,2,128]{2,1,0:T(2,128)} %reshape.173) | copy-start | bytes 12292
  81.8 4.9 %copy-start.19 = (bf16[4,1,256,128]{3,2,0,1:T(8,128)(2,1)S(1)}, bf16[4,1,256,128]{3,2,0,1:T(8,128)(2,1)}, u32[]{:S(2)}) copy-start(bf16[4,1,256,128]{3,2,0,1:T(8,128)(2,1)} %copy-done.18) | copy-start | bytes 786436
  81.8 4.9 %copy-start.30 = (f32[4,2,256]{2,1,0:T(2,128)S(1)}, f32[4,2,256]{2,1,0:T(2,128)}, u32[]{:S(2)}) copy-start(f32[4,2,256]{2,1,0:T(2,128)} %get-tuple-element.17) | copy-start | bytes 24580
  82.8 16.6 %all-to-all-start.3 = ((f32[32,40,128]{2,1,0:T(8,128)}), f32[32,40,128]{2,1,0:T(8,128)S(1)}, u32[]{:S(2)}, u32[]{:S(2)}) async-start(f32[32,40,128]{2,1,0:T(8,128)} %bitcast.38), calls=%async_computation.3 | async-start | bytes 1310720 | tf_op jit(solution)/shard_map/all_to_all | solution.py:40
  86.7 3.9 %copy-start.23 = (f32[4,2,256,32]{2,3,1,0:T(8,128)S(1)}, f32[4,2,256,32]{2,3,1,0:T(8,128)}, u32[]{:S(2)}) copy-start(f32[4,2,256,32]{2,3,1,0:T(8,128)} %copy-done.22) | copy-start | bytes 786436
  88.2 4.4 %copy-start.2 = (bf16[4,512,128]{2,1,0:T(8,128)(2,1)S(1)}, bf16[4,512,128]{2,1,0:T(8,128)(2,1)}, u32[]{:S(2)}) copy-start(bf16[4,512,128]{2,1,0:T(8,128)(2,1)} %copy-done) | copy-start | bytes 1572868
  88.2 4.4 %copy-start.5 = (bf16[4,2,256,128]{3,2,1,0:T(8,128)(2,1)S(1)}, bf16[4,2,256,128]{3,2,1,0:T(8,128)(2,1)}, u32[]{:S(2)}) copy-start(bf16[4,2,256,128]{3,2,1,0:T(8,128)(2,1)} %copy-done.4) | copy-start | bytes 1572868
  88.2 4.4 %copy-start.25 = (f32[4,2,256,256]{2,3,1,0:T(8,128)S(1)}, f32[4,2,256,256]{2,3,1,0:T(8,128)}, u32[]{:S(2)}) copy-start(f32[4,2,256,256]{2,3,1,0:T(8,128)} %get-tuple-element.25) | copy-start | bytes 6291460
  88.2 4.4 %copy-start.29 = (pred[256,256]{0,1:T(8,128)(4,1)S(1)}, pred[256,256]{0,1:T(8,128)(4,1)}, u32[]{:S(2)}) copy-start(pred[256,256]{0,1:T(8,128)(4,1)} %copy-done.28) | copy-start | bytes 196612
  100.9 17.2 %all-to-all-start.4 = ((f32[32,40,128]{2,1,0:T(8,128)}), f32[32,40,128]{2,1,0:T(8,128)}, u32[]{:S(2)}, u32[]{:S(2)}) async-start(f32[32,40,128]{2,1,0:T(8,128)} %pad_add_fusion), calls=%async_computation.4 | async-start | bytes 1310720 | tf_op jit(solution)/shard_map/all_to_all | solution.py:46
  105.3 2.3 %copy-start.8 = (bf16[512,512]{1,0:T(8,128)(2,1)S(1)}, bf16[512,512]{1,0:T(8,128)(2,1)}, u32[]{:S(2)}) copy-start(bf16[512,512]{1,0:T(8,128)(2,1)} %param.7) | copy-start | bytes 1572868
  105.3 2.3 %copy-start.37 = (f32[512]{0:T(512)S(1)}, f32[512]{0:T(512)}, u32[]{:S(2)}) copy-start(f32[512]{0:T(512)} %param.11) | copy-start | bytes 6148
  105.3 2.5 %copy-start.6 = (bf16[4,2,256,128]{3,2,1,0:T(8,128)(2,1)S(1)}, bf16[4,2,256,128]{3,2,1,0:T(8,128)(2,1)}, u32[]{:S(2)}) copy-start(bf16[4,2,256,128]{3,2,1,0:T(8,128)(2,1)} %copy-done.4) | copy-start | bytes 1572868
  107.9 13.3 %copy-start.42 = (f32[4,2,1,256]{3,0,1,2:T(4,128)S(1)}, f32[4,2,1,256]{3,0,1,2:T(4,128)}, u32[]{:S(2)}) copy-start(f32[4,2,1,256]{3,0,1,2:T(4,128)} %copy.153) | copy-start | bytes 24580
  119.8 3.9 %copy-start.3 = (bf16[4,512,128]{2,1,0:T(8,128)(2,1)S(1)}, bf16[4,512,128]{2,1,0:T(8,128)(2,1)}, u32[]{:S(2)}) copy-start(bf16[4,512,128]{2,1,0:T(8,128)(2,1)} %copy-done) | copy-start | bytes 1572868
  123.7 0.9 copy-start.27
  123.7 3.2 %copy-start.21 = (f32[4,2,256,32]{2,3,1,0:T(8,128)S(1)}, f32[4,2,256,32]{2,3,1,0:T(8,128)}, u32[]{:S(2)}) copy-start(f32[4,2,256,32]{2,3,1,0:T(8,128)} %copy-done.20) | copy-start | bytes 786436
  124.7 3.4 %copy-start.13 = (bf16[4,512,128]{2,1,0:T(8,128)(2,1)S(1)}, bf16[4,512,128]{2,1,0:T(8,128)(2,1)}, u32[]{:S(2)}) copy-start(bf16[4,512,128]{2,1,0:T(8,128)(2,1)} %copy-done.12) | copy-start | bytes 1572868
  124.7 3.4 %copy-start.15 = (bf16[4,2,256,256]{2,3,1,0:T(8,128)(2,1)S(1)}, bf16[4,2,256,256]{2,3,1,0:T(8,128)(2,1)}, u32[]{:S(2)}) copy-start(bf16[4,2,256,256]{2,3,1,0:T(8,128)(2,1)} %fusion.6) | copy-start | bytes 3145732
  128.0 1.0 copy-start.11
  128.0 1.0 copy-start.39
  128.5 11.5 %copy-start.9 = (bf16[512,512]{1,0:T(8,128)(2,1)S(1)}, bf16[512,512]{1,0:T(8,128)(2,1)}, u32[]{:S(2)}) copy-start(bf16[512,512]{1,0:T(8,128)(2,1)} %param.7) | copy-start | bytes 1572868
  128.5 11.5 %copy-start.33 = (f32[1,512]{1,0:T(1,128)S(1)}, f32[1,512]{1,0:T(1,128)}, u32[]{:S(2)}) copy-start(f32[1,512]{1,0:T(1,128)} %copy-done.32) | copy-start | bytes 6148
  128.6 11.5 %copy-start.35 = (f32[1,512]{1,0:T(1,128)S(1)}, f32[1,512]{1,0:T(1,128)}, u32[]{:S(2)}) copy-start(f32[1,512]{1,0:T(1,128)} %copy-done.34) | copy-start | bytes 6148
  128.6 11.5 %copy-start.44 = (f32[512]{0:T(512)S(1)}, f32[512]{0:T(512)}, u32[]{:S(2)}) copy-start(f32[512]{0:T(512)} %multiply_multiply_fusion.5) | copy-start | bytes 6148
  128.6 11.5 %copy-start.45 = (f32[512]{0:T(512)S(1)}, f32[512]{0:T(512)}, u32[]{:S(2)}) copy-start(f32[512]{0:T(512)} %multiply_multiply_fusion.4) | copy-start | bytes 6148
  129.9 10.1 %all-to-all-start.5 = ((f32[8,2,512]{2,1,0:T(2,128)}), f32[8,2,512]{2,1,0:T(2,128)S(1)}, u32[]{:S(2)}, u32[]{:S(2)}) async-start(f32[8,2,512]{2,1,0:T(2,128)} %broadcast_in_dim.19), calls=%async_computation.5 | async-start | bytes 65536 | tf_op jit(solution)/shard_map/all_to_all | solution.py:54

commit v4 on v1

--- a/solution.py
+++ b/solution.py
@@ -11,6 +11,15 @@
 
 EPSILON = 1e-06
 HIGHEST_PREC = lax.Precision.HIGHEST
+
+
+def shift_rows(rows, step, reverse):
+    widths = [(0, 0)] * rows.ndim
+    if reverse:
+        widths[0] = (0, step)
+        return jnp.pad(rows[step:], widths)
+    widths[0] = (step, 0)
+    return jnp.pad(rows[:-step], widths)
 
 
 def carried_in(state, totals, axis, reverse):
@@ -28,12 +37,11 @@
         axis=1,
     ).reshape(count, room, lanes)
     mine = lax.all_to_all(stacked, axis, 0, 0, tiled=True)
-    dest = lax.broadcasted_iota(jnp.int32, (count, count), 0)
-    source = lax.broadcasted_iota(jnp.int32, (count, count), 1)
-    taken = (source > dest) if reverse else (source < dest)
-    shifted = jnp.einsum(
-        "ij,jrc->irc", taken.astype(jnp.float32), mine, precision=HIGHEST_PREC
-    )
+    shifted = shift_rows(mine, 1, reverse)
+    step = 1
+    while step < count:
+        shifted = shifted + shift_rows(shifted, step, reverse)
+        step *= 2
     back = lax.all_to_all(shifted, axis, 0, 0, tiled=True).reshape(heads_here, padded, lanes)
     return (back[:, :rows], back[:, rows : rows + total_rows].reshape(totals.shape))
 

time: 139 us -> 138 us (level)
  matrix products: 21.2 us -> 18.1 us
  other arithmetic: 26.2 us -> 28.8 us
    dot_general x2 -> x0, matrix products: 3.12 us -> none  [carried_in(): jnp.einsum('ij,jrc->irc', taken.astype(jnp.float32), mine, precision=HIGH...]
    add x0 -> x10, other arithmetic: none -> 2.56 us  [carried_in(): shifted = shifted + shift_rows(shifted, step, reverse)]
    slice x0 -> x10, local copies, waits for them, and re-layouts: none -> 2.52 us  [the longest x5 1.26 us: shift_rows(): return jnp.pad(rows[step:], widths)]
    dot_general x2 -> x0, local copies, waits for them, and re-layouts: 2.5 us -> none  [carried_in(): jnp.einsum('ij,jrc->irc', taken.astype(jnp.float32), mine, precision=HIGH...]
  transfers between devices with their start and end apart: 6 -> 6, of which waited for: 6 -> 6; matrix products, arithmetic and copies ran while one was open for 19% -> 20% of each run, Pallas kernels for 0% -> 0%
where the time goes in v4:
time: 138 us; the launch traced here: 137 us
  waiting for transfers between devices  35.4 us (26%)
  starting transfers between devices  35.1 us (25%)
  other arithmetic  28.8 us (21%)
  local copies, waits for them, and re-layouts  18.3 us (13%)
  matrix products  18.1 us (13%)
  between operations  1.51 us (1%)
    all_to_all x2, waiting for transfers between devices, carried_in(): mine = lax.all_to_all(stacked, axis, 0, 0, tiled=True)  17.2 us
    dot_general x14, matrix products, product_of(): return jnp.einsum(spec, lhs, rhs, preferred_element_type=jnp.float32)  14.7 us
    all_to_all x2, starting transfers between devices, carried_in(): mine = lax.all_to_all(stacked, axis, 0, 0, tiled=True)  13.9 us
    all_to_all x2, starting transfers between devices, head_sum(): gathered = lax.all_to_all(spread, axis, 0, 0, tiled=True)  12.3 us
    all_to_all x2, waiting for transfers between devices, carried_in(): lax.all_to_all(shifted, axis, 0, 0, tiled=True)  10.7 us
    all_to_all x2, starting transfers between devices, carried_in(): lax.all_to_all(shifted, axis, 0, 0, tiled=True)  8.8 us
    all_to_all x2, waiting for transfers between devices, head_sum(): gathered = lax.all_to_all(spread, axis, 0, 0, tiled=True)  7.54 us
    reduce_sum x2, other arithmetic, sketch_back(): sketch_grad = jnp.sum(symmetric * sketched[..., None, :], axis=-1)  6.36 us
  transfers between devices with their start and end apart: 6, of which 6 were waited for; matrix products, arithmetic and copies ran while one was open for 20% of the time, Pallas kernels for 0%

profile of v4, /device:TPU:1, one launch (start us, length us, event | category | flops | bytes accessed | tf_op | source)
XLA Modules:
  0.0 137.2 jit_solution(12231583357762007668)
XLA Ops:
  0.6 1.3 fusion.14
  1.9 1.3 fusion.23
  3.2 0.6 broadcast_in_dim.17
  3.9 9.0 %all-to-all-start = ((f32[8,2,512]{2,1,0:T(2,128)}), f32[8,2,512]{2,1,0:T(2,128)S(1)}, u32[]{:S(2)}, u32[]{:S(2)}) async-start(f32[8,2,512]{2,1,0:T(2,128)} %broadcast_in_dim.17), calls=%async_computation | async-start | bytes 65536 | tf_op jit(solution)/shard_map/all_to_all | solution.py:53
  12.9 0.7 fusion.46
  13.6 1.2 reshape.169
  14.9 1.0 copy_bitcast_fusion
  16.0 0.6 iota_compare_fusion
  16.6 3.1 %all-to-all-done = f32[8,2,512]{2,1,0:T(2,128)S(1)} async-done(((f32[8,2,512]{2,1,0:T(2,128)}), f32[8,2,512]{2,1,0:T(2,128)S(1)}, u32[]{:S(2)}, u32[]{:S(2)}) %all-to-all-start) | async-done | bytes 32800 | tf_op jit(solution)/shard_map/all_to_all | solution.py:53
  21.5 1.0 convert_reduce_fusion
  22.6 0.4 fusion.61
  23.1 1.0 maximum_maximum_fusion
  24.0 9.2 %all-to-all-start.1 = ((f32[32,40,128]{2,1,0:T(8,128)}), f32[32,40,128]{2,1,0:T(8,128)}, u32[]{:S(2)}, u32[]{:S(2)}) async-start(f32[32,40,128]{2,1,0:T(8,128)} %bitcast.17), calls=%async_computation.1 | async-start | bytes 1310720 | tf_op jit(solution)/shard_map/all_to_all | solution.py:39
  33.3 0.6 multiply_multiply_fusion.5
  34.1 12.1 %all-to-all-done.1 = f32[32,40,128]{2,1,0:T(8,128)} async-done(((f32[32,40,128]{2,1,0:T(8,128)}), f32[32,40,128]{2,1,0:T(8,128)}, u32[]{:S(2)}, u32[]{:S(2)}) %all-to-all-start.1) | async-done | bytes 655392 | tf_op jit(solution)/shard_map/all_to_all | solution.py:39
  46.2 1.1 slice.110
  47.9 0.9 pad_add_fusion.4
  48.8 4.4 %all-to-all-start.2 = ((f32[32,40,128]{2,1,0:T(8,128)}), f32[32,40,128]{2,1,0:T(8,128)}, u32[]{:S(2)}, u32[]{:S(2)}) async-start(f32[32,40,128]{2,1,0:T(8,128)} %pad_add_fusion.4), calls=%async_computation.2 | async-start | bytes 1310720 | tf_op jit(solution)/shard_map/all_to_all | solution.py:45
  53.3 0.6 multiply_multiply_fusion.4
  53.8 0.9 reduce_sum.144
  54.8 0.6 reduce_window_sum.35
  55.4 3.7 %convert_reduce_fusion.2 = (f32[4,2,256]{2,1,0:T(2,128)}, bf16[4,2,256,256]{2,3,1,0:T(8,128)(2,1)S(1)}, f32[4,2,256,256]{2,3,1,0:T(8,128)}) fusion(pred[256,256]{0,1:T(8,128)(4,1)} %iota_compare_fusion, bf16[4,2,256,128]{3,2,1,0:T(8,128)(2,1)} %bitcast.161, bf16[4,2,256,128]{3,2,1,0:T(8,128)(2,1)} %bitcast.164), kind=kOutput, calls=%fused_computation.18 | convolution fusion | flops 137885696 | bytes 4268032 | tf_op jit(solution)/shard_map/...id,...jd->...ij/dot_general | solution.py:59
  59.1 1.0 copy-done
  60.1 1.5 %fusion.64 = f32[4,2,256,128]{3,2,1,0:T(8,128)} fusion(bf16[4,2,256,256]{2,3,1,0:T(8,128)(2,1)S(1)} %get-tuple-element.9, bf16[4,2,256,128]{3,2,1,0:T(8,128)(2,1)S(1)} %bitcast.157), kind=kOutput, calls=%fused_computation.138 | convolution fusion | flops 134217728 | bytes 2621440 | tf_op jit(solution)/shard_map/...ij,...jd->...id/dot_general | solution.py:59
  61.6 4.4 %all-to-all-done.2 = f32[32,40,128]{2,1,0:T(8,128)} async-done(((f32[32,40,128]{2,1,0:T(8,128)}), f32[32,40,128]{2,1,0:T(8,128)}, u32[]{:S(2)}, u32[]{:S(2)}) %all-to-all-start.2) | async-done | bytes 655392 | tf_op jit(solution)/shard_map/all_to_all | solution.py:45
  66.0 0.7 slice_bitcast_fusion.1
  66.7 1.1 slice.116
  68.0 0.5 fusion.44
  68.6 0.5 copy-done.20
  69.4 0.6 multiply_reduce_fusion
  70.4 1.2 divide_convert_fusion
  71.6 1.2 fusion.62
  72.9 1.8 %multiply_add_fusion = f32[4,2,256,256]{2,3,1,0:T(8,128)} fusion(bf16[4,2,256,128]{3,2,1,0:T(8,128)(2,1)S(1)} %get-tuple-element.17, bf16[4,2,256,128]{3,2,1,0:T(8,128)(2,1)S(1)} %fusion.12, f32[4,2,256]{2,1,0:T(2,128)S(1)} %add_subtract_fusion.1, f32[4,2,256]{2,1,0:T(2,128)S(1)} %get-tuple-element.6), kind=kOutput, calls=%fused_computation.17 | convolution fusion | flops 135266304 | bytes 3162112 | tf_op jit(solution)/shard_map/...id,...rd->...ir/dot_general | solution.py:59
  74.6 0.9 fusion.42
  75.6 2.0 %maximum_maximum_fusion.1 = f32[4,320,128]{2,1,0:T(8,128)} fusion(f32[4,2,128]{2,1,0:T(2,128)S(1)} %reshape.179, f32[4,256,128]{2,1,0:T(8,128)} %get-tuple-element.28, f32[320]{0:T(512)} %copy-done.44), kind=kLoop, calls=%fused_computation.65 | loop fusion | flops 327680 | bytes 1185024 | tf_op jit(solution)/shard_map/concatenate | solution.py:31
  77.7 4.7 %all-to-all-start.3 = ((f32[32,40,128]{2,1,0:T(8,128)}), f32[32,40,128]{2,1,0:T(8,128)}, u32[]{:S(2)}, u32[]{:S(2)}) async-start(f32[32,40,128]{2,1,0:T(8,128)} %bitcast.33), calls=%async_computation.3 | async-start | bytes 1310720 | tf_op jit(solution)/shard_map/all_to_all | solution.py:39
  82.4 4.0 %fusion.10 = f32[4,2,256,16]{2,3,1,0:T(8,128)S(1)} fusion(f32[4,2,256,16,16]{2,4,3,1,0:T(8,128)} %bitcast.154, f32[4,2,256,16]{2,3,1,0:T(8,128)S(1)} %multiply_multiply_fusion.3), kind=kLoop, calls=%fused_computation.16 | loop fusion | flops 1540096 | bytes 2359296 | tf_op jit(solution)/shard_map/reduce_sum | solution.py:87
  86.5 1.0 fusion.34
  87.6 0.8 fusion.6
  88.4 1.0 copy-done.17
  89.3 0.5 convolution_add_fusion.3
  89.8 5.1 %all-to-all-done.3 = f32[32,40,128]{2,1,0:T(8,128)} async-done(((f32[32,40,128]{2,1,0:T(8,128)}), f32[32,40,128]{2,1,0:T(8,128)}, u32[]{:S(2)}, u32[]{:S(2)}) %all-to-all-start.3) | async-done | bytes 655392 | tf_op jit(solution)/shard_map/all_to_all | solution.py:39
  94.9 1.1 slice.118
  96.6 0.9 pad_add_fusion
  97.5 4.4 %all-to-all-start.4 = ((f32[32,40,128]{2,1,0:T(8,128)}), f32[32,40,128]{2,1,0:T(8,128)}, u32[]{:S(2)}, u32[]{:S(2)}) async-start(f32[32,40,128]{2,1,0:T(8,128)} %pad_add_fusion), calls=%async_computation.4 | async-start | bytes 1310720 | tf_op jit(solution)/shard_map/all_to_all | solution.py:45
  101.9 1.3 fusion.22
  103.4 1.0 rev.14
  104.5 2.4 %fusion.63 = f32[4,2,256,128]{3,2,1,0:T(8,128)} fusion(f32[4,2,256,128]{3,2,1,0:T(8,128)} %rev.14), kind=kOutput, calls=%fused_computation.137 | output fusion | flops 262144 | bytes 2097152 | tf_op jit(solution)/shard_map/jit(cumsum)/reduce_window_sum | solution.py:111
  106.9 1.4 %fusion.65 = f32[4,2,256,128]{3,2,1,0:T(8,128)} fusion(bf16[4,2,256,256]{2,3,1,0:T(8,128)(2,1)S(1)} %copy-done.1, bf16[4,2,256,128]{3,2,1,0:T(8,128)(2,1)S(1)} %copy-done.8), kind=kOutput, calls=%fused_computation.139 | convolution fusion | flops 134217728 | bytes 2621440 | tf_op jit(solution)/shard_map/...ij,...id->...jd/dot_general | solution.py:59
  108.3 6.3 %all-to-all-done.4 = f32[32,40,128]{2,1,0:T(8,128)} async-done(((f32[32,40,128]{2,1,0:T(8,128)}), f32[32,40,128]{2,1,0:T(8,128)}, u32[]{:S(2)}, u32[]{:S(2)}) %all-to-all-start.4) | async-done | bytes 655392 | tf_op jit(solution)/shard_map/all_to_all | solution.py:45
  114.6 0.7 slice_bitcast_fusion
  115.3 1.2 slice.124
  116.5 1.4 %subtract_convert_fusion = bf16[4,2,256,128]{3,2,1,0:T(8,128)(2,1)S(1)} fusion(f32[4,2,256,128]{3,2,1,0:T(8,128)S(1)} %get-tuple-element.29, f32[4,2,256,128]{3,2,1,0:T(8,128)} %fusion.63, f32[4,256,128]{2,1,0:T(8,128)S(1)} %slice.124), kind=kLoop, calls=%fused_computation.60 | loop fusion | flops 786432 | bytes 3145728 | tf_op jit(solution)/shard_map/convert_element_type | solution.py:163
  118.0 1.3 fusion.13
  119.3 0.4 convolution_add_fusion
  119.7 0.5 copy-done.28
  120.2 2.3 %fusion.8 = f32[4,2,256,16]{2,3,1,0:T(8,128)S(1)} fusion(f32[4,2,256,16,16]{2,4,3,1,0:T(8,128)S(1)} %bitcast.155, f32[4,2,256,16]{2,3,1,0:T(8,128)S(1)} %copy-done.28), kind=kLoop, calls=%fused_computation.13 | loop fusion | flops 1540096 | bytes 2359296 | tf_op jit(solution)/shard_map/reduce_sum | solution.py:87
  122.5 1.0 fusion.37
  124.1 0.5 copy-done.12
  124.8 0.6 broadcast_in_dim.19
  125.5 3.3 %all-to-all-start.5 = ((f32[8,2,512]{2,1,0:T(2,128)}), f32[8,2,512]{2,1,0:T(2,128)S(1)}, u32[]{:S(2)}, u32[]{:S(2)}) async-start(f32[8,2,512]{2,1,0:T(2,128)} %broadcast_in_dim.19), calls=%async_computation.5 | async-start | bytes 65536 | tf_op jit(solution)/shard_map/all_to_all | solution.py:53
  128.8 2.3 %copy_bitcast_fusion.1 = (bf16[512,512]{1,0:T(8,128)(2,1)}, bf16[512,512]{1,0:T(8,128)(2,1)}) fusion(bf16[4,64,8,128]{3,2,1,0:T(8,128)(2,1)} %bitcast.171, bf16[4,64,8,128]{3,2,1,0:T(8,128)(2,1)} %bitcast.167), kind=kLoop, calls=%fused_computation.80 | loop fusion | bytes 2097152 | tf_op jit(solution)/shard_map/convert_element_type | solution.py:255
  131.1 4.4 %all-to-all-done.5 = f32[8,2,512]{2,1,0:T(2,128)S(1)} async-done(((f32[8,2,512]{2,1,0:T(2,128)}), f32[8,2,512]{2,1,0:T(2,128)S(1)}, u32[]{:S(2)}, u32[]{:S(2)}) %all-to-all-start.5) | async-done | bytes 32800 | tf_op jit(solution)/shard_map/all_to_all | solution.py:53
  135.6 1.6 %fusion.20 = (bf16[512,512]{1,0:T(8,128)(2,1)}, bf16[512,512]{1,0:T(8,128)(2,1)}) fusion(bf16[512,512]{1,0:T(8,128)(2,1)S(1)} %copy-done.10, f32[4,64,8,128]{3,2,1,0:T(8,128)S(1)} %bitcast.151, f32[512]{0:T(512)S(1)} %bitcast.185, f32[512]{0:T(512)S(1)} %copy-done.45, f32[512]{0:T(512)S(1)} %copy-done.41, f32[512]{0:T(512)S(1)} %bitcast.179, ...), kind=kLoop, calls=%fused_computation.44 | loop fusion | flops 4194304 | bytes 4210688 | tf_op jit(solution)/shard_map/convert_element_type | solution.py:178
  (142 shorter events, 5.2 us)
Async XLA Ops:
  0.6 14.2 %copy-start.24 = (bf16[512,512]{1,0:T(8,128)(2,1)S(1)}, bf16[512,512]{1,0:T(8,128)(2,1)}, u32[]{:S(2)}) copy-start(bf16[512,512]{1,0:T(8,128)(2,1)} %param.10) | copy-start | bytes 1572868
  1.9 17.9 %copy-start.9 = (bf16[512,512]{1,0:T(8,128)(2,1)S(1)}, bf16[512,512]{1,0:T(8,128)(2,1)}, u32[]{:S(2)}) copy-start(bf16[512,512]{1,0:T(8,128)(2,1)} %param.7) | copy-start | bytes 1572868
  1.9 17.9 %copy-start.40 = (f32[512]{0:T(512)S(1)}, f32[512]{0:T(512)}, u32[]{:S(2)}) copy-start(f32[512]{0:T(512)} %param.11) | copy-start | bytes 6148
  3.9 15.9 %all-to-all-start = ((f32[8,2,512]{2,1,0:T(2,128)}), f32[8,2,512]{2,1,0:T(2,128)S(1)}, u32[]{:S(2)}, u32[]{:S(2)}) async-start(f32[8,2,512]{2,1,0:T(2,128)} %broadcast_in_dim.17), calls=%async_computation | async-start | bytes 65536 | tf_op jit(solution)/shard_map/all_to_all | solution.py:53
  14.8 7.8 %copy-start.2 = (bf16[4,512,128]{2,1,0:T(8,128)(2,1)}, bf16[4,512,128]{2,1,0:T(8,128)(2,1)S(1)}, u32[]{:S(2)}) copy-start(bf16[4,512,128]{2,1,0:T(8,128)(2,1)S(1)} %copy.60) | copy-start | bytes 1572868
  14.8 5.4 %copy-start.11 = (bf16[512,512]{1,0:T(8,128)(2,1)S(1)}, bf16[512,512]{1,0:T(8,128)(2,1)}, u32[]{:S(2)}) copy-start(bf16[512,512]{1,0:T(8,128)(2,1)} %param.8) | copy-start | bytes 1572868
  14.9 5.4 %copy-start.42 = (f32[512]{0:T(512)S(1)}, f32[512]{0:T(512)}, u32[]{:S(2)}) copy-start(f32[512]{0:T(512)} %param.12) | copy-start | bytes 6148
  16.0 7.1 %copy-start.44 = (f32[320]{0:T(512)}, f32[320]{0:T(512)S(1)}, u32[]{:S(2)}) copy-start(f32[320]{0:T(512)S(1)} %pad.69.clone) | copy-start | bytes 3844
  19.8 13.5 %copy-start.37 = (f32[1,512]{1,0:T(1,128)}, f32[1,512]{1,0:T(1,128)S(1)}, u32[]{:S(2)}) copy-start(f32[1,512]{1,0:T(1,128)S(1)} %get-tuple-element.22) | copy-start | bytes 6148
  19.8 33.5 %copy-start.35 = (f32[1,512]{1,0:T(1,128)}, f32[1,512]{1,0:T(1,128)S(1)}, u32[]{:S(2)}) copy-start(f32[1,512]{1,0:T(1,128)S(1)} %get-tuple-element.21) | copy-start | bytes 6148
  20.2 1.0 copy-start.13
  20.7 0.8 copy-start.15
  20.9 12.9 %copy-start.22 = (f32[4,2,256,32]{2,3,1,0:T(8,128)}, f32[4,2,256,32]{2,3,1,0:T(8,128)S(1)}, u32[]{:S(2)}) copy-start(f32[4,2,256,32]{2,3,1,0:T(8,128)S(1)} %fusion.57) | copy-start | bytes 786436
  21.5 1.6 %copy-start.27 = (f32[4,2,256,16]{2,3,1,0:T(8,128)}, f32[4,2,256,16]{2,3,1,0:T(8,128)S(1)}, u32[]{:S(2)}) copy-start(f32[4,2,256,16]{2,3,1,0:T(8,128)S(1)} %multiply_multiply_fusion.2) | copy-start | bytes 393220
  24.0 22.2 %all-to-all-start.1 = ((f32[32,40,128]{2,1,0:T(8,128)}), f32[32,40,128]{2,1,0:T(8,128)}, u32[]{:S(2)}, u32[]{:S(2)}) async-start(f32[32,40,128]{2,1,0:T(8,128)} %bitcast.17), calls=%async_computation.1 | async-start | bytes 1310720 | tf_op jit(solution)/shard_map/all_to_all | solution.py:39
  48.8 17.1 %all-to-all-start.2 = ((f32[32,40,128]{2,1,0:T(8,128)}), f32[32,40,128]{2,1,0:T(8,128)}, u32[]{:S(2)}, u32[]{:S(2)}) async-start(f32[32,40,128]{2,1,0:T(8,128)} %pad_add_fusion.4), calls=%async_computation.2 | async-start | bytes 1310720 | tf_op jit(solution)/shard_map/all_to_all | solution.py:45
  54.8 4.4 %copy-start.32 = (f32[4,2,256]{2,1,0:T(2,128)}, f32[4,2,256]{2,1,0:T(2,128)S(1)}, u32[]{:S(2)}) copy-start(f32[4,2,256]{2,1,0:T(2,128)S(1)} %reduce_sum.144) | copy-start | bytes 24580
  55.4 4.7 %copy-start.3 = (bf16[4,512,128]{2,1,0:T(8,128)(2,1)S(1)}, bf16[4,512,128]{2,1,0:T(8,128)(2,1)}, u32[]{:S(2)}) copy-start(bf16[4,512,128]{2,1,0:T(8,128)(2,1)} %copy-done.2) | copy-start | bytes 1572868
  59.1 1.0 copy-start
  66.7 1.3 copy-start.33
  66.7 1.3 copy-start.39
  67.8 1.2 copy-start.20
  67.8 1.5 %copy-start.21 = (f32[4,2,256,128]{3,2,1,0:T(8,128)S(1)}, f32[4,2,256,128]{3,2,1,0:T(8,128)}, u32[]{:S(2)}) copy-start(f32[4,2,256,128]{3,2,1,0:T(8,128)} %fusion.64) | copy-start | bytes 3145732
  69.4 0.7 copy-start.34
  69.4 1.1 copy-start.25
  70.1 4.6 %copy-start.30 = (f32[4,2,256]{2,1,0:T(2,128)}, f32[4,2,256]{2,1,0:T(2,128)S(1)}, u32[]{:S(2)}) copy-start(f32[4,2,256]{2,1,0:T(2,128)S(1)} %get-tuple-element.6) | copy-start | bytes 24580
  71.6 3.0 %copy-start.6 = (bf16[4,2,256,128]{3,2,1,0:T(8,128)(2,1)}, bf16[4,2,256,128]{3,2,1,0:T(8,128)(2,1)S(1)}, u32[]{:S(2)}) copy-start(bf16[4,2,256,128]{3,2,1,0:T(8,128)(2,1)S(1)} %get-tuple-element.17) | copy-start | bytes 1572868
  77.6 8.8 %copy-start.23 = (f32[4,2,256,32]{2,3,1,0:T(8,128)S(1)}, f32[4,2,256,32]{2,3,1,0:T(8,128)}, u32[]{:S(2)}) copy-start(f32[4,2,256,32]{2,3,1,0:T(8,128)} %copy-done.22) | copy-start | bytes 786436
  77.7 17.3 %all-to-all-start.3 = ((f32[32,40,128]{2,1,0:T(8,128)}), f32[32,40,128]{2,1,0:T(8,128)}, u32[]{:S(2)}, u32[]{:S(2)}) async-start(f32[32,40,128]{2,1,0:T(8,128)} %bitcast.33), calls=%async_computation.3 | async-start | bytes 1310720 | tf_op jit(solution)/shard_map/all_to_all | solution.py:39
  82.4 5.2 %copy-start.4 = (bf16[4,512,128]{2,1,0:T(8,128)(2,1)S(1)}, bf16[4,512,128]{2,1,0:T(8,128)(2,1)}, u32[]{:S(2)}) copy-start(bf16[4,512,128]{2,1,0:T(8,128)(2,1)} %copy-done.2) | copy-start | bytes 1572868
  82.4 5.2 %copy-start.7 = (bf16[4,2,256,128]{3,2,1,0:T(8,128)(2,1)S(1)}, bf16[4,2,256,128]{3,2,1,0:T(8,128)(2,1)}, u32[]{:S(2)}) copy-start(bf16[4,2,256,128]{3,2,1,0:T(8,128)(2,1)} %copy-done.6) | copy-start | bytes 1572868
  82.4 5.2 %copy-start.26 = (f32[4,2,256,256]{2,3,1,0:T(8,128)S(1)}, f32[4,2,256,256]{2,3,1,0:T(8,128)}, u32[]{:S(2)}) copy-start(f32[4,2,256,256]{2,3,1,0:T(8,128)} %get-tuple-element.23) | copy-start | bytes 6291460
  82.4 5.2 %copy-start.29 = (pred[256,256]{0,1:T(8,128)(4,1)S(1)}, pred[256,256]{0,1:T(8,128)(4,1)}, u32[]{:S(2)}) copy-start(pred[256,256]{0,1:T(8,128)(4,1)} %iota_compare_fusion) | copy-start | bytes 196612
  82.4 5.2 %copy-start.31 = (f32[4,2,256]{2,1,0:T(2,128)S(1)}, f32[4,2,256]{2,1,0:T(2,128)}, u32[]{:S(2)}) copy-start(f32[4,2,256]{2,1,0:T(2,128)} %copy-done.30) | copy-start | bytes 24580
  87.6 1.8 %copy-start.16 = (bf16[4,512,128]{2,1,0:T(8,128)(2,1)S(1)}, bf16[4,512,128]{2,1,0:T(8,128)(2,1)}, u32[]{:S(2)}) copy-start(bf16[4,512,128]{2,1,0:T(8,128)(2,1)} %copy-done.15) | copy-start | bytes 1572868
  88.4 1.0 copy-start.17
  96.5 5.4 %copy-start.41 = (f32[512]{0:T(512)S(1)}, f32[512]{0:T(512)}, u32[]{:S(2)}) copy-start(f32[512]{0:T(512)} %param.11) | copy-start | bytes 6148
  97.5 17.1 %all-to-all-start.4 = ((f32[32,40,128]{2,1,0:T(8,128)}), f32[32,40,128]{2,1,0:T(8,128)}, u32[]{:S(2)}, u32[]{:S(2)}) async-start(f32[32,40,128]{2,1,0:T(8,128)} %pad_add_fusion), calls=%async_computation.4 | async-start | bytes 1310720 | tf_op jit(solution)/shard_map/all_to_all | solution.py:45
  104.5 2.4 %copy-start.1 = (bf16[4,2,256,256]{2,3,1,0:T(8,128)(2,1)S(1)}, bf16[4,2,256,256]{2,3,1,0:T(8,128)(2,1)}, u32[]{:S(2)}) copy-start(bf16[4,2,256,256]{2,3,1,0:T(8,128)(2,1)} %copy-done) | copy-start | bytes 3145732
  104.5 2.4 %copy-start.8 = (bf16[4,2,256,128]{3,2,1,0:T(8,128)(2,1)S(1)}, bf16[4,2,256,128]{3,2,1,0:T(8,128)(2,1)}, u32[]{:S(2)}) copy-start(bf16[4,2,256,128]{3,2,1,0:T(8,128)(2,1)} %copy-done.6) | copy-start | bytes 1572868
  115.3 2.6 %copy-start.19 = (f32[4,2,256,128]{3,2,1,0:T(8,128)S(1)}, f32[4,2,256,128]{3,2,1,0:T(8,128)}, u32[]{:S(2)}) copy-start(f32[4,2,256,128]{3,2,1,0:T(8,128)} %fusion.65) | copy-start | bytes 3145732
  118.0 1.3 copy-start.5
  119.3 0.9 copy-start.28
  120.2 3.4 %copy-start.14 = (bf16[4,512,128]{2,1,0:T(8,128)(2,1)S(1)}, bf16[4,512,128]{2,1,0:T(8,128)(2,1)}, u32[]{:S(2)}) copy-start(bf16[4,512,128]{2,1,0:T(8,128)(2,1)} %copy-done.13) | copy-start | bytes 1572868
  120.2 3.4 %copy-start.18 = (bf16[4,2,256,256]{2,3,1,0:T(8,128)(2,1)S(1)}, bf16[4,2,256,256]{2,3,1,0:T(8,128)(2,1)}, u32[]{:S(2)}) copy-start(bf16[4,2,256,256]{2,3,1,0:T(8,128)(2,1)} %copy-done.17) | copy-start | bytes 3145732
  123.6 1.0 copy-start.12
  123.6 1.0 copy-start.43
  124.0 11.6 %copy-start.10 = (bf16[512,512]{1,0:T(8,128)(2,1)S(1)}, bf16[512,512]{1,0:T(8,128)(2,1)}, u32[]{:S(2)}) copy-start(bf16[512,512]{1,0:T(8,128)(2,1)} %param.7) | copy-start | bytes 1572868
  124.0 11.6 %copy-start.36 = (f32[1,512]{1,0:T(1,128)S(1)}, f32[1,512]{1,0:T(1,128)}, u32[]{:S(2)}) copy-start(f32[1,512]{1,0:T(1,128)} %copy-done.35) | copy-start | bytes 6148
  124.0 11.6 %copy-start.38 = (f32[1,512]{1,0:T(1,128)S(1)}, f32[1,512]{1,0:T(1,128)}, u32[]{:S(2)}) copy-start(f32[1,512]{1,0:T(1,128)} %copy-done.37) | copy-start | bytes 6148
  124.1 11.6 %copy-start.45 = (f32[512]{0:T(512)S(1)}, f32[512]{0:T(512)}, u32[]{:S(2)}) copy-start(f32[512]{0:T(512)} %multiply_multiply_fusion.5) | copy-start | bytes 6148
  124.1 11.6 %copy-start.46 = (f32[512]{0:T(512)S(1)}, f32[512]{0:T(512)}, u32[]{:S(2)}) copy-start(f32[512]{0:T(512)} %multiply_multiply_fusion.4) | copy-start | bytes 6148
  125.5 10.1 %all-to-all-start.5 = ((f32[8,2,512]{2,1,0:T(2,128)}), f32[8,2,512]{2,1,0:T(2,128)S(1)}, u32[]{:S(2)}, u32[]{:S(2)}) async-start(f32[8,2,512]{2,1,0:T(2,128)} %broadcast_in_dim.19), calls=%async_computation.5 | async-start | bytes 65536 | tf_op jit(solution)/shard_map/all_to_all | solution.py:53

commit v5 on v4

--- a/solution.py
+++ b/solution.py
@@ -1,3 +1,4 @@
+import numpy as np
 import jax
 import jax.numpy as jnp
 from jax import lax
@@ -91,12 +92,34 @@
     return precise_product("...r,dr->...d", both_grad, sign_pair)
 
 
+def pair_tables():
+    upper = [r * RS + c for r in range(RS) for c in range(r, RS)]
+    low = np.minimum.outer(np.arange(RS), np.arange(RS)).reshape(-1)
+    high = np.maximum.outer(np.arange(RS), np.arange(RS)).reshape(-1)
+    owner = np.array([upper.index(a * RS + b) for a, b in zip(low, high)])
+    pick = np.zeros((RS * RS, len(upper)), np.float32)
+    pick[upper, np.arange(len(upper))] = 1.0
+    spread = np.zeros((RS * RS, len(upper)), np.float32)
+    spread[np.arange(RS * RS), owner] = 1.0
+    return pick, spread
+
+
+def pick_pairs(feats):
+    pick = jnp.asarray(pair_tables()[0], jnp.bfloat16)
+    return product_of("...f,fp->...p", feats, pick).astype(jnp.bfloat16)
+
+
+def spread_pairs(half):
+    spread = jnp.asarray(pair_tables()[1])
+    return jnp.einsum("...pd,fp->...fd", half, spread, precision=HIGHEST_PREC)
+
+
 def forward_blocks(q_normed, k_normed, values, sign_pair):
     scores = product_of("...id,...jd->...ij", q_normed, k_normed) * DH ** (-0.5)
     weights = jnp.where(causal_mask(), scores**4, 0.0).astype(jnp.bfloat16)
     q_parts = sketch(q_normed, sign_pair)
     k_parts = sketch(k_normed, sign_pair)
-    block_kv = product_of("...jr,...jd->...rd", k_parts[0], values)
+    block_kv = product_of("...jr,...jd->...rd", pick_pairs(k_parts[0]), values)
     block_keys = jnp.sum(k_parts[0].astype(jnp.float32), axis=-2)
     return (scores, weights, q_parts, k_parts, block_kv, block_keys)
 
@@ -154,7 +177,7 @@
         product_of("...id,...rd->...ir", scaled_grad, state_half)
         + den_grad[..., None] * key_total[..., None, :]
     )
-    block_u = product_of("...ir,...id->...rd", q_feats, scaled_grad)
+    block_u = product_of("...ir,...id->...rd", pick_pairs(q_feats), scaled_grad)
     block_w = precise_product("...ir,...i->...r", q_feats, den_grad)
     return (q_diag, k_diag, v_diag, qf_grad, block_u, block_w)
 
@@ -216,6 +239,7 @@
     sum_keys = jnp.sum(block_keys, axis=1)
     prior_kv, prior_keys = carried_in(sum_kv, sum_keys, "ctx", False)
     key_state, key_total = before_blocks(block_kv, block_keys, prior_kv, prior_keys)
+    key_state = spread_pairs(key_state)
     state_half, numerator, denominator, attended = finish_forward(
         weights, v_heads, q_parts[0], key_state, key_total
     )
@@ -236,6 +260,7 @@
         jnp.sum(block_u, axis=1), jnp.sum(block_w, axis=1), "ctx", True
     )
     later_state, later_total = after_blocks(block_u, block_w, later_u, later_w)
+    later_state = spread_pairs(later_state)
     kf_grad, v_grad = finish_backward(v_heads, k_parts[0], later_state, later_total, v_diag)
     qn_grad = join_heads(
         q_diag + sketch_back(qf_grad, q_parts[1], q_parts[2], q_parts[3], sign_pair)

time: 138 us -> 142 us (1.029)
  matrix products: 18.1 us -> 31.2 us
  waiting for transfers between devices: 35.4 us -> 24.4 us
    all_to_all x2, waiting for transfers between devices: 17.2 us -> 8.62 us  [carried_in(): mine = lax.all_to_all(stacked, axis, 0, 0, tiled=True)]
    dot_general x14, matrix products: 14.7 us -> 22.9 us  [product_of(): return jnp.einsum(spec, lhs, rhs, preferred_element_type=jnp.float32)]
    dot_general x0 -> x2, matrix products: none -> 4.93 us  [spread_pairs(): return jnp.einsum('...pd,fp->...fd', half, spread, precision=HIGHEST_PREC)]
    rev x1 -> x2, local copies, waits for them, and re-layouts: 1.04 us -> 3.06 us  [after_blocks(): rev_u = jnp.flip(jnp.cumsum(jnp.flip(block_u, -3), axis=-3), -3)]
    all_to_all x2, waiting for transfers between devices: 10.7 us -> 8.79 us  [carried_in(): lax.all_to_all(shifted, axis, 0, 0, tiled=True)]
    another operation x1, other arithmetic: 2.4 us -> 0.87 us  [after_blocks(): rev_u = jnp.flip(jnp.cumsum(jnp.flip(block_u, -3), axis=-3), -3)]
    unnamed x98 -> x102, local copies, waits for them, and re-layouts: 6.01 us -> 4.66 us
  transfers between devices with their start and end apart: 6 -> 6, of which waited for: 6 -> 6; matrix products, arithmetic and copies ran while one was open for 20% -> 21% of each run, Pallas kernels for 0% -> 0%
where the time goes in v5:
time: 142 us; the launch traced here: 141 us
  starting transfers between devices  35.3 us (25%)
  matrix products  31.2 us (22%)
  other arithmetic  28.9 us (20%)
  waiting for transfers between devices  24.4 us (17%)
  local copies, waits for them, and re-layouts  19.4 us (14%)
  between operations  1.55 us (1%)
    dot_general x14, matrix products, product_of(): return jnp.einsum(spec, lhs, rhs, preferred_element_type=jnp.float32)  22.9 us
    all_to_all x2, starting transfers between devices, carried_in(): mine = lax.all_to_all(stacked, axis, 0, 0, tiled=True)  13.8 us
    all_to_all x2, starting transfers between devices, head_sum(): gathered = lax.all_to_all(spread, axis, 0, 0, tiled=True)  12.3 us
    all_to_all x2, starting transfers between devices, carried_in(): lax.all_to_all(shifted, axis, 0, 0, tiled=True)  9.12 us
    all_to_all x2, waiting for transfers between devices, carried_in(): lax.all_to_all(shifted, axis, 0, 0, tiled=True)  8.79 us
    all_to_all x2, waiting for transfers between devices, carried_in(): mine = lax.all_to_all(stacked, axis, 0, 0, tiled=True)  8.62 us
    all_to_all x2, waiting for transfers between devices, head_sum(): gathered = lax.all_to_all(spread, axis, 0, 0, tiled=True)  6.98 us
    reduce_sum x2, other arithmetic, sketch_back(): sketch_grad = jnp.sum(symmetric * sketched[..., None, :], axis=-1)  6.29 us
  transfers between devices with their start and end apart: 6, of which 6 were waited for; matrix products, arithmetic and copies ran while one was open for 21% of the time, Pallas kernels for 0%

profile of v5, /device:TPU:1, one launch (start us, length us, event | category | flops | bytes accessed | tf_op | source)
XLA Modules:
  0.0 140.8 jit_solution(18198788118975999119)
XLA Ops:
  0.6 1.3 fusion.15
  1.9 1.3 fusion.24
  3.2 0.6 broadcast_in_dim.17
  3.9 9.0 %all-to-all-start = ((f32[8,2,512]{2,1,0:T(2,128)}), f32[8,2,512]{2,1,0:T(2,128)S(1)}, u32[]{:S(2)}, u32[]{:S(2)}) async-start(f32[8,2,512]{2,1,0:T(2,128)} %broadcast_in_dim.17), calls=%async_computation | async-start | bytes 65536 | tf_op jit(solution)/shard_map/all_to_all | solution.py:54
  12.9 0.7 fusion.50
  13.6 1.2 reshape.169
  14.9 1.1 copy_bitcast_fusion
  16.0 0.6 pad.69.clone
  16.6 0.6 iota_compare_fusion
  17.2 2.5 %all-to-all-done = f32[8,2,512]{2,1,0:T(2,128)S(1)} async-done(((f32[8,2,512]{2,1,0:T(2,128)}), f32[8,2,512]{2,1,0:T(2,128)S(1)}, u32[]{:S(2)}, u32[]{:S(2)}) %all-to-all-start) | async-done | bytes 32800 | tf_op jit(solution)/shard_map/all_to_all | solution.py:54
  20.3 0.8 copy-done.8
  21.3 0.7 copy-done.18
  23.5 1.0 convert_reduce_fusion
  24.7 1.4 fusion.65
  26.0 0.8 maximum_maximum_fusion
  26.9 9.2 %all-to-all-start.1 = ((f32[32,24,128]{2,1,0:T(8,128)}), f32[32,24,128]{2,1,0:T(8,128)}, u32[]{:S(2)}, u32[]{:S(2)}) async-start(f32[32,24,128]{2,1,0:T(8,128)} %bitcast.19), calls=%async_computation.1 | async-start | bytes 786432 | tf_op jit(solution)/shard_map/all_to_all | solution.py:40
  36.7 3.7 %convert_reduce_fusion.2 = (f32[4,2,256]{2,1,0:T(2,128)}, bf16[4,2,256,256]{2,3,1,0:T(8,128)(2,1)S(1)}, f32[4,2,256,256]{2,3,1,0:T(8,128)}) fusion(pred[256,256]{0,1:T(8,128)(4,1)} %iota_compare_fusion, bf16[4,2,256,128]{3,2,1,0:T(8,128)(2,1)} %bitcast.172, bf16[4,2,256,128]{3,2,1,0:T(8,128)(2,1)} %bitcast.175), kind=kOutput, calls=%fused_computation.18 | convolution fusion | flops 137885696 | bytes 4268032 | tf_op jit(solution)/shard_map/...id,...jd->...ij/dot_general | solution.py:60
  40.4 6.1 %all-to-all-done.1 = f32[32,24,128]{2,1,0:T(8,128)} async-done(((f32[32,24,128]{2,1,0:T(8,128)}), f32[32,24,128]{2,1,0:T(8,128)}, u32[]{:S(2)}, u32[]{:S(2)}) %all-to-all-start.1) | async-done | bytes 393248 | tf_op jit(solution)/shard_map/all_to_all | solution.py:40
  46.5 1.0 slice.110
  47.8 0.8 pad_add_fusion.4
  48.6 4.4 %all-to-all-start.2 = ((f32[32,24,128]{2,1,0:T(8,128)}), f32[32,24,128]{2,1,0:T(8,128)}, u32[]{:S(2)}, u32[]{:S(2)}) async-start(f32[32,24,128]{2,1,0:T(8,128)} %pad_add_fusion.4), calls=%async_computation.2 | async-start | bytes 786432 | tf_op jit(solution)/shard_map/all_to_all | solution.py:46
  53.6 0.9 reduce_sum.144
  54.5 0.6 reduce_window_sum.35
  55.2 2.5 %fusion.68 = f32[4,2,256,128]{3,2,1,0:T(8,128)} fusion(bf16[4,2,256,256]{2,3,1,0:T(8,128)(2,1)S(1)} %get-tuple-element.9, bf16[4,2,256,128]{3,2,1,0:T(8,128)(2,1)} %bitcast.168), kind=kOutput, calls=%fused_computation.145 | convolution fusion | flops 134217728 | bytes 2621440 | tf_op jit(solution)/shard_map/...ij,...jd->...id/dot_general | solution.py:60
  57.7 5.5 %all-to-all-done.2 = f32[32,24,128]{2,1,0:T(8,128)} async-done(((f32[32,24,128]{2,1,0:T(8,128)}), f32[32,24,128]{2,1,0:T(8,128)}, u32[]{:S(2)}, u32[]{:S(2)}) %all-to-all-start.2) | async-done | bytes 393248 | tf_op jit(solution)/shard_map/all_to_all | solution.py:46
  63.2 0.8 slice_bitcast_fusion.1
  63.9 1.0 slice.116
  64.9 1.4 %fusion.11 = f32[4,2,136,128]{3,2,1,0:T(8,128)S(1)} fusion(f32[4,2,136,128]{3,2,1,0:T(8,128)} %get-tuple-element.25, f32[4,136,128]{2,1,0:T(8,128)S(1)} %slice.116), kind=kOutput, calls=%fused_computation.37 | output fusion | flops 417792 | bytes 1392640 | tf_op jit(solution)/shard_map/jit(cumsum)/reduce_window_sum | solution.py:128
  66.4 1.8 %convolution_convert_fusion.3 = bf16[4,2,128,256]{3,2,1,0:T(8,128)(2,1)S(1)} fusion(f32[4,2,136,128]{3,2,1,0:T(8,128)S(1)} %fusion.11, f32[256,136,1,1]{0,1,3,2:T(8,128)S(1)} %copy-done.25), kind=kOutput, calls=%fused_computation.40 | convolution fusion | flops 428081152 | bytes 1220608 | tf_op jit(solution)/shard_map/...pd,fp->...fd/dot_general | solution.py:114
  68.2 0.8 add_subtract_fusion.1
  69.5 0.6 multiply_reduce_fusion
  70.2 0.6 multiply_divide_fusion
  70.8 1.4 divide_convert_fusion
  72.2 3.1 %fusion.66 = (f32[4,136,128]{2,1,0:T(8,128)}, f32[4,2,136,128]{3,2,1,0:T(8,128)}) fusion(bf16[4,2,256,128]{3,2,1,0:T(8,128)(2,1)} %get-tuple-element.17, bf16[4,2,256,256]{2,3,1,0:T(8,128)(2,1)S(1)} %bitcast.157, bf16[256,136,1,1]{0,1,3,2:T(8,128)(2,1)} %constant.67), kind=kOutput, calls=%fused_computation.143 | convolution fusion | flops 214257664 | bytes 2478080 | tf_op jit(solution)/shard_map/...ir,...id->...rd/dot_general | solution.py:60
  75.3 3.2 %multiply_add_fusion = f32[4,2,256,256]{2,3,1,0:T(8,128)} fusion(bf16[4,2,256,128]{3,2,1,0:T(8,128)(2,1)} %get-tuple-element.17, bf16[4,2,128,256]{3,2,1,0:T(8,128)(2,1)} %copy-done.12, f32[4,2,256]{2,1,0:T(2,128)S(1)} %add_subtract_fusion.1, f32[4,2,256]{2,1,0:T(2,128)} %get-tuple-element.6), kind=kOutput, calls=%fused_computation.17 | convolution fusion | flops 135266304 | bytes 3162112 | tf_op jit(solution)/shard_map/...id,...rd->...ir/dot_general | solution.py:60
  78.5 2.6 %fusion.6 = bf16[4,2,256,256]{2,3,1,0:T(8,128)(2,1)} fusion(f32[4,2,256,256]{2,3,1,0:T(8,128)S(1)} %copy-done.22, bf16[4,2,256,128]{3,2,1,0:T(8,128)(2,1)S(1)} %copy-done, bf16[4,2,256,128]{3,2,1,0:T(8,128)(2,1)S(1)} %bitcast.169, f32[4,2,256]{2,1,0:T(2,128)S(1)} %copy-done.32, pred[256,256]{0,1:T(8,128)(4,1)} %iota_compare_fusion), kind=kOutput, calls=%fused_computation.10 | convolution fusion | flops 138936320 | bytes 4268032 | tf_op jit(solution)/shard_map/...id,...jd->...ij/dot_general | solution.py:60
  81.1 0.9 fusion.46
  82.1 1.8 %maximum_maximum_fusion.1 = f32[4,192,128]{2,1,0:T(8,128)} fusion(f32[4,2,128]{2,1,0:T(2,128)S(1)} %reshape.179, f32[4,136,128]{2,1,0:T(8,128)} %get-tuple-element.28, f32[192]{0:T(256)} %pad.69.clone), kind=kLoop, calls=%fused_computation.73 | loop fusion | flops 196608 | bytes 676608 | tf_op jit(solution)/shard_map/concatenate | solution.py:32
  83.9 4.6 %all-to-all-start.3 = ((f32[32,24,128]{2,1,0:T(8,128)}), f32[32,24,128]{2,1,0:T(8,128)}, u32[]{:S(2)}, u32[]{:S(2)}) async-start(f32[32,24,128]{2,1,0:T(8,128)} %bitcast.38), calls=%async_computation.3 | async-start | bytes 786432 | tf_op jit(solution)/shard_map/all_to_all | solution.py:40
  88.5 1.1 rev.14
  89.6 0.9 fusion.67
  90.5 4.0 %fusion.10 = f32[4,2,256,16]{2,3,1,0:T(8,128)S(1)} fusion(f32[4,2,256,16,16]{2,4,3,1,0:T(8,128)} %bitcast.165, f32[4,2,256,16]{2,3,1,0:T(8,128)S(1)} %multiply_multiply_fusion.3), kind=kLoop, calls=%fused_computation.16 | loop fusion | flops 1540096 | bytes 2359296 | tf_op jit(solution)/shard_map/reduce_sum | solution.py:88
  94.6 1.0 fusion.38
  96.1 2.5 %all-to-all-done.3 = f32[32,24,128]{2,1,0:T(8,128)} async-done(((f32[32,24,128]{2,1,0:T(8,128)}), f32[32,24,128]{2,1,0:T(8,128)}, u32[]{:S(2)}, u32[]{:S(2)}) %all-to-all-start.3) | async-done | bytes 393248 | tf_op jit(solution)/shard_map/all_to_all | solution.py:40
  98.7 1.0 slice.118
  100.0 0.8 pad_add_fusion
  100.8 4.7 %all-to-all-start.4 = ((f32[32,24,128]{2,1,0:T(8,128)}), f32[32,24,128]{2,1,0:T(8,128)}, u32[]{:S(2)}, u32[]{:S(2)}) async-start(f32[32,24,128]{2,1,0:T(8,128)} %pad_add_fusion), calls=%async_computation.4 | async-start | bytes 786432 | tf_op jit(solution)/shard_map/all_to_all | solution.py:46
  105.6 1.8 %fusion.23 = f32[512]{0:T(512)} fusion(bf16[512,512]{1,0:T(8,128)(2,1)} %param.11, f32[4,64,8,128]{3,2,1,0:T(8,128)S(1)} %bitcast.161, f32[512]{0:T(512)S(1)} %copy-done.41), kind=kLoop, calls=%fused_computation.51 | loop fusion | flops 1048064 | bytes 1576960 | tf_op jit(solution)/shard_map/reduce_sum | solution.py:273
  107.5 0.7 rev.17
  108.2 1.9 %rev.15 = f32[4,2,136,128]{3,2,1,0:T(8,128)} reverse(f32[4,2,136,128]{3,2,1,0:T(8,128)} %fusion.67), dimensions={1} | reverse | bytes 1114112 | tf_op jit(solution)/shard_map/jit(_flip)/rev | solution.py:134
  110.1 2.5 %fusion.69 = f32[4,2,256,128]{3,2,1,0:T(8,128)} fusion(bf16[4,2,256,256]{2,3,1,0:T(8,128)(2,1)S(1)} %get-tuple-element.9, bf16[4,2,256,128]{3,2,1,0:T(8,128)(2,1)} %get-tuple-element.17), kind=kOutput, calls=%fused_computation.146 | convolution fusion | flops 134217728 | bytes 2621440 | tf_op jit(solution)/shard_map/...ij,...id->...jd/dot_general | solution.py:60
  112.5 3.3 %all-to-all-done.4 = f32[32,24,128]{2,1,0:T(8,128)} async-done(((f32[32,24,128]{2,1,0:T(8,128)}), f32[32,24,128]{2,1,0:T(8,128)}, u32[]{:S(2)}, u32[]{:S(2)}) %all-to-all-start.4) | async-done | bytes 393248 | tf_op jit(solution)/shard_map/all_to_all | solution.py:46
  115.9 0.8 slice_bitcast_fusion
  116.7 1.0 slice.124
  117.7 0.7 add_subtract_fusion
  118.4 3.1 %convolution_convert_fusion.2 = bf16[4,2,128,256]{3,2,1,0:T(8,128)(2,1)S(1)} fusion(f32[256,136,1,1]{0,1,3,2:T(8,128)S(1)} %copy-done.26, f32[4,2,136,128]{3,2,1,0:T(8,128)} %get-tuple-element.29, f32[4,2,136,128]{3,2,1,0:T(8,128)} %rev.15, f32[4,136,128]{2,1,0:T(8,128)S(1)} %slice.124), kind=kOutput, calls=%fused_computation.39 | convolution fusion | flops 428359680 | bytes 2056192 | tf_op jit(solution)/shard_map/...pd,fp->...fd/dot_general | solution.py:114
  121.5 1.3 fusion.12
  123.7 2.3 %fusion.8 = f32[4,2,256,16]{2,3,1,0:T(8,128)S(1)} fusion(f32[4,2,256,16,16]{2,4,3,1,0:T(8,128)S(1)} %bitcast.166, f32[4,2,256,16]{2,3,1,0:T(8,128)S(1)} %copy-done.24), kind=kLoop, calls=%fused_computation.13 | loop fusion | flops 1540096 | bytes 2359296 | tf_op jit(solution)/shard_map/reduce_sum | solution.py:88
  126.1 1.0 fusion.41
  128.4 0.6 broadcast_in_dim.19
  129.0 3.3 %all-to-all-start.5 = ((f32[8,2,512]{2,1,0:T(2,128)}), f32[8,2,512]{2,1,0:T(2,128)S(1)}, u32[]{:S(2)}, u32[]{:S(2)}) async-start(f32[8,2,512]{2,1,0:T(2,128)} %broadcast_in_dim.19), calls=%async_computation.5 | async-start | bytes 65536 | tf_op jit(solution)/shard_map/all_to_all | solution.py:54
  132.4 2.3 %copy_bitcast_fusion.1 = (bf16[512,512]{1,0:T(8,128)(2,1)}, bf16[512,512]{1,0:T(8,128)(2,1)}) fusion(bf16[4,64,8,128]{3,2,1,0:T(8,128)(2,1)} %bitcast.182, bf16[4,64,8,128]{3,2,1,0:T(8,128)(2,1)} %bitcast.178), kind=kLoop, calls=%fused_computation.70 | loop fusion | bytes 2097152 | tf_op jit(solution)/shard_map/convert_element_type | solution.py:280
  134.7 4.5 %all-to-all-done.5 = f32[8,2,512]{2,1,0:T(2,128)S(1)} async-done(((f32[8,2,512]{2,1,0:T(2,128)}), f32[8,2,512]{2,1,0:T(2,128)S(1)}, u32[]{:S(2)}, u32[]{:S(2)}) %all-to-all-start.5) | async-done | bytes 32800 | tf_op jit(solution)/shard_map/all_to_all | solution.py:54
  139.2 1.6 %fusion.21 = (bf16[512,512]{1,0:T(8,128)(2,1)}, bf16[512,512]{1,0:T(8,128)(2,1)}) fusion(bf16[512,512]{1,0:T(8,128)(2,1)S(1)} %copy-done.5, f32[4,64,8,128]{3,2,1,0:T(8,128)S(1)} %bitcast.162, f32[512]{0:T(512)S(1)} %bitcast.196, f32[512]{0:T(512)S(1)} %copy-done.46, f32[512]{0:T(512)S(1)} %copy-done.42, f32[512]{0:T(512)S(1)} %bitcast.190, ...), kind=kLoop, calls=%fused_computation.49 | loop fusion | flops 4194304 | bytes 4210688 | tf_op jit(solution)/shard_map/convert_element_type | solution.py:201
  (148 shorter events, 7.6 us)
Async XLA Ops:
  0.6 14.2 %copy-start.20 = (bf16[512,512]{1,0:T(8,128)(2,1)S(1)}, bf16[512,512]{1,0:T(8,128)(2,1)}, u32[]{:S(2)}) copy-start(bf16[512,512]{1,0:T(8,128)(2,1)} %param.14) | copy-start | bytes 1572868
  1.9 17.9 %copy-start.4 = (bf16[512,512]{1,0:T(8,128)(2,1)S(1)}, bf16[512,512]{1,0:T(8,128)(2,1)}, u32[]{:S(2)}) copy-start(bf16[512,512]{1,0:T(8,128)(2,1)} %param.11) | copy-start | bytes 1572868
  1.9 17.9 %copy-start.40 = (f32[512]{0:T(512)S(1)}, f32[512]{0:T(512)}, u32[]{:S(2)}) copy-start(f32[512]{0:T(512)} %param.15) | copy-start | bytes 6148
  3.9 15.9 %all-to-all-start = ((f32[8,2,512]{2,1,0:T(2,128)}), f32[8,2,512]{2,1,0:T(2,128)S(1)}, u32[]{:S(2)}, u32[]{:S(2)}) async-start(f32[8,2,512]{2,1,0:T(2,128)} %broadcast_in_dim.17), calls=%async_computation | async-start | bytes 65536 | tf_op jit(solution)/shard_map/all_to_all | solution.py:54
  13.6 81.0 %copy-start.28 = (bf16[128,16]{0,1:T(8,128)(2,1)}, bf16[128,16]{0,1:T(8,128)(2,1)S(1)}, u32[]{:S(2)}) copy-start(bf16[128,16]{0,1:T(8,128)(2,1)S(1)} %get-tuple-element.15) | copy-start | bytes 12292
  13.6 81.0 %copy-start.30 = (bf16[128,16]{0,1:T(8,128)(2,1)}, bf16[128,16]{0,1:T(8,128)(2,1)S(1)}, u32[]{:S(2)}) copy-start(bf16[128,16]{0,1:T(8,128)(2,1)S(1)} %get-tuple-element.16) | copy-start | bytes 12292
  14.8 9.8 %copy-start.1 = (bf16[4,512,128]{2,1,0:T(8,128)(2,1)}, bf16[4,512,128]{2,1,0:T(8,128)(2,1)S(1)}, u32[]{:S(2)}) copy-start(bf16[4,512,128]{2,1,0:T(8,128)(2,1)S(1)} %copy.71) | copy-start | bytes 1572868
  19.8 16.3 %copy-start.37 = (f32[1,512]{1,0:T(1,128)}, f32[1,512]{1,0:T(1,128)S(1)}, u32[]{:S(2)}) copy-start(f32[1,512]{1,0:T(1,128)S(1)} %get-tuple-element.22) | copy-start | bytes 6148
  19.8 33.2 %copy-start.35 = (f32[1,512]{1,0:T(1,128)}, f32[1,512]{1,0:T(1,128)S(1)}, u32[]{:S(2)}) copy-start(f32[1,512]{1,0:T(1,128)S(1)} %get-tuple-element.21) | copy-start | bytes 6148
  19.8 2.2 %copy-start.6 = (bf16[512,512]{1,0:T(8,128)(2,1)S(1)}, bf16[512,512]{1,0:T(8,128)(2,1)}, u32[]{:S(2)}) copy-start(bf16[512,512]{1,0:T(8,128)(2,1)} %param.12) | copy-start | bytes 1572868
  19.8 2.2 %copy-start.43 = (f32[512]{0:T(512)S(1)}, f32[512]{0:T(512)}, u32[]{:S(2)}) copy-start(f32[512]{0:T(512)} %param.16) | copy-start | bytes 6148
  20.2 0.8 copy-start.8
  21.3 0.7 copy-start.18
  22.5 0.8 copy-start.10
  22.5 2.2 %copy-start.27 = (bf16[256,136,1,1]{0,1,3,2:T(8,128)(2,1)S(1)}, bf16[256,136,1,1]{0,1,3,2:T(8,128)(2,1)}, u32[]{:S(2)}) copy-start(bf16[256,136,1,1]{0,1,3,2:T(8,128)(2,1)} %constant.67) | copy-start | bytes 208900
  23.3 2.7 %copy-start.23 = (f32[4,2,256,16]{2,3,1,0:T(8,128)}, f32[4,2,256,16]{2,3,1,0:T(8,128)S(1)}, u32[]{:S(2)}) copy-start(f32[4,2,256,16]{2,3,1,0:T(8,128)S(1)} %multiply_multiply_fusion.2) | copy-start | bytes 393220
  23.5 2.5 %copy-start.45 = (f32[192]{0:T(256)S(1)}, f32[192]{0:T(256)}, u32[]{:S(2)}) copy-start(f32[192]{0:T(256)} %pad.69.clone) | copy-start | bytes 2308
  26.9 19.6 %all-to-all-start.1 = ((f32[32,24,128]{2,1,0:T(8,128)}), f32[32,24,128]{2,1,0:T(8,128)}, u32[]{:S(2)}, u32[]{:S(2)}) async-start(f32[32,24,128]{2,1,0:T(8,128)} %bitcast.19), calls=%async_computation.1 | async-start | bytes 786432 | tf_op jit(solution)/shard_map/all_to_all | solution.py:40
  48.6 14.6 %all-to-all-start.2 = ((f32[32,24,128]{2,1,0:T(8,128)}), f32[32,24,128]{2,1,0:T(8,128)}, u32[]{:S(2)}, u32[]{:S(2)}) async-start(f32[32,24,128]{2,1,0:T(8,128)} %pad_add_fusion.4), calls=%async_computation.2 | async-start | bytes 786432 | tf_op jit(solution)/shard_map/all_to_all | solution.py:46
  54.5 11.8 %copy-start.33 = (f32[4,2,256]{2,1,0:T(2,128)}, f32[4,2,256]{2,1,0:T(2,128)S(1)}, u32[]{:S(2)}) copy-start(f32[4,2,256]{2,1,0:T(2,128)S(1)} %reduce_sum.144) | copy-start | bytes 24580
  63.2 3.2 %copy-start.25 = (f32[256,136,1,1]{0,1,3,2:T(8,128)S(1)}, f32[256,136,1,1]{0,1,3,2:T(8,128)}, u32[]{:S(2)}) copy-start(f32[256,136,1,1]{0,1,3,2:T(8,128)} %constant.68) | copy-start | bytes 417796
  63.2 5.1 %copy-start.39 = (f32[4,2,256]{2,1,0:T(2,128)S(1)}, f32[4,2,256]{2,1,0:T(2,128)}, u32[]{:S(2)}) copy-start(f32[4,2,256]{2,1,0:T(2,128)} %reduce_window_sum.35) | copy-start | bytes 24580
  64.9 4.6 %copy-start.16 = (f32[512,4,128]{2,0,1:T(8,128)S(1)}, f32[512,4,128]{2,0,1:T(8,128)}, u32[]{:S(2)}) copy-start(f32[512,4,128]{2,0,1:T(8,128)} %copy_bitcast_fusion) | copy-start | bytes 3145732
  64.9 4.6 %copy-start.17 = (f32[4,2,256,128]{3,2,1,0:T(8,128)S(1)}, f32[4,2,256,128]{3,2,1,0:T(8,128)}, u32[]{:S(2)}) copy-start(f32[4,2,256,128]{3,2,1,0:T(8,128)} %fusion.68) | copy-start | bytes 3145732
  68.2 2.0 %copy-start.12 = (bf16[4,2,128,256]{3,2,1,0:T(8,128)(2,1)}, bf16[4,2,128,256]{3,2,1,0:T(8,128)(2,1)S(1)}, u32[]{:S(2)}) copy-start(bf16[4,2,128,256]{3,2,1,0:T(8,128)(2,1)S(1)} %convolution_convert_fusion.3) | copy-start | bytes 1572868
  69.5 0.7 copy-start.34
  69.5 1.3 copy-start.21
  75.3 3.2 %copy-start = (bf16[4,2,256,128]{3,2,1,0:T(8,128)(2,1)S(1)}, bf16[4,2,256,128]{3,2,1,0:T(8,128)(2,1)}, u32[]{:S(2)}) copy-start(bf16[4,2,256,128]{3,2,1,0:T(8,128)(2,1)} %get-tuple-element.17) | copy-start | bytes 1572868
  75.3 3.2 %copy-start.2 = (bf16[4,512,128]{2,1,0:T(8,128)(2,1)S(1)}, bf16[4,512,128]{2,1,0:T(8,128)(2,1)}, u32[]{:S(2)}) copy-start(bf16[4,512,128]{2,1,0:T(8,128)(2,1)} %copy-done.1) | copy-start | bytes 1572868
  75.3 3.2 %copy-start.22 = (f32[4,2,256,256]{2,3,1,0:T(8,128)S(1)}, f32[4,2,256,256]{2,3,1,0:T(8,128)}, u32[]{:S(2)}) copy-start(f32[4,2,256,256]{2,3,1,0:T(8,128)} %get-tuple-element.23) | copy-start | bytes 6291460
  75.3 3.2 %copy-start.32 = (f32[4,2,256]{2,1,0:T(2,128)S(1)}, f32[4,2,256]{2,1,0:T(2,128)}, u32[]{:S(2)}) copy-start(f32[4,2,256]{2,1,0:T(2,128)} %get-tuple-element.6) | copy-start | bytes 24580
  83.9 14.7 %all-to-all-start.3 = ((f32[32,24,128]{2,1,0:T(8,128)}), f32[32,24,128]{2,1,0:T(8,128)}, u32[]{:S(2)}, u32[]{:S(2)}) async-start(f32[32,24,128]{2,1,0:T(8,128)} %bitcast.38), calls=%async_computation.3 | async-start | bytes 786432 | tf_op jit(solution)/shard_map/all_to_all | solution.py:40
  88.5 6.0 %copy-start.19 = (f32[4,2,256,32]{2,3,1,0:T(8,128)S(1)}, f32[4,2,256,32]{2,3,1,0:T(8,128)}, u32[]{:S(2)}) copy-start(f32[4,2,256,32]{2,3,1,0:T(8,128)} %copy-done.18) | copy-start | bytes 786436
  90.5 5.1 %copy-start.11 = (bf16[4,512,128]{2,1,0:T(8,128)(2,1)S(1)}, bf16[4,512,128]{2,1,0:T(8,128)(2,1)}, u32[]{:S(2)}) copy-start(bf16[4,512,128]{2,1,0:T(8,128)(2,1)} %copy-done.10) | copy-start | bytes 1572868
  90.5 5.1 %copy-start.13 = (bf16[4,2,256,256]{2,3,1,0:T(8,128)(2,1)S(1)}, bf16[4,2,256,256]{2,3,1,0:T(8,128)(2,1)}, u32[]{:S(2)}) copy-start(bf16[4,2,256,256]{2,3,1,0:T(8,128)(2,1)} %fusion.6) | copy-start | bytes 3145732
  99.9 5.6 %copy-start.41 = (f32[512]{0:T(512)S(1)}, f32[512]{0:T(512)}, u32[]{:S(2)}) copy-start(f32[512]{0:T(512)} %param.15) | copy-start | bytes 6148
  100.8 15.1 %all-to-all-start.4 = ((f32[32,24,128]{2,1,0:T(8,128)}), f32[32,24,128]{2,1,0:T(8,128)}, u32[]{:S(2)}, u32[]{:S(2)}) async-start(f32[32,24,128]{2,1,0:T(8,128)} %pad_add_fusion), calls=%async_computation.4 | async-start | bytes 786432 | tf_op jit(solution)/shard_map/all_to_all | solution.py:46
  108.2 10.2 %copy-start.26 = (f32[256,136,1,1]{0,1,3,2:T(8,128)S(1)}, f32[256,136,1,1]{0,1,3,2:T(8,128)}, u32[]{:S(2)}) copy-start(f32[256,136,1,1]{0,1,3,2:T(8,128)} %constant.68) | copy-start | bytes 417796
  115.9 5.6 %copy-start.15 = (f32[4,2,256,128]{3,2,1,0:T(8,128)S(1)}, f32[4,2,256,128]{3,2,1,0:T(8,128)}, u32[]{:S(2)}) copy-start(f32[4,2,256,128]{3,2,1,0:T(8,128)} %fusion.69) | copy-start | bytes 3145732
  118.4 4.4 %copy-start.3 = (bf16[4,512,128]{2,1,0:T(8,128)(2,1)S(1)}, bf16[4,512,128]{2,1,0:T(8,128)(2,1)}, u32[]{:S(2)}) copy-start(bf16[4,512,128]{2,1,0:T(8,128)(2,1)} %copy-done.1) | copy-start | bytes 1572868
  122.8 0.9 copy-start.24
  123.3 2.7 %copy-start.29 = (bf16[128,16]{0,1:T(8,128)(2,1)S(1)}, bf16[128,16]{0,1:T(8,128)(2,1)}, u32[]{:S(2)}) copy-start(bf16[128,16]{0,1:T(8,128)(2,1)} %copy-done.28) | copy-start | bytes 12292
  123.4 2.7 %copy-start.31 = (bf16[128,16]{0,1:T(8,128)(2,1)S(1)}, bf16[128,16]{0,1:T(8,128)(2,1)}, u32[]{:S(2)}) copy-start(bf16[128,16]{0,1:T(8,128)(2,1)} %copy-done.30) | copy-start | bytes 12292
  123.7 3.4 %copy-start.9 = (bf16[4,512,128]{2,1,0:T(8,128)(2,1)S(1)}, bf16[4,512,128]{2,1,0:T(8,128)(2,1)}, u32[]{:S(2)}) copy-start(bf16[4,512,128]{2,1,0:T(8,128)(2,1)} %copy-done.8) | copy-start | bytes 1572868
  123.7 3.4 %copy-start.14 = (bf16[4,2,256,256]{2,3,1,0:T(8,128)(2,1)S(1)}, bf16[4,2,256,256]{2,3,1,0:T(8,128)(2,1)}, u32[]{:S(2)}) copy-start(bf16[4,2,256,256]{2,3,1,0:T(8,128)(2,1)} %fusion.6) | copy-start | bytes 3145732
  127.1 1.0 copy-start.7
  127.1 1.0 copy-start.44
  127.1 1.2 copy-start.48
  127.6 11.6 %copy-start.5 = (bf16[512,512]{1,0:T(8,128)(2,1)S(1)}, bf16[512,512]{1,0:T(8,128)(2,1)}, u32[]{:S(2)}) copy-start(bf16[512,512]{1,0:T(8,128)(2,1)} %param.11) | copy-start | bytes 1572868
  127.6 11.5 %copy-start.36 = (f32[1,512]{1,0:T(1,128)S(1)}, f32[1,512]{1,0:T(1,128)}, u32[]{:S(2)}) copy-start(f32[1,512]{1,0:T(1,128)} %copy-done.35) | copy-start | bytes 6148
  127.6 11.5 %copy-start.38 = (f32[1,512]{1,0:T(1,128)S(1)}, f32[1,512]{1,0:T(1,128)}, u32[]{:S(2)}) copy-start(f32[1,512]{1,0:T(1,128)} %copy-done.37) | copy-start | bytes 6148
  127.7 11.5 %copy-start.42 = (f32[512]{0:T(512)S(1)}, f32[512]{0:T(512)}, u32[]{:S(2)}) copy-start(f32[512]{0:T(512)} %param.15) | copy-start | bytes 6148
  127.7 11.5 %copy-start.46 = (f32[512]{0:T(512)S(1)}, f32[512]{0:T(512)}, u32[]{:S(2)}) copy-start(f32[512]{0:T(512)} %multiply_multiply_fusion.5) | copy-start | bytes 6148
  127.7 11.5 %copy-start.47 = (f32[512]{0:T(512)S(1)}, f32[512]{0:T(512)}, u32[]{:S(2)}) copy-start(f32[512]{0:T(512)} %multiply_multiply_fusion.4) | copy-start | bytes 6148
  129.0 10.1 %all-to-all-start.5 = ((f32[8,2,512]{2,1,0:T(2,128)}), f32[8,2,512]{2,1,0:T(2,128)S(1)}, u32[]{:S(2)}, u32[]{:S(2)}) async-start(f32[8,2,512]{2,1,0:T(2,128)} %broadcast_in_dim.19), calls=%async_computation.5 | async-start | bytes 65536 | tf_op jit(solution)/shard_map/all_to_all | solution.py:54

commit v6 on v5

--- a/solution.py
+++ b/solution.py
@@ -110,8 +110,8 @@
 
 
 def spread_pairs(half):
-    spread = jnp.asarray(pair_tables()[1])
-    return jnp.einsum("...pd,fp->...fd", half, spread, precision=HIGHEST_PREC)
+    spread = jnp.asarray(pair_tables()[1], jnp.bfloat16)
+    return product_of("...pd,fp->...fd", half.astype(jnp.bfloat16), spread).astype(jnp.bfloat16)
 
 
 def forward_blocks(q_normed, k_normed, values, sign_pair):
@@ -137,7 +137,7 @@
 
 
 def finish_forward(weights, values, q_feats, key_state, key_total):
-    state_half = key_state.astype(jnp.bfloat16)
+    state_half = key_state
     numerator = product_of("...ij,...jd->...id", weights, values) + product_of(
         "...ir,...rd->...id", q_feats, state_half
     )
@@ -183,7 +183,7 @@
 
 
 def finish_backward(values, k_feats, later_state, later_total, v_diag):
-    later_half = later_state.astype(jnp.bfloat16)
+    later_half = later_state
     kf_grad = product_of("...jd,...rd->...jr", values, later_half) + later_total[..., None, :]
     v_grad = v_diag + product_of("...jr,...rd->...jd", k_feats, later_half)
     return (kf_grad, v_grad)

time: 142 us -> 138 us (0.972)
  matrix products: 31.2 us -> 27.1 us
  waiting for transfers between devices: 24.4 us -> 27.2 us
  local copies, waits for them, and re-layouts: 19.4 us -> 17.2 us
    dot_general x2 -> x0, matrix products: 4.93 us -> none  [spread_pairs(): return jnp.einsum('...pd,fp->...fd', half, spread, precision=HIGHEST_PREC)]
    all_to_all x2, waiting for transfers between devices: 8.79 us -> 11.8 us  [carried_in(): lax.all_to_all(shifted, axis, 0, 0, tiled=True)]
    rev x2 -> x1, local copies, waits for them, and re-layouts: 3.06 us -> 1.13 us  [after_blocks(): rev_u = jnp.flip(jnp.cumsum(jnp.flip(block_u, -3), axis=-3), -3)]
    dot_general x14 -> x16, matrix products: 22.9 us -> 23.7 us  [product_of(): return jnp.einsum(spec, lhs, rhs, preferred_element_type=jnp.float32)]
    unnamed x102 -> x90, local copies, waits for them, and re-layouts: 4.66 us -> 4.77 us
  transfers between devices with their start and end apart: 6 -> 6, of which waited for: 6 -> 6; matrix products, arithmetic and copies ran while one was open for 21% -> 20% of each run, Pallas kernels for 0% -> 0%
where the time goes in v6:
time: 138 us; the launch traced here: 137 us
  starting transfers between devices  35.2 us (26%)
  other arithmetic  28.8 us (21%)
  waiting for transfers between devices  27.2 us (20%)
  matrix products  27.1 us (20%)
  local copies, waits for them, and re-layouts  17.2 us (12%)
  between operations  1.48 us (1%)
    dot_general x16, matrix products, product_of(): return jnp.einsum(spec, lhs, rhs, preferred_element_type=jnp.float32)  23.7 us
    all_to_all x2, starting transfers between devices, carried_in(): mine = lax.all_to_all(stacked, axis, 0, 0, tiled=True)  13.8 us
    all_to_all x2, starting transfers between devices, head_sum(): gathered = lax.all_to_all(spread, axis, 0, 0, tiled=True)  12.3 us
    all_to_all x2, waiting for transfers between devices, carried_in(): lax.all_to_all(shifted, axis, 0, 0, tiled=True)  11.8 us
    all_to_all x2, starting transfers between devices, carried_in(): lax.all_to_all(shifted, axis, 0, 0, tiled=True)  9.08 us
    all_to_all x2, waiting for transfers between devices, carried_in(): mine = lax.all_to_all(stacked, axis, 0, 0, tiled=True)  8.47 us
    all_to_all x2, waiting for transfers between devices, head_sum(): gathered = lax.all_to_all(spread, axis, 0, 0, tiled=True)  6.98 us
    reduce_sum x2, other arithmetic, sketch_back(): sketch_grad = jnp.sum(symmetric * sketched[..., None, :], axis=-1)  6.29 us
  transfers between devices with their start and end apart: 6, of which 6 were waited for; matrix products, arithmetic and copies ran while one was open for 20% of the time, Pallas kernels for 0%

profile of v6, /device:TPU:1, one launch (start us, length us, event | category | flops | bytes accessed | tf_op | source)
XLA Modules:
  0.0 137.1 jit_solution(6737804437171718617)
XLA Ops:
  0.6 1.3 fusion.16
  1.9 1.3 fusion.25
  3.2 0.6 broadcast_in_dim.17
  3.9 9.0 %all-to-all-start = ((f32[8,2,512]{2,1,0:T(2,128)}), f32[8,2,512]{2,1,0:T(2,128)S(1)}, u32[]{:S(2)}, u32[]{:S(2)}) async-start(f32[8,2,512]{2,1,0:T(2,128)} %broadcast_in_dim.17), calls=%async_computation | async-start | bytes 65536 | tf_op jit(solution)/shard_map/all_to_all | solution.py:54
  12.9 0.7 fusion.48
  13.6 1.2 reshape.169
  14.8 1.1 copy_bitcast_fusion
  16.0 0.7 pad.69.clone
  16.6 0.6 iota_compare_fusion
  17.3 2.5 %all-to-all-done = f32[8,2,512]{2,1,0:T(2,128)S(1)} async-done(((f32[8,2,512]{2,1,0:T(2,128)}), f32[8,2,512]{2,1,0:T(2,128)S(1)}, u32[]{:S(2)}, u32[]{:S(2)}) %all-to-all-start) | async-done | bytes 32800 | tf_op jit(solution)/shard_map/all_to_all | solution.py:54
  20.3 0.8 copy-done.8
  21.3 0.7 copy-done.18
  22.8 0.5 copy-done.10
  23.6 1.0 convert_reduce_fusion
  24.7 1.4 %fusion.63 = (f32[4,136,128]{2,1,0:T(8,128)S(1)}, f32[4,2,136,128]{3,2,1,0:T(8,128)}) fusion(bf16[4,2,256,128]{3,2,1,0:T(8,128)(2,1)S(1)} %bitcast.168, bf16[4,2,256,256]{2,3,1,0:T(8,128)(2,1)S(1)} %bitcast.160, bf16[256,136,1,1]{0,1,3,2:T(8,128)(2,1)S(1)} %copy-done.25), kind=kOutput, calls=%fused_computation.141 | convolution fusion | flops 214257664 | bytes 2478080 | tf_op jit(solution)/shard_map/...jr,...jd->...rd/dot_general | solution.py:60
  26.1 0.8 maximum_maximum_fusion
  26.9 9.2 %all-to-all-start.1 = ((f32[32,24,128]{2,1,0:T(8,128)}), f32[32,24,128]{2,1,0:T(8,128)}, u32[]{:S(2)}, u32[]{:S(2)}) async-start(f32[32,24,128]{2,1,0:T(8,128)} %bitcast.19), calls=%async_computation.1 | async-start | bytes 786432 | tf_op jit(solution)/shard_map/all_to_all | solution.py:40
  36.2 0.6 multiply_multiply_fusion.5
  36.8 3.7 %convert_reduce_fusion.2 = (f32[4,2,256]{2,1,0:T(2,128)}, bf16[4,2,256,256]{2,3,1,0:T(8,128)(2,1)S(1)}, f32[4,2,256,256]{2,3,1,0:T(8,128)}) fusion(pred[256,256]{0,1:T(8,128)(4,1)} %iota_compare_fusion, bf16[4,2,256,128]{3,2,1,0:T(8,128)(2,1)} %bitcast.173, bf16[4,2,256,128]{3,2,1,0:T(8,128)(2,1)} %bitcast.176), kind=kOutput, calls=%fused_computation.18 | convolution fusion | flops 137885696 | bytes 4268032 | tf_op jit(solution)/shard_map/...id,...jd->...ij/dot_general | solution.py:60
  40.4 6.1 %all-to-all-done.1 = f32[32,24,128]{2,1,0:T(8,128)} async-done(((f32[32,24,128]{2,1,0:T(8,128)}), f32[32,24,128]{2,1,0:T(8,128)}, u32[]{:S(2)}, u32[]{:S(2)}) %all-to-all-start.1) | async-done | bytes 393248 | tf_op jit(solution)/shard_map/all_to_all | solution.py:40
  46.5 1.0 slice.110
  47.9 0.8 pad_add_fusion.4
  48.6 4.4 %all-to-all-start.2 = ((f32[32,24,128]{2,1,0:T(8,128)}), f32[32,24,128]{2,1,0:T(8,128)}, u32[]{:S(2)}, u32[]{:S(2)}) async-start(f32[32,24,128]{2,1,0:T(8,128)} %pad_add_fusion.4), calls=%async_computation.2 | async-start | bytes 786432 | tf_op jit(solution)/shard_map/all_to_all | solution.py:46
  53.0 0.6 multiply_multiply_fusion.4
  53.6 0.9 reduce_sum.144
  54.6 0.6 reduce_window_sum.35
  55.2 2.5 %fusion.66 = f32[4,2,256,128]{3,2,1,0:T(8,128)} fusion(bf16[4,2,256,256]{2,3,1,0:T(8,128)(2,1)S(1)} %get-tuple-element.9, bf16[4,2,256,128]{3,2,1,0:T(8,128)(2,1)} %bitcast.169), kind=kOutput, calls=%fused_computation.144 | convolution fusion | flops 134217728 | bytes 2621440 | tf_op jit(solution)/shard_map/...ij,...jd->...id/dot_general | solution.py:60
  57.7 5.5 %all-to-all-done.2 = f32[32,24,128]{2,1,0:T(8,128)} async-done(((f32[32,24,128]{2,1,0:T(8,128)}), f32[32,24,128]{2,1,0:T(8,128)}, u32[]{:S(2)}, u32[]{:S(2)}) %all-to-all-start.2) | async-done | bytes 393248 | tf_op jit(solution)/shard_map/all_to_all | solution.py:46
  63.2 0.8 slice_bitcast_fusion.1
  64.0 1.1 slice.116
  65.1 1.3 fusion.15
  66.4 0.7 add_subtract_fusion.1
  67.1 0.5 fusion.46
  68.1 0.6 multiply_reduce_fusion
  68.8 0.6 multiply_divide_fusion
  69.4 1.4 %divide_convert_fusion = (bf16[4,2,256,128]{3,2,1,0:T(8,128)(2,1)}, bf16[4,2,256,128]{3,2,1,0:T(8,128)(2,1)}) fusion(f32[4,2,256]{2,1,0:T(2,128)S(1)} %get-tuple-element.7, f32[4,2,256,128]{3,2,1,0:T(8,128)S(1)} %get-tuple-element.27, bf16[512,512]{1,0:T(8,128)(2,1)S(1)} %copy-done.21), kind=kLoop, calls=%fused_computation.67 | loop fusion | flops 1310720 | bytes 2629632 | tf_op jit(solution)/shard_map/convert_element_type | solution.py:167
  70.8 3.2 %fusion.64 = (f32[4,136,128]{2,1,0:T(8,128)}, f32[4,2,136,128]{3,2,1,0:T(8,128)}) fusion(bf16[4,2,256,128]{3,2,1,0:T(8,128)(2,1)} %get-tuple-element.17, bf16[4,2,256,256]{2,3,1,0:T(8,128)(2,1)S(1)} %bitcast.158, bf16[256,136,1,1]{0,1,3,2:T(8,128)(2,1)} %constant.67), kind=kOutput, calls=%fused_computation.142 | convolution fusion | flops 214257664 | bytes 2478080 | tf_op jit(solution)/shard_map/...ir,...id->...rd/dot_general | solution.py:60
  74.0 3.2 %multiply_add_fusion = f32[4,2,256,256]{2,3,1,0:T(8,128)} fusion(bf16[4,2,256,128]{3,2,1,0:T(8,128)(2,1)} %get-tuple-element.17, bf16[4,2,128,256]{3,2,1,0:T(8,128)(2,1)} %copy-done.12, f32[4,2,256]{2,1,0:T(2,128)S(1)} %add_subtract_fusion.1, f32[4,2,256]{2,1,0:T(2,128)} %get-tuple-element.6), kind=kOutput, calls=%fused_computation.17 | convolution fusion | flops 135266304 | bytes 3162112 | tf_op jit(solution)/shard_map/...id,...rd->...ir/dot_general | solution.py:60
  77.2 2.6 %fusion.6 = bf16[4,2,256,256]{2,3,1,0:T(8,128)(2,1)} fusion(f32[4,2,256,256]{2,3,1,0:T(8,128)S(1)} %copy-done.22, bf16[4,2,256,128]{3,2,1,0:T(8,128)(2,1)S(1)} %copy-done, bf16[4,2,256,128]{3,2,1,0:T(8,128)(2,1)S(1)} %bitcast.170, f32[4,2,256]{2,1,0:T(2,128)S(1)} %copy-done.28, pred[256,256]{0,1:T(8,128)(4,1)} %iota_compare_fusion), kind=kOutput, calls=%fused_computation.10 | convolution fusion | flops 138936320 | bytes 4268032 | tf_op jit(solution)/shard_map/...id,...jd->...ij/dot_general | solution.py:60
  79.8 0.9 fusion.44
  80.7 1.8 %maximum_maximum_fusion.1 = f32[4,192,128]{2,1,0:T(8,128)} fusion(f32[4,2,128]{2,1,0:T(2,128)S(1)} %reshape.179, f32[4,136,128]{2,1,0:T(8,128)} %get-tuple-element.28, f32[192]{0:T(256)} %pad.69.clone), kind=kLoop, calls=%fused_computation.73 | loop fusion | flops 196608 | bytes 676608 | tf_op jit(solution)/shard_map/concatenate | solution.py:32
  82.6 4.6 %all-to-all-start.3 = ((f32[32,24,128]{2,1,0:T(8,128)}), f32[32,24,128]{2,1,0:T(8,128)}, u32[]{:S(2)}, u32[]{:S(2)}) async-start(f32[32,24,128]{2,1,0:T(8,128)} %bitcast.38), calls=%async_computation.3 | async-start | bytes 786432 | tf_op jit(solution)/shard_map/all_to_all | solution.py:40
  87.1 1.1 rev.14
  88.3 0.8 fusion.65
  89.1 4.0 %fusion.10 = f32[4,2,256,16]{2,3,1,0:T(8,128)S(1)} fusion(f32[4,2,256,16,16]{2,4,3,1,0:T(8,128)} %bitcast.166, f32[4,2,256,16]{2,3,1,0:T(8,128)S(1)} %multiply_multiply_fusion.3), kind=kLoop, calls=%fused_computation.16 | loop fusion | flops 1540096 | bytes 2359296 | tf_op jit(solution)/shard_map/reduce_sum | solution.py:88
  93.2 1.0 fusion.36
  94.7 2.4 %all-to-all-done.3 = f32[32,24,128]{2,1,0:T(8,128)} async-done(((f32[32,24,128]{2,1,0:T(8,128)}), f32[32,24,128]{2,1,0:T(8,128)}, u32[]{:S(2)}, u32[]{:S(2)}) %all-to-all-start.3) | async-done | bytes 393248 | tf_op jit(solution)/shard_map/all_to_all | solution.py:40
  97.1 1.0 slice.118
  98.5 0.8 pad_add_fusion
  99.3 4.7 %all-to-all-start.4 = ((f32[32,24,128]{2,1,0:T(8,128)}), f32[32,24,128]{2,1,0:T(8,128)}, u32[]{:S(2)}, u32[]{:S(2)}) async-start(f32[32,24,128]{2,1,0:T(8,128)} %pad_add_fusion), calls=%async_computation.4 | async-start | bytes 786432 | tf_op jit(solution)/shard_map/all_to_all | solution.py:46
  104.0 1.3 fusion.24
  105.5 2.5 %fusion.67 = f32[4,2,256,128]{3,2,1,0:T(8,128)} fusion(bf16[4,2,256,256]{2,3,1,0:T(8,128)(2,1)S(1)} %get-tuple-element.9, bf16[4,2,256,128]{3,2,1,0:T(8,128)(2,1)} %get-tuple-element.17), kind=kOutput, calls=%fused_computation.145 | convolution fusion | flops 134217728 | bytes 2621440 | tf_op jit(solution)/shard_map/...ij,...id->...jd/dot_general | solution.py:60
  108.0 6.3 %all-to-all-done.4 = f32[32,24,128]{2,1,0:T(8,128)} async-done(((f32[32,24,128]{2,1,0:T(8,128)}), f32[32,24,128]{2,1,0:T(8,128)}, u32[]{:S(2)}, u32[]{:S(2)}) %all-to-all-start.4) | async-done | bytes 393248 | tf_op jit(solution)/shard_map/all_to_all | solution.py:46
  114.3 0.8 slice_bitcast_fusion
  115.1 1.0 slice.124
  116.1 1.3 subtract_convert_fusion
  117.8 1.3 fusion.12
  120.0 2.3 %fusion.8 = f32[4,2,256,16]{2,3,1,0:T(8,128)S(1)} fusion(f32[4,2,256,16,16]{2,4,3,1,0:T(8,128)S(1)} %bitcast.167, f32[4,2,256,16]{2,3,1,0:T(8,128)S(1)} %copy-done.24), kind=kLoop, calls=%fused_computation.13 | loop fusion | flops 1540096 | bytes 2359296 | tf_op jit(solution)/shard_map/reduce_sum | solution.py:88
  122.4 1.0 fusion.39
  124.7 0.6 broadcast_in_dim.19
  125.3 3.3 %all-to-all-start.5 = ((f32[8,2,512]{2,1,0:T(2,128)}), f32[8,2,512]{2,1,0:T(2,128)S(1)}, u32[]{:S(2)}, u32[]{:S(2)}) async-start(f32[8,2,512]{2,1,0:T(2,128)} %broadcast_in_dim.19), calls=%async_computation.5 | async-start | bytes 65536 | tf_op jit(solution)/shard_map/all_to_all | solution.py:54
  128.6 2.3 %copy_bitcast_fusion.1 = (bf16[512,512]{1,0:T(8,128)(2,1)}, bf16[512,512]{1,0:T(8,128)(2,1)}) fusion(bf16[4,64,8,128]{3,2,1,0:T(8,128)(2,1)} %bitcast.183, bf16[4,64,8,128]{3,2,1,0:T(8,128)(2,1)} %bitcast.179), kind=kLoop, calls=%fused_computation.70 | loop fusion | bytes 2097152 | tf_op jit(solution)/shard_map/convert_element_type | solution.py:280
  130.9 4.5 %all-to-all-done.5 = f32[8,2,512]{2,1,0:T(2,128)S(1)} async-done(((f32[8,2,512]{2,1,0:T(2,128)}), f32[8,2,512]{2,1,0:T(2,128)S(1)}, u32[]{:S(2)}, u32[]{:S(2)}) %all-to-all-start.5) | async-done | bytes 32800 | tf_op jit(solution)/shard_map/all_to_all | solution.py:54
  135.5 1.6 %fusion.22 = (bf16[512,512]{1,0:T(8,128)(2,1)}, bf16[512,512]{1,0:T(8,128)(2,1)}) fusion(bf16[512,512]{1,0:T(8,128)(2,1)S(1)} %copy-done.5, f32[4,64,8,128]{3,2,1,0:T(8,128)S(1)} %bitcast.163, f32[512]{0:T(512)S(1)} %bitcast.197, f32[512]{0:T(512)S(1)} %copy-done.41, f32[512]{0:T(512)S(1)} %copy-done.37, f32[512]{0:T(512)S(1)} %bitcast.191, ...), kind=kLoop, calls=%fused_computation.50 | loop fusion | flops 4194304 | bytes 4210688 | tf_op jit(solution)/shard_map/convert_element_type | solution.py:201
  (136 shorter events, 6.4 us)
Async XLA Ops:
  0.6 14.2 %copy-start.20 = (bf16[512,512]{1,0:T(8,128)(2,1)S(1)}, bf16[512,512]{1,0:T(8,128)(2,1)}, u32[]{:S(2)}) copy-start(bf16[512,512]{1,0:T(8,128)(2,1)} %param.14) | copy-start | bytes 1572868
  1.9 17.9 %copy-start.4 = (bf16[512,512]{1,0:T(8,128)(2,1)S(1)}, bf16[512,512]{1,0:T(8,128)(2,1)}, u32[]{:S(2)}) copy-start(bf16[512,512]{1,0:T(8,128)(2,1)} %param.11) | copy-start | bytes 1572868
  1.9 17.9 %copy-start.36 = (f32[512]{0:T(512)S(1)}, f32[512]{0:T(512)}, u32[]{:S(2)}) copy-start(f32[512]{0:T(512)} %param.15) | copy-start | bytes 6148
  3.9 15.9 %all-to-all-start = ((f32[8,2,512]{2,1,0:T(2,128)}), f32[8,2,512]{2,1,0:T(2,128)S(1)}, u32[]{:S(2)}, u32[]{:S(2)}) async-start(f32[8,2,512]{2,1,0:T(2,128)} %broadcast_in_dim.17), calls=%async_computation | async-start | bytes 65536 | tf_op jit(solution)/shard_map/all_to_all | solution.py:54
  14.8 9.8 %copy-start.1 = (bf16[4,512,128]{2,1,0:T(8,128)(2,1)}, bf16[4,512,128]{2,1,0:T(8,128)(2,1)S(1)}, u32[]{:S(2)}) copy-start(bf16[4,512,128]{2,1,0:T(8,128)(2,1)S(1)} %copy.71) | copy-start | bytes 1572868
  19.8 16.4 %copy-start.33 = (f32[1,512]{1,0:T(1,128)}, f32[1,512]{1,0:T(1,128)S(1)}, u32[]{:S(2)}) copy-start(f32[1,512]{1,0:T(1,128)S(1)} %get-tuple-element.22) | copy-start | bytes 6148
  19.8 33.2 %copy-start.31 = (f32[1,512]{1,0:T(1,128)}, f32[1,512]{1,0:T(1,128)S(1)}, u32[]{:S(2)}) copy-start(f32[1,512]{1,0:T(1,128)S(1)} %get-tuple-element.21) | copy-start | bytes 6148
  19.8 2.2 %copy-start.6 = (bf16[512,512]{1,0:T(8,128)(2,1)S(1)}, bf16[512,512]{1,0:T(8,128)(2,1)}, u32[]{:S(2)}) copy-start(bf16[512,512]{1,0:T(8,128)(2,1)} %param.12) | copy-start | bytes 1572868
  19.8 2.2 %copy-start.38 = (f32[512]{0:T(512)S(1)}, f32[512]{0:T(512)}, u32[]{:S(2)}) copy-start(f32[512]{0:T(512)} %param.16) | copy-start | bytes 6148
  20.2 0.8 copy-start.8
  21.3 0.7 copy-start.18
  22.5 0.8 copy-start.10
  22.5 2.2 %copy-start.25 = (bf16[256,136,1,1]{0,1,3,2:T(8,128)(2,1)S(1)}, bf16[256,136,1,1]{0,1,3,2:T(8,128)(2,1)}, u32[]{:S(2)}) copy-start(bf16[256,136,1,1]{0,1,3,2:T(8,128)(2,1)} %constant.67) | copy-start | bytes 208900
  23.3 2.8 %copy-start.23 = (f32[4,2,256,16]{2,3,1,0:T(8,128)}, f32[4,2,256,16]{2,3,1,0:T(8,128)S(1)}, u32[]{:S(2)}) copy-start(f32[4,2,256,16]{2,3,1,0:T(8,128)S(1)} %multiply_multiply_fusion.2) | copy-start | bytes 393220
  23.6 2.5 %copy-start.40 = (f32[192]{0:T(256)S(1)}, f32[192]{0:T(256)}, u32[]{:S(2)}) copy-start(f32[192]{0:T(256)} %pad.69.clone) | copy-start | bytes 2308
  26.9 19.6 %all-to-all-start.1 = ((f32[32,24,128]{2,1,0:T(8,128)}), f32[32,24,128]{2,1,0:T(8,128)}, u32[]{:S(2)}, u32[]{:S(2)}) async-start(f32[32,24,128]{2,1,0:T(8,128)} %bitcast.19), calls=%async_computation.1 | async-start | bytes 786432 | tf_op jit(solution)/shard_map/all_to_all | solution.py:40
  48.6 14.6 %all-to-all-start.2 = ((f32[32,24,128]{2,1,0:T(8,128)}), f32[32,24,128]{2,1,0:T(8,128)}, u32[]{:S(2)}, u32[]{:S(2)}) async-start(f32[32,24,128]{2,1,0:T(8,128)} %pad_add_fusion.4), calls=%async_computation.2 | async-start | bytes 786432 | tf_op jit(solution)/shard_map/all_to_all | solution.py:46
  54.6 11.8 %copy-start.29 = (f32[4,2,256]{2,1,0:T(2,128)}, f32[4,2,256]{2,1,0:T(2,128)S(1)}, u32[]{:S(2)}) copy-start(f32[4,2,256]{2,1,0:T(2,128)S(1)} %reduce_sum.144) | copy-start | bytes 24580
  63.2 3.2 %copy-start.35 = (f32[4,2,256]{2,1,0:T(2,128)S(1)}, f32[4,2,256]{2,1,0:T(2,128)}, u32[]{:S(2)}) copy-start(f32[4,2,256]{2,1,0:T(2,128)} %reduce_window_sum.35) | copy-start | bytes 24580
  63.2 4.4 %copy-start.26 = (bf16[256,136,1,1]{0,1,3,2:T(8,128)(2,1)S(1)}, bf16[256,136,1,1]{0,1,3,2:T(8,128)(2,1)}, u32[]{:S(2)}) copy-start(bf16[256,136,1,1]{0,1,3,2:T(8,128)(2,1)} %constant.68) | copy-start | bytes 208900
  64.0 4.1 %copy-start.16 = (f32[512,4,128]{2,0,1:T(8,128)S(1)}, f32[512,4,128]{2,0,1:T(8,128)}, u32[]{:S(2)}) copy-start(f32[512,4,128]{2,0,1:T(8,128)} %copy_bitcast_fusion) | copy-start | bytes 3145732
  64.0 4.1 %copy-start.17 = (f32[4,2,256,128]{3,2,1,0:T(8,128)S(1)}, f32[4,2,256,128]{3,2,1,0:T(8,128)}, u32[]{:S(2)}) copy-start(f32[4,2,256,128]{3,2,1,0:T(8,128)} %fusion.66) | copy-start | bytes 3145732
  68.0 0.8 copy-start.12
  68.0 0.8 copy-start.30
  68.1 1.4 %copy-start.21 = (bf16[512,512]{1,0:T(8,128)(2,1)S(1)}, bf16[512,512]{1,0:T(8,128)(2,1)}, u32[]{:S(2)}) copy-start(bf16[512,512]{1,0:T(8,128)(2,1)} %param.14) | copy-start | bytes 1572868
  74.0 3.2 %copy-start = (bf16[4,2,256,128]{3,2,1,0:T(8,128)(2,1)S(1)}, bf16[4,2,256,128]{3,2,1,0:T(8,128)(2,1)}, u32[]{:S(2)}) copy-start(bf16[4,2,256,128]{3,2,1,0:T(8,128)(2,1)} %get-tuple-element.17) | copy-start | bytes 1572868
  74.0 3.2 %copy-start.2 = (bf16[4,512,128]{2,1,0:T(8,128)(2,1)S(1)}, bf16[4,512,128]{2,1,0:T(8,128)(2,1)}, u32[]{:S(2)}) copy-start(bf16[4,512,128]{2,1,0:T(8,128)(2,1)} %copy-done.1) | copy-start | bytes 1572868
  74.0 3.2 %copy-start.22 = (f32[4,2,256,256]{2,3,1,0:T(8,128)S(1)}, f32[4,2,256,256]{2,3,1,0:T(8,128)}, u32[]{:S(2)}) copy-start(f32[4,2,256,256]{2,3,1,0:T(8,128)} %get-tuple-element.23) | copy-start | bytes 6291460
  74.0 3.2 %copy-start.28 = (f32[4,2,256]{2,1,0:T(2,128)S(1)}, f32[4,2,256]{2,1,0:T(2,128)}, u32[]{:S(2)}) copy-start(f32[4,2,256]{2,1,0:T(2,128)} %get-tuple-element.6) | copy-start | bytes 24580
  82.6 14.6 %all-to-all-start.3 = ((f32[32,24,128]{2,1,0:T(8,128)}), f32[32,24,128]{2,1,0:T(8,128)}, u32[]{:S(2)}, u32[]{:S(2)}) async-start(f32[32,24,128]{2,1,0:T(8,128)} %bitcast.38), calls=%async_computation.3 | async-start | bytes 786432 | tf_op jit(solution)/shard_map/all_to_all | solution.py:40
  87.1 6.0 %copy-start.19 = (f32[4,2,256,32]{2,3,1,0:T(8,128)S(1)}, f32[4,2,256,32]{2,3,1,0:T(8,128)}, u32[]{:S(2)}) copy-start(f32[4,2,256,32]{2,3,1,0:T(8,128)} %copy-done.18) | copy-start | bytes 786436
  89.1 5.1 %copy-start.11 = (bf16[4,512,128]{2,1,0:T(8,128)(2,1)S(1)}, bf16[4,512,128]{2,1,0:T(8,128)(2,1)}, u32[]{:S(2)}) copy-start(bf16[4,512,128]{2,1,0:T(8,128)(2,1)} %copy-done.10) | copy-start | bytes 1572868
  89.1 5.1 %copy-start.13 = (bf16[4,2,256,256]{2,3,1,0:T(8,128)(2,1)S(1)}, bf16[4,2,256,256]{2,3,1,0:T(8,128)(2,1)}, u32[]{:S(2)}) copy-start(bf16[4,2,256,256]{2,3,1,0:T(8,128)(2,1)} %fusion.6) | copy-start | bytes 3145732
  98.4 5.6 %copy-start.37 = (f32[512]{0:T(512)S(1)}, f32[512]{0:T(512)}, u32[]{:S(2)}) copy-start(f32[512]{0:T(512)} %param.15) | copy-start | bytes 6148
  99.3 15.0 %all-to-all-start.4 = ((f32[32,24,128]{2,1,0:T(8,128)}), f32[32,24,128]{2,1,0:T(8,128)}, u32[]{:S(2)}, u32[]{:S(2)}) async-start(f32[32,24,128]{2,1,0:T(8,128)} %pad_add_fusion), calls=%async_computation.4 | async-start | bytes 786432 | tf_op jit(solution)/shard_map/all_to_all | solution.py:46
  105.5 11.9 %copy-start.27 = (bf16[256,136,1,1]{0,1,3,2:T(8,128)(2,1)S(1)}, bf16[256,136,1,1]{0,1,3,2:T(8,128)(2,1)}, u32[]{:S(2)}) copy-start(bf16[256,136,1,1]{0,1,3,2:T(8,128)(2,1)} %constant.68) | copy-start | bytes 208900
  114.3 3.5 %copy-start.15 = (f32[4,2,256,128]{3,2,1,0:T(8,128)S(1)}, f32[4,2,256,128]{3,2,1,0:T(8,128)}, u32[]{:S(2)}) copy-start(f32[4,2,256,128]{3,2,1,0:T(8,128)} %fusion.67) | copy-start | bytes 3145732
  117.4 1.7 %copy-start.3 = (bf16[4,512,128]{2,1,0:T(8,128)(2,1)S(1)}, bf16[4,512,128]{2,1,0:T(8,128)(2,1)}, u32[]{:S(2)}) copy-start(bf16[4,512,128]{2,1,0:T(8,128)(2,1)} %copy-done.1) | copy-start | bytes 1572868
  119.1 0.9 copy-start.24
  120.0 3.3 %copy-start.9 = (bf16[4,512,128]{2,1,0:T(8,128)(2,1)S(1)}, bf16[4,512,128]{2,1,0:T(8,128)(2,1)}, u32[]{:S(2)}) copy-start(bf16[4,512,128]{2,1,0:T(8,128)(2,1)} %copy-done.8) | copy-start | bytes 1572868
  120.0 3.3 %copy-start.14 = (bf16[4,2,256,256]{2,3,1,0:T(8,128)(2,1)S(1)}, bf16[4,2,256,256]{2,3,1,0:T(8,128)(2,1)}, u32[]{:S(2)}) copy-start(bf16[4,2,256,256]{2,3,1,0:T(8,128)(2,1)} %fusion.6) | copy-start | bytes 3145732
  123.4 1.0 copy-start.7
  123.4 1.0 copy-start.39
  123.9 11.6 %copy-start.5 = (bf16[512,512]{1,0:T(8,128)(2,1)S(1)}, bf16[512,512]{1,0:T(8,128)(2,1)}, u32[]{:S(2)}) copy-start(bf16[512,512]{1,0:T(8,128)(2,1)} %param.11) | copy-start | bytes 1572868
  123.9 11.6 %copy-start.32 = (f32[1,512]{1,0:T(1,128)S(1)}, f32[1,512]{1,0:T(1,128)}, u32[]{:S(2)}) copy-start(f32[1,512]{1,0:T(1,128)} %copy-done.31) | copy-start | bytes 6148
  123.9 11.6 %copy-start.34 = (f32[1,512]{1,0:T(1,128)S(1)}, f32[1,512]{1,0:T(1,128)}, u32[]{:S(2)}) copy-start(f32[1,512]{1,0:T(1,128)} %copy-done.33) | copy-start | bytes 6148
  123.9 11.6 %copy-start.41 = (f32[512]{0:T(512)S(1)}, f32[512]{0:T(512)}, u32[]{:S(2)}) copy-start(f32[512]{0:T(512)} %multiply_multiply_fusion.5) | copy-start | bytes 6148
  123.9 11.6 %copy-start.42 = (f32[512]{0:T(512)S(1)}, f32[512]{0:T(512)}, u32[]{:S(2)}) copy-start(f32[512]{0:T(512)} %multiply_multiply_fusion.4) | copy-start | bytes 6148
  125.3 10.1 %all-to-all-start.5 = ((f32[8,2,512]{2,1,0:T(2,128)}), f32[8,2,512]{2,1,0:T(2,128)S(1)}, u32[]{:S(2)}, u32[]{:S(2)}) async-start(f32[8,2,512]{2,1,0:T(2,128)} %broadcast_in_dim.19), calls=%async_computation.5 | async-start | bytes 65536 | tf_op jit(solution)/shard_map/all_to_all | solution.py:54

commit v7 on v6

--- a/solution.py
+++ b/solution.py
@@ -106,12 +106,14 @@
 
 def pick_pairs(feats):
     pick = jnp.asarray(pair_tables()[0], jnp.bfloat16)
-    return product_of("...f,fp->...p", feats, pick).astype(jnp.bfloat16)
+    return lax.optimization_barrier(product_of("...f,fp->...p", feats, pick).astype(jnp.bfloat16))
 
 
 def spread_pairs(half):
     spread = jnp.asarray(pair_tables()[1], jnp.bfloat16)
-    return product_of("...pd,fp->...fd", half.astype(jnp.bfloat16), spread).astype(jnp.bfloat16)
+    return lax.optimization_barrier(
+        product_of("...pd,fp->...fd", half.astype(jnp.bfloat16), spread).astype(jnp.bfloat16)
+    )
 
 
 def forward_blocks(q_normed, k_normed, values, sign_pair):

time: 138 us -> 135 us (0.978)
  matrix products: 27.1 us -> 24.4 us
    dot_general x16 -> x18, matrix products: 23.7 us -> 21 us  [product_of(): return jnp.einsum(spec, lhs, rhs, preferred_element_type=jnp.float32)]
  transfers between devices with their start and end apart: 6 -> 6, of which waited for: 6 -> 6; matrix products, arithmetic and copies ran while one was open for 20% -> 21% of each run, Pallas kernels for 0% -> 0%
where the time goes in v7:
time: 135 us; the launch traced here: 133 us
  starting transfers between devices  36.1 us (27%)
  other arithmetic  27.6 us (20%)
  waiting for transfers between devices  26.4 us (20%)
  matrix products  24.4 us (18%)
  local copies, waits for them, and re-layouts  17.2 us (13%)
  between operations  1.5 us (1%)
    dot_general x18, matrix products, product_of(): return jnp.einsum(spec, lhs, rhs, preferred_element_type=jnp.float32)  21 us
    all_to_all x2, starting transfers between devices, carried_in(): mine = lax.all_to_all(stacked, axis, 0, 0, tiled=True)  13.8 us
    all_to_all x2, starting transfers between devices, head_sum(): gathered = lax.all_to_all(spread, axis, 0, 0, tiled=True)  12.3 us
    all_to_all x2, waiting for transfers between devices, carried_in(): lax.all_to_all(shifted, axis, 0, 0, tiled=True)  11.8 us
    all_to_all x2, starting transfers between devices, carried_in(): lax.all_to_all(shifted, axis, 0, 0, tiled=True)  9.9 us
    all_to_all x2, waiting for transfers between devices, carried_in(): mine = lax.all_to_all(stacked, axis, 0, 0, tiled=True)  7.67 us
    all_to_all x2, waiting for transfers between devices, head_sum(): gathered = lax.all_to_all(spread, axis, 0, 0, tiled=True)  6.99 us
    reduce_sum x2, other arithmetic, sketch_back(): sketch_grad = jnp.sum(symmetric * sketched[..., None, :], axis=-1)  6.33 us
  transfers between devices with their start and end apart: 6, of which 6 were waited for; matrix products, arithmetic and copies ran while one was open for 21% of the time, Pallas kernels for 0%

profile of v7, /device:TPU:1, one launch (start us, length us, event | category | flops | bytes accessed | tf_op | source)
XLA Modules:
  0.0 133.2 jit_solution(11466171513164363125)
XLA Ops:
  0.6 1.3 fusion.16
  1.9 1.3 fusion.25
  3.2 0.6 broadcast_in_dim.17
  3.9 9.0 %all-to-all-start = ((f32[8,2,512]{2,1,0:T(2,128)}), f32[8,2,512]{2,1,0:T(2,128)S(1)}, u32[]{:S(2)}, u32[]{:S(2)}) async-start(f32[8,2,512]{2,1,0:T(2,128)} %broadcast_in_dim.17), calls=%async_computation | async-start | bytes 65536 | tf_op jit(solution)/shard_map/all_to_all | solution.py:54
  12.9 0.7 fusion.48
  13.6 1.2 reshape.169
  14.8 1.1 copy_bitcast_fusion
  16.0 0.6 pad.69.clone
  16.6 0.7 iota_compare_fusion
  17.2 2.5 %all-to-all-done = f32[8,2,512]{2,1,0:T(2,128)S(1)} async-done(((f32[8,2,512]{2,1,0:T(2,128)}), f32[8,2,512]{2,1,0:T(2,128)S(1)}, u32[]{:S(2)}, u32[]{:S(2)}) %all-to-all-start) | async-done | bytes 32800 | tf_op jit(solution)/shard_map/all_to_all | solution.py:54
  20.5 0.7 copy-done.19
  22.7 1.0 convert_reduce_fusion
  23.9 1.1 convolution_convert_fusion
  25.3 1.1 fusion.63
  26.5 0.8 maximum_maximum_fusion
  27.3 9.2 %all-to-all-start.1 = ((f32[32,24,128]{2,1,0:T(8,128)}), f32[32,24,128]{2,1,0:T(8,128)}, u32[]{:S(2)}, u32[]{:S(2)}) async-start(f32[32,24,128]{2,1,0:T(8,128)} %bitcast.19), calls=%async_computation.1 | async-start | bytes 786432 | tf_op jit(solution)/shard_map/all_to_all | solution.py:40
  36.6 0.6 multiply_multiply_fusion.5
  37.2 3.6 %convert_reduce_fusion.2 = (f32[4,2,256]{2,1,0:T(2,128)}, bf16[4,2,256,256]{2,3,1,0:T(8,128)(2,1)S(1)}, f32[4,2,256,256]{2,3,1,0:T(8,128)}) fusion(pred[256,256]{0,1:T(8,128)(4,1)} %iota_compare_fusion, bf16[4,2,256,128]{3,2,1,0:T(8,128)(2,1)} %bitcast.179, bf16[4,2,256,128]{3,2,1,0:T(8,128)(2,1)} %bitcast.182), kind=kOutput, calls=%fused_computation.18 | convolution fusion | flops 137885696 | bytes 4268032 | tf_op jit(solution)/shard_map/...id,...jd->...ij/dot_general | solution.py:60
  40.8 6.1 %all-to-all-done.1 = f32[32,24,128]{2,1,0:T(8,128)} async-done(((f32[32,24,128]{2,1,0:T(8,128)}), f32[32,24,128]{2,1,0:T(8,128)}, u32[]{:S(2)}, u32[]{:S(2)}) %all-to-all-start.1) | async-done | bytes 393248 | tf_op jit(solution)/shard_map/all_to_all | solution.py:40
  46.9 1.0 slice.110
  48.3 0.8 pad_add_fusion.4
  49.0 4.4 %all-to-all-start.2 = ((f32[32,24,128]{2,1,0:T(8,128)}), f32[32,24,128]{2,1,0:T(8,128)}, u32[]{:S(2)}, u32[]{:S(2)}) async-start(f32[32,24,128]{2,1,0:T(8,128)} %pad_add_fusion.4), calls=%async_computation.2 | async-start | bytes 786432 | tf_op jit(solution)/shard_map/all_to_all | solution.py:46
  53.4 0.6 multiply_multiply_fusion.4
  54.0 0.9 reduce_sum.144
  54.9 0.6 reduce_window_sum.35
  55.6 2.5 %fusion.66 = f32[4,2,256,128]{3,2,1,0:T(8,128)} fusion(bf16[4,2,256,256]{2,3,1,0:T(8,128)(2,1)S(1)} %get-tuple-element.9, bf16[4,2,256,128]{3,2,1,0:T(8,128)(2,1)} %bitcast.175), kind=kOutput, calls=%fused_computation.144 | convolution fusion | flops 134217728 | bytes 2621440 | tf_op jit(solution)/shard_map/...ij,...jd->...id/dot_general | solution.py:60
  58.1 5.5 %all-to-all-done.2 = f32[32,24,128]{2,1,0:T(8,128)} async-done(((f32[32,24,128]{2,1,0:T(8,128)}), f32[32,24,128]{2,1,0:T(8,128)}, u32[]{:S(2)}, u32[]{:S(2)}) %all-to-all-start.2) | async-done | bytes 393248 | tf_op jit(solution)/shard_map/all_to_all | solution.py:46
  63.6 0.8 slice_bitcast_fusion.1
  64.4 1.1 slice.116
  65.5 0.7 add_subtract_fusion.1
  66.3 0.5 fusion.46
  67.3 0.6 multiply_reduce_fusion
  68.3 1.2 divide_convert_fusion
  69.5 1.8 %multiply_add_fusion = f32[4,2,256,256]{2,3,1,0:T(8,128)} fusion(bf16[4,2,256,128]{3,2,1,0:T(8,128)(2,1)S(1)} %get-tuple-element.17, bf16[4,2,256,128]{2,3,1,0:T(8,128)(2,1)S(1)} %fusion.14, f32[4,2,256]{2,1,0:T(2,128)S(1)} %add_subtract_fusion.1, f32[4,2,256]{2,1,0:T(2,128)S(1)} %get-tuple-element.6), kind=kOutput, calls=%fused_computation.17 | convolution fusion | flops 135266304 | bytes 3162112 | tf_op jit(solution)/shard_map/...id,...rd->...ir/dot_general | solution.py:60
  71.3 0.9 copy-done.23
  72.2 1.7 %fusion.6 = bf16[4,2,256,256]{2,3,1,0:T(8,128)(2,1)} fusion(f32[4,2,256,256]{2,3,1,0:T(8,128)S(1)} %copy-done.23, bf16[4,2,256,128]{3,2,1,0:T(8,128)(2,1)S(1)} %get-tuple-element.17, bf16[4,2,256,128]{3,2,1,0:T(8,128)(2,1)S(1)} %bitcast.176, f32[4,2,256]{2,1,0:T(2,128)S(1)} %get-tuple-element.6, pred[256,256]{0,1:T(8,128)(4,1)S(1)} %copy-done.29), kind=kOutput, calls=%fused_computation.10 | convolution fusion | flops 138936320 | bytes 4268032 | tf_op jit(solution)/shard_map/...id,...jd->...ij/dot_general | solution.py:60
  73.9 0.9 fusion.44
  74.9 1.5 %fusion.64 = (f32[4,136,128]{2,1,0:T(8,128)S(1)}, f32[4,2,136,128]{3,2,1,0:T(8,128)S(1)}) fusion(bf16[4,2,256,136]{2,3,1,0:T(8,128)(2,1)} %convolution_convert_fusion, bf16[4,2,256,128]{3,2,1,0:T(8,128)(2,1)} %copy-done.3), kind=kOutput, calls=%fused_computation.142 | convolution fusion | flops 71372800 | bytes 1916928 | tf_op jit(solution)/shard_map/...ir,...id->...rd/dot_general | solution.py:60
  76.4 1.5 %maximum_maximum_fusion.1 = f32[4,192,128]{2,1,0:T(8,128)} fusion(f32[4,2,128]{2,1,0:T(2,128)S(1)} %reshape.179, f32[4,136,128]{2,1,0:T(8,128)S(1)} %get-tuple-element.28, f32[192]{0:T(256)} %pad.69.clone), kind=kLoop, calls=%fused_computation.73 | loop fusion | flops 196608 | bytes 676608 | tf_op jit(solution)/shard_map/concatenate | solution.py:32
  77.9 4.6 %all-to-all-start.3 = ((f32[32,24,128]{2,1,0:T(8,128)}), f32[32,24,128]{2,1,0:T(8,128)}, u32[]{:S(2)}, u32[]{:S(2)}) async-start(f32[32,24,128]{2,1,0:T(8,128)} %bitcast.39), calls=%async_computation.3 | async-start | bytes 786432 | tf_op jit(solution)/shard_map/all_to_all | solution.py:40
  82.5 0.9 rev.14
  83.4 1.9 %fusion.65 = f32[4,2,136,128]{3,2,1,0:T(8,128)} fusion(f32[4,2,136,128]{3,2,1,0:T(8,128)} %rev.14), kind=kOutput, calls=%fused_computation.143 | output fusion | flops 139264 | bytes 1114112 | tf_op jit(solution)/shard_map/jit(cumsum)/reduce_window_sum | solution.py:136
  85.3 4.0 %fusion.10 = f32[4,2,256,16]{2,3,1,0:T(8,128)S(1)} fusion(f32[4,2,256,16,16]{2,4,3,1,0:T(8,128)} %bitcast.172, f32[4,2,256,16]{2,3,1,0:T(8,128)S(1)} %multiply_multiply_fusion.3), kind=kLoop, calls=%fused_computation.16 | loop fusion | flops 1540096 | bytes 2359296 | tf_op jit(solution)/shard_map/reduce_sum | solution.py:88
  89.4 1.0 fusion.36
  90.9 1.6 %all-to-all-done.3 = f32[32,24,128]{2,1,0:T(8,128)} async-done(((f32[32,24,128]{2,1,0:T(8,128)}), f32[32,24,128]{2,1,0:T(8,128)}, u32[]{:S(2)}, u32[]{:S(2)}) %all-to-all-start.3) | async-done | bytes 393248 | tf_op jit(solution)/shard_map/all_to_all | solution.py:40
  92.5 1.0 slice.118
  93.8 0.8 pad_add_fusion
  94.6 5.5 %all-to-all-start.4 = ((f32[32,24,128]{2,1,0:T(8,128)}), f32[32,24,128]{2,1,0:T(8,128)}, u32[]{:S(2)}, u32[]{:S(2)}) async-start(f32[32,24,128]{2,1,0:T(8,128)} %pad_add_fusion), calls=%async_computation.4 | async-start | bytes 786432 | tf_op jit(solution)/shard_map/all_to_all | solution.py:46
  100.2 1.3 fusion.24
  101.7 2.5 %fusion.67 = f32[4,2,256,128]{3,2,1,0:T(8,128)} fusion(bf16[4,2,256,256]{2,3,1,0:T(8,128)(2,1)S(1)} %get-tuple-element.9, bf16[4,2,256,128]{3,2,1,0:T(8,128)(2,1)} %copy-done.3), kind=kOutput, calls=%fused_computation.145 | convolution fusion | flops 134217728 | bytes 2621440 | tf_op jit(solution)/shard_map/...ij,...id->...jd/dot_general | solution.py:60
  104.2 6.3 %all-to-all-done.4 = f32[32,24,128]{2,1,0:T(8,128)} async-done(((f32[32,24,128]{2,1,0:T(8,128)}), f32[32,24,128]{2,1,0:T(8,128)}, u32[]{:S(2)}, u32[]{:S(2)}) %all-to-all-start.4) | async-done | bytes 393248 | tf_op jit(solution)/shard_map/all_to_all | solution.py:46
  110.5 0.7 slice_bitcast_fusion
  111.2 1.0 slice.124
  112.2 1.3 subtract_convert_fusion
  113.9 1.3 fusion.12
  115.2 0.5 convolution_add_fusion
  116.1 2.3 %fusion.8 = f32[4,2,256,16]{2,3,1,0:T(8,128)S(1)} fusion(f32[4,2,256,16,16]{2,4,3,1,0:T(8,128)S(1)} %bitcast.173, f32[4,2,256,16]{2,3,1,0:T(8,128)S(1)} %copy-done.25), kind=kLoop, calls=%fused_computation.13 | loop fusion | flops 1540096 | bytes 2359296 | tf_op jit(solution)/shard_map/reduce_sum | solution.py:88
  118.5 1.0 fusion.39
  120.0 0.5 copy-done.7
  120.8 0.6 broadcast_in_dim.19
  121.4 3.3 %all-to-all-start.5 = ((f32[8,2,512]{2,1,0:T(2,128)}), f32[8,2,512]{2,1,0:T(2,128)S(1)}, u32[]{:S(2)}, u32[]{:S(2)}) async-start(f32[8,2,512]{2,1,0:T(2,128)} %broadcast_in_dim.19), calls=%async_computation.5 | async-start | bytes 65536 | tf_op jit(solution)/shard_map/all_to_all | solution.py:54
  124.7 2.3 %copy_bitcast_fusion.1 = (bf16[512,512]{1,0:T(8,128)(2,1)}, bf16[512,512]{1,0:T(8,128)(2,1)}) fusion(bf16[4,64,8,128]{3,2,1,0:T(8,128)(2,1)} %bitcast.189, bf16[4,64,8,128]{3,2,1,0:T(8,128)(2,1)} %bitcast.185), kind=kLoop, calls=%fused_computation.70 | loop fusion | bytes 2097152 | tf_op jit(solution)/shard_map/convert_element_type | solution.py:282
  127.0 4.5 %all-to-all-done.5 = f32[8,2,512]{2,1,0:T(2,128)S(1)} async-done(((f32[8,2,512]{2,1,0:T(2,128)}), f32[8,2,512]{2,1,0:T(2,128)S(1)}, u32[]{:S(2)}, u32[]{:S(2)}) %all-to-all-start.5) | async-done | bytes 32800 | tf_op jit(solution)/shard_map/all_to_all | solution.py:54
  131.6 1.6 %fusion.22 = (bf16[512,512]{1,0:T(8,128)(2,1)}, bf16[512,512]{1,0:T(8,128)(2,1)}) fusion(bf16[512,512]{1,0:T(8,128)(2,1)S(1)} %copy-done.5, f32[4,64,8,128]{3,2,1,0:T(8,128)S(1)} %bitcast.169, f32[512]{0:T(512)S(1)} %bitcast.203, f32[512]{0:T(512)S(1)} %copy-done.41, f32[512]{0:T(512)S(1)} %copy-done.37, f32[512]{0:T(512)S(1)} %bitcast.197, ...), kind=kLoop, calls=%fused_computation.50 | loop fusion | flops 4194304 | bytes 4210688 | tf_op jit(solution)/shard_map/convert_element_type | solution.py:203
  (138 shorter events, 6.5 us)
Async XLA Ops:
  0.6 14.2 %copy-start.21 = (bf16[512,512]{1,0:T(8,128)(2,1)S(1)}, bf16[512,512]{1,0:T(8,128)(2,1)}, u32[]{:S(2)}) copy-start(bf16[512,512]{1,0:T(8,128)(2,1)} %param.14) | copy-start | bytes 1572868
  1.9 17.9 %copy-start.4 = (bf16[512,512]{1,0:T(8,128)(2,1)S(1)}, bf16[512,512]{1,0:T(8,128)(2,1)}, u32[]{:S(2)}) copy-start(bf16[512,512]{1,0:T(8,128)(2,1)} %param.11) | copy-start | bytes 1572868
  1.9 17.9 %copy-start.36 = (f32[512]{0:T(512)S(1)}, f32[512]{0:T(512)}, u32[]{:S(2)}) copy-start(f32[512]{0:T(512)} %param.15) | copy-start | bytes 6148
  3.9 15.9 %all-to-all-start = ((f32[8,2,512]{2,1,0:T(2,128)}), f32[8,2,512]{2,1,0:T(2,128)S(1)}, u32[]{:S(2)}, u32[]{:S(2)}) async-start(f32[8,2,512]{2,1,0:T(2,128)} %broadcast_in_dim.17), calls=%async_computation | async-start | bytes 65536 | tf_op jit(solution)/shard_map/all_to_all | solution.py:54
  14.8 10.5 %copy-start = (bf16[4,512,128]{2,1,0:T(8,128)(2,1)}, bf16[4,512,128]{2,1,0:T(8,128)(2,1)S(1)}, u32[]{:S(2)}) copy-start(bf16[4,512,128]{2,1,0:T(8,128)(2,1)S(1)} %copy.77) | copy-start | bytes 1572868
  19.8 16.8 %copy-start.34 = (f32[1,512]{1,0:T(1,128)}, f32[1,512]{1,0:T(1,128)S(1)}, u32[]{:S(2)}) copy-start(f32[1,512]{1,0:T(1,128)S(1)} %get-tuple-element.22) | copy-start | bytes 6148
  19.8 33.6 %copy-start.32 = (f32[1,512]{1,0:T(1,128)}, f32[1,512]{1,0:T(1,128)S(1)}, u32[]{:S(2)}) copy-start(f32[1,512]{1,0:T(1,128)S(1)} %get-tuple-element.21) | copy-start | bytes 6148
  19.8 1.4 %copy-start.6 = (bf16[512,512]{1,0:T(8,128)(2,1)S(1)}, bf16[512,512]{1,0:T(8,128)(2,1)}, u32[]{:S(2)}) copy-start(bf16[512,512]{1,0:T(8,128)(2,1)} %param.12) | copy-start | bytes 1572868
  19.8 1.4 %copy-start.38 = (f32[512]{0:T(512)S(1)}, f32[512]{0:T(512)}, u32[]{:S(2)}) copy-start(f32[512]{0:T(512)} %param.16) | copy-start | bytes 6148
  20.2 1.4 %copy-start.8 = (bf16[4,512,128]{2,1,0:T(8,128)(2,1)}, bf16[4,512,128]{2,1,0:T(8,128)(2,1)S(1)}, u32[]{:S(2)}) copy-start(bf16[4,512,128]{2,1,0:T(8,128)(2,1)S(1)} %copy.75) | copy-start | bytes 1572868
  20.5 0.7 copy-start.19
  21.7 0.8 copy-start.10
  21.7 2.1 %copy-start.26 = (bf16[256,136,1,1]{0,1,3,2:T(8,128)(2,1)S(1)}, bf16[256,136,1,1]{0,1,3,2:T(8,128)(2,1)}, u32[]{:S(2)}) copy-start(bf16[256,136,1,1]{0,1,3,2:T(8,128)(2,1)} %constant.67) | copy-start | bytes 208900
  22.5 2.5 %copy-start.24 = (f32[4,2,256,16]{2,3,1,0:T(8,128)}, f32[4,2,256,16]{2,3,1,0:T(8,128)S(1)}, u32[]{:S(2)}) copy-start(f32[4,2,256,16]{2,3,1,0:T(8,128)S(1)} %multiply_multiply_fusion.2) | copy-start | bytes 393220
  25.0 1.5 %copy-start.40 = (f32[192]{0:T(256)S(1)}, f32[192]{0:T(256)}, u32[]{:S(2)}) copy-start(f32[192]{0:T(256)} %pad.69.clone) | copy-start | bytes 2308
  27.3 19.6 %all-to-all-start.1 = ((f32[32,24,128]{2,1,0:T(8,128)}), f32[32,24,128]{2,1,0:T(8,128)}, u32[]{:S(2)}, u32[]{:S(2)}) async-start(f32[32,24,128]{2,1,0:T(8,128)} %bitcast.19), calls=%async_computation.1 | async-start | bytes 786432 | tf_op jit(solution)/shard_map/all_to_all | solution.py:40
  49.0 14.6 %all-to-all-start.2 = ((f32[32,24,128]{2,1,0:T(8,128)}), f32[32,24,128]{2,1,0:T(8,128)}, u32[]{:S(2)}, u32[]{:S(2)}) async-start(f32[32,24,128]{2,1,0:T(8,128)} %pad_add_fusion.4), calls=%async_computation.2 | async-start | bytes 786432 | tf_op jit(solution)/shard_map/all_to_all | solution.py:46
  54.9 10.6 %copy-start.30 = (f32[4,2,256]{2,1,0:T(2,128)}, f32[4,2,256]{2,1,0:T(2,128)S(1)}, u32[]{:S(2)}) copy-start(f32[4,2,256]{2,1,0:T(2,128)S(1)} %reduce_sum.144) | copy-start | bytes 24580
  63.6 3.2 %copy-start.13 = (f32[4,2,136,128]{3,2,1,0:T(8,128)S(1)}, f32[4,2,136,128]{3,2,1,0:T(8,128)}, u32[]{:S(2)}) copy-start(f32[4,2,136,128]{3,2,1,0:T(8,128)} %get-tuple-element.25) | copy-start | bytes 1671172
  63.6 3.3 %copy-start.27 = (bf16[256,136,1,1]{0,1,3,2:T(8,128)(2,1)S(1)}, bf16[256,136,1,1]{0,1,3,2:T(8,128)(2,1)}, u32[]{:S(2)}) copy-start(bf16[256,136,1,1]{0,1,3,2:T(8,128)(2,1)} %constant.68) | copy-start | bytes 208900
  64.4 2.9 %copy-start.17 = (f32[512,4,128]{2,0,1:T(8,128)S(1)}, f32[512,4,128]{2,0,1:T(8,128)}, u32[]{:S(2)}) copy-start(f32[512,4,128]{2,0,1:T(8,128)} %copy_bitcast_fusion) | copy-start | bytes 3145732
  64.4 2.9 %copy-start.18 = (f32[4,2,256,128]{3,2,1,0:T(8,128)S(1)}, f32[4,2,256,128]{3,2,1,0:T(8,128)}, u32[]{:S(2)}) copy-start(f32[4,2,256,128]{3,2,1,0:T(8,128)} %fusion.66) | copy-start | bytes 3145732
  67.2 0.7 copy-start.31
  67.3 1.0 copy-start.22
  69.5 4.4 %copy-start.3 = (bf16[4,2,256,128]{3,2,1,0:T(8,128)(2,1)}, bf16[4,2,256,128]{3,2,1,0:T(8,128)(2,1)S(1)}, u32[]{:S(2)}) copy-start(bf16[4,2,256,128]{3,2,1,0:T(8,128)(2,1)S(1)} %get-tuple-element.17) | copy-start | bytes 1572868
  69.5 1.8 %copy-start.1 = (bf16[4,512,128]{2,1,0:T(8,128)(2,1)S(1)}, bf16[4,512,128]{2,1,0:T(8,128)(2,1)}, u32[]{:S(2)}) copy-start(bf16[4,512,128]{2,1,0:T(8,128)(2,1)} %copy-done) | copy-start | bytes 1572868
  69.5 2.7 %copy-start.23 = (f32[4,2,256,256]{2,3,1,0:T(8,128)S(1)}, f32[4,2,256,256]{2,3,1,0:T(8,128)}, u32[]{:S(2)}) copy-start(f32[4,2,256,256]{2,3,1,0:T(8,128)} %get-tuple-element.23) | copy-start | bytes 6291460
  69.5 2.7 %copy-start.29 = (pred[256,256]{0,1:T(8,128)(4,1)S(1)}, pred[256,256]{0,1:T(8,128)(4,1)}, u32[]{:S(2)}) copy-start(pred[256,256]{0,1:T(8,128)(4,1)} %iota_compare_fusion) | copy-start | bytes 196612
  76.4 12.9 %copy-start.12 = (f32[4,2,136,128]{3,2,1,0:T(8,128)}, f32[4,2,136,128]{3,2,1,0:T(8,128)S(1)}, u32[]{:S(2)}) copy-start(f32[4,2,136,128]{3,2,1,0:T(8,128)S(1)} %get-tuple-element.29) | copy-start | bytes 1671172
  77.9 14.6 %all-to-all-start.3 = ((f32[32,24,128]{2,1,0:T(8,128)}), f32[32,24,128]{2,1,0:T(8,128)}, u32[]{:S(2)}, u32[]{:S(2)}) async-start(f32[32,24,128]{2,1,0:T(8,128)} %bitcast.39), calls=%async_computation.3 | async-start | bytes 786432 | tf_op jit(solution)/shard_map/all_to_all | solution.py:40
  82.5 6.8 %copy-start.20 = (f32[4,2,256,32]{2,3,1,0:T(8,128)S(1)}, f32[4,2,256,32]{2,3,1,0:T(8,128)}, u32[]{:S(2)}) copy-start(f32[4,2,256,32]{2,3,1,0:T(8,128)} %copy-done.19) | copy-start | bytes 786436
  85.3 5.1 %copy-start.11 = (bf16[4,512,128]{2,1,0:T(8,128)(2,1)S(1)}, bf16[4,512,128]{2,1,0:T(8,128)(2,1)}, u32[]{:S(2)}) copy-start(bf16[4,512,128]{2,1,0:T(8,128)(2,1)} %copy-done.10) | copy-start | bytes 1572868
  85.3 5.1 %copy-start.14 = (bf16[4,2,256,256]{2,3,1,0:T(8,128)(2,1)S(1)}, bf16[4,2,256,256]{2,3,1,0:T(8,128)(2,1)}, u32[]{:S(2)}) copy-start(bf16[4,2,256,256]{2,3,1,0:T(8,128)(2,1)} %fusion.6) | copy-start | bytes 3145732
  93.7 6.4 %copy-start.37 = (f32[512]{0:T(512)S(1)}, f32[512]{0:T(512)}, u32[]{:S(2)}) copy-start(f32[512]{0:T(512)} %param.15) | copy-start | bytes 6148
  94.6 15.9 %all-to-all-start.4 = ((f32[32,24,128]{2,1,0:T(8,128)}), f32[32,24,128]{2,1,0:T(8,128)}, u32[]{:S(2)}, u32[]{:S(2)}) async-start(f32[32,24,128]{2,1,0:T(8,128)} %pad_add_fusion), calls=%async_computation.4 | async-start | bytes 786432 | tf_op jit(solution)/shard_map/all_to_all | solution.py:46
  101.7 11.8 %copy-start.28 = (bf16[256,136,1,1]{0,1,3,2:T(8,128)(2,1)S(1)}, bf16[256,136,1,1]{0,1,3,2:T(8,128)(2,1)}, u32[]{:S(2)}) copy-start(bf16[256,136,1,1]{0,1,3,2:T(8,128)(2,1)} %constant.68) | copy-start | bytes 208900
  104.2 9.7 %copy-start.16 = (f32[4,2,256,128]{3,2,1,0:T(8,128)S(1)}, f32[4,2,256,128]{3,2,1,0:T(8,128)}, u32[]{:S(2)}) copy-start(f32[4,2,256,128]{3,2,1,0:T(8,128)} %fusion.67) | copy-start | bytes 3145732
  113.5 1.7 %copy-start.2 = (bf16[4,512,128]{2,1,0:T(8,128)(2,1)S(1)}, bf16[4,512,128]{2,1,0:T(8,128)(2,1)}, u32[]{:S(2)}) copy-start(bf16[4,512,128]{2,1,0:T(8,128)(2,1)} %copy-done) | copy-start | bytes 1572868
  115.2 0.9 copy-start.25
  116.1 3.4 %copy-start.9 = (bf16[4,512,128]{2,1,0:T(8,128)(2,1)S(1)}, bf16[4,512,128]{2,1,0:T(8,128)(2,1)}, u32[]{:S(2)}) copy-start(bf16[4,512,128]{2,1,0:T(8,128)(2,1)} %copy-done.8) | copy-start | bytes 1572868
  116.1 3.4 %copy-start.15 = (bf16[4,2,256,256]{2,3,1,0:T(8,128)(2,1)S(1)}, bf16[4,2,256,256]{2,3,1,0:T(8,128)(2,1)}, u32[]{:S(2)}) copy-start(bf16[4,2,256,256]{2,3,1,0:T(8,128)(2,1)} %fusion.6) | copy-start | bytes 3145732
  119.5 1.0 copy-start.7
  119.5 1.0 copy-start.39
  120.0 11.6 %copy-start.5 = (bf16[512,512]{1,0:T(8,128)(2,1)S(1)}, bf16[512,512]{1,0:T(8,128)(2,1)}, u32[]{:S(2)}) copy-start(bf16[512,512]{1,0:T(8,128)(2,1)} %param.11) | copy-start | bytes 1572868
  120.0 11.6 %copy-start.33 = (f32[1,512]{1,0:T(1,128)S(1)}, f32[1,512]{1,0:T(1,128)}, u32[]{:S(2)}) copy-start(f32[1,512]{1,0:T(1,128)} %copy-done.32) | copy-start | bytes 6148
  120.0 11.6 %copy-start.35 = (f32[1,512]{1,0:T(1,128)S(1)}, f32[1,512]{1,0:T(1,128)}, u32[]{:S(2)}) copy-start(f32[1,512]{1,0:T(1,128)} %copy-done.34) | copy-start | bytes 6148
  120.0 11.6 %copy-start.41 = (f32[512]{0:T(512)S(1)}, f32[512]{0:T(512)}, u32[]{:S(2)}) copy-start(f32[512]{0:T(512)} %multiply_multiply_fusion.5) | copy-start | bytes 6148
  120.0 11.6 %copy-start.42 = (f32[512]{0:T(512)S(1)}, f32[512]{0:T(512)}, u32[]{:S(2)}) copy-start(f32[512]{0:T(512)} %multiply_multiply_fusion.4) | copy-start | bytes 6148
  121.4 10.1 %all-to-all-start.5 = ((f32[8,2,512]{2,1,0:T(2,128)}), f32[8,2,512]{2,1,0:T(2,128)S(1)}, u32[]{:S(2)}, u32[]{:S(2)}) async-start(f32[8,2,512]{2,1,0:T(2,128)} %broadcast_in_dim.19), calls=%async_computation.5 | async-start | bytes 65536 | tf_op jit(solution)/shard_map/all_to_all | solution.py:54

commit v8 on v7

--- a/solution.py
+++ b/solution.py
@@ -23,7 +23,7 @@
     return jnp.pad(rows[:-step], widths)
 
 
-def carried_in(state, totals, axis, reverse):
+def carried_in(state, totals, axis, reverse, along=()):
     count = lax.axis_size(axis)
     heads_here, rows, lanes = state.shape
     total_rows = totals.shape[1] // lanes
@@ -37,6 +37,7 @@
         ],
         axis=1,
     ).reshape(count, room, lanes)
+    stacked, along = lax.optimization_barrier((stacked, along))
     mine = lax.all_to_all(stacked, axis, 0, 0, tiled=True)
     shifted = shift_rows(mine, 1, reverse)
     step = 1
@@ -44,16 +45,16 @@
         shifted = shifted + shift_rows(shifted, step, reverse)
         step *= 2
     back = lax.all_to_all(shifted, axis, 0, 0, tiled=True).reshape(heads_here, padded, lanes)
-    return (back[:, :rows], back[:, rows : rows + total_rows].reshape(totals.shape))
-
-
-def head_sum(parts, axis):
+    return (back[:, :rows], back[:, rows : rows + total_rows].reshape(totals.shape), along)
+
+
+def head_sum(parts, axis, along=()):
     count = lax.axis_size(axis)
-    stacked = jnp.stack(parts)
+    stacked, along = lax.optimization_barrier((jnp.stack(parts), along))
     spread = jnp.broadcast_to(stacked[None], (count,) + stacked.shape)
     gathered = lax.all_to_all(spread, axis, 0, 0, tiled=True)
     summed = jnp.sum(gathered, axis=0)
-    return tuple(summed[i] for i in range(len(parts)))
+    return (tuple(summed[i] for i in range(len(parts))), along)
 
 
 def product_of(spec, lhs, rhs):
@@ -148,26 +149,29 @@
         + jnp.sum(weights.astype(jnp.float32), axis=-1)
         + precise_product("...ir,...r->...i", q_feats, key_total)
     )
-    attended = (numerator / denominator[..., None]).astype(jnp.bfloat16)
-    return (state_half, numerator, denominator, attended)
+    return (state_half, numerator, denominator)
+
+
+def backward_states(grad_in, numerator, denominator, q_feats):
+    grad_float = grad_in.astype(jnp.float32)
+    scaled_grad = (grad_float / denominator[..., None]).astype(jnp.bfloat16)
+    den_grad = -jnp.sum(grad_float * numerator, axis=-1) / (denominator * denominator)
+    block_u = product_of("...ir,...id->...rd", pick_pairs(q_feats), scaled_grad)
+    block_w = precise_product("...ir,...i->...r", q_feats, den_grad)
+    return (scaled_grad, den_grad, block_u, block_w)
 
 
 def backward_blocks(
-    grad_in,
-    numerator,
-    denominator,
+    scaled_grad,
+    den_grad,
     scores,
     weights,
     values,
     q_normed,
     k_normed,
-    q_feats,
     state_half,
     key_total,
 ):
-    grad_float = grad_in.astype(jnp.float32)
-    scaled_grad = (grad_float / denominator[..., None]).astype(jnp.bfloat16)
-    den_grad = -jnp.sum(grad_float * numerator, axis=-1) / (denominator * denominator)
     weight_grad = product_of("...id,...jd->...ij", scaled_grad, values) + den_grad[..., None]
     score_grad = jnp.where(
         causal_mask(), 4.0 * scores**3 * weight_grad * DH ** (-0.5), 0.0
@@ -179,9 +183,7 @@
         product_of("...id,...rd->...ir", scaled_grad, state_half)
         + den_grad[..., None] * key_total[..., None, :]
     )
-    block_u = product_of("...ir,...id->...rd", pick_pairs(q_feats), scaled_grad)
-    block_w = precise_product("...ir,...i->...r", q_feats, den_grad)
-    return (q_diag, k_diag, v_diag, qf_grad, block_u, block_w)
+    return (q_diag, k_diag, v_diag, qf_grad)
 
 
 def finish_backward(values, k_feats, later_state, later_total, v_diag):
@@ -210,7 +212,7 @@
     sign_pair = jnp.concatenate([2 * signs[0] - 1, 2 * signs[1] - 1], axis=1).astype(jnp.bfloat16)
     q_float = queries.astype(jnp.float32)
     k_float = keys.astype(jnp.float32)
-    q_total, k_total = head_sum(
+    (q_total, k_total), _ = head_sum(
         (jnp.sum(q_float * q_float, axis=-1), jnp.sum(k_float * k_float, axis=-1)), "head"
     )
     q_scale, q_normed = normalize(queries, q_gain, q_total)
@@ -239,44 +241,52 @@
     )
     sum_kv = jnp.sum(block_kv, axis=1)
     sum_keys = jnp.sum(block_keys, axis=1)
-    prior_kv, prior_keys = carried_in(sum_kv, sum_keys, "ctx", False)
+    prior_kv, prior_keys, _ = carried_in(sum_kv, sum_keys, "ctx", False)
     key_state, key_total = before_blocks(block_kv, block_keys, prior_kv, prior_keys)
     key_state = spread_pairs(key_state)
-    state_half, numerator, denominator, attended = finish_forward(
+    state_half, numerator, denominator = finish_forward(
         weights, v_heads, q_parts[0], key_state, key_total
     )
-    q_diag, k_diag, v_diag, qf_grad, block_u, block_w = backward_blocks(
-        g_heads,
-        numerator,
-        denominator,
+    scaled_grad, den_grad, block_u, block_w = backward_states(
+        g_heads, numerator, denominator, q_parts[0]
+    )
+    later_u, later_w, (scaled_grad, den_grad, numerator, denominator) = carried_in(
+        jnp.sum(block_u, axis=1),
+        jnp.sum(block_w, axis=1),
+        "ctx",
+        True,
+        (scaled_grad, den_grad, numerator, denominator),
+    )
+    attended = (numerator / denominator[..., None]).astype(jnp.bfloat16)
+    q_diag, k_diag, v_diag, qf_grad = backward_blocks(
+        scaled_grad,
+        den_grad,
         scores,
         weights,
         v_heads,
         q_heads,
         k_heads,
-        q_parts[0],
         state_half,
         key_total,
     )
-    later_u, later_w = carried_in(
-        jnp.sum(block_u, axis=1), jnp.sum(block_w, axis=1), "ctx", True
-    )
     later_state, later_total = after_blocks(block_u, block_w, later_u, later_w)
     later_state = spread_pairs(later_state)
-    kf_grad, v_grad = finish_backward(v_heads, k_parts[0], later_state, later_total, v_diag)
+    kf_grad, _ = finish_backward(v_heads, k_parts[0], later_state, later_total, v_diag)
     qn_grad = join_heads(
         q_diag + sketch_back(qf_grad, q_parts[1], q_parts[2], q_parts[3], sign_pair)
     )
     kn_grad = join_heads(
         k_diag + sketch_back(kf_grad, k_parts[1], k_parts[2], k_parts[3], sign_pair)
     )
-    q_dot, k_dot = head_sum(
+    (q_dot, k_dot), (v_diag, later_state) = head_sum(
         (
             jnp.sum(q_float * q_gain * qn_grad, axis=-1),
             jnp.sum(k_float * k_gain * kn_grad, axis=-1),
         ),
         "head",
-    )
+        (v_diag, later_state),
+    )
+    _, v_grad = finish_backward(v_heads, k_parts[0], later_state, later_total, v_diag)
     q_grad = norm_back(queries, q_gain, q_scale, qn_grad, q_dot)
     k_grad = norm_back(keys, k_gain, k_scale, kn_grad, k_dot)
     return (join_heads(attended), q_grad, k_grad, join_heads(v_grad).astype(jnp.bfloat16))

time: 135 us -> 133 us (0.985)
  waiting for transfers between devices: 26.4 us -> 12.8 us
  local copies, waits for them, and re-layouts: 17.2 us -> 23.3 us
  starting transfers between devices: 36.1 us -> 39.4 us
  other arithmetic: 27.6 us -> 29.2 us
    all_to_all x2, waiting for transfers between devices: 11.8 us -> 5.58 us  [carried_in(): lax.all_to_all(shifted, axis, 0, 0, tiled=True)]
    convert_element_type x0 -> x3, local copies, waits for them, and re-layouts: none -> 4.97 us  [the longest x2 2.92 us: backward_states(): grad_float = grad_in.astype(jnp.float32)]
    all_to_all x2, waiting for transfers between devices: 7.67 us -> 3.1 us  [carried_in(): mine = lax.all_to_all(stacked, axis, 0, 0, tiled=True)]
    all_to_all x2, waiting for transfers between devices: 6.99 us -> 4.08 us  [head_sum(): gathered = lax.all_to_all(spread, axis, 0, 0, tiled=True)]
    all_to_all x2, starting transfers between devices: 12.3 us -> 14.9 us  [head_sum(): gathered = lax.all_to_all(spread, axis, 0, 0, tiled=True)]
    transpose x0 -> x1, local copies, waits for them, and re-layouts: none -> 2.04 us  [join_heads(): return array.reshape(heads_here, tok_rows, DH).transpose(1, 0, 2).reshape...]
    reduce_sum x2, other arithmetic: 6.33 us -> 4.64 us  [sketch_back(): sketch_grad = jnp.sum(symmetric * sketched[..., None, :], axis=-1)]
    all_to_all x2, starting transfers between devices: 9.9 us -> 11.5 us  [carried_in(): lax.all_to_all(shifted, axis, 0, 0, tiled=True)]
  transfers between devices with their start and end apart: 6 -> 6, of which waited for: 6 -> 5; matrix products, arithmetic and copies ran while one was open for 21% -> 31% of each run, Pallas kernels for 0% -> 0%
where the time goes in v8:
time: 133 us; the launch traced here: 131 us
  starting transfers between devices  39.4 us (30%)
  other arithmetic  29.2 us (22%)
  matrix products  24.6 us (18%)
  local copies, waits for them, and re-layouts  23.3 us (18%)
  waiting for transfers between devices  12.8 us (10%)
  between operations  1.62 us (1%)
    dot_general x18, matrix products, product_of(): return jnp.einsum(spec, lhs, rhs, preferred_element_type=jnp.float32)  21.2 us
    all_to_all x2, starting transfers between devices, head_sum(): gathered = lax.all_to_all(spread, axis, 0, 0, tiled=True)  14.9 us
    all_to_all x2, starting transfers between devices, carried_in(): mine = lax.all_to_all(stacked, axis, 0, 0, tiled=True)  13 us
    all_to_all x2, starting transfers between devices, carried_in(): lax.all_to_all(shifted, axis, 0, 0, tiled=True)  11.5 us
    unnamed x114, local copies, waits for them, and re-layouts  6.07 us
    all_to_all x2, waiting for transfers between devices, carried_in(): lax.all_to_all(shifted, axis, 0, 0, tiled=True)  5.58 us
    reduce_sum x2, other arithmetic, sketch_back(): sketch_grad = jnp.sum(symmetric * sketched[..., None, :], axis=-1)  4.64 us
    all_to_all x2, waiting for transfers between devices, head_sum(): gathered = lax.all_to_all(spread, axis, 0, 0, tiled=True)  4.08 us
  transfers between devices with their start and end apart: 6, of which 5 were waited for; matrix products, arithmetic and copies ran while one was open for 31% of the time, Pallas kernels for 0%

profile of v8, /device:TPU:1, one launch (start us, length us, event | category | flops | bytes accessed | tf_op | source)
XLA Modules:
  0.0 131.0 jit_solution(9989968997571342531)
XLA Ops:
  0.6 1.3 fusion.16
  1.9 1.2 fusion.25
  3.2 0.6 broadcast_in_dim.16
  3.8 9.0 %all-to-all-start = ((f32[8,2,512]{2,1,0:T(2,128)}), f32[8,2,512]{2,1,0:T(2,128)S(1)}, u32[]{:S(2)}, u32[]{:S(2)}) async-start(f32[8,2,512]{2,1,0:T(2,128)} %broadcast_in_dim.16), calls=%async_computation | async-start | bytes 65536 | tf_op jit(solution)/shard_map/all_to_all | solution.py:55
  12.8 0.7 fusion.48
  13.5 1.2 reshape.170
  15.0 1.1 convert_bitcast_fusion
  16.1 1.6 %copy.109 = f32[4,512,128]{2,1,0:T(8,128)S(1)} copy(f32[4,512,128]{1,2,0:T(8,128)} %convert_bitcast_fusion) | data formatting | bytes 2097152 | tf_op jit(solution)/shard_map/convert_element_type | solution.py:156
  17.7 1.3 %copy.116 = f32[4,2,256,128]{2,3,1,0:T(8,128)} copy(f32[4,2,256,128]{3,2,1,0:T(8,128)S(1)} %bitcast.160) | data formatting | bytes 2097152 | tf_op jit(solution)/shard_map/convert_element_type | solution.py:156
  19.1 0.6 iota_compare_fusion
  21.1 1.2 convert_reduce_fusion.1
  22.3 1.1 convolution_convert_fusion
  23.5 2.2 %fusion.63 = (f32[4,136,128]{2,1,0:T(8,128)S(1)}, f32[4,2,136,128]{3,2,1,0:T(8,128)}) fusion(bf16[4,2,256,136]{2,3,1,0:T(8,128)(2,1)} %convolution_convert_fusion, bf16[4,2,256,128]{3,2,1,0:T(8,128)(2,1)S(1)} %bitcast.168), kind=kOutput, calls=%fused_computation.139 | convolution fusion | flops 71372800 | bytes 1916928 | tf_op jit(solution)/shard_map/...jr,...jd->...rd/dot_general | solution.py:61
  25.8 0.8 maximum_maximum_fusion
  26.6 9.1 %all-to-all-start.1 = ((f32[32,24,128]{2,1,0:T(8,128)}), f32[32,24,128]{2,1,0:T(8,128)}, u32[]{:S(2)}, u32[]{:S(2)}) async-start(f32[32,24,128]{2,1,0:T(8,128)} %bitcast.23), calls=%async_computation.1 | async-start | bytes 786432 | tf_op jit(solution)/shard_map/all_to_all | solution.py:41
  35.8 1.0 fusion.18
  36.7 1.2 reshape.166
  38.3 0.7 copy-done.23
  39.3 1.1 convolution_convert_fusion.1
  40.4 0.6 multiply_multiply_fusion.4
  41.0 2.8 %convert_reduce_fusion.2 = (f32[4,2,256]{2,1,0:T(2,128)}, bf16[4,2,256,256]{2,3,1,0:T(8,128)(2,1)}, f32[4,2,256,256]{2,3,1,0:T(8,128)}) fusion(pred[256,256]{0,1:T(8,128)(4,1)S(1)} %copy-done.33, bf16[4,2,256,128]{3,2,1,0:T(8,128)(2,1)S(1)} %bitcast.173, bf16[4,2,256,128]{3,2,1,0:T(8,128)(2,1)S(1)} %bitcast.176), kind=kOutput, calls=%fused_computation.19 | convolution fusion | flops 137885696 | bytes 4268032 | tf_op jit(solution)/shard_map/...id,...jd->...ij/dot_general | solution.py:61
  43.8 2.3 %all-to-all-done.1 = f32[32,24,128]{2,1,0:T(8,128)} async-done(((f32[32,24,128]{2,1,0:T(8,128)}), f32[32,24,128]{2,1,0:T(8,128)}, u32[]{:S(2)}, u32[]{:S(2)}) %all-to-all-start.1) | async-done | bytes 393248 | tf_op jit(solution)/shard_map/all_to_all | solution.py:41
  46.1 1.0 slice.110
  47.4 0.8 pad_add_fusion.4
  48.2 5.2 %all-to-all-start.2 = ((f32[32,24,128]{2,1,0:T(8,128)}), f32[32,24,128]{2,1,0:T(8,128)}, u32[]{:S(2)}, u32[]{:S(2)}) async-start(f32[32,24,128]{2,1,0:T(8,128)} %pad_add_fusion.4), calls=%async_computation.2 | async-start | bytes 786432 | tf_op jit(solution)/shard_map/all_to_all | solution.py:47
  53.4 0.6 multiply_multiply_fusion.5
  54.0 0.9 reduce_sum.144
  54.9 0.6 reduce_window_sum.34
  55.5 2.7 %fusion.66 = f32[4,2,256,128]{2,3,1,0:T(8,128)} fusion(bf16[4,2,256,256]{2,3,1,0:T(8,128)(2,1)} %get-tuple-element.37, bf16[4,2,256,128]{3,2,1,0:T(8,128)(2,1)} %bitcast.169), kind=kOutput, calls=%fused_computation.142 | convolution fusion | flops 134217728 | bytes 2621440 | tf_op jit(solution)/shard_map/...ij,...jd->...id/dot_general | solution.py:61
  58.2 5.5 %all-to-all-done.2 = f32[32,24,128]{2,1,0:T(8,128)} async-done(((f32[32,24,128]{2,1,0:T(8,128)}), f32[32,24,128]{2,1,0:T(8,128)}, u32[]{:S(2)}, u32[]{:S(2)}) %all-to-all-start.2) | async-done | bytes 393248 | tf_op jit(solution)/shard_map/all_to_all | solution.py:47
  63.7 0.8 slice_bitcast_fusion.1
  64.5 1.1 slice.117
  65.7 0.7 add_subtract_fusion.1
  67.4 1.3 multiply_reduce_fusion
  68.8 1.1 divide_convert_fusion.1
  69.9 0.9 fusion.44
  70.9 1.5 %fusion.64 = (f32[4,136,128]{2,1,0:T(8,128)S(1)}, f32[4,2,136,128]{3,2,1,0:T(8,128)S(1)}) fusion(bf16[4,2,256,136]{2,3,1,0:T(8,128)(2,1)} %convolution_convert_fusion.1, bf16[4,2,256,128]{3,2,1,0:T(8,128)(2,1)} %divide_convert_fusion.1), kind=kOutput, calls=%fused_computation.140 | convolution fusion | flops 71372800 | bytes 1916928 | tf_op jit(solution)/shard_map/...ir,...id->...rd/dot_general | solution.py:61
  72.5 1.6 %maximum_maximum_fusion.1 = f32[4,192,128]{2,1,0:T(8,128)} fusion(f32[4,2,128]{2,1,0:T(2,128)S(1)} %reshape.175, f32[4,136,128]{2,1,0:T(8,128)S(1)} %get-tuple-element.54, f32[192]{0:T(256)} %copy-done.51), kind=kLoop, calls=%fused_computation.71 | loop fusion | flops 196608 | bytes 676608 | tf_op jit(solution)/shard_map/concatenate | solution.py:32
  74.1 3.8 %all-to-all-start.3 = ((f32[32,24,128]{2,1,0:T(8,128)}), f32[32,24,128]{2,1,0:T(8,128)S(1)}, u32[]{:S(2)}, u32[]{:S(2)}) async-start(f32[32,24,128]{2,1,0:T(8,128)} %bitcast.32), calls=%async_computation.3 | async-start | bytes 786432 | tf_op jit(solution)/shard_map/all_to_all | solution.py:41
  77.9 0.8 rev.14
  78.8 2.1 %fusion.65 = f32[4,2,136,128]{3,2,1,0:T(8,128)} fusion(f32[4,2,136,128]{3,2,1,0:T(8,128)} %rev.14), kind=kOutput, calls=%fused_computation.141 | output fusion | flops 139264 | bytes 1114112 | tf_op jit(solution)/shard_map/jit(cumsum)/reduce_window_sum | solution.py:137
  81.4 0.8 fusion.6
  82.3 2.3 %fusion.10 = f32[4,2,256,16]{2,3,1,0:T(8,128)S(1)} fusion(f32[4,2,256,16,16]{2,4,3,1,0:T(8,128)S(1)} %bitcast.166, f32[4,2,256,16]{2,3,1,0:T(8,128)S(1)} %multiply_multiply_fusion.3), kind=kLoop, calls=%fused_computation.16 | loop fusion | flops 1540096 | bytes 2359296 | tf_op jit(solution)/shard_map/reduce_sum | solution.py:89
  84.7 0.9 divide_convert_fusion
  85.6 1.0 fusion.36
  87.1 0.8 all-to-all-done.3
  88.3 0.8 pad_add_fusion
  89.1 6.4 %all-to-all-start.4 = ((f32[32,24,128]{2,1,0:T(8,128)}), f32[32,24,128]{2,1,0:T(8,128)}, u32[]{:S(2)}, u32[]{:S(2)}) async-start(f32[32,24,128]{2,1,0:T(8,128)} %pad_add_fusion), calls=%async_computation.4 | async-start | bytes 786432 | tf_op jit(solution)/shard_map/all_to_all | solution.py:47
  95.5 1.3 %fusion.24 = f32[512]{0:T(512)S(1)} fusion(bf16[512,512]{1,0:T(8,128)(2,1)} %param.11, f32[4,64,8,128]{3,2,1,0:T(8,128)S(1)} %bitcast.162, f32[512]{0:T(512)S(1)} %copy-done.48), kind=kLoop, calls=%fused_computation.52 | loop fusion | flops 1048064 | bytes 1576960 | tf_op jit(solution)/shard_map/reduce_sum | solution.py:283
  97.1 2.0 %copy.117 = bf16[4,2,256,128]{3,2,1,0:T(8,128)(2,1)} copy(bf16[4,2,256,128]{2,3,1,0:T(8,128)(2,1)} %divide_convert_fusion) | data formatting | bytes 1048576 | tf_op jit(solution)/shard_map/convert_element_type | solution.py:260
  99.2 2.0 %copy.118 = bf16[512,4,128]{0,2,1:T(8,128)(2,1)} copy(bf16[512,4,128]{2,0,1:T(8,128)(2,1)} %bitcast.181) | data formatting | bytes 1048576 | tf_op jit(solution)/shard_map/transpose | solution.py:231
  101.2 2.0 %copy.131 = bf16[512,512]{1,0:T(8,128)(2,1)} copy(bf16[512,512]{0,1:T(8,128)(2,1)} %bitcast.182) | data formatting | bytes 1048576
  103.3 2.5 %fusion.67 = f32[4,2,256,128]{3,2,1,0:T(8,128)} fusion(bf16[4,2,256,256]{2,3,1,0:T(8,128)(2,1)S(1)} %copy-done, bf16[4,2,256,128]{3,2,1,0:T(8,128)(2,1)} %divide_convert_fusion.1), kind=kOutput, calls=%fused_computation.143 | convolution fusion | flops 134217728 | bytes 2621440 | tf_op jit(solution)/shard_map/...ij,...id->...jd/dot_general | solution.py:61
  105.8 0.8 slice_bitcast_fusion
  106.6 1.0 slice.124
  107.6 1.3 subtract_convert_fusion
  110.0 2.3 %fusion.8 = f32[4,2,256,16]{2,3,1,0:T(8,128)S(1)} fusion(f32[4,2,256,16,16]{2,4,3,1,0:T(8,128)S(1)} %bitcast.167, f32[4,2,256,16]{2,3,1,0:T(8,128)S(1)} %copy-done.27), kind=kLoop, calls=%fused_computation.13 | loop fusion | flops 1540096 | bytes 2359296 | tf_op jit(solution)/shard_map/reduce_sum | solution.py:89
  112.4 1.0 fusion.39
  114.7 0.6 broadcast_in_dim.19
  115.3 5.9 %all-to-all-start.5 = ((f32[8,2,512]{2,1,0:T(2,128)}), f32[8,2,512]{2,1,0:T(2,128)S(1)}, u32[]{:S(2)}, u32[]{:S(2)}) async-start(f32[8,2,512]{2,1,0:T(2,128)} %broadcast_in_dim.19), calls=%async_computation.5 | async-start | bytes 65536 | tf_op jit(solution)/shard_map/all_to_all | solution.py:55
  121.3 1.9 %fusion.12 = bf16[4,2,256,128]{3,2,1,0:T(8,128)(2,1)S(1)} fusion(f32[4,2,256,128]{3,2,1,0:T(8,128)} %fusion.67, bf16[4,2,256,256]{2,3,1,0:T(8,128)(2,1)S(1)} %bitcast.159, bf16[4,2,256,128]{2,3,1,0:T(8,128)(2,1)} %copy-done.17), kind=kOutput, calls=%fused_computation.38 | convolution fusion | flops 134742016 | bytes 3145728 | tf_op jit(solution)/shard_map/...jr,...rd->...jd/dot_general | solution.py:61
  123.2 0.9 copy.181
  124.0 4.1 %all-to-all-done.5 = f32[8,2,512]{2,1,0:T(2,128)S(1)} async-done(((f32[8,2,512]{2,1,0:T(2,128)}), f32[8,2,512]{2,1,0:T(2,128)S(1)}, u32[]{:S(2)}, u32[]{:S(2)}) %all-to-all-start.5) | async-done | bytes 32800 | tf_op jit(solution)/shard_map/all_to_all | solution.py:55
  128.2 2.8 %fusion.22 = (bf16[512,512]{1,0:T(8,128)(2,1)}, bf16[512,512]{1,0:T(8,128)(2,1)}) fusion(bf16[512,512]{1,0:T(8,128)(2,1)} %param.11, f32[4,64,8,128]{3,2,1,0:T(8,128)S(1)} %bitcast.163, f32[512]{0:T(512)S(1)} %bitcast.199, f32[512]{0:T(512)S(1)} %copy-done.53, f32[512]{0:T(512)S(1)} %copy-done.48, f32[512]{0:T(512)S(1)} %bitcast.193, f32[512]{0:T(512)S(1)} %bitcast.198, ...), kind=kLoop, calls=%fused_computation.50 | loop fusion | flops 4194304 | bytes 4210688 | tf_op jit(solution)/shard_map/convert_element_type | solution.py:205
  (167 shorter events, 7.9 us)
Async XLA Ops:
  0.6 14.1 %copy-start.28 = (bf16[512,512]{1,0:T(8,128)(2,1)S(1)}, bf16[512,512]{1,0:T(8,128)(2,1)}, u32[]{:S(2)}) copy-start(bf16[512,512]{1,0:T(8,128)(2,1)} %param.14) | copy-start | bytes 1572868
  3.8 16.0 %all-to-all-start = ((f32[8,2,512]{2,1,0:T(2,128)}), f32[8,2,512]{2,1,0:T(2,128)S(1)}, u32[]{:S(2)}, u32[]{:S(2)}) async-start(f32[8,2,512]{2,1,0:T(2,128)} %broadcast_in_dim.16), calls=%async_computation | async-start | bytes 65536 | tf_op jit(solution)/shard_map/all_to_all | solution.py:55
  14.8 8.8 %copy-start.1 = (bf16[4,512,128]{2,1,0:T(8,128)(2,1)}, bf16[4,512,128]{2,1,0:T(8,128)(2,1)S(1)}, u32[]{:S(2)}) copy-start(bf16[4,512,128]{2,1,0:T(8,128)(2,1)S(1)} %copy.112) | copy-start | bytes 1572868
  16.1 3.7 %copy-start.6 = (bf16[512,512]{1,0:T(8,128)(2,1)S(1)}, bf16[512,512]{1,0:T(8,128)(2,1)}, u32[]{:S(2)}) copy-start(bf16[512,512]{1,0:T(8,128)(2,1)} %param.12) | copy-start | bytes 1572868
  16.1 3.7 %copy-start.49 = (f32[512]{0:T(512)S(1)}, f32[512]{0:T(512)}, u32[]{:S(2)}) copy-start(f32[512]{0:T(512)} %param.16) | copy-start | bytes 6148
  19.1 6.6 %copy-start.51 = (f32[192]{0:T(256)}, f32[192]{0:T(256)S(1)}, u32[]{:S(2)}) copy-start(f32[192]{0:T(256)S(1)} %pad.69.clone) | copy-start | bytes 2308
  19.8 20.6 %copy-start.43 = (f32[1,512]{1,0:T(1,128)}, f32[1,512]{1,0:T(1,128)S(1)}, u32[]{:S(2)}) copy-start(f32[1,512]{1,0:T(1,128)S(1)} %get-tuple-element.47) | copy-start | bytes 6148
  19.8 33.6 %copy-start.45 = (f32[1,512]{1,0:T(1,128)}, f32[1,512]{1,0:T(1,128)S(1)}, u32[]{:S(2)}) copy-start(f32[1,512]{1,0:T(1,128)S(1)} %get-tuple-element.48) | copy-start | bytes 6148
  20.0 2.2 %copy-start.29 = (bf16[256,136,1,1]{0,1,3,2:T(8,128)(2,1)S(1)}, bf16[256,136,1,1]{0,1,3,2:T(8,128)(2,1)}, u32[]{:S(2)}) copy-start(bf16[256,136,1,1]{0,1,3,2:T(8,128)(2,1)} %constant.67) | copy-start | bytes 208900
  20.3 0.8 copy-start.10
  21.1 1.2 copy-start.26
  23.4 12.3 %copy-start.5 = (bf16[512,512]{1,0:T(8,128)(2,1)S(1)}, bf16[512,512]{1,0:T(8,128)(2,1)}, u32[]{:S(2)}) copy-start(bf16[512,512]{1,0:T(8,128)(2,1)} %param.11) | copy-start | bytes 1572868
  23.4 12.3 %copy-start.47 = (f32[512]{0:T(512)S(1)}, f32[512]{0:T(512)}, u32[]{:S(2)}) copy-start(f32[512]{0:T(512)} %param.15) | copy-start | bytes 6148
  26.6 19.5 %all-to-all-start.1 = ((f32[32,24,128]{2,1,0:T(8,128)}), f32[32,24,128]{2,1,0:T(8,128)}, u32[]{:S(2)}, u32[]{:S(2)}) async-start(f32[32,24,128]{2,1,0:T(8,128)} %bitcast.23), calls=%async_computation.1 | async-start | bytes 786432 | tf_op jit(solution)/shard_map/all_to_all | solution.py:41
  37.9 1.4 %copy-start.30 = (bf16[256,136,1,1]{0,1,3,2:T(8,128)(2,1)S(1)}, bf16[256,136,1,1]{0,1,3,2:T(8,128)(2,1)}, u32[]{:S(2)}) copy-start(bf16[256,136,1,1]{0,1,3,2:T(8,128)(2,1)} %constant.67) | copy-start | bytes 208900
  38.0 3.0 %copy-start.8 = (bf16[4,512,128]{2,1,0:T(8,128)(2,1)}, bf16[4,512,128]{2,1,0:T(8,128)(2,1)S(1)}, u32[]{:S(2)}) copy-start(bf16[4,512,128]{2,1,0:T(8,128)(2,1)S(1)} %copy.106) | copy-start | bytes 1572868
  38.0 3.0 %copy-start.11 = (bf16[4,512,128]{2,1,0:T(8,128)(2,1)S(1)}, bf16[4,512,128]{2,1,0:T(8,128)(2,1)}, u32[]{:S(2)}) copy-start(bf16[4,512,128]{2,1,0:T(8,128)(2,1)} %copy-done.10) | copy-start | bytes 1572868
  38.0 3.0 %copy-start.33 = (pred[256,256]{0,1:T(8,128)(4,1)S(1)}, pred[256,256]{0,1:T(8,128)(4,1)}, u32[]{:S(2)}) copy-start(pred[256,256]{0,1:T(8,128)(4,1)} %iota_compare_fusion) | copy-start | bytes 196612
  38.3 0.7 copy-start.23
  48.2 15.5 %all-to-all-start.2 = ((f32[32,24,128]{2,1,0:T(8,128)}), f32[32,24,128]{2,1,0:T(8,128)}, u32[]{:S(2)}, u32[]{:S(2)}) async-start(f32[32,24,128]{2,1,0:T(8,128)} %pad_add_fusion.4), calls=%async_computation.2 | async-start | bytes 786432 | tf_op jit(solution)/shard_map/all_to_all | solution.py:47
  54.9 10.8 %copy-start.41 = (f32[4,2,256]{2,1,0:T(2,128)}, f32[4,2,256]{2,1,0:T(2,128)S(1)}, u32[]{:S(2)}) copy-start(f32[4,2,256]{2,1,0:T(2,128)S(1)} %reduce_sum.144) | copy-start | bytes 24580
  63.7 3.2 %copy-start.14 = (f32[4,2,136,128]{3,2,1,0:T(8,128)S(1)}, f32[4,2,136,128]{3,2,1,0:T(8,128)}, u32[]{:S(2)}) copy-start(f32[4,2,136,128]{3,2,1,0:T(8,128)} %get-tuple-element.51) | copy-start | bytes 1671172
  63.7 3.3 %copy-start.31 = (bf16[256,136,1,1]{0,1,3,2:T(8,128)(2,1)S(1)}, bf16[256,136,1,1]{0,1,3,2:T(8,128)(2,1)}, u32[]{:S(2)}) copy-start(bf16[256,136,1,1]{0,1,3,2:T(8,128)(2,1)} %constant.68) | copy-start | bytes 208900
  64.5 2.9 %copy-start.20 = (f32[4,2,256,128]{2,3,1,0:T(8,128)S(1)}, f32[4,2,256,128]{2,3,1,0:T(8,128)}, u32[]{:S(2)}) copy-start(f32[4,2,256,128]{2,3,1,0:T(8,128)} %copy.116) | copy-start | bytes 3145732
  64.5 2.9 %copy-start.22 = (f32[4,2,256,128]{2,3,1,0:T(8,128)S(1)}, f32[4,2,256,128]{2,3,1,0:T(8,128)}, u32[]{:S(2)}) copy-start(f32[4,2,256,128]{2,3,1,0:T(8,128)} %fusion.66) | copy-start | bytes 3145732
  66.4 2.3 %copy-start.35 = (f32[4,2,256]{2,1,0:T(2,128)}, f32[4,2,256]{2,1,0:T(2,128)S(1)}, u32[]{:S(2)}) copy-start(f32[4,2,256]{2,1,0:T(2,128)S(1)} %add_subtract_fusion.1) | copy-start | bytes 24580
  67.4 1.3 %copy-start.15 = (bf16[4,2,256,128]{2,3,1,0:T(8,128)(2,1)}, bf16[4,2,256,128]{2,3,1,0:T(8,128)(2,1)S(1)}, u32[]{:S(2)}) copy-start(bf16[4,2,256,128]{2,3,1,0:T(8,128)(2,1)S(1)} %fusion.14) | copy-start | bytes 1572868
  67.4 1.3 %copy-start.42 = (f32[4,2,256]{2,1,0:T(2,128)S(1)}, f32[4,2,256]{2,1,0:T(2,128)}, u32[]{:S(2)}) copy-start(f32[4,2,256]{2,1,0:T(2,128)} %get-tuple-element.36) | copy-start | bytes 24580
  68.7 1.2 copy-start.37
  68.7 2.1 %copy-start.39 = (f32[4,2,256]{2,1,0:T(2,128)}, f32[4,2,256]{2,1,0:T(2,128)S(1)}, u32[]{:S(2)}) copy-start(f32[4,2,256]{2,1,0:T(2,128)S(1)} %get-tuple-element.15) | copy-start | bytes 24580
  72.4 9.0 %copy-start.13 = (f32[4,2,136,128]{3,2,1,0:T(8,128)}, f32[4,2,136,128]{3,2,1,0:T(8,128)S(1)}, u32[]{:S(2)}) copy-start(f32[4,2,136,128]{3,2,1,0:T(8,128)S(1)} %get-tuple-element.55) | copy-start | bytes 1671172
  72.4 8.4 %copy-start.4 = (bf16[4,2,256,128]{3,2,1,0:T(8,128)(2,1)S(1)}, bf16[4,2,256,128]{3,2,1,0:T(8,128)(2,1)}, u32[]{:S(2)}) copy-start(bf16[4,2,256,128]{3,2,1,0:T(8,128)(2,1)} %divide_convert_fusion.1) | copy-start | bytes 1572868
  72.4 8.4 %copy-start.16 = (bf16[4,2,256,128]{2,3,1,0:T(8,128)(2,1)S(1)}, bf16[4,2,256,128]{2,3,1,0:T(8,128)(2,1)}, u32[]{:S(2)}) copy-start(bf16[4,2,256,128]{2,3,1,0:T(8,128)(2,1)} %copy-done.15) | copy-start | bytes 1572868
  72.4 8.4 %copy-start.36 = (f32[4,2,256]{2,1,0:T(2,128)S(1)}, f32[4,2,256]{2,1,0:T(2,128)}, u32[]{:S(2)}) copy-start(f32[4,2,256]{2,1,0:T(2,128)} %copy-done.35) | copy-start | bytes 24580
  72.4 8.4 %copy-start.40 = (f32[4,2,256]{2,1,0:T(2,128)S(1)}, f32[4,2,256]{2,1,0:T(2,128)}, u32[]{:S(2)}) copy-start(f32[4,2,256]{2,1,0:T(2,128)} %copy-done.39) | copy-start | bytes 24580
  74.1 13.9 %all-to-all-start.3 = ((f32[32,24,128]{2,1,0:T(8,128)}), f32[32,24,128]{2,1,0:T(8,128)S(1)}, u32[]{:S(2)}, u32[]{:S(2)}) async-start(f32[32,24,128]{2,1,0:T(8,128)} %bitcast.32), calls=%async_computation.3 | async-start | bytes 786432 | tf_op jit(solution)/shard_map/all_to_all | solution.py:41
  78.8 2.6 %copy-start.2 = (bf16[4,512,128]{2,1,0:T(8,128)(2,1)S(1)}, bf16[4,512,128]{2,1,0:T(8,128)(2,1)}, u32[]{:S(2)}) copy-start(bf16[4,512,128]{2,1,0:T(8,128)(2,1)} %copy-done.1) | copy-start | bytes 1572868
  78.8 2.6 %copy-start.25 = (f32[4,2,256,256]{2,3,1,0:T(8,128)S(1)}, f32[4,2,256,256]{2,3,1,0:T(8,128)}, u32[]{:S(2)}) copy-start(f32[4,2,256,256]{2,3,1,0:T(8,128)} %get-tuple-element.49) | copy-start | bytes 6291460
  78.8 2.6 %copy-start.34 = (pred[256,256]{0,1:T(8,128)(4,1)S(1)}, pred[256,256]{0,1:T(8,128)(4,1)}, u32[]{:S(2)}) copy-start(pred[256,256]{0,1:T(8,128)(4,1)} %iota_compare_fusion) | copy-start | bytes 196612
  82.2 4.4 %copy-start.18 = (bf16[4,2,256,256]{2,3,1,0:T(8,128)(2,1)}, bf16[4,2,256,256]{2,3,1,0:T(8,128)(2,1)S(1)}, u32[]{:S(2)}) copy-start(bf16[4,2,256,256]{2,3,1,0:T(8,128)(2,1)S(1)} %fusion.6) | copy-start | bytes 3145732
  82.3 2.4 %copy-start.24 = (f32[4,2,256,32]{2,3,1,0:T(8,128)S(1)}, f32[4,2,256,32]{2,3,1,0:T(8,128)}, u32[]{:S(2)}) copy-start(f32[4,2,256,32]{2,3,1,0:T(8,128)} %copy-done.23) | copy-start | bytes 786436
  82.3 2.4 %copy-start.21 = (f32[4,2,256,128]{2,3,1,0:T(8,128)S(1)}, f32[4,2,256,128]{2,3,1,0:T(8,128)}, u32[]{:S(2)}) copy-start(f32[4,2,256,128]{2,3,1,0:T(8,128)} %get-tuple-element.12) | copy-start | bytes 3145732
  82.3 2.4 %copy-start.38 = (f32[4,2,256]{2,1,0:T(2,128)S(1)}, f32[4,2,256]{2,1,0:T(2,128)}, u32[]{:S(2)}) copy-start(f32[4,2,256]{2,1,0:T(2,128)} %copy-done.37) | copy-start | bytes 24580
  84.6 2.0 %copy-start.12 = (bf16[4,512,128]{2,1,0:T(8,128)(2,1)S(1)}, bf16[4,512,128]{2,1,0:T(8,128)(2,1)}, u32[]{:S(2)}) copy-start(bf16[4,512,128]{2,1,0:T(8,128)(2,1)} %copy-done.10) | copy-start | bytes 1572868
  88.2 7.3 %copy-start.48 = (f32[512]{0:T(512)S(1)}, f32[512]{0:T(512)}, u32[]{:S(2)}) copy-start(f32[512]{0:T(512)} %param.15) | copy-start | bytes 6148
  89.1 16.7 %all-to-all-start.4 = ((f32[32,24,128]{2,1,0:T(8,128)}), f32[32,24,128]{2,1,0:T(8,128)}, u32[]{:S(2)}, u32[]{:S(2)}) async-start(f32[32,24,128]{2,1,0:T(8,128)} %pad_add_fusion), calls=%async_computation.4 | async-start | bytes 786432 | tf_op jit(solution)/shard_map/all_to_all | solution.py:47
  95.5 7.8 %copy-start = (bf16[4,2,256,256]{2,3,1,0:T(8,128)(2,1)S(1)}, bf16[4,2,256,256]{2,3,1,0:T(8,128)(2,1)}, u32[]{:S(2)}) copy-start(bf16[4,2,256,256]{2,3,1,0:T(8,128)(2,1)} %get-tuple-element.37) | copy-start | bytes 3145732
  103.3 5.6 %copy-start.32 = (bf16[256,136,1,1]{0,1,3,2:T(8,128)(2,1)S(1)}, bf16[256,136,1,1]{0,1,3,2:T(8,128)(2,1)}, u32[]{:S(2)}) copy-start(bf16[256,136,1,1]{0,1,3,2:T(8,128)(2,1)} %constant.68) | copy-start | bytes 208900
  105.7 3.6 %copy-start.3 = (bf16[4,512,128]{2,1,0:T(8,128)(2,1)S(1)}, bf16[4,512,128]{2,1,0:T(8,128)(2,1)}, u32[]{:S(2)}) copy-start(bf16[4,512,128]{2,1,0:T(8,128)(2,1)} %copy-done.1) | copy-start | bytes 1572868
  108.9 1.2 copy-start.27
  109.2 0.8 copy-start.17
  110.0 3.4 %copy-start.9 = (bf16[4,512,128]{2,1,0:T(8,128)(2,1)S(1)}, bf16[4,512,128]{2,1,0:T(8,128)(2,1)}, u32[]{:S(2)}) copy-start(bf16[4,512,128]{2,1,0:T(8,128)(2,1)} %copy-done.8) | copy-start | bytes 1572868
  110.0 3.4 %copy-start.19 = (bf16[4,2,256,256]{2,3,1,0:T(8,128)(2,1)S(1)}, bf16[4,2,256,256]{2,3,1,0:T(8,128)(2,1)}, u32[]{:S(2)}) copy-start(bf16[4,2,256,256]{2,3,1,0:T(8,128)(2,1)} %copy-done.18) | copy-start | bytes 3145732
  113.4 1.0 copy-start.7
  113.5 1.0 copy-start.50
  115.3 12.8 %all-to-all-start.5 = ((f32[8,2,512]{2,1,0:T(2,128)}), f32[8,2,512]{2,1,0:T(2,128)S(1)}, u32[]{:S(2)}, u32[]{:S(2)}) async-start(f32[8,2,512]{2,1,0:T(2,128)} %broadcast_in_dim.19), calls=%async_computation.5 | async-start | bytes 65536 | tf_op jit(solution)/shard_map/all_to_all | solution.py:55
  121.2 6.9 %copy-start.44 = (f32[1,512]{1,0:T(1,128)S(1)}, f32[1,512]{1,0:T(1,128)}, u32[]{:S(2)}) copy-start(f32[1,512]{1,0:T(1,128)} %copy-done.43) | copy-start | bytes 6148
  121.2 6.9 %copy-start.46 = (f32[1,512]{1,0:T(1,128)S(1)}, f32[1,512]{1,0:T(1,128)}, u32[]{:S(2)}) copy-start(f32[1,512]{1,0:T(1,128)} %copy-done.45) | copy-start | bytes 6148
  121.2 6.9 %copy-start.52 = (f32[512]{0:T(512)S(1)}, f32[512]{0:T(512)}, u32[]{:S(2)}) copy-start(f32[512]{0:T(512)} %multiply_multiply_fusion.4) | copy-start | bytes 6148
  121.2 6.9 %copy-start.53 = (f32[512]{0:T(512)S(1)}, f32[512]{0:T(512)}, u32[]{:S(2)}) copy-start(f32[512]{0:T(512)} %multiply_multiply_fusion.5) | copy-start | bytes 6148

commit v9 on v8

--- a/solution.py
+++ b/solution.py
@@ -250,14 +250,13 @@
     scaled_grad, den_grad, block_u, block_w = backward_states(
         g_heads, numerator, denominator, q_parts[0]
     )
-    later_u, later_w, (scaled_grad, den_grad, numerator, denominator) = carried_in(
+    later_u, later_w, (scaled_grad, den_grad) = carried_in(
         jnp.sum(block_u, axis=1),
         jnp.sum(block_w, axis=1),
         "ctx",
         True,
-        (scaled_grad, den_grad, numerator, denominator),
-    )
-    attended = (numerator / denominator[..., None]).astype(jnp.bfloat16)
+        (scaled_grad, den_grad),
+    )
     q_diag, k_diag, v_diag, qf_grad = backward_blocks(
         scaled_grad,
         den_grad,
@@ -278,14 +277,15 @@
     kn_grad = join_heads(
         k_diag + sketch_back(kf_grad, k_parts[1], k_parts[2], k_parts[3], sign_pair)
     )
-    (q_dot, k_dot), (v_diag, later_state) = head_sum(
+    (q_dot, k_dot), (v_diag, later_state, numerator, denominator) = head_sum(
         (
             jnp.sum(q_float * q_gain * qn_grad, axis=-1),
             jnp.sum(k_float * k_gain * kn_grad, axis=-1),
         ),
         "head",
-        (v_diag, later_state),
-    )
+        (v_diag, later_state, numerator, denominator),
+    )
+    attended = (numerator / denominator[..., None]).astype(jnp.bfloat16)
     _, v_grad = finish_backward(v_heads, k_parts[0], later_state, later_total, v_diag)
     q_grad = norm_back(queries, q_gain, q_scale, qn_grad, q_dot)
     k_grad = norm_back(keys, k_gain, k_scale, kn_grad, k_dot)

time: 133 us -> 137 us (1.030)
  waiting for transfers between devices: 12.8 us -> 19.5 us
  starting transfers between devices: 39.4 us -> 37.6 us
  other arithmetic: 29.2 us -> 27.7 us
    all_to_all x2, waiting for transfers between devices: 5.58 us -> 11.4 us  [carried_in(): lax.all_to_all(shifted, axis, 0, 0, tiled=True)]
    all_to_all x2, waiting for transfers between devices: 3.1 us -> 8.07 us  [carried_in(): mine = lax.all_to_all(stacked, axis, 0, 0, tiled=True)]
    all_to_all x2, waiting for transfers between devices: 4.08 us -> 0.01 us  [head_sum(): gathered = lax.all_to_all(spread, axis, 0, 0, tiled=True)]
    all_to_all x2, starting transfers between devices: 11.5 us -> 9.76 us  [carried_in(): lax.all_to_all(shifted, axis, 0, 0, tiled=True)]
    unnamed x114 -> x118, local copies, waits for them, and re-layouts: 6.07 us -> 6.06 us
  transfers between devices with their start and end apart: 6 -> 6, of which waited for: 5 -> 4; matrix products, arithmetic and copies ran while one was open for 31% -> 27% of each run, Pallas kernels for 0% -> 0%
where the time goes in v9:
time: 137 us; the launch traced here: 135 us
  starting transfers between devices  37.6 us (27%)
  other arithmetic  27.7 us (20%)
  matrix products  25.6 us (19%)
  local copies, waits for them, and re-layouts  23.3 us (17%)
  waiting for transfers between devices  19.5 us (14%)
  between operations  1.62 us (1%)
    dot_general x18, matrix products, product_of(): return jnp.einsum(spec, lhs, rhs, preferred_element_type=jnp.float32)  22.2 us
    all_to_all x2, starting transfers between devices, head_sum(): gathered = lax.all_to_all(spread, axis, 0, 0, tiled=True)  14.9 us
    all_to_all x2, starting transfers between devices, carried_in(): mine = lax.all_to_all(stacked, axis, 0, 0, tiled=True)  12.9 us
    all_to_all x2, waiting for transfers between devices, carried_in(): lax.all_to_all(shifted, axis, 0, 0, tiled=True)  11.4 us
    all_to_all x2, starting transfers between devices, carried_in(): lax.all_to_all(shifted, axis, 0, 0, tiled=True)  9.76 us
    all_to_all x2, waiting for transfers between devices, carried_in(): mine = lax.all_to_all(stacked, axis, 0, 0, tiled=True)  8.07 us
    unnamed x118, local copies, waits for them, and re-layouts  6.06 us
    reduce_sum x2, other arithmetic, sketch_back(): sketch_grad = jnp.sum(symmetric * sketched[..., None, :], axis=-1)  4.64 us
  transfers between devices with their start and end apart: 6, of which 4 were waited for; matrix products, arithmetic and copies ran while one was open for 27% of the time, Pallas kernels for 0%

profile of v9, /device:TPU:1, one launch (start us, length us, event | category | flops | bytes accessed | tf_op | source)
XLA Modules:
  0.0 135.3 jit_solution(5236752733940020722)
XLA Ops:
  0.6 1.3 fusion.18
  1.9 1.2 fusion.25
  3.2 0.6 broadcast_in_dim.17
  3.8 9.0 %all-to-all-start = ((f32[8,2,512]{2,1,0:T(2,128)}), f32[8,2,512]{2,1,0:T(2,128)S(1)}, u32[]{:S(2)}, u32[]{:S(2)}) async-start(f32[8,2,512]{2,1,0:T(2,128)} %broadcast_in_dim.17), calls=%async_computation | async-start | bytes 65536 | tf_op jit(solution)/shard_map/all_to_all | solution.py:55
  12.8 0.7 fusion.48
  13.5 1.2 reshape.170
  15.0 1.1 convert_bitcast_fusion
  16.1 1.6 %copy.110 = f32[4,512,128]{2,1,0:T(8,128)S(1)} copy(f32[4,512,128]{1,2,0:T(8,128)} %convert_bitcast_fusion) | data formatting | bytes 2097152 | tf_op jit(solution)/shard_map/convert_element_type | solution.py:156
  17.7 1.3 copy.116
  19.1 0.6 iota_compare_fusion
  21.1 1.2 convert_reduce_fusion.1
  22.3 1.1 convolution_convert_fusion
  23.5 2.2 %fusion.63 = (f32[4,136,128]{2,1,0:T(8,128)S(1)}, f32[4,2,136,128]{3,2,1,0:T(8,128)}) fusion(bf16[4,2,256,136]{2,3,1,0:T(8,128)(2,1)} %convolution_convert_fusion, bf16[4,2,256,128]{3,2,1,0:T(8,128)(2,1)S(1)} %bitcast.168), kind=kOutput, calls=%fused_computation.139 | convolution fusion | flops 71372800 | bytes 1916928 | tf_op jit(solution)/shard_map/...jr,...jd->...rd/dot_general | solution.py:61
  25.7 0.8 maximum_maximum_fusion
  26.6 9.1 %all-to-all-start.1 = ((f32[32,24,128]{2,1,0:T(8,128)}), f32[32,24,128]{2,1,0:T(8,128)}, u32[]{:S(2)}, u32[]{:S(2)}) async-start(f32[32,24,128]{2,1,0:T(8,128)} %bitcast.23), calls=%async_computation.1 | async-start | bytes 786432 | tf_op jit(solution)/shard_map/all_to_all | solution.py:41
  35.7 1.0 fusion.20
  36.7 1.2 reshape.166
  38.3 0.7 copy-done.25
  39.3 1.1 convolution_convert_fusion.1
  41.0 2.8 %convert_reduce_fusion.2 = (f32[4,2,256]{2,1,0:T(2,128)}, bf16[4,2,256,256]{2,3,1,0:T(8,128)(2,1)}, f32[4,2,256,256]{2,3,1,0:T(8,128)}) fusion(pred[256,256]{0,1:T(8,128)(4,1)S(1)} %copy-done.35, bf16[4,2,256,128]{3,2,1,0:T(8,128)(2,1)S(1)} %bitcast.173, bf16[4,2,256,128]{3,2,1,0:T(8,128)(2,1)S(1)} %bitcast.176), kind=kOutput, calls=%fused_computation.19 | convolution fusion | flops 137885696 | bytes 4268032 | tf_op jit(solution)/shard_map/...id,...jd->...ij/dot_general | solution.py:61
  43.8 2.3 %all-to-all-done.1 = f32[32,24,128]{2,1,0:T(8,128)} async-done(((f32[32,24,128]{2,1,0:T(8,128)}), f32[32,24,128]{2,1,0:T(8,128)}, u32[]{:S(2)}, u32[]{:S(2)}) %all-to-all-start.1) | async-done | bytes 393248 | tf_op jit(solution)/shard_map/all_to_all | solution.py:41
  46.1 1.0 slice.110
  47.4 0.8 pad_add_fusion.4
  48.2 5.2 %all-to-all-start.2 = ((f32[32,24,128]{2,1,0:T(8,128)}), f32[32,24,128]{2,1,0:T(8,128)}, u32[]{:S(2)}, u32[]{:S(2)}) async-start(f32[32,24,128]{2,1,0:T(8,128)} %pad_add_fusion.4), calls=%async_computation.2 | async-start | bytes 786432 | tf_op jit(solution)/shard_map/all_to_all | solution.py:47
  53.4 0.6 multiply_multiply_fusion.5
  54.0 0.9 reduce_sum.144
  54.9 0.6 reduce_window_sum.34
  55.5 2.7 %fusion.66 = f32[4,2,256,128]{2,3,1,0:T(8,128)} fusion(bf16[4,2,256,256]{2,3,1,0:T(8,128)(2,1)} %get-tuple-element.37, bf16[4,2,256,128]{3,2,1,0:T(8,128)(2,1)} %bitcast.169), kind=kOutput, calls=%fused_computation.142 | convolution fusion | flops 134217728 | bytes 2621440 | tf_op jit(solution)/shard_map/...ij,...jd->...id/dot_general | solution.py:61
  58.2 5.5 %all-to-all-done.2 = f32[32,24,128]{2,1,0:T(8,128)} async-done(((f32[32,24,128]{2,1,0:T(8,128)}), f32[32,24,128]{2,1,0:T(8,128)}, u32[]{:S(2)}, u32[]{:S(2)}) %all-to-all-start.2) | async-done | bytes 393248 | tf_op jit(solution)/shard_map/all_to_all | solution.py:47
  63.7 0.8 slice_bitcast_fusion.1
  64.5 1.1 slice.117
  65.6 0.7 add_subtract_fusion.1
  67.4 1.3 multiply_reduce_fusion
  68.7 0.6 multiply_divide_fusion
  69.3 0.9 fusion.44
  70.3 1.1 divide_convert_fusion.1
  71.4 1.6 %fusion.64 = (f32[4,136,128]{2,1,0:T(8,128)S(1)}, f32[4,2,136,128]{3,2,1,0:T(8,128)S(1)}) fusion(bf16[4,2,256,136]{2,3,1,0:T(8,128)(2,1)} %convolution_convert_fusion.1, bf16[4,2,256,128]{3,2,1,0:T(8,128)(2,1)S(1)} %divide_convert_fusion.1), kind=kOutput, calls=%fused_computation.140 | convolution fusion | flops 71372800 | bytes 1916928 | tf_op jit(solution)/shard_map/...ir,...id->...rd/dot_general | solution.py:61
  73.0 0.9 maximum_maximum_fusion.1
  74.5 2.3 %fusion.10 = f32[4,2,256,16]{2,3,1,0:T(8,128)S(1)} fusion(f32[4,2,256,16,16]{2,4,3,1,0:T(8,128)S(1)} %bitcast.166, f32[4,2,256,16]{2,3,1,0:T(8,128)S(1)} %multiply_multiply_fusion.3), kind=kLoop, calls=%fused_computation.16 | loop fusion | flops 1540096 | bytes 2359296 | tf_op jit(solution)/shard_map/reduce_sum | solution.py:89
  76.9 1.8 %fusion.4 = bf16[4,2,256,256]{2,3,1,0:T(8,128)(2,1)} fusion(f32[4,2,256,256]{2,3,1,0:T(8,128)S(1)} %copy-done.27, bf16[4,2,256,128]{3,2,1,0:T(8,128)(2,1)S(1)} %divide_convert_fusion.1, bf16[4,2,256,128]{3,2,1,0:T(8,128)(2,1)S(1)} %bitcast.170, f32[4,2,256]{2,1,0:T(2,128)S(1)} %copy-done.41, pred[256,256]{0,1:T(8,128)(4,1)S(1)} %copy-done.36), kind=kOutput, calls=%fused_computation.8 | convolution fusion | flops 138936320 | bytes 4268032 | tf_op jit(solution)/shard_map/...id,...jd->...ij/dot_general | solution.py:61
  78.7 3.8 %all-to-all-start.3 = ((f32[32,24,128]{2,1,0:T(8,128)}), f32[32,24,128]{2,1,0:T(8,128)S(1)}, u32[]{:S(2)}, u32[]{:S(2)}) async-start(f32[32,24,128]{2,1,0:T(8,128)} %bitcast.32), calls=%async_computation.3 | async-start | bytes 786432 | tf_op jit(solution)/shard_map/all_to_all | solution.py:41
  82.5 0.9 rev.14
  83.3 2.0 %fusion.65 = f32[4,2,136,128]{3,2,1,0:T(8,128)} fusion(f32[4,2,136,128]{3,2,1,0:T(8,128)} %rev.14), kind=kOutput, calls=%fused_computation.141 | output fusion | flops 139264 | bytes 1114112 | tf_op jit(solution)/shard_map/jit(cumsum)/reduce_window_sum | solution.py:137
  85.3 1.0 fusion.36
  86.9 5.8 %all-to-all-done.3 = f32[32,24,128]{2,1,0:T(8,128)S(1)} async-done(((f32[32,24,128]{2,1,0:T(8,128)}), f32[32,24,128]{2,1,0:T(8,128)S(1)}, u32[]{:S(2)}, u32[]{:S(2)}) %all-to-all-start.3) | async-done | bytes 393248 | tf_op jit(solution)/shard_map/all_to_all | solution.py:41
  93.0 0.8 pad_add_fusion
  93.8 4.6 %all-to-all-start.4 = ((f32[32,24,128]{2,1,0:T(8,128)}), f32[32,24,128]{2,1,0:T(8,128)}, u32[]{:S(2)}, u32[]{:S(2)}) async-start(f32[32,24,128]{2,1,0:T(8,128)} %pad_add_fusion), calls=%async_computation.4 | async-start | bytes 786432 | tf_op jit(solution)/shard_map/all_to_all | solution.py:47
  98.4 1.3 fusion.17
  100.0 2.5 %fusion.67 = f32[4,2,256,128]{3,2,1,0:T(8,128)} fusion(bf16[4,2,256,256]{2,3,1,0:T(8,128)(2,1)S(1)} %copy-done, bf16[4,2,256,128]{3,2,1,0:T(8,128)(2,1)} %copy-done.4), kind=kOutput, calls=%fused_computation.143 | convolution fusion | flops 134217728 | bytes 2621440 | tf_op jit(solution)/shard_map/...ij,...id->...jd/dot_general | solution.py:61
  102.4 5.9 %all-to-all-done.4 = f32[32,24,128]{2,1,0:T(8,128)} async-done(((f32[32,24,128]{2,1,0:T(8,128)}), f32[32,24,128]{2,1,0:T(8,128)}, u32[]{:S(2)}, u32[]{:S(2)}) %all-to-all-start.4) | async-done | bytes 393248 | tf_op jit(solution)/shard_map/all_to_all | solution.py:47
  108.4 0.7 slice_bitcast_fusion
  109.1 1.0 slice.124
  110.1 1.3 subtract_convert_fusion
  112.6 2.3 %fusion.8 = f32[4,2,256,16]{2,3,1,0:T(8,128)S(1)} fusion(f32[4,2,256,16,16]{2,4,3,1,0:T(8,128)S(1)} %bitcast.167, f32[4,2,256,16]{2,3,1,0:T(8,128)S(1)} %copy-done.29), kind=kLoop, calls=%fused_computation.13 | loop fusion | flops 1540096 | bytes 2359296 | tf_op jit(solution)/shard_map/reduce_sum | solution.py:89
  114.9 1.0 fusion.39
  117.2 0.6 broadcast_in_dim.19
  117.8 5.9 %all-to-all-start.5 = ((f32[8,2,512]{2,1,0:T(2,128)}), f32[8,2,512]{2,1,0:T(2,128)S(1)}, u32[]{:S(2)}, u32[]{:S(2)}) async-start(f32[8,2,512]{2,1,0:T(2,128)} %broadcast_in_dim.19), calls=%async_computation.5 | async-start | bytes 65536 | tf_op jit(solution)/shard_map/all_to_all | solution.py:55
  123.7 2.0 %fusion.12 = bf16[4,2,256,128]{3,2,1,0:T(8,128)(2,1)S(1)} fusion(f32[4,2,256,128]{3,2,1,0:T(8,128)} %fusion.67, bf16[4,2,256,256]{2,3,1,0:T(8,128)(2,1)S(1)} %bitcast.159, bf16[4,2,256,128]{2,3,1,0:T(8,128)(2,1)} %copy-done.19), kind=kOutput, calls=%fused_computation.38 | convolution fusion | flops 134742016 | bytes 3145728 | tf_op jit(solution)/shard_map/...jr,...rd->...jd/dot_general | solution.py:61
  125.7 0.9 divide_convert_fusion
  126.7 0.9 copy.181
  127.5 2.0 %copy.125 = bf16[4,2,256,128]{3,2,1,0:T(8,128)(2,1)} copy(bf16[4,2,256,128]{2,3,1,0:T(8,128)(2,1)} %divide_convert_fusion) | data formatting | bytes 1048576 | tf_op jit(solution)/shard_map/convert_element_type | solution.py:288
  129.6 2.0 %copy.126 = bf16[512,4,128]{0,2,1:T(8,128)(2,1)} copy(bf16[512,4,128]{2,0,1:T(8,128)(2,1)} %bitcast.181) | data formatting | bytes 1048576 | tf_op jit(solution)/shard_map/transpose | solution.py:231
  131.6 2.0 %copy.131 = bf16[512,512]{1,0:T(8,128)(2,1)} copy(bf16[512,512]{0,1:T(8,128)(2,1)} %bitcast.182) | data formatting | bytes 1048576
  133.8 1.6 %fusion.24 = (bf16[512,512]{1,0:T(8,128)(2,1)}, bf16[512,512]{1,0:T(8,128)(2,1)}) fusion(bf16[512,512]{1,0:T(8,128)(2,1)S(1)} %copy-done.6, f32[4,64,8,128]{3,2,1,0:T(8,128)S(1)} %bitcast.163, f32[512]{0:T(512)S(1)} %bitcast.199, f32[512]{0:T(512)S(1)} %copy-done.55, f32[512]{0:T(512)S(1)} %bitcast.193, f32[512]{0:T(512)S(1)} %copy-done.49, ...), kind=kLoop, calls=%fused_computation.52 | loop fusion | flops 4194304 | bytes 4210688 | tf_op jit(solution)/shard_map/convert_element_type | solution.py:205
  (171 shorter events, 8.4 us)
Async XLA Ops:
  0.6 14.1 %copy-start.30 = (bf16[512,512]{1,0:T(8,128)(2,1)S(1)}, bf16[512,512]{1,0:T(8,128)(2,1)}, u32[]{:S(2)}) copy-start(bf16[512,512]{1,0:T(8,128)(2,1)} %param.14) | copy-start | bytes 1572868
  3.8 16.0 %all-to-all-start = ((f32[8,2,512]{2,1,0:T(2,128)}), f32[8,2,512]{2,1,0:T(2,128)S(1)}, u32[]{:S(2)}, u32[]{:S(2)}) async-start(f32[8,2,512]{2,1,0:T(2,128)} %broadcast_in_dim.17), calls=%async_computation | async-start | bytes 65536 | tf_op jit(solution)/shard_map/all_to_all | solution.py:55
  14.8 8.7 %copy-start.1 = (bf16[4,512,128]{2,1,0:T(8,128)(2,1)}, bf16[4,512,128]{2,1,0:T(8,128)(2,1)S(1)}, u32[]{:S(2)}) copy-start(bf16[4,512,128]{2,1,0:T(8,128)(2,1)S(1)} %copy.112) | copy-start | bytes 1572868
  16.1 3.7 %copy-start.7 = (bf16[512,512]{1,0:T(8,128)(2,1)S(1)}, bf16[512,512]{1,0:T(8,128)(2,1)}, u32[]{:S(2)}) copy-start(bf16[512,512]{1,0:T(8,128)(2,1)} %param.12) | copy-start | bytes 1572868
  16.1 3.7 %copy-start.50 = (f32[512]{0:T(512)S(1)}, f32[512]{0:T(512)}, u32[]{:S(2)}) copy-start(f32[512]{0:T(512)} %param.16) | copy-start | bytes 6148
  19.1 6.6 %copy-start.52 = (f32[192]{0:T(256)}, f32[192]{0:T(256)S(1)}, u32[]{:S(2)}) copy-start(f32[192]{0:T(256)S(1)} %pad.69.clone) | copy-start | bytes 2308
  19.8 20.6 %copy-start.44 = (f32[1,512]{1,0:T(1,128)}, f32[1,512]{1,0:T(1,128)S(1)}, u32[]{:S(2)}) copy-start(f32[1,512]{1,0:T(1,128)S(1)} %get-tuple-element.47) | copy-start | bytes 6148
  19.8 33.6 %copy-start.46 = (f32[1,512]{1,0:T(1,128)}, f32[1,512]{1,0:T(1,128)S(1)}, u32[]{:S(2)}) copy-start(f32[1,512]{1,0:T(1,128)S(1)} %get-tuple-element.48) | copy-start | bytes 6148
  20.0 2.2 %copy-start.31 = (bf16[256,136,1,1]{0,1,3,2:T(8,128)(2,1)S(1)}, bf16[256,136,1,1]{0,1,3,2:T(8,128)(2,1)}, u32[]{:S(2)}) copy-start(bf16[256,136,1,1]{0,1,3,2:T(8,128)(2,1)} %constant.67) | copy-start | bytes 208900
  20.3 0.8 copy-start.12
  21.1 1.2 copy-start.28
  23.4 12.3 %copy-start.5 = (bf16[512,512]{1,0:T(8,128)(2,1)S(1)}, bf16[512,512]{1,0:T(8,128)(2,1)}, u32[]{:S(2)}) copy-start(bf16[512,512]{1,0:T(8,128)(2,1)} %param.11) | copy-start | bytes 1572868
  23.4 12.3 %copy-start.48 = (f32[512]{0:T(512)S(1)}, f32[512]{0:T(512)}, u32[]{:S(2)}) copy-start(f32[512]{0:T(512)} %param.15) | copy-start | bytes 6148
  26.6 19.5 %all-to-all-start.1 = ((f32[32,24,128]{2,1,0:T(8,128)}), f32[32,24,128]{2,1,0:T(8,128)}, u32[]{:S(2)}, u32[]{:S(2)}) async-start(f32[32,24,128]{2,1,0:T(8,128)} %bitcast.23), calls=%async_computation.1 | async-start | bytes 786432 | tf_op jit(solution)/shard_map/all_to_all | solution.py:41
  37.9 1.4 %copy-start.32 = (bf16[256,136,1,1]{0,1,3,2:T(8,128)(2,1)S(1)}, bf16[256,136,1,1]{0,1,3,2:T(8,128)(2,1)}, u32[]{:S(2)}) copy-start(bf16[256,136,1,1]{0,1,3,2:T(8,128)(2,1)} %constant.67) | copy-start | bytes 208900
  38.0 3.0 %copy-start.10 = (bf16[4,512,128]{2,1,0:T(8,128)(2,1)}, bf16[4,512,128]{2,1,0:T(8,128)(2,1)S(1)}, u32[]{:S(2)}) copy-start(bf16[4,512,128]{2,1,0:T(8,128)(2,1)S(1)} %copy.106) | copy-start | bytes 1572868
  38.0 3.0 %copy-start.13 = (bf16[4,512,128]{2,1,0:T(8,128)(2,1)S(1)}, bf16[4,512,128]{2,1,0:T(8,128)(2,1)}, u32[]{:S(2)}) copy-start(bf16[4,512,128]{2,1,0:T(8,128)(2,1)} %copy-done.12) | copy-start | bytes 1572868
  38.0 3.0 %copy-start.35 = (pred[256,256]{0,1:T(8,128)(4,1)S(1)}, pred[256,256]{0,1:T(8,128)(4,1)}, u32[]{:S(2)}) copy-start(pred[256,256]{0,1:T(8,128)(4,1)} %iota_compare_fusion) | copy-start | bytes 196612
  38.3 0.7 copy-start.25
  48.2 15.5 %all-to-all-start.2 = ((f32[32,24,128]{2,1,0:T(8,128)}), f32[32,24,128]{2,1,0:T(8,128)}, u32[]{:S(2)}, u32[]{:S(2)}) async-start(f32[32,24,128]{2,1,0:T(8,128)} %pad_add_fusion.4), calls=%async_computation.2 | async-start | bytes 786432 | tf_op jit(solution)/shard_map/all_to_all | solution.py:47
  54.9 10.7 %copy-start.42 = (f32[4,2,256]{2,1,0:T(2,128)}, f32[4,2,256]{2,1,0:T(2,128)S(1)}, u32[]{:S(2)}) copy-start(f32[4,2,256]{2,1,0:T(2,128)S(1)} %reduce_sum.144) | copy-start | bytes 24580
  63.7 3.2 %copy-start.16 = (f32[4,2,136,128]{3,2,1,0:T(8,128)S(1)}, f32[4,2,136,128]{3,2,1,0:T(8,128)}, u32[]{:S(2)}) copy-start(f32[4,2,136,128]{3,2,1,0:T(8,128)} %get-tuple-element.51) | copy-start | bytes 1671172
  63.7 3.3 %copy-start.33 = (bf16[256,136,1,1]{0,1,3,2:T(8,128)(2,1)S(1)}, bf16[256,136,1,1]{0,1,3,2:T(8,128)(2,1)}, u32[]{:S(2)}) copy-start(bf16[256,136,1,1]{0,1,3,2:T(8,128)(2,1)} %constant.68) | copy-start | bytes 208900
  64.5 2.9 %copy-start.23 = (f32[4,2,256,128]{2,3,1,0:T(8,128)S(1)}, f32[4,2,256,128]{2,3,1,0:T(8,128)}, u32[]{:S(2)}) copy-start(f32[4,2,256,128]{2,3,1,0:T(8,128)} %copy.116) | copy-start | bytes 3145732
  64.5 2.9 %copy-start.24 = (f32[4,2,256,128]{2,3,1,0:T(8,128)S(1)}, f32[4,2,256,128]{2,3,1,0:T(8,128)}, u32[]{:S(2)}) copy-start(f32[4,2,256,128]{2,3,1,0:T(8,128)} %fusion.66) | copy-start | bytes 3145732
  66.4 2.3 %copy-start.38 = (f32[4,2,256]{2,1,0:T(2,128)}, f32[4,2,256]{2,1,0:T(2,128)S(1)}, u32[]{:S(2)}) copy-start(f32[4,2,256]{2,1,0:T(2,128)S(1)} %add_subtract_fusion.1) | copy-start | bytes 24580
  67.4 1.3 copy-start.17
  67.4 1.3 copy-start.43
  69.3 0.9 copy-start.40
  70.2 2.8 %copy-start.53 = (f32[192]{0:T(256)S(1)}, f32[192]{0:T(256)}, u32[]{:S(2)}) copy-start(f32[192]{0:T(256)} %copy-done.52) | copy-start | bytes 2308
  70.2 3.7 %copy-start.18 = (bf16[4,2,256,128]{2,3,1,0:T(8,128)(2,1)S(1)}, bf16[4,2,256,128]{2,3,1,0:T(8,128)(2,1)}, u32[]{:S(2)}) copy-start(bf16[4,2,256,128]{2,3,1,0:T(8,128)(2,1)} %copy-done.17) | copy-start | bytes 1572868
  70.2 3.7 %copy-start.39 = (f32[4,2,256]{2,1,0:T(2,128)S(1)}, f32[4,2,256]{2,1,0:T(2,128)}, u32[]{:S(2)}) copy-start(f32[4,2,256]{2,1,0:T(2,128)} %copy-done.38) | copy-start | bytes 24580
  70.2 3.7 %copy-start.41 = (f32[4,2,256]{2,1,0:T(2,128)S(1)}, f32[4,2,256]{2,1,0:T(2,128)}, u32[]{:S(2)}) copy-start(f32[4,2,256]{2,1,0:T(2,128)} %copy-done.40) | copy-start | bytes 24580
  71.4 5.5 %copy-start.4 = (bf16[4,2,256,128]{3,2,1,0:T(8,128)(2,1)}, bf16[4,2,256,128]{3,2,1,0:T(8,128)(2,1)S(1)}, u32[]{:S(2)}) copy-start(bf16[4,2,256,128]{3,2,1,0:T(8,128)(2,1)S(1)} %divide_convert_fusion.1) | copy-start | bytes 1572868
  72.9 9.5 %copy-start.15 = (f32[4,2,136,128]{3,2,1,0:T(8,128)}, f32[4,2,136,128]{3,2,1,0:T(8,128)S(1)}, u32[]{:S(2)}) copy-start(f32[4,2,136,128]{3,2,1,0:T(8,128)S(1)} %get-tuple-element.55) | copy-start | bytes 1671172
  73.9 2.9 %copy-start.26 = (f32[4,2,256,32]{2,3,1,0:T(8,128)S(1)}, f32[4,2,256,32]{2,3,1,0:T(8,128)}, u32[]{:S(2)}) copy-start(f32[4,2,256,32]{2,3,1,0:T(8,128)} %copy-done.25) | copy-start | bytes 786436
  74.4 2.4 %copy-start.2 = (bf16[4,512,128]{2,1,0:T(8,128)(2,1)S(1)}, bf16[4,512,128]{2,1,0:T(8,128)(2,1)}, u32[]{:S(2)}) copy-start(bf16[4,512,128]{2,1,0:T(8,128)(2,1)} %copy-done.1) | copy-start | bytes 1572868
  74.5 2.4 %copy-start.27 = (f32[4,2,256,256]{2,3,1,0:T(8,128)S(1)}, f32[4,2,256,256]{2,3,1,0:T(8,128)}, u32[]{:S(2)}) copy-start(f32[4,2,256,256]{2,3,1,0:T(8,128)} %get-tuple-element.49) | copy-start | bytes 6291460
  74.5 2.4 %copy-start.36 = (pred[256,256]{0,1:T(8,128)(4,1)S(1)}, pred[256,256]{0,1:T(8,128)(4,1)}, u32[]{:S(2)}) copy-start(pred[256,256]{0,1:T(8,128)(4,1)} %iota_compare_fusion) | copy-start | bytes 196612
  78.7 7.7 %copy-start.14 = (bf16[4,512,128]{2,1,0:T(8,128)(2,1)S(1)}, bf16[4,512,128]{2,1,0:T(8,128)(2,1)}, u32[]{:S(2)}) copy-start(bf16[4,512,128]{2,1,0:T(8,128)(2,1)} %copy-done.12) | copy-start | bytes 1572868
  78.7 14.0 %all-to-all-start.3 = ((f32[32,24,128]{2,1,0:T(8,128)}), f32[32,24,128]{2,1,0:T(8,128)S(1)}, u32[]{:S(2)}, u32[]{:S(2)}) async-start(f32[32,24,128]{2,1,0:T(8,128)} %bitcast.32), calls=%async_computation.3 | async-start | bytes 786432 | tf_op jit(solution)/shard_map/all_to_all | solution.py:41
  83.3 3.0 %copy-start.20 = (bf16[4,2,256,256]{2,3,1,0:T(8,128)(2,1)S(1)}, bf16[4,2,256,256]{2,3,1,0:T(8,128)(2,1)}, u32[]{:S(2)}) copy-start(bf16[4,2,256,256]{2,3,1,0:T(8,128)(2,1)} %fusion.4) | copy-start | bytes 3145732
  92.9 5.5 %copy-start.49 = (f32[512]{0:T(512)S(1)}, f32[512]{0:T(512)}, u32[]{:S(2)}) copy-start(f32[512]{0:T(512)} %param.15) | copy-start | bytes 6148
  93.0 7.0 %copy-start = (bf16[4,2,256,256]{2,3,1,0:T(8,128)(2,1)S(1)}, bf16[4,2,256,256]{2,3,1,0:T(8,128)(2,1)}, u32[]{:S(2)}) copy-start(bf16[4,2,256,256]{2,3,1,0:T(8,128)(2,1)} %get-tuple-element.37) | copy-start | bytes 3145732
  93.8 14.6 %all-to-all-start.4 = ((f32[32,24,128]{2,1,0:T(8,128)}), f32[32,24,128]{2,1,0:T(8,128)}, u32[]{:S(2)}, u32[]{:S(2)}) async-start(f32[32,24,128]{2,1,0:T(8,128)} %pad_add_fusion), calls=%async_computation.4 | async-start | bytes 786432 | tf_op jit(solution)/shard_map/all_to_all | solution.py:47
  100.0 11.4 %copy-start.34 = (bf16[256,136,1,1]{0,1,3,2:T(8,128)(2,1)S(1)}, bf16[256,136,1,1]{0,1,3,2:T(8,128)(2,1)}, u32[]{:S(2)}) copy-start(bf16[256,136,1,1]{0,1,3,2:T(8,128)(2,1)} %constant.68) | copy-start | bytes 208900
  102.4 9.3 %copy-start.3 = (bf16[4,512,128]{2,1,0:T(8,128)(2,1)S(1)}, bf16[4,512,128]{2,1,0:T(8,128)(2,1)}, u32[]{:S(2)}) copy-start(bf16[4,512,128]{2,1,0:T(8,128)(2,1)} %copy-done.1) | copy-start | bytes 1572868
  111.4 1.2 copy-start.29
  111.8 0.8 copy-start.19
  112.5 3.4 %copy-start.11 = (bf16[4,512,128]{2,1,0:T(8,128)(2,1)S(1)}, bf16[4,512,128]{2,1,0:T(8,128)(2,1)}, u32[]{:S(2)}) copy-start(bf16[4,512,128]{2,1,0:T(8,128)(2,1)} %copy-done.10) | copy-start | bytes 1572868
  112.6 3.4 %copy-start.21 = (bf16[4,2,256,256]{2,3,1,0:T(8,128)(2,1)S(1)}, bf16[4,2,256,256]{2,3,1,0:T(8,128)(2,1)}, u32[]{:S(2)}) copy-start(bf16[4,2,256,256]{2,3,1,0:T(8,128)(2,1)} %fusion.4) | copy-start | bytes 3145732
  115.9 1.0 copy-start.8
  116.0 1.0 copy-start.51
  117.0 8.7 %copy-start.37 = (f32[4,2,256]{2,1,0:T(2,128)S(1)}, f32[4,2,256]{2,1,0:T(2,128)}, u32[]{:S(2)}) copy-start(f32[4,2,256]{2,1,0:T(2,128)} %get-tuple-element.16) | copy-start | bytes 24580
  117.8 15.8 %all-to-all-start.5 = ((f32[8,2,512]{2,1,0:T(2,128)}), f32[8,2,512]{2,1,0:T(2,128)S(1)}, u32[]{:S(2)}, u32[]{:S(2)}) async-start(f32[8,2,512]{2,1,0:T(2,128)} %broadcast_in_dim.19), calls=%async_computation.5 | async-start | bytes 65536 | tf_op jit(solution)/shard_map/all_to_all | solution.py:55
  123.7 2.0 %copy-start.22 = (f32[4,2,256,128]{2,3,1,0:T(8,128)S(1)}, f32[4,2,256,128]{2,3,1,0:T(8,128)}, u32[]{:S(2)}) copy-start(f32[4,2,256,128]{2,3,1,0:T(8,128)} %get-tuple-element.15) | copy-start | bytes 3145732
  126.6 7.1 %copy-start.6 = (bf16[512,512]{1,0:T(8,128)(2,1)S(1)}, bf16[512,512]{1,0:T(8,128)(2,1)}, u32[]{:S(2)}) copy-start(bf16[512,512]{1,0:T(8,128)(2,1)} %param.11) | copy-start | bytes 1572868
  126.6 7.1 %copy-start.9 = (bf16[512,512]{1,0:T(8,128)(2,1)S(1)}, bf16[512,512]{1,0:T(8,128)(2,1)}, u32[]{:S(2)}) copy-start(bf16[512,512]{1,0:T(8,128)(2,1)} %param.12) | copy-start | bytes 1572868
  126.6 7.1 %copy-start.45 = (f32[1,512]{1,0:T(1,128)S(1)}, f32[1,512]{1,0:T(1,128)}, u32[]{:S(2)}) copy-start(f32[1,512]{1,0:T(1,128)} %copy-done.44) | copy-start | bytes 6148
  126.6 7.1 %copy-start.47 = (f32[1,512]{1,0:T(1,128)S(1)}, f32[1,512]{1,0:T(1,128)}, u32[]{:S(2)}) copy-start(f32[1,512]{1,0:T(1,128)} %copy-done.46) | copy-start | bytes 6148
  126.6 7.1 %copy-start.54 = (f32[512]{0:T(512)S(1)}, f32[512]{0:T(512)}, u32[]{:S(2)}) copy-start(f32[512]{0:T(512)} %multiply_multiply_fusion.4) | copy-start | bytes 6148
  126.6 7.1 %copy-start.55 = (f32[512]{0:T(512)S(1)}, f32[512]{0:T(512)}, u32[]{:S(2)}) copy-start(f32[512]{0:T(512)} %multiply_multiply_fusion.5) | copy-start | bytes 6148

commit v10 on v9

--- a/solution.py
+++ b/solution.py
@@ -250,6 +250,7 @@
     scaled_grad, den_grad, block_u, block_w = backward_states(
         g_heads, numerator, denominator, q_parts[0]
     )
+    attended = (numerator / denominator[..., None]).astype(jnp.bfloat16)
     later_u, later_w, (scaled_grad, den_grad) = carried_in(
         jnp.sum(block_u, axis=1),
         jnp.sum(block_w, axis=1),
@@ -277,15 +278,14 @@
     kn_grad = join_heads(
         k_diag + sketch_back(kf_grad, k_parts[1], k_parts[2], k_parts[3], sign_pair)
     )
-    (q_dot, k_dot), (v_diag, later_state, numerator, denominator) = head_sum(
+    (q_dot, k_dot), (v_diag, later_state) = head_sum(
         (
             jnp.sum(q_float * q_gain * qn_grad, axis=-1),
             jnp.sum(k_float * k_gain * kn_grad, axis=-1),
         ),
         "head",
-        (v_diag, later_state, numerator, denominator),
-    )
-    attended = (numerator / denominator[..., None]).astype(jnp.bfloat16)
+        (v_diag, later_state),
+    )
     _, v_grad = finish_backward(v_heads, k_parts[0], later_state, later_total, v_diag)
     q_grad = norm_back(queries, q_gain, q_scale, qn_grad, q_dot)
     k_grad = norm_back(keys, k_gain, k_scale, kn_grad, k_dot)

time: 137 us -> 134 us (0.978)
  local copies, waits for them, and re-layouts: 23.3 us -> 14.5 us
  waiting for transfers between devices: 19.5 us -> 25.6 us
  starting transfers between devices: 37.6 us -> 36 us
    all_to_all x2, waiting for transfers between devices: 0.01 us -> 6.16 us  [head_sum(): gathered = lax.all_to_all(spread, axis, 0, 0, tiled=True)]
    convert_element_type x3 -> x0, local copies, waits for them, and re-layouts: 4.95 us -> none  [the longest x2 2.91 us: backward_states(): grad_float = grad_in.astype(jnp.float32)]
    unnamed x118 -> x106, local copies, waits for them, and re-layouts: 6.06 us -> 3.48 us
    all_to_all x2, starting transfers between devices: 14.9 us -> 12.3 us  [head_sum(): gathered = lax.all_to_all(spread, axis, 0, 0, tiled=True)]
    transpose x1 -> x0, local copies, waits for them, and re-layouts: 2.04 us -> none  [join_heads(): return array.reshape(heads_here, tok_rows, DH).transpose(1, 0, 2).reshape...]
    reduce_sum x2, other arithmetic: 4.64 us -> 6.3 us  [sketch_back(): sketch_grad = jnp.sum(symmetric * sketched[..., None, :], axis=-1)]
    convert_element_type x1, other arithmetic: 1.09 us -> 2.56 us  [backward_states(): scaled_grad = (grad_float / denominator[..., None]).astype(jnp.bfloat16)]
  transfers between devices with their start and end apart: 6 -> 6, of which waited for: 4 -> 6; matrix products, arithmetic and copies ran while one was open for 27% -> 22% of each run, Pallas kernels for 0% -> 0%
where the time goes in v10:
time: 134 us; the launch traced here: 133 us
  starting transfers between devices  36 us (27%)
  other arithmetic  29 us (22%)
  matrix products  26 us (19%)
  waiting for transfers between devices  25.6 us (19%)
  local copies, waits for them, and re-layouts  14.5 us (11%)
  between operations  1.64 us (1%)
    dot_general x18, matrix products, product_of(): return jnp.einsum(spec, lhs, rhs, preferred_element_type=jnp.float32)  22.6 us
    all_to_all x2, starting transfers between devices, carried_in(): mine = lax.all_to_all(stacked, axis, 0, 0, tiled=True)  13.8 us
    all_to_all x2, starting transfers between devices, head_sum(): gathered = lax.all_to_all(spread, axis, 0, 0, tiled=True)  12.3 us
    all_to_all x2, waiting for transfers between devices, carried_in(): lax.all_to_all(shifted, axis, 0, 0, tiled=True)  11.8 us
    all_to_all x2, starting transfers between devices, carried_in(): lax.all_to_all(shifted, axis, 0, 0, tiled=True)  9.88 us
    all_to_all x2, waiting for transfers between devices, carried_in(): mine = lax.all_to_all(stacked, axis, 0, 0, tiled=True)  7.67 us
    reduce_sum x2, other arithmetic, sketch_back(): sketch_grad = jnp.sum(symmetric * sketched[..., None, :], axis=-1)  6.3 us
    all_to_all x2, waiting for transfers between devices, head_sum(): gathered = lax.all_to_all(spread, axis, 0, 0, tiled=True)  6.16 us
  transfers between devices with their start and end apart: 6, of which 6 were waited for; matrix products, arithmetic and copies ran while one was open for 22% of the time, Pallas kernels for 0%

profile of v10, /device:TPU:1, one launch (start us, length us, event | category | flops | bytes accessed | tf_op | source)
XLA Modules:
  0.0 132.8 jit_solution(11861151689562527890)
XLA Ops:
  0.6 1.3 fusion.16
  1.9 1.3 fusion.25
  3.2 0.6 broadcast_in_dim.17
  3.9 9.0 %all-to-all-start = ((f32[8,2,512]{2,1,0:T(2,128)}), f32[8,2,512]{2,1,0:T(2,128)S(1)}, u32[]{:S(2)}, u32[]{:S(2)}) async-start(f32[8,2,512]{2,1,0:T(2,128)} %broadcast_in_dim.17), calls=%async_computation | async-start | bytes 65536 | tf_op jit(solution)/shard_map/all_to_all | solution.py:55
  12.9 0.7 fusion.48
  13.6 1.2 reshape.169
  14.8 1.1 copy_bitcast_fusion
  16.0 0.7 pad.69.clone
  16.6 0.7 iota_compare_fusion
  17.3 2.4 %all-to-all-done = f32[8,2,512]{2,1,0:T(2,128)S(1)} async-done(((f32[8,2,512]{2,1,0:T(2,128)}), f32[8,2,512]{2,1,0:T(2,128)S(1)}, u32[]{:S(2)}, u32[]{:S(2)}) %all-to-all-start) | async-done | bytes 32800 | tf_op jit(solution)/shard_map/all_to_all | solution.py:55
  20.5 0.7 copy-done.22
  22.7 1.0 convert_reduce_fusion
  23.9 1.1 convolution_convert_fusion
  25.3 1.1 fusion.63
  26.5 0.8 maximum_maximum_fusion
  27.3 9.2 %all-to-all-start.1 = ((f32[32,24,128]{2,1,0:T(8,128)}), f32[32,24,128]{2,1,0:T(8,128)}, u32[]{:S(2)}, u32[]{:S(2)}) async-start(f32[32,24,128]{2,1,0:T(8,128)} %bitcast.19), calls=%async_computation.1 | async-start | bytes 786432 | tf_op jit(solution)/shard_map/all_to_all | solution.py:41
  36.6 0.6 multiply_multiply_fusion.5
  37.2 3.7 %convert_reduce_fusion.2 = (f32[4,2,256]{2,1,0:T(2,128)}, bf16[4,2,256,256]{2,3,1,0:T(8,128)(2,1)S(1)}, f32[4,2,256,256]{2,3,1,0:T(8,128)}) fusion(pred[256,256]{0,1:T(8,128)(4,1)} %iota_compare_fusion, bf16[4,2,256,128]{3,2,1,0:T(8,128)(2,1)} %bitcast.179, bf16[4,2,256,128]{3,2,1,0:T(8,128)(2,1)} %bitcast.182), kind=kOutput, calls=%fused_computation.18 | convolution fusion | flops 137885696 | bytes 4268032 | tf_op jit(solution)/shard_map/...id,...jd->...ij/dot_general | solution.py:61
  40.8 6.1 %all-to-all-done.1 = f32[32,24,128]{2,1,0:T(8,128)} async-done(((f32[32,24,128]{2,1,0:T(8,128)}), f32[32,24,128]{2,1,0:T(8,128)}, u32[]{:S(2)}, u32[]{:S(2)}) %all-to-all-start.1) | async-done | bytes 393248 | tf_op jit(solution)/shard_map/all_to_all | solution.py:41
  46.9 1.0 slice.110
  48.3 0.8 pad_add_fusion.4
  49.1 4.4 %all-to-all-start.2 = ((f32[32,24,128]{2,1,0:T(8,128)}), f32[32,24,128]{2,1,0:T(8,128)}, u32[]{:S(2)}, u32[]{:S(2)}) async-start(f32[32,24,128]{2,1,0:T(8,128)} %pad_add_fusion.4), calls=%async_computation.2 | async-start | bytes 786432 | tf_op jit(solution)/shard_map/all_to_all | solution.py:47
  53.5 0.6 multiply_multiply_fusion.4
  54.0 0.9 reduce_sum.144
  55.0 0.6 reduce_window_sum.35
  55.6 2.5 %fusion.66 = f32[4,2,256,128]{3,2,1,0:T(8,128)} fusion(bf16[4,2,256,256]{2,3,1,0:T(8,128)(2,1)S(1)} %get-tuple-element.21, bf16[4,2,256,128]{3,2,1,0:T(8,128)(2,1)} %bitcast.175), kind=kOutput, calls=%fused_computation.144 | convolution fusion | flops 134217728 | bytes 2621440 | tf_op jit(solution)/shard_map/...ij,...jd->...id/dot_general | solution.py:61
  58.1 5.5 %all-to-all-done.2 = f32[32,24,128]{2,1,0:T(8,128)} async-done(((f32[32,24,128]{2,1,0:T(8,128)}), f32[32,24,128]{2,1,0:T(8,128)}, u32[]{:S(2)}, u32[]{:S(2)}) %all-to-all-start.2) | async-done | bytes 393248 | tf_op jit(solution)/shard_map/all_to_all | solution.py:47
  63.6 0.8 slice_bitcast_fusion.1
  64.4 1.1 slice.116
  65.6 0.7 add_subtract_fusion.1
  66.3 0.5 fusion.46
  67.3 1.6 %multiply_reduce_fusion = (f32[4,2,256]{2,1,0:T(2,128)S(1)}, f32[4,2,256,128]{3,2,1,0:T(8,128)}) fusion(f32[4,2,256,128]{3,2,1,0:T(8,128)S(1)} %bitcast.184, f32[4,2,256,128]{3,2,1,0:T(8,128)S(1)} %copy-done.21, bf16[4,2,256,256]{2,3,1,0:T(8,128)(2,1)S(1)} %bitcast.164, bf16[4,2,256,128]{2,3,1,0:T(8,128)(2,1)S(1)} %fusion.14), kind=kOutput, calls=%fused_computation.66 | convolution fusion | flops 135002112 | bytes 4726784 | tf_op jit(solution)/shard_map/...ir,...rd->...id/dot_general | solution.py:61
  68.9 0.6 multiply_divide_fusion
  69.5 0.9 fusion.44
  70.5 2.6 %divide_convert_fusion = (bf16[4,2,256,128]{3,2,1,0:T(8,128)(2,1)S(1)}, bf16[4,2,256,128]{3,2,1,0:T(8,128)(2,1)}) fusion(f32[4,2,256]{2,1,0:T(2,128)} %get-tuple-element.19, f32[4,2,256,128]{3,2,1,0:T(8,128)} %get-tuple-element.39, bf16[512,512]{1,0:T(8,128)(2,1)} %param.14), kind=kLoop, calls=%fused_computation.67 | loop fusion | flops 1310720 | bytes 2629632 | tf_op jit(solution)/shard_map/convert_element_type | solution.py:157
  73.1 1.6 %fusion.64 = (f32[4,136,128]{2,1,0:T(8,128)S(1)}, f32[4,2,136,128]{3,2,1,0:T(8,128)S(1)}) fusion(bf16[4,2,256,136]{2,3,1,0:T(8,128)(2,1)} %convolution_convert_fusion, bf16[4,2,256,128]{3,2,1,0:T(8,128)(2,1)S(1)} %get-tuple-element.10), kind=kOutput, calls=%fused_computation.142 | convolution fusion | flops 71372800 | bytes 1916928 | tf_op jit(solution)/shard_map/...ir,...id->...rd/dot_general | solution.py:61
  74.7 0.9 maximum_maximum_fusion.1
  75.5 1.8 %multiply_add_fusion = f32[4,2,256,256]{2,3,1,0:T(8,128)} fusion(bf16[4,2,256,128]{3,2,1,0:T(8,128)(2,1)S(1)} %get-tuple-element.10, bf16[4,2,256,128]{2,3,1,0:T(8,128)(2,1)S(1)} %copy-done.16, f32[4,2,256]{2,1,0:T(2,128)S(1)} %copy-done.34, f32[4,2,256]{2,1,0:T(2,128)S(1)} %copy-done.36), kind=kOutput, calls=%fused_computation.17 | convolution fusion | flops 135266304 | bytes 3162112 | tf_op jit(solution)/shard_map/...id,...rd->...ir/dot_general | solution.py:61
  77.4 1.8 %fusion.6 = bf16[4,2,256,256]{2,3,1,0:T(8,128)(2,1)} fusion(f32[4,2,256,256]{2,3,1,0:T(8,128)S(1)} %copy-done.25, bf16[4,2,256,128]{3,2,1,0:T(8,128)(2,1)S(1)} %get-tuple-element.10, bf16[4,2,256,128]{3,2,1,0:T(8,128)(2,1)S(1)} %bitcast.176, f32[4,2,256]{2,1,0:T(2,128)S(1)} %copy-done.36, pred[256,256]{0,1:T(8,128)(4,1)S(1)} %copy-done.32), kind=kOutput, calls=%fused_computation.10 | convolution fusion | flops 138936320 | bytes 4268032 | tf_op jit(solution)/shard_map/...id,...jd->...ij/dot_general | solution.py:61
  79.1 4.6 %all-to-all-start.3 = ((f32[32,24,128]{2,1,0:T(8,128)}), f32[32,24,128]{2,1,0:T(8,128)}, u32[]{:S(2)}, u32[]{:S(2)}) async-start(f32[32,24,128]{2,1,0:T(8,128)} %bitcast.34), calls=%async_computation.3 | async-start | bytes 786432 | tf_op jit(solution)/shard_map/all_to_all | solution.py:41
  83.7 0.9 rev.14
  84.6 1.9 %fusion.65 = f32[4,2,136,128]{3,2,1,0:T(8,128)} fusion(f32[4,2,136,128]{3,2,1,0:T(8,128)} %rev.14), kind=kOutput, calls=%fused_computation.143 | output fusion | flops 139264 | bytes 1114112 | tf_op jit(solution)/shard_map/jit(cumsum)/reduce_window_sum | solution.py:137
  86.5 4.0 %fusion.10 = f32[4,2,256,16]{2,3,1,0:T(8,128)S(1)} fusion(f32[4,2,256,16,16]{2,4,3,1,0:T(8,128)} %bitcast.172, f32[4,2,256,16]{2,3,1,0:T(8,128)S(1)} %multiply_multiply_fusion.3), kind=kLoop, calls=%fused_computation.16 | loop fusion | flops 1540096 | bytes 2359296 | tf_op jit(solution)/shard_map/reduce_sum | solution.py:89
  90.6 1.0 fusion.36
  92.1 1.6 %all-to-all-done.3 = f32[32,24,128]{2,1,0:T(8,128)} async-done(((f32[32,24,128]{2,1,0:T(8,128)}), f32[32,24,128]{2,1,0:T(8,128)}, u32[]{:S(2)}, u32[]{:S(2)}) %all-to-all-start.3) | async-done | bytes 393248 | tf_op jit(solution)/shard_map/all_to_all | solution.py:41
  93.7 1.0 slice.118
  95.1 0.8 pad_add_fusion
  95.8 5.5 %all-to-all-start.4 = ((f32[32,24,128]{2,1,0:T(8,128)}), f32[32,24,128]{2,1,0:T(8,128)}, u32[]{:S(2)}, u32[]{:S(2)}) async-start(f32[32,24,128]{2,1,0:T(8,128)} %pad_add_fusion), calls=%async_computation.4 | async-start | bytes 786432 | tf_op jit(solution)/shard_map/all_to_all | solution.py:47
  101.4 1.3 fusion.24
  102.9 2.5 %fusion.67 = f32[4,2,256,128]{3,2,1,0:T(8,128)} fusion(bf16[4,2,256,256]{2,3,1,0:T(8,128)(2,1)S(1)} %get-tuple-element.21, bf16[4,2,256,128]{3,2,1,0:T(8,128)(2,1)} %copy-done.3), kind=kOutput, calls=%fused_computation.145 | convolution fusion | flops 134217728 | bytes 2621440 | tf_op jit(solution)/shard_map/...ij,...id->...jd/dot_general | solution.py:61
  105.4 6.3 %all-to-all-done.4 = f32[32,24,128]{2,1,0:T(8,128)} async-done(((f32[32,24,128]{2,1,0:T(8,128)}), f32[32,24,128]{2,1,0:T(8,128)}, u32[]{:S(2)}, u32[]{:S(2)}) %all-to-all-start.4) | async-done | bytes 393248 | tf_op jit(solution)/shard_map/all_to_all | solution.py:47
  111.7 0.7 slice_bitcast_fusion
  112.4 1.0 slice.124
  113.4 1.3 subtract_convert_fusion
  115.1 0.5 convolution_add_fusion
  115.7 2.3 %fusion.8 = f32[4,2,256,16]{2,3,1,0:T(8,128)S(1)} fusion(f32[4,2,256,16,16]{2,4,3,1,0:T(8,128)S(1)} %bitcast.173, f32[4,2,256,16]{2,3,1,0:T(8,128)S(1)} %copy-done.28), kind=kLoop, calls=%fused_computation.13 | loop fusion | flops 1540096 | bytes 2359296 | tf_op jit(solution)/shard_map/reduce_sum | solution.py:89
  118.0 1.0 fusion.39
  119.5 0.6 copy-done.7
  120.3 0.6 broadcast_in_dim.19
  120.9 3.3 %all-to-all-start.5 = ((f32[8,2,512]{2,1,0:T(2,128)}), f32[8,2,512]{2,1,0:T(2,128)S(1)}, u32[]{:S(2)}, u32[]{:S(2)}) async-start(f32[8,2,512]{2,1,0:T(2,128)} %broadcast_in_dim.19), calls=%async_computation.5 | async-start | bytes 65536 | tf_op jit(solution)/shard_map/all_to_all | solution.py:55
  124.3 1.9 %fusion.12 = bf16[4,2,256,128]{3,2,1,0:T(8,128)(2,1)S(1)} fusion(f32[4,2,256,128]{3,2,1,0:T(8,128)} %fusion.67, bf16[4,2,256,256]{2,3,1,0:T(8,128)(2,1)S(1)} %bitcast.167, bf16[4,2,256,128]{2,3,1,0:T(8,128)(2,1)} %copy-done.17), kind=kOutput, calls=%fused_computation.38 | convolution fusion | flops 134742016 | bytes 3145728 | tf_op jit(solution)/shard_map/...jr,...rd->...jd/dot_general | solution.py:61
  126.3 1.1 copy_bitcast_fusion.1
  127.4 3.7 %all-to-all-done.5 = f32[8,2,512]{2,1,0:T(2,128)S(1)} async-done(((f32[8,2,512]{2,1,0:T(2,128)}), f32[8,2,512]{2,1,0:T(2,128)S(1)}, u32[]{:S(2)}, u32[]{:S(2)}) %all-to-all-start.5) | async-done | bytes 32800 | tf_op jit(solution)/shard_map/all_to_all | solution.py:55
  131.2 1.6 %fusion.22 = (bf16[512,512]{1,0:T(8,128)(2,1)}, bf16[512,512]{1,0:T(8,128)(2,1)}) fusion(bf16[512,512]{1,0:T(8,128)(2,1)S(1)} %copy-done.5, f32[4,64,8,128]{3,2,1,0:T(8,128)S(1)} %bitcast.169, f32[512]{0:T(512)S(1)} %bitcast.203, f32[512]{0:T(512)S(1)} %copy-done.49, f32[512]{0:T(512)S(1)} %copy-done.44, f32[512]{0:T(512)S(1)} %bitcast.197, ...), kind=kLoop, calls=%fused_computation.50 | loop fusion | flops 4194304 | bytes 4210688 | tf_op jit(solution)/shard_map/convert_element_type | solution.py:205
  (154 shorter events, 5.8 us)
Async XLA Ops:
  0.6 14.2 %copy-start.24 = (bf16[512,512]{1,0:T(8,128)(2,1)S(1)}, bf16[512,512]{1,0:T(8,128)(2,1)}, u32[]{:S(2)}) copy-start(bf16[512,512]{1,0:T(8,128)(2,1)} %param.14) | copy-start | bytes 1572868
  1.9 17.9 %copy-start.4 = (bf16[512,512]{1,0:T(8,128)(2,1)S(1)}, bf16[512,512]{1,0:T(8,128)(2,1)}, u32[]{:S(2)}) copy-start(bf16[512,512]{1,0:T(8,128)(2,1)} %param.11) | copy-start | bytes 1572868
  1.9 17.9 %copy-start.43 = (f32[512]{0:T(512)S(1)}, f32[512]{0:T(512)}, u32[]{:S(2)}) copy-start(f32[512]{0:T(512)} %param.15) | copy-start | bytes 6148
  3.9 15.9 %all-to-all-start = ((f32[8,2,512]{2,1,0:T(2,128)}), f32[8,2,512]{2,1,0:T(2,128)S(1)}, u32[]{:S(2)}, u32[]{:S(2)}) async-start(f32[8,2,512]{2,1,0:T(2,128)} %broadcast_in_dim.17), calls=%async_computation | async-start | bytes 65536 | tf_op jit(solution)/shard_map/all_to_all | solution.py:55
  14.8 10.5 %copy-start = (bf16[4,512,128]{2,1,0:T(8,128)(2,1)}, bf16[4,512,128]{2,1,0:T(8,128)(2,1)S(1)}, u32[]{:S(2)}) copy-start(bf16[4,512,128]{2,1,0:T(8,128)(2,1)S(1)} %copy.77) | copy-start | bytes 1572868
  19.8 16.8 %copy-start.41 = (f32[1,512]{1,0:T(1,128)}, f32[1,512]{1,0:T(1,128)S(1)}, u32[]{:S(2)}) copy-start(f32[1,512]{1,0:T(1,128)S(1)} %get-tuple-element.34) | copy-start | bytes 6148
  19.8 33.7 %copy-start.39 = (f32[1,512]{1,0:T(1,128)}, f32[1,512]{1,0:T(1,128)S(1)}, u32[]{:S(2)}) copy-start(f32[1,512]{1,0:T(1,128)S(1)} %get-tuple-element.33) | copy-start | bytes 6148
  19.8 1.4 %copy-start.6 = (bf16[512,512]{1,0:T(8,128)(2,1)S(1)}, bf16[512,512]{1,0:T(8,128)(2,1)}, u32[]{:S(2)}) copy-start(bf16[512,512]{1,0:T(8,128)(2,1)} %param.12) | copy-start | bytes 1572868
  19.8 1.4 %copy-start.45 = (f32[512]{0:T(512)S(1)}, f32[512]{0:T(512)}, u32[]{:S(2)}) copy-start(f32[512]{0:T(512)} %param.16) | copy-start | bytes 6148
  20.2 1.4 %copy-start.9 = (bf16[4,512,128]{2,1,0:T(8,128)(2,1)}, bf16[4,512,128]{2,1,0:T(8,128)(2,1)S(1)}, u32[]{:S(2)}) copy-start(bf16[4,512,128]{2,1,0:T(8,128)(2,1)S(1)} %copy.75) | copy-start | bytes 1572868
  20.5 0.7 copy-start.22
  21.7 0.8 copy-start.11
  21.7 2.1 %copy-start.29 = (bf16[256,136,1,1]{0,1,3,2:T(8,128)(2,1)S(1)}, bf16[256,136,1,1]{0,1,3,2:T(8,128)(2,1)}, u32[]{:S(2)}) copy-start(bf16[256,136,1,1]{0,1,3,2:T(8,128)(2,1)} %constant.67) | copy-start | bytes 208900
  22.5 2.5 %copy-start.27 = (f32[4,2,256,16]{2,3,1,0:T(8,128)}, f32[4,2,256,16]{2,3,1,0:T(8,128)S(1)}, u32[]{:S(2)}) copy-start(f32[4,2,256,16]{2,3,1,0:T(8,128)S(1)} %multiply_multiply_fusion.2) | copy-start | bytes 393220
  25.0 1.5 %copy-start.47 = (f32[192]{0:T(256)S(1)}, f32[192]{0:T(256)}, u32[]{:S(2)}) copy-start(f32[192]{0:T(256)} %pad.69.clone) | copy-start | bytes 2308
  27.3 19.6 %all-to-all-start.1 = ((f32[32,24,128]{2,1,0:T(8,128)}), f32[32,24,128]{2,1,0:T(8,128)}, u32[]{:S(2)}, u32[]{:S(2)}) async-start(f32[32,24,128]{2,1,0:T(8,128)} %bitcast.19), calls=%async_computation.1 | async-start | bytes 786432 | tf_op jit(solution)/shard_map/all_to_all | solution.py:41
  49.1 14.6 %all-to-all-start.2 = ((f32[32,24,128]{2,1,0:T(8,128)}), f32[32,24,128]{2,1,0:T(8,128)}, u32[]{:S(2)}, u32[]{:S(2)}) async-start(f32[32,24,128]{2,1,0:T(8,128)} %pad_add_fusion.4), calls=%async_computation.2 | async-start | bytes 786432 | tf_op jit(solution)/shard_map/all_to_all | solution.py:47
  55.0 10.6 %copy-start.37 = (f32[4,2,256]{2,1,0:T(2,128)}, f32[4,2,256]{2,1,0:T(2,128)S(1)}, u32[]{:S(2)}) copy-start(f32[4,2,256]{2,1,0:T(2,128)S(1)} %reduce_sum.144) | copy-start | bytes 24580
  63.6 3.2 %copy-start.14 = (f32[4,2,136,128]{3,2,1,0:T(8,128)S(1)}, f32[4,2,136,128]{3,2,1,0:T(8,128)}, u32[]{:S(2)}) copy-start(f32[4,2,136,128]{3,2,1,0:T(8,128)} %get-tuple-element.37) | copy-start | bytes 1671172
  63.6 3.3 %copy-start.30 = (bf16[256,136,1,1]{0,1,3,2:T(8,128)(2,1)S(1)}, bf16[256,136,1,1]{0,1,3,2:T(8,128)(2,1)}, u32[]{:S(2)}) copy-start(bf16[256,136,1,1]{0,1,3,2:T(8,128)(2,1)} %constant.68) | copy-start | bytes 208900
  64.4 2.9 %copy-start.20 = (f32[512,4,128]{2,0,1:T(8,128)S(1)}, f32[512,4,128]{2,0,1:T(8,128)}, u32[]{:S(2)}) copy-start(f32[512,4,128]{2,0,1:T(8,128)} %copy_bitcast_fusion) | copy-start | bytes 3145732
  64.4 2.9 %copy-start.21 = (f32[4,2,256,128]{3,2,1,0:T(8,128)S(1)}, f32[4,2,256,128]{3,2,1,0:T(8,128)}, u32[]{:S(2)}) copy-start(f32[4,2,256,128]{3,2,1,0:T(8,128)} %fusion.66) | copy-start | bytes 3145732
  66.3 2.6 %copy-start.33 = (f32[4,2,256]{2,1,0:T(2,128)}, f32[4,2,256]{2,1,0:T(2,128)S(1)}, u32[]{:S(2)}) copy-start(f32[4,2,256]{2,1,0:T(2,128)S(1)} %add_subtract_fusion.1) | copy-start | bytes 24580
  67.3 1.6 %copy-start.15 = (bf16[4,2,256,128]{2,3,1,0:T(8,128)(2,1)}, bf16[4,2,256,128]{2,3,1,0:T(8,128)(2,1)S(1)}, u32[]{:S(2)}) copy-start(bf16[4,2,256,128]{2,3,1,0:T(8,128)(2,1)S(1)} %fusion.14) | copy-start | bytes 1572868
  67.3 1.6 %copy-start.38 = (f32[4,2,256]{2,1,0:T(2,128)S(1)}, f32[4,2,256]{2,1,0:T(2,128)}, u32[]{:S(2)}) copy-start(f32[4,2,256]{2,1,0:T(2,128)} %get-tuple-element.20) | copy-start | bytes 24580
  69.5 0.9 copy-start.35
  70.5 4.2 %copy-start.48 = (f32[192]{0:T(256)S(1)}, f32[192]{0:T(256)}, u32[]{:S(2)}) copy-start(f32[192]{0:T(256)} %pad.69.clone) | copy-start | bytes 2308
  70.5 5.1 %copy-start.16 = (bf16[4,2,256,128]{2,3,1,0:T(8,128)(2,1)S(1)}, bf16[4,2,256,128]{2,3,1,0:T(8,128)(2,1)}, u32[]{:S(2)}) copy-start(bf16[4,2,256,128]{2,3,1,0:T(8,128)(2,1)} %copy-done.15) | copy-start | bytes 1572868
  70.5 5.1 %copy-start.34 = (f32[4,2,256]{2,1,0:T(2,128)S(1)}, f32[4,2,256]{2,1,0:T(2,128)}, u32[]{:S(2)}) copy-start(f32[4,2,256]{2,1,0:T(2,128)} %copy-done.33) | copy-start | bytes 24580
  70.5 5.1 %copy-start.36 = (f32[4,2,256]{2,1,0:T(2,128)S(1)}, f32[4,2,256]{2,1,0:T(2,128)}, u32[]{:S(2)}) copy-start(f32[4,2,256]{2,1,0:T(2,128)} %copy-done.35) | copy-start | bytes 24580
  73.1 4.3 %copy-start.3 = (bf16[4,2,256,128]{3,2,1,0:T(8,128)(2,1)}, bf16[4,2,256,128]{3,2,1,0:T(8,128)(2,1)S(1)}, u32[]{:S(2)}) copy-start(bf16[4,2,256,128]{3,2,1,0:T(8,128)(2,1)S(1)} %get-tuple-element.10) | copy-start | bytes 1572868
  74.6 9.1 %copy-start.13 = (f32[4,2,136,128]{3,2,1,0:T(8,128)}, f32[4,2,136,128]{3,2,1,0:T(8,128)S(1)}, u32[]{:S(2)}) copy-start(f32[4,2,136,128]{3,2,1,0:T(8,128)S(1)} %get-tuple-element.41) | copy-start | bytes 1671172
  74.6 2.7 %copy-start.1 = (bf16[4,512,128]{2,1,0:T(8,128)(2,1)S(1)}, bf16[4,512,128]{2,1,0:T(8,128)(2,1)}, u32[]{:S(2)}) copy-start(bf16[4,512,128]{2,1,0:T(8,128)(2,1)} %copy-done) | copy-start | bytes 1572868
  74.6 2.7 %copy-start.25 = (f32[4,2,256,256]{2,3,1,0:T(8,128)S(1)}, f32[4,2,256,256]{2,3,1,0:T(8,128)}, u32[]{:S(2)}) copy-start(f32[4,2,256,256]{2,3,1,0:T(8,128)} %get-tuple-element.35) | copy-start | bytes 6291460
  74.7 2.7 %copy-start.32 = (pred[256,256]{0,1:T(8,128)(4,1)S(1)}, pred[256,256]{0,1:T(8,128)(4,1)}, u32[]{:S(2)}) copy-start(pred[256,256]{0,1:T(8,128)(4,1)} %iota_compare_fusion) | copy-start | bytes 196612
  79.1 14.6 %all-to-all-start.3 = ((f32[32,24,128]{2,1,0:T(8,128)}), f32[32,24,128]{2,1,0:T(8,128)}, u32[]{:S(2)}, u32[]{:S(2)}) async-start(f32[32,24,128]{2,1,0:T(8,128)} %bitcast.34), calls=%async_computation.3 | async-start | bytes 786432 | tf_op jit(solution)/shard_map/all_to_all | solution.py:41
  83.7 6.8 %copy-start.23 = (f32[4,2,256,32]{2,3,1,0:T(8,128)S(1)}, f32[4,2,256,32]{2,3,1,0:T(8,128)}, u32[]{:S(2)}) copy-start(f32[4,2,256,32]{2,3,1,0:T(8,128)} %copy-done.22) | copy-start | bytes 786436
  86.5 5.1 %copy-start.12 = (bf16[4,512,128]{2,1,0:T(8,128)(2,1)S(1)}, bf16[4,512,128]{2,1,0:T(8,128)(2,1)}, u32[]{:S(2)}) copy-start(bf16[4,512,128]{2,1,0:T(8,128)(2,1)} %copy-done.11) | copy-start | bytes 1572868
  86.5 5.1 %copy-start.18 = (bf16[4,2,256,256]{2,3,1,0:T(8,128)(2,1)S(1)}, bf16[4,2,256,256]{2,3,1,0:T(8,128)(2,1)}, u32[]{:S(2)}) copy-start(bf16[4,2,256,256]{2,3,1,0:T(8,128)(2,1)} %fusion.6) | copy-start | bytes 3145732
  95.0 6.4 %copy-start.44 = (f32[512]{0:T(512)S(1)}, f32[512]{0:T(512)}, u32[]{:S(2)}) copy-start(f32[512]{0:T(512)} %param.15) | copy-start | bytes 6148
  95.8 15.8 %all-to-all-start.4 = ((f32[32,24,128]{2,1,0:T(8,128)}), f32[32,24,128]{2,1,0:T(8,128)}, u32[]{:S(2)}, u32[]{:S(2)}) async-start(f32[32,24,128]{2,1,0:T(8,128)} %pad_add_fusion), calls=%async_computation.4 | async-start | bytes 786432 | tf_op jit(solution)/shard_map/all_to_all | solution.py:47
  102.9 11.8 %copy-start.31 = (bf16[256,136,1,1]{0,1,3,2:T(8,128)(2,1)S(1)}, bf16[256,136,1,1]{0,1,3,2:T(8,128)(2,1)}, u32[]{:S(2)}) copy-start(bf16[256,136,1,1]{0,1,3,2:T(8,128)(2,1)} %constant.68) | copy-start | bytes 208900
  105.4 9.7 %copy-start.2 = (bf16[4,512,128]{2,1,0:T(8,128)(2,1)S(1)}, bf16[4,512,128]{2,1,0:T(8,128)(2,1)}, u32[]{:S(2)}) copy-start(bf16[4,512,128]{2,1,0:T(8,128)(2,1)} %copy-done) | copy-start | bytes 1572868
  114.7 0.9 copy-start.28
  115.1 2.9 %copy-start.17 = (bf16[4,2,256,128]{2,3,1,0:T(8,128)(2,1)}, bf16[4,2,256,128]{2,3,1,0:T(8,128)(2,1)S(1)}, u32[]{:S(2)}) copy-start(bf16[4,2,256,128]{2,3,1,0:T(8,128)(2,1)S(1)} %fusion.15) | copy-start | bytes 1572868
  115.6 3.4 %copy-start.10 = (bf16[4,512,128]{2,1,0:T(8,128)(2,1)S(1)}, bf16[4,512,128]{2,1,0:T(8,128)(2,1)}, u32[]{:S(2)}) copy-start(bf16[4,512,128]{2,1,0:T(8,128)(2,1)} %copy-done.9) | copy-start | bytes 1572868
  115.7 3.4 %copy-start.19 = (bf16[4,2,256,256]{2,3,1,0:T(8,128)(2,1)S(1)}, bf16[4,2,256,256]{2,3,1,0:T(8,128)(2,1)}, u32[]{:S(2)}) copy-start(bf16[4,2,256,256]{2,3,1,0:T(8,128)(2,1)} %fusion.6) | copy-start | bytes 3145732
  119.0 1.0 copy-start.7
  119.1 1.0 copy-start.46
  120.9 10.2 %all-to-all-start.5 = ((f32[8,2,512]{2,1,0:T(2,128)}), f32[8,2,512]{2,1,0:T(2,128)S(1)}, u32[]{:S(2)}, u32[]{:S(2)}) async-start(f32[8,2,512]{2,1,0:T(2,128)} %broadcast_in_dim.19), calls=%async_computation.5 | async-start | bytes 65536 | tf_op jit(solution)/shard_map/all_to_all | solution.py:55
  124.3 2.0 %copy-start.26 = (bf16[4,2,256,128]{3,2,1,0:T(8,128)(2,1)S(1)}, bf16[4,2,256,128]{3,2,1,0:T(8,128)(2,1)}, u32[]{:S(2)}) copy-start(bf16[4,2,256,128]{3,2,1,0:T(8,128)(2,1)} %get-tuple-element.30) | copy-start | bytes 1572868
  124.3 6.8 %copy-start.40 = (f32[1,512]{1,0:T(1,128)S(1)}, f32[1,512]{1,0:T(1,128)}, u32[]{:S(2)}) copy-start(f32[1,512]{1,0:T(1,128)} %copy-done.39) | copy-start | bytes 6148
  124.3 6.8 %copy-start.42 = (f32[1,512]{1,0:T(1,128)S(1)}, f32[1,512]{1,0:T(1,128)}, u32[]{:S(2)}) copy-start(f32[1,512]{1,0:T(1,128)} %copy-done.41) | copy-start | bytes 6148
  124.3 6.8 %copy-start.49 = (f32[512]{0:T(512)S(1)}, f32[512]{0:T(512)}, u32[]{:S(2)}) copy-start(f32[512]{0:T(512)} %multiply_multiply_fusion.5) | copy-start | bytes 6148
  124.3 6.8 %copy-start.50 = (f32[512]{0:T(512)S(1)}, f32[512]{0:T(512)}, u32[]{:S(2)}) copy-start(f32[512]{0:T(512)} %multiply_multiply_fusion.4) | copy-start | bytes 6148
  126.3 4.9 %copy-start.5 = (bf16[512,512]{1,0:T(8,128)(2,1)S(1)}, bf16[512,512]{1,0:T(8,128)(2,1)}, u32[]{:S(2)}) copy-start(bf16[512,512]{1,0:T(8,128)(2,1)} %param.11) | copy-start | bytes 1572868
  126.3 4.9 %copy-start.8 = (bf16[512,512]{1,0:T(8,128)(2,1)S(1)}, bf16[512,512]{1,0:T(8,128)(2,1)}, u32[]{:S(2)}) copy-start(bf16[512,512]{1,0:T(8,128)(2,1)} %param.12) | copy-start | bytes 1572868

commit v11 on v8

--- a/solution.py
+++ b/solution.py
@@ -257,7 +257,10 @@
         True,
         (scaled_grad, den_grad, numerator, denominator),
     )
-    attended = (numerator / denominator[..., None]).astype(jnp.bfloat16)
+    spread_den = jnp.broadcast_to(
+        denominator.reshape(heads_here, tok_rows)[..., None], (heads_here, tok_rows, DH)
+    )
+    attended = (join_heads(numerator) / join_heads(spread_den)).astype(jnp.bfloat16)
     q_diag, k_diag, v_diag, qf_grad = backward_blocks(
         scaled_grad,
         den_grad,
@@ -289,7 +292,7 @@
     _, v_grad = finish_backward(v_heads, k_parts[0], later_state, later_total, v_diag)
     q_grad = norm_back(queries, q_gain, q_scale, qn_grad, q_dot)
     k_grad = norm_back(keys, k_gain, k_scale, kn_grad, k_dot)
-    return (join_heads(attended), q_grad, k_grad, join_heads(v_grad).astype(jnp.bfloat16))
+    return (attended, q_grad, k_grad, join_heads(v_grad).astype(jnp.bfloat16))
 
 
 def solution(mesh):

time: 133 us -> 137 us (1.030)
  matrix products: 24.6 us -> 26.5 us
    all_to_all x2, waiting for transfers between devices: 5.58 us -> 7.69 us  [carried_in(): lax.all_to_all(shifted, axis, 0, 0, tiled=True)]
    transpose x1 -> x0, local copies, waits for them, and re-layouts: 2.04 us -> none  [join_heads(): return array.reshape(heads_here, tok_rows, DH).transpose(1, 0, 2).reshape...]
    optimization_barrier x0 -> x1, local copies, waits for them, and re-layouts: none -> 1.61 us  [carried_in(): stacked, along = lax.optimization_barrier((stacked, along))]
    unnamed x114 -> x113, local copies, waits for them, and re-layouts: 6.07 us -> 6.02 us
  transfers between devices with their start and end apart: 6 -> 6, of which waited for: 5 -> 4; matrix products, arithmetic and copies ran while one was open for 31% -> 32% of each run, Pallas kernels for 0% -> 0%
where the time goes in v11:
time: 137 us; the launch traced here: 135 us
  starting transfers between devices  40.3 us (29%)
  other arithmetic  30.1 us (22%)
  matrix products  26.5 us (19%)
  local copies, waits for them, and re-layouts  22.9 us (17%)
  waiting for transfers between devices  14 us (10%)
  between operations  1.58 us (1%)
    dot_general x18, matrix products, product_of(): return jnp.einsum(spec, lhs, rhs, preferred_element_type=jnp.float32)  22.2 us
    all_to_all x2, starting transfers between devices, head_sum(): gathered = lax.all_to_all(spread, axis, 0, 0, tiled=True)  14.9 us
    all_to_all x2, starting transfers between devices, carried_in(): mine = lax.all_to_all(stacked, axis, 0, 0, tiled=True)  13 us
    all_to_all x2, starting transfers between devices, carried_in(): lax.all_to_all(shifted, axis, 0, 0, tiled=True)  12.5 us
    all_to_all x2, waiting for transfers between devices, carried_in(): lax.all_to_all(shifted, axis, 0, 0, tiled=True)  7.69 us
    unnamed x113, local copies, waits for them, and re-layouts  6.02 us
    reduce_sum x2, other arithmetic, sketch_back(): sketch_grad = jnp.sum(symmetric * sketched[..., None, :], axis=-1)  4.65 us
    dot_general x4, matrix products, precise_product(): jnp.einsum(spec, lhs.astype(jnp.float32), rhs.astype(jnp.float32), precis...  4.33 us
  transfers between devices with their start and end apart: 6, of which 4 were waited for; matrix products, arithmetic and copies ran while one was open for 32% of the time, Pallas kernels for 0%

profile of v11, /device:TPU:1, one launch (start us, length us, event | category | flops | bytes accessed | tf_op | source)
XLA Modules:
  0.0 135.4 jit_solution(8380323209708810794)
XLA Ops:
  0.6 1.3 fusion.16
  1.9 1.2 fusion.25
  3.2 0.6 broadcast_in_dim.20
  3.8 9.0 %all-to-all-start = ((f32[8,2,512]{2,1,0:T(2,128)}), f32[8,2,512]{2,1,0:T(2,128)S(1)}, u32[]{:S(2)}, u32[]{:S(2)}) async-start(f32[8,2,512]{2,1,0:T(2,128)} %broadcast_in_dim.20), calls=%async_computation | async-start | bytes 65536 | tf_op jit(solution)/shard_map/all_to_all | solution.py:55
  12.8 0.7 fusion.49
  13.5 1.2 reshape.171
  15.0 1.1 convert_bitcast_fusion
  16.1 1.6 %copy.110 = f32[4,512,128]{2,1,0:T(8,128)S(1)} copy(f32[4,512,128]{1,2,0:T(8,128)} %convert_bitcast_fusion) | data formatting | bytes 2097152 | tf_op jit(solution)/shard_map/convert_element_type | solution.py:156
  17.7 1.3 copy.117
  19.1 0.6 iota_compare_fusion
  21.1 1.2 convert_reduce_fusion.1
  22.3 1.1 convolution_convert_fusion
  23.5 2.2 %fusion.64 = (f32[4,136,128]{2,1,0:T(8,128)S(1)}, f32[4,2,136,128]{3,2,1,0:T(8,128)}) fusion(bf16[4,2,256,136]{2,3,1,0:T(8,128)(2,1)} %convolution_convert_fusion, bf16[4,2,256,128]{3,2,1,0:T(8,128)(2,1)S(1)} %bitcast.172), kind=kOutput, calls=%fused_computation.140 | convolution fusion | flops 71372800 | bytes 1916928 | tf_op jit(solution)/shard_map/...jr,...jd->...rd/dot_general | solution.py:61
  25.8 0.8 maximum_maximum_fusion
  26.6 9.1 %all-to-all-start.1 = ((f32[32,24,128]{2,1,0:T(8,128)}), f32[32,24,128]{2,1,0:T(8,128)}, u32[]{:S(2)}, u32[]{:S(2)}) async-start(f32[32,24,128]{2,1,0:T(8,128)} %bitcast.23), calls=%async_computation.1 | async-start | bytes 786432 | tf_op jit(solution)/shard_map/all_to_all | solution.py:41
  35.8 1.0 fusion.18
  36.8 1.2 reshape.167
  38.3 0.7 copy-done.22
  39.3 1.1 convolution_convert_fusion.1
  40.4 0.6 multiply_multiply_fusion.4
  41.0 2.8 %convert_reduce_fusion.2 = (f32[4,2,256]{2,1,0:T(2,128)}, bf16[4,2,256,256]{2,3,1,0:T(8,128)(2,1)}, f32[4,2,256,256]{2,3,1,0:T(8,128)}) fusion(pred[256,256]{0,1:T(8,128)(4,1)S(1)} %copy-done.32, bf16[4,2,256,128]{3,2,1,0:T(8,128)(2,1)S(1)} %bitcast.177, bf16[4,2,256,128]{3,2,1,0:T(8,128)(2,1)S(1)} %bitcast.180), kind=kOutput, calls=%fused_computation.19 | convolution fusion | flops 137885696 | bytes 4268032 | tf_op jit(solution)/shard_map/...id,...jd->...ij/dot_general | solution.py:61
  43.8 2.3 %all-to-all-done.1 = f32[32,24,128]{2,1,0:T(8,128)} async-done(((f32[32,24,128]{2,1,0:T(8,128)}), f32[32,24,128]{2,1,0:T(8,128)}, u32[]{:S(2)}, u32[]{:S(2)}) %all-to-all-start.1) | async-done | bytes 393248 | tf_op jit(solution)/shard_map/all_to_all | solution.py:41
  46.1 1.0 slice.110
  47.5 0.8 pad_add_fusion.4
  48.2 5.2 %all-to-all-start.2 = ((f32[32,24,128]{2,1,0:T(8,128)}), f32[32,24,128]{2,1,0:T(8,128)}, u32[]{:S(2)}, u32[]{:S(2)}) async-start(f32[32,24,128]{2,1,0:T(8,128)} %pad_add_fusion.4), calls=%async_computation.2 | async-start | bytes 786432 | tf_op jit(solution)/shard_map/all_to_all | solution.py:47
  54.0 0.9 reduce_sum.144
  55.0 0.6 reduce_window_sum.34
  55.6 2.7 %fusion.67 = f32[4,2,256,128]{2,3,1,0:T(8,128)} fusion(bf16[4,2,256,256]{2,3,1,0:T(8,128)(2,1)} %get-tuple-element.37, bf16[4,2,256,128]{3,2,1,0:T(8,128)(2,1)} %bitcast.173), kind=kOutput, calls=%fused_computation.143 | convolution fusion | flops 134217728 | bytes 2621440 | tf_op jit(solution)/shard_map/...ij,...jd->...id/dot_general | solution.py:61
  58.3 5.5 %all-to-all-done.2 = f32[32,24,128]{2,1,0:T(8,128)} async-done(((f32[32,24,128]{2,1,0:T(8,128)}), f32[32,24,128]{2,1,0:T(8,128)}, u32[]{:S(2)}, u32[]{:S(2)}) %all-to-all-start.2) | async-done | bytes 393248 | tf_op jit(solution)/shard_map/all_to_all | solution.py:47
  63.8 0.8 slice_bitcast_fusion.1
  64.5 1.1 slice.117
  65.7 0.7 add_subtract_fusion.1
  67.4 1.3 multiply_reduce_fusion
  68.8 1.1 divide_convert_fusion
  69.9 0.9 fusion.45
  70.9 1.5 %fusion.65 = (f32[4,136,128]{2,1,0:T(8,128)S(1)}, f32[4,2,136,128]{3,2,1,0:T(8,128)S(1)}) fusion(bf16[4,2,256,136]{2,3,1,0:T(8,128)(2,1)} %convolution_convert_fusion.1, bf16[4,2,256,128]{3,2,1,0:T(8,128)(2,1)} %divide_convert_fusion), kind=kOutput, calls=%fused_computation.141 | convolution fusion | flops 71372800 | bytes 1916928 | tf_op jit(solution)/shard_map/...ir,...id->...rd/dot_general | solution.py:61
  72.5 1.7 %maximum_maximum_fusion.1 = f32[4,192,128]{2,1,0:T(8,128)} fusion(f32[4,2,128]{2,1,0:T(2,128)S(1)} %reshape.176, f32[4,136,128]{2,1,0:T(8,128)S(1)} %get-tuple-element.54, f32[192]{0:T(256)} %copy-done.50), kind=kLoop, calls=%fused_computation.72 | loop fusion | flops 196608 | bytes 676608 | tf_op jit(solution)/shard_map/concatenate | solution.py:32
  74.2 3.8 %all-to-all-start.3 = ((f32[32,24,128]{2,1,0:T(8,128)}), f32[32,24,128]{2,1,0:T(8,128)S(1)}, u32[]{:S(2)}, u32[]{:S(2)}) async-start(f32[32,24,128]{2,1,0:T(8,128)} %bitcast.32), calls=%async_computation.3 | async-start | bytes 786432 | tf_op jit(solution)/shard_map/all_to_all | solution.py:41
  78.0 0.8 rev.14
  78.9 2.1 %fusion.66 = f32[4,2,136,128]{3,2,1,0:T(8,128)} fusion(f32[4,2,136,128]{3,2,1,0:T(8,128)} %rev.14), kind=kOutput, calls=%fused_computation.142 | output fusion | flops 139264 | bytes 1114112 | tf_op jit(solution)/shard_map/jit(cumsum)/reduce_window_sum | solution.py:137
  81.5 1.8 %fusion.6 = bf16[4,2,256,256]{2,3,1,0:T(8,128)(2,1)} fusion(f32[4,2,256,256]{2,3,1,0:T(8,128)S(1)} %copy-done.24, bf16[4,2,256,128]{3,2,1,0:T(8,128)(2,1)S(1)} %copy-done.4, bf16[4,2,256,128]{3,2,1,0:T(8,128)(2,1)S(1)} %bitcast.174, f32[4,2,256]{2,1,0:T(2,128)S(1)} %copy-done.37, pred[256,256]{0,1:T(8,128)(4,1)S(1)} %copy-done.33), kind=kOutput, calls=%fused_computation.10 | convolution fusion | flops 138936320 | bytes 4268032 | tf_op jit(solution)/shard_map/...id,...jd->...ij/dot_general | solution.py:61
  83.3 2.3 %fusion.10 = f32[4,2,256,16]{2,3,1,0:T(8,128)S(1)} fusion(f32[4,2,256,16,16]{2,4,3,1,0:T(8,128)S(1)} %bitcast.170, f32[4,2,256,16]{2,3,1,0:T(8,128)S(1)} %multiply_multiply_fusion.3), kind=kLoop, calls=%fused_computation.16 | loop fusion | flops 1540096 | bytes 2359296 | tf_op jit(solution)/shard_map/reduce_sum | solution.py:89
  85.6 0.7 slice_multiply_fusion.2
  86.3 1.6 %copy.118 = f32[4,2,256,128]{3,2,1,0:T(8,128)S(1)} copy(f32[4,2,256,128]{2,3,1,0:T(8,128)} %get-tuple-element.12) | data formatting | bytes 2097152 | tf_op jit(solution)/shard_map/optimization_barrier | solution.py:40
  87.9 1.1 fusion.34
  89.1 1.9 %fusion.37 = f32[4,2,256,128]{3,2,1,0:T(8,128)S(1)} fusion(f32[4,2,256,16]{2,3,1,0:T(8,128)} %get-tuple-element.41, f32[4,2,256,16]{2,3,1,0:T(8,128)S(1)} %get-tuple-element.40, bf16[128,16]{0,1:T(8,128)(2,1)S(1)} %get-tuple-element.44, bf16[128,16]{0,1:T(8,128)(2,1)S(1)} %get-tuple-element.43), kind=kOutput, calls=%fused_computation.88 | convolution fusion | flops 100810752 | bytes 1318912 | tf_op jit(solution)/shard_map/...r,dr->...d/dot_general | solution.py:65
  91.9 0.8 pad_add_fusion
  92.7 7.3 %all-to-all-start.4 = ((f32[32,24,128]{2,1,0:T(8,128)}), f32[32,24,128]{2,1,0:T(8,128)}, u32[]{:S(2)}, u32[]{:S(2)}) async-start(f32[32,24,128]{2,1,0:T(8,128)} %pad_add_fusion), calls=%async_computation.4 | async-start | bytes 786432 | tf_op jit(solution)/shard_map/all_to_all | solution.py:47
  100.0 1.3 fusion.24
  101.6 2.0 %copy.119 = bf16[512,4,128]{0,2,1:T(8,128)(2,1)} copy(bf16[512,4,128]{2,0,1:T(8,128)(2,1)} %bitcast.182) | data formatting | bytes 1048576 | tf_op jit(solution)/shard_map/convert_element_type | solution.py:263
  103.6 2.0 %copy.132 = bf16[512,512]{1,0:T(8,128)(2,1)} copy(bf16[512,512]{0,1:T(8,128)(2,1)} %bitcast.186) | data formatting | bytes 1048576
  105.6 2.5 %fusion.68 = f32[4,2,256,128]{3,2,1,0:T(8,128)} fusion(bf16[4,2,256,256]{2,3,1,0:T(8,128)(2,1)S(1)} %copy-done, bf16[4,2,256,128]{3,2,1,0:T(8,128)(2,1)} %divide_convert_fusion), kind=kOutput, calls=%fused_computation.144 | convolution fusion | flops 134217728 | bytes 2621440 | tf_op jit(solution)/shard_map/...ij,...id->...jd/dot_general | solution.py:61
  108.1 2.2 %all-to-all-done.4 = f32[32,24,128]{2,1,0:T(8,128)} async-done(((f32[32,24,128]{2,1,0:T(8,128)}), f32[32,24,128]{2,1,0:T(8,128)}, u32[]{:S(2)}, u32[]{:S(2)}) %all-to-all-start.4) | async-done | bytes 393248 | tf_op jit(solution)/shard_map/all_to_all | solution.py:47
  110.3 0.7 slice_bitcast_fusion
  111.1 1.0 slice.124
  112.1 1.3 subtract_convert_fusion
  114.5 2.3 %fusion.8 = f32[4,2,256,16]{2,3,1,0:T(8,128)S(1)} fusion(f32[4,2,256,16,16]{2,4,3,1,0:T(8,128)S(1)} %bitcast.171, f32[4,2,256,16]{2,3,1,0:T(8,128)S(1)} %copy-done.26), kind=kLoop, calls=%fused_computation.13 | loop fusion | flops 1540096 | bytes 2359296 | tf_op jit(solution)/shard_map/reduce_sum | solution.py:89
  116.9 1.0 fusion.40
  119.2 0.6 broadcast_in_dim.25
  119.8 5.9 %all-to-all-start.5 = ((f32[8,2,512]{2,1,0:T(2,128)}), f32[8,2,512]{2,1,0:T(2,128)S(1)}, u32[]{:S(2)}, u32[]{:S(2)}) async-start(f32[8,2,512]{2,1,0:T(2,128)} %broadcast_in_dim.25), calls=%async_computation.5 | async-start | bytes 65536 | tf_op jit(solution)/shard_map/all_to_all | solution.py:55
  125.8 1.9 %fusion.12 = bf16[4,2,256,128]{3,2,1,0:T(8,128)(2,1)S(1)} fusion(f32[4,2,256,128]{3,2,1,0:T(8,128)} %fusion.68, bf16[4,2,256,256]{2,3,1,0:T(8,128)(2,1)S(1)} %bitcast.163, bf16[4,2,256,128]{2,3,1,0:T(8,128)(2,1)} %copy-done.17), kind=kOutput, calls=%fused_computation.38 | convolution fusion | flops 134742016 | bytes 3145728 | tf_op jit(solution)/shard_map/...jr,...rd->...jd/dot_general | solution.py:61
  127.7 0.9 copy.183
  128.5 4.0 %all-to-all-done.5 = f32[8,2,512]{2,1,0:T(2,128)S(1)} async-done(((f32[8,2,512]{2,1,0:T(2,128)}), f32[8,2,512]{2,1,0:T(2,128)S(1)}, u32[]{:S(2)}, u32[]{:S(2)}) %all-to-all-start.5) | async-done | bytes 32800 | tf_op jit(solution)/shard_map/all_to_all | solution.py:55
  132.6 2.8 %fusion.22 = (bf16[512,512]{1,0:T(8,128)(2,1)}, bf16[512,512]{1,0:T(8,128)(2,1)}) fusion(bf16[512,512]{1,0:T(8,128)(2,1)} %param.11, f32[4,64,8,128]{3,2,1,0:T(8,128)S(1)} %bitcast.167, f32[512]{0:T(512)S(1)} %bitcast.205, f32[512]{0:T(512)S(1)} %copy-done.52, f32[512]{0:T(512)S(1)} %copy-done.47, f32[512]{0:T(512)S(1)} %bitcast.199, f32[512]{0:T(512)S(1)} %bitcast.204, ...), kind=kLoop, calls=%fused_computation.50 | loop fusion | flops 4194304 | bytes 4210688 | tf_op jit(solution)/shard_map/convert_element_type | solution.py:205
  (166 shorter events, 8.4 us)
Async XLA Ops:
  0.6 14.1 %copy-start.27 = (bf16[512,512]{1,0:T(8,128)(2,1)S(1)}, bf16[512,512]{1,0:T(8,128)(2,1)}, u32[]{:S(2)}) copy-start(bf16[512,512]{1,0:T(8,128)(2,1)} %param.14) | copy-start | bytes 1572868
  3.8 16.0 %all-to-all-start = ((f32[8,2,512]{2,1,0:T(2,128)}), f32[8,2,512]{2,1,0:T(2,128)S(1)}, u32[]{:S(2)}, u32[]{:S(2)}) async-start(f32[8,2,512]{2,1,0:T(2,128)} %broadcast_in_dim.20), calls=%async_computation | async-start | bytes 65536 | tf_op jit(solution)/shard_map/all_to_all | solution.py:55
  14.8 8.8 %copy-start.1 = (bf16[4,512,128]{2,1,0:T(8,128)(2,1)}, bf16[4,512,128]{2,1,0:T(8,128)(2,1)S(1)}, u32[]{:S(2)}) copy-start(bf16[4,512,128]{2,1,0:T(8,128)(2,1)S(1)} %copy.113) | copy-start | bytes 1572868
  16.1 3.7 %copy-start.6 = (bf16[512,512]{1,0:T(8,128)(2,1)S(1)}, bf16[512,512]{1,0:T(8,128)(2,1)}, u32[]{:S(2)}) copy-start(bf16[512,512]{1,0:T(8,128)(2,1)} %param.12) | copy-start | bytes 1572868
  16.1 3.8 %copy-start.48 = (f32[512]{0:T(512)S(1)}, f32[512]{0:T(512)}, u32[]{:S(2)}) copy-start(f32[512]{0:T(512)} %param.16) | copy-start | bytes 6148
  19.1 6.7 %copy-start.50 = (f32[192]{0:T(256)}, f32[192]{0:T(256)S(1)}, u32[]{:S(2)}) copy-start(f32[192]{0:T(256)S(1)} %pad.69.clone) | copy-start | bytes 2308
  19.8 20.6 %copy-start.42 = (f32[1,512]{1,0:T(1,128)}, f32[1,512]{1,0:T(1,128)S(1)}, u32[]{:S(2)}) copy-start(f32[1,512]{1,0:T(1,128)S(1)} %get-tuple-element.47) | copy-start | bytes 6148
  19.8 33.6 %copy-start.44 = (f32[1,512]{1,0:T(1,128)}, f32[1,512]{1,0:T(1,128)S(1)}, u32[]{:S(2)}) copy-start(f32[1,512]{1,0:T(1,128)S(1)} %get-tuple-element.48) | copy-start | bytes 6148
  20.1 2.2 %copy-start.28 = (bf16[256,136,1,1]{0,1,3,2:T(8,128)(2,1)S(1)}, bf16[256,136,1,1]{0,1,3,2:T(8,128)(2,1)}, u32[]{:S(2)}) copy-start(bf16[256,136,1,1]{0,1,3,2:T(8,128)(2,1)} %constant.67) | copy-start | bytes 208900
  20.3 0.8 copy-start.10
  21.1 1.2 copy-start.25
  23.5 12.3 %copy-start.5 = (bf16[512,512]{1,0:T(8,128)(2,1)S(1)}, bf16[512,512]{1,0:T(8,128)(2,1)}, u32[]{:S(2)}) copy-start(bf16[512,512]{1,0:T(8,128)(2,1)} %param.11) | copy-start | bytes 1572868
  23.5 12.3 %copy-start.46 = (f32[512]{0:T(512)S(1)}, f32[512]{0:T(512)}, u32[]{:S(2)}) copy-start(f32[512]{0:T(512)} %param.15) | copy-start | bytes 6148
  26.6 19.5 %all-to-all-start.1 = ((f32[32,24,128]{2,1,0:T(8,128)}), f32[32,24,128]{2,1,0:T(8,128)}, u32[]{:S(2)}, u32[]{:S(2)}) async-start(f32[32,24,128]{2,1,0:T(8,128)} %bitcast.23), calls=%async_computation.1 | async-start | bytes 786432 | tf_op jit(solution)/shard_map/all_to_all | solution.py:41
  37.9 1.4 %copy-start.29 = (bf16[256,136,1,1]{0,1,3,2:T(8,128)(2,1)S(1)}, bf16[256,136,1,1]{0,1,3,2:T(8,128)(2,1)}, u32[]{:S(2)}) copy-start(bf16[256,136,1,1]{0,1,3,2:T(8,128)(2,1)} %constant.67) | copy-start | bytes 208900
  38.0 3.0 %copy-start.8 = (bf16[4,512,128]{2,1,0:T(8,128)(2,1)}, bf16[4,512,128]{2,1,0:T(8,128)(2,1)S(1)}, u32[]{:S(2)}) copy-start(bf16[4,512,128]{2,1,0:T(8,128)(2,1)S(1)} %copy.107) | copy-start | bytes 1572868
  38.0 3.0 %copy-start.11 = (bf16[4,512,128]{2,1,0:T(8,128)(2,1)S(1)}, bf16[4,512,128]{2,1,0:T(8,128)(2,1)}, u32[]{:S(2)}) copy-start(bf16[4,512,128]{2,1,0:T(8,128)(2,1)} %copy-done.10) | copy-start | bytes 1572868
  38.0 3.0 %copy-start.32 = (pred[256,256]{0,1:T(8,128)(4,1)S(1)}, pred[256,256]{0,1:T(8,128)(4,1)}, u32[]{:S(2)}) copy-start(pred[256,256]{0,1:T(8,128)(4,1)} %iota_compare_fusion) | copy-start | bytes 196612
  38.3 0.7 copy-start.22
  48.2 15.5 %all-to-all-start.2 = ((f32[32,24,128]{2,1,0:T(8,128)}), f32[32,24,128]{2,1,0:T(8,128)}, u32[]{:S(2)}, u32[]{:S(2)}) async-start(f32[32,24,128]{2,1,0:T(8,128)} %pad_add_fusion.4), calls=%async_computation.2 | async-start | bytes 786432 | tf_op jit(solution)/shard_map/all_to_all | solution.py:47
  54.9 10.7 %copy-start.40 = (f32[4,2,256]{2,1,0:T(2,128)}, f32[4,2,256]{2,1,0:T(2,128)S(1)}, u32[]{:S(2)}) copy-start(f32[4,2,256]{2,1,0:T(2,128)S(1)} %reduce_sum.144) | copy-start | bytes 24580
  63.7 3.2 %copy-start.14 = (f32[4,2,136,128]{3,2,1,0:T(8,128)S(1)}, f32[4,2,136,128]{3,2,1,0:T(8,128)}, u32[]{:S(2)}) copy-start(f32[4,2,136,128]{3,2,1,0:T(8,128)} %get-tuple-element.51) | copy-start | bytes 1671172
  63.7 3.3 %copy-start.30 = (bf16[256,136,1,1]{0,1,3,2:T(8,128)(2,1)S(1)}, bf16[256,136,1,1]{0,1,3,2:T(8,128)(2,1)}, u32[]{:S(2)}) copy-start(bf16[256,136,1,1]{0,1,3,2:T(8,128)(2,1)} %constant.68) | copy-start | bytes 208900
  64.5 2.9 %copy-start.20 = (f32[4,2,256,128]{2,3,1,0:T(8,128)S(1)}, f32[4,2,256,128]{2,3,1,0:T(8,128)}, u32[]{:S(2)}) copy-start(f32[4,2,256,128]{2,3,1,0:T(8,128)} %copy.117) | copy-start | bytes 3145732
  64.5 2.9 %copy-start.21 = (f32[4,2,256,128]{2,3,1,0:T(8,128)S(1)}, f32[4,2,256,128]{2,3,1,0:T(8,128)}, u32[]{:S(2)}) copy-start(f32[4,2,256,128]{2,3,1,0:T(8,128)} %fusion.67) | copy-start | bytes 3145732
  66.4 2.3 %copy-start.34 = (f32[4,2,256]{2,1,0:T(2,128)}, f32[4,2,256]{2,1,0:T(2,128)S(1)}, u32[]{:S(2)}) copy-start(f32[4,2,256]{2,1,0:T(2,128)S(1)} %add_subtract_fusion.1) | copy-start | bytes 24580
  67.4 1.3 copy-start.15
  67.4 1.3 copy-start.41
  68.8 1.2 copy-start.38
  68.8 2.1 %copy-start.36 = (f32[4,2,256]{2,1,0:T(2,128)}, f32[4,2,256]{2,1,0:T(2,128)S(1)}, u32[]{:S(2)}) copy-start(f32[4,2,256]{2,1,0:T(2,128)S(1)} %get-tuple-element.15) | copy-start | bytes 24580
  72.4 9.0 %copy-start.13 = (f32[4,2,136,128]{3,2,1,0:T(8,128)}, f32[4,2,136,128]{3,2,1,0:T(8,128)S(1)}, u32[]{:S(2)}) copy-start(f32[4,2,136,128]{3,2,1,0:T(8,128)S(1)} %get-tuple-element.55) | copy-start | bytes 1671172
  72.4 8.5 %copy-start.4 = (bf16[4,2,256,128]{3,2,1,0:T(8,128)(2,1)S(1)}, bf16[4,2,256,128]{3,2,1,0:T(8,128)(2,1)}, u32[]{:S(2)}) copy-start(bf16[4,2,256,128]{3,2,1,0:T(8,128)(2,1)} %divide_convert_fusion) | copy-start | bytes 1572868
  72.5 8.5 %copy-start.16 = (bf16[4,2,256,128]{2,3,1,0:T(8,128)(2,1)S(1)}, bf16[4,2,256,128]{2,3,1,0:T(8,128)(2,1)}, u32[]{:S(2)}) copy-start(bf16[4,2,256,128]{2,3,1,0:T(8,128)(2,1)} %copy-done.15) | copy-start | bytes 1572868
  72.5 8.5 %copy-start.35 = (f32[4,2,256]{2,1,0:T(2,128)S(1)}, f32[4,2,256]{2,1,0:T(2,128)}, u32[]{:S(2)}) copy-start(f32[4,2,256]{2,1,0:T(2,128)} %copy-done.34) | copy-start | bytes 24580
  72.5 8.5 %copy-start.37 = (f32[4,2,256]{2,1,0:T(2,128)S(1)}, f32[4,2,256]{2,1,0:T(2,128)}, u32[]{:S(2)}) copy-start(f32[4,2,256]{2,1,0:T(2,128)} %copy-done.36) | copy-start | bytes 24580
  74.2 17.4 %all-to-all-start.3 = ((f32[32,24,128]{2,1,0:T(8,128)}), f32[32,24,128]{2,1,0:T(8,128)S(1)}, u32[]{:S(2)}, u32[]{:S(2)}) async-start(f32[32,24,128]{2,1,0:T(8,128)} %bitcast.32), calls=%async_computation.3 | async-start | bytes 786432 | tf_op jit(solution)/shard_map/all_to_all | solution.py:41
  78.9 2.6 %copy-start.2 = (bf16[4,512,128]{2,1,0:T(8,128)(2,1)S(1)}, bf16[4,512,128]{2,1,0:T(8,128)(2,1)}, u32[]{:S(2)}) copy-start(bf16[4,512,128]{2,1,0:T(8,128)(2,1)} %copy-done.1) | copy-start | bytes 1572868
  78.9 2.6 %copy-start.24 = (f32[4,2,256,256]{2,3,1,0:T(8,128)S(1)}, f32[4,2,256,256]{2,3,1,0:T(8,128)}, u32[]{:S(2)}) copy-start(f32[4,2,256,256]{2,3,1,0:T(8,128)} %get-tuple-element.49) | copy-start | bytes 6291460
  78.9 2.6 %copy-start.33 = (pred[256,256]{0,1:T(8,128)(4,1)S(1)}, pred[256,256]{0,1:T(8,128)(4,1)}, u32[]{:S(2)}) copy-start(pred[256,256]{0,1:T(8,128)(4,1)} %iota_compare_fusion) | copy-start | bytes 196612
  83.3 2.3 %copy-start.23 = (f32[4,2,256,32]{2,3,1,0:T(8,128)S(1)}, f32[4,2,256,32]{2,3,1,0:T(8,128)}, u32[]{:S(2)}) copy-start(f32[4,2,256,32]{2,3,1,0:T(8,128)} %copy-done.22) | copy-start | bytes 786436
  83.3 4.6 %copy-start.39 = (f32[4,2,256]{2,1,0:T(2,128)S(1)}, f32[4,2,256]{2,1,0:T(2,128)}, u32[]{:S(2)}) copy-start(f32[4,2,256]{2,1,0:T(2,128)} %copy-done.38) | copy-start | bytes 24580
  86.3 4.7 %copy-start.12 = (bf16[4,512,128]{2,1,0:T(8,128)(2,1)S(1)}, bf16[4,512,128]{2,1,0:T(8,128)(2,1)}, u32[]{:S(2)}) copy-start(bf16[4,512,128]{2,1,0:T(8,128)(2,1)} %copy-done.10) | copy-start | bytes 1572868
  87.9 3.1 %copy-start.18 = (bf16[4,2,256,256]{2,3,1,0:T(8,128)(2,1)S(1)}, bf16[4,2,256,256]{2,3,1,0:T(8,128)(2,1)}, u32[]{:S(2)}) copy-start(bf16[4,2,256,256]{2,3,1,0:T(8,128)(2,1)} %fusion.6) | copy-start | bytes 3145732
  91.8 8.2 %copy-start.47 = (f32[512]{0:T(512)S(1)}, f32[512]{0:T(512)}, u32[]{:S(2)}) copy-start(f32[512]{0:T(512)} %param.15) | copy-start | bytes 6148
  92.7 12.9 %copy-start = (bf16[4,2,256,256]{2,3,1,0:T(8,128)(2,1)S(1)}, bf16[4,2,256,256]{2,3,1,0:T(8,128)(2,1)}, u32[]{:S(2)}) copy-start(bf16[4,2,256,256]{2,3,1,0:T(8,128)(2,1)} %get-tuple-element.37) | copy-start | bytes 3145732
  92.7 17.6 %all-to-all-start.4 = ((f32[32,24,128]{2,1,0:T(8,128)}), f32[32,24,128]{2,1,0:T(8,128)}, u32[]{:S(2)}, u32[]{:S(2)}) async-start(f32[32,24,128]{2,1,0:T(8,128)} %pad_add_fusion), calls=%async_computation.4 | async-start | bytes 786432 | tf_op jit(solution)/shard_map/all_to_all | solution.py:47
  105.6 7.7 %copy-start.31 = (bf16[256,136,1,1]{0,1,3,2:T(8,128)(2,1)S(1)}, bf16[256,136,1,1]{0,1,3,2:T(8,128)(2,1)}, u32[]{:S(2)}) copy-start(bf16[256,136,1,1]{0,1,3,2:T(8,128)(2,1)} %constant.68) | copy-start | bytes 208900
  108.1 5.6 %copy-start.3 = (bf16[4,512,128]{2,1,0:T(8,128)(2,1)S(1)}, bf16[4,512,128]{2,1,0:T(8,128)(2,1)}, u32[]{:S(2)}) copy-start(bf16[4,512,128]{2,1,0:T(8,128)(2,1)} %copy-done.1) | copy-start | bytes 1572868
  113.4 1.2 copy-start.26
  113.7 0.8 copy-start.17
  114.5 3.4 %copy-start.9 = (bf16[4,512,128]{2,1,0:T(8,128)(2,1)S(1)}, bf16[4,512,128]{2,1,0:T(8,128)(2,1)}, u32[]{:S(2)}) copy-start(bf16[4,512,128]{2,1,0:T(8,128)(2,1)} %copy-done.8) | copy-start | bytes 1572868
  114.5 3.4 %copy-start.19 = (bf16[4,2,256,256]{2,3,1,0:T(8,128)(2,1)S(1)}, bf16[4,2,256,256]{2,3,1,0:T(8,128)(2,1)}, u32[]{:S(2)}) copy-start(bf16[4,2,256,256]{2,3,1,0:T(8,128)(2,1)} %fusion.6) | copy-start | bytes 3145732
  117.9 1.0 copy-start.7
  117.9 1.0 copy-start.49
  119.8 12.7 %all-to-all-start.5 = ((f32[8,2,512]{2,1,0:T(2,128)}), f32[8,2,512]{2,1,0:T(2,128)S(1)}, u32[]{:S(2)}, u32[]{:S(2)}) async-start(f32[8,2,512]{2,1,0:T(2,128)} %broadcast_in_dim.25), calls=%async_computation.5 | async-start | bytes 65536 | tf_op jit(solution)/shard_map/all_to_all | solution.py:55
  125.7 6.9 %copy-start.43 = (f32[1,512]{1,0:T(1,128)S(1)}, f32[1,512]{1,0:T(1,128)}, u32[]{:S(2)}) copy-start(f32[1,512]{1,0:T(1,128)} %copy-done.42) | copy-start | bytes 6148
  125.7 6.9 %copy-start.45 = (f32[1,512]{1,0:T(1,128)S(1)}, f32[1,512]{1,0:T(1,128)}, u32[]{:S(2)}) copy-start(f32[1,512]{1,0:T(1,128)} %copy-done.44) | copy-start | bytes 6148
  125.7 6.9 %copy-start.51 = (f32[512]{0:T(512)S(1)}, f32[512]{0:T(512)}, u32[]{:S(2)}) copy-start(f32[512]{0:T(512)} %multiply_multiply_fusion.4) | copy-start | bytes 6148
  125.8 6.9 %copy-start.52 = (f32[512]{0:T(512)S(1)}, f32[512]{0:T(512)}, u32[]{:S(2)}) copy-start(f32[512]{0:T(512)} %multiply_multiply_fusion.5) | copy-start | bytes 6148

commit v12 on v8

--- a/solution.py
+++ b/solution.py
@@ -198,11 +198,13 @@
     return (scale, (raw.astype(jnp.float32) * scale * gain).astype(jnp.bfloat16))
 
 
-def norm_back(raw, gain, scale, normed_grad, dot_total):
-    raw_float = raw.astype(jnp.float32)
-    return (
-        scale * gain * normed_grad - raw_float * scale**3 * dot_total[:, None] / (HEADS * DH)
-    ).astype(jnp.bfloat16)
+def norm_terms(raw, gain, scale, normed_grad):
+    return (scale * gain * normed_grad, raw.astype(jnp.float32) * scale**3)
+
+
+def norm_back(terms, dot_total):
+    direct, cross = terms
+    return (direct - cross * dot_total[:, None] / (HEADS * DH)).astype(jnp.bfloat16)
 
 
 def on_device(queries, keys, values, out_grad, q_gain, k_gain, signs):
@@ -278,17 +280,19 @@
     kn_grad = join_heads(
         k_diag + sketch_back(kf_grad, k_parts[1], k_parts[2], k_parts[3], sign_pair)
     )
-    (q_dot, k_dot), (v_diag, later_state) = head_sum(
+    q_terms = norm_terms(queries, q_gain, q_scale, qn_grad)
+    k_terms = norm_terms(keys, k_gain, k_scale, kn_grad)
+    (q_dot, k_dot), (v_diag, later_state, q_terms, k_terms) = head_sum(
         (
             jnp.sum(q_float * q_gain * qn_grad, axis=-1),
             jnp.sum(k_float * k_gain * kn_grad, axis=-1),
         ),
         "head",
-        (v_diag, later_state),
+        (v_diag, later_state, q_terms, k_terms),
     )
     _, v_grad = finish_backward(v_heads, k_parts[0], later_state, later_total, v_diag)
-    q_grad = norm_back(queries, q_gain, q_scale, qn_grad, q_dot)
-    k_grad = norm_back(keys, k_gain, k_scale, kn_grad, k_dot)
+    q_grad = norm_back(q_terms, q_dot)
+    k_grad = norm_back(k_terms, k_dot)
     return (join_heads(attended), q_grad, k_grad, join_heads(v_grad).astype(jnp.bfloat16))
 
 

time: 133 us -> 140 us (1.053)
  waiting for transfers between devices: 12.8 us -> 17.9 us
  matrix products: 24.6 us -> 27 us
  other arithmetic: 29.2 us -> 31.4 us
    mul x0 -> x1, other arithmetic: none -> 2.66 us  [norm_terms(): return (scale * gain * normed_grad, raw.astype(jnp.float32) * scale ** 3)]
    all_to_all x2, waiting for transfers between devices: 5.58 us -> 7.63 us  [carried_in(): lax.all_to_all(shifted, axis, 0, 0, tiled=True)]
    dot_general x4, matrix products: 3.43 us -> 5.46 us  [precise_product(): jnp.einsum(spec, lhs.astype(jnp.float32), rhs.astype(jnp.float32), precis...]
    all_to_all x2, waiting for transfers between devices: 3.1 us -> 4.88 us  [carried_in(): mine = lax.all_to_all(stacked, axis, 0, 0, tiled=True)]
    all_to_all x2, starting transfers between devices: 11.5 us -> 9.83 us  [carried_in(): lax.all_to_all(shifted, axis, 0, 0, tiled=True)]
    reduce_sum x2 -> x0, other arithmetic: 1.55 us -> none  [the longest x1 1.34 us: on_device(): jnp.sum(q_float * q_gain * qn_grad, axis=-1)]
    convert_element_type x1 -> x2, other arithmetic: 2.77 us -> 3.5 us  [norm_back(): (direct - cross * dot_total[:, None] / (HEADS * DH)).astype(jnp.bfloat16)]
    unnamed x114 -> x98, local copies, waits for them, and re-layouts: 6.07 us -> 6.2 us
  transfers between devices with their start and end apart: 6 -> 6, of which waited for: 5 -> 5; matrix products, arithmetic and copies ran while one was open for 31% -> 26% of each run, Pallas kernels for 0% -> 0%
where the time goes in v12:
time: 140 us; the launch traced here: 138 us
  starting transfers between devices  38.2 us (27%)
  other arithmetic  31.4 us (22%)
  matrix products  27 us (19%)
  local copies, waits for them, and re-layouts  22.4 us (16%)
  waiting for transfers between devices  17.9 us (13%)
  between operations  1.43 us (1%)
    dot_general x18, matrix products, product_of(): return jnp.einsum(spec, lhs, rhs, preferred_element_type=jnp.float32)  21.5 us
    all_to_all x2, starting transfers between devices, head_sum(): gathered = lax.all_to_all(spread, axis, 0, 0, tiled=True)  14.9 us
    all_to_all x2, starting transfers between devices, carried_in(): mine = lax.all_to_all(stacked, axis, 0, 0, tiled=True)  13.5 us
    all_to_all x2, starting transfers between devices, carried_in(): lax.all_to_all(shifted, axis, 0, 0, tiled=True)  9.83 us
    all_to_all x2, waiting for transfers between devices, carried_in(): lax.all_to_all(shifted, axis, 0, 0, tiled=True)  7.63 us
    unnamed x98, local copies, waits for them, and re-layouts  6.2 us
    dot_general x4, matrix products, precise_product(): jnp.einsum(spec, lhs.astype(jnp.float32), rhs.astype(jnp.float32), precis...  5.46 us
    all_to_all x2, waiting for transfers between devices, head_sum(): gathered = lax.all_to_all(spread, axis, 0, 0, tiled=True)  5.43 us
  transfers between devices with their start and end apart: 6, of which 5 were waited for; matrix products, arithmetic and copies ran while one was open for 26% of the time, Pallas kernels for 0%

profile of v12, /device:TPU:1, one launch (start us, length us, event | category | flops | bytes accessed | tf_op | source)
XLA Modules:
  0.0 138.4 jit_solution(8348195064344299662)
XLA Ops:
  0.6 1.3 fusion.16
  1.9 1.2 fusion.21
  3.2 0.6 broadcast_in_dim.16
  3.8 9.0 %all-to-all-start = ((f32[8,2,512]{2,1,0:T(2,128)}), f32[8,2,512]{2,1,0:T(2,128)S(1)}, u32[]{:S(2)}, u32[]{:S(2)}) async-start(f32[8,2,512]{2,1,0:T(2,128)} %broadcast_in_dim.16), calls=%async_computation | async-start | bytes 65536 | tf_op jit(solution)/shard_map/all_to_all | solution.py:55
  12.8 0.7 fusion.40
  13.5 1.2 reshape.170
  15.0 1.1 convert_bitcast_fusion
  16.1 1.6 %copy.109 = f32[4,512,128]{2,1,0:T(8,128)S(1)} copy(f32[4,512,128]{1,2,0:T(8,128)} %convert_bitcast_fusion) | data formatting | bytes 2097152 | tf_op jit(solution)/shard_map/convert_element_type | solution.py:156
  17.7 1.3 copy.116
  19.1 0.6 iota_compare_fusion
  21.1 1.2 convert_reduce_fusion.1
  22.3 1.1 convolution_convert_fusion
  23.5 2.3 %fusion.55 = (f32[4,136,128]{2,1,0:T(8,128)S(1)}, f32[4,2,136,128]{3,2,1,0:T(8,128)}) fusion(bf16[4,2,256,136]{2,3,1,0:T(8,128)(2,1)} %convolution_convert_fusion, bf16[4,2,256,128]{3,2,1,0:T(8,128)(2,1)S(1)} %bitcast.160), kind=kOutput, calls=%fused_computation.133 | convolution fusion | flops 71372800 | bytes 1916928 | tf_op jit(solution)/shard_map/...jr,...jd->...rd/dot_general | solution.py:61
  25.7 0.8 maximum_maximum_fusion
  26.6 9.2 %all-to-all-start.1 = ((f32[32,24,128]{2,1,0:T(8,128)}), f32[32,24,128]{2,1,0:T(8,128)}, u32[]{:S(2)}, u32[]{:S(2)}) async-start(f32[32,24,128]{2,1,0:T(8,128)} %bitcast.23), calls=%async_computation.1 | async-start | bytes 786432 | tf_op jit(solution)/shard_map/all_to_all | solution.py:41
  35.8 1.0 fusion.18
  36.7 1.2 reshape.166
  38.3 0.7 copy-done.23
  39.0 0.6 copy-done.25
  39.9 1.1 convolution_convert_fusion.1
  41.6 2.2 %convert_reduce_fusion.2 = (f32[4,2,256]{2,1,0:T(2,128)S(1)}, bf16[4,2,256,256]{2,3,1,0:T(8,128)(2,1)}, f32[4,2,256,256]{2,3,1,0:T(8,128)}) fusion(pred[256,256]{0,1:T(8,128)(4,1)S(1)} %copy-done.34, bf16[4,2,256,128]{3,2,1,0:T(8,128)(2,1)S(1)} %bitcast.165, bf16[4,2,256,128]{3,2,1,0:T(8,128)(2,1)S(1)} %bitcast.168), kind=kOutput, calls=%fused_computation.19 | convolution fusion | flops 137885696 | bytes 4268032 | tf_op jit(solution)/shard_map/...id,...jd->...ij/dot_general | solution.py:61
  43.8 2.3 %all-to-all-done.1 = f32[32,24,128]{2,1,0:T(8,128)} async-done(((f32[32,24,128]{2,1,0:T(8,128)}), f32[32,24,128]{2,1,0:T(8,128)}, u32[]{:S(2)}, u32[]{:S(2)}) %all-to-all-start.1) | async-done | bytes 393248 | tf_op jit(solution)/shard_map/all_to_all | solution.py:41
  46.1 1.0 slice.110
  47.4 0.8 pad_add_fusion.4
  48.2 5.2 %all-to-all-start.2 = ((f32[32,24,128]{2,1,0:T(8,128)}), f32[32,24,128]{2,1,0:T(8,128)}, u32[]{:S(2)}, u32[]{:S(2)}) async-start(f32[32,24,128]{2,1,0:T(8,128)} %pad_add_fusion.4), calls=%async_computation.2 | async-start | bytes 786432 | tf_op jit(solution)/shard_map/all_to_all | solution.py:47
  54.1 2.7 %fusion.58 = f32[4,2,256,128]{2,3,1,0:T(8,128)} fusion(bf16[4,2,256,256]{2,3,1,0:T(8,128)(2,1)} %get-tuple-element.45, bf16[4,2,256,128]{3,2,1,0:T(8,128)(2,1)} %bitcast.161), kind=kOutput, calls=%fused_computation.136 | convolution fusion | flops 134217728 | bytes 2621440 | tf_op jit(solution)/shard_map/...ij,...jd->...id/dot_general | solution.py:61
  56.8 6.9 %all-to-all-done.2 = f32[32,24,128]{2,1,0:T(8,128)} async-done(((f32[32,24,128]{2,1,0:T(8,128)}), f32[32,24,128]{2,1,0:T(8,128)}, u32[]{:S(2)}, u32[]{:S(2)}) %all-to-all-start.2) | async-done | bytes 393248 | tf_op jit(solution)/shard_map/all_to_all | solution.py:47
  63.7 0.8 slice_bitcast_fusion.1
  64.5 1.1 slice.117
  66.7 1.3 multiply_reduce_fusion
  68.0 1.1 divide_convert_fusion.1
  69.1 0.9 fusion.36
  70.7 1.5 %fusion.56 = (f32[4,136,128]{2,1,0:T(8,128)S(1)}, f32[4,2,136,128]{3,2,1,0:T(8,128)S(1)}) fusion(bf16[4,2,256,136]{2,3,1,0:T(8,128)(2,1)} %convolution_convert_fusion.1, bf16[4,2,256,128]{3,2,1,0:T(8,128)(2,1)} %divide_convert_fusion.1), kind=kOutput, calls=%fused_computation.134 | convolution fusion | flops 71372800 | bytes 1916928 | tf_op jit(solution)/shard_map/...ir,...id->...rd/dot_general | solution.py:61
  72.2 1.6 %maximum_maximum_fusion.1 = f32[4,192,128]{2,1,0:T(8,128)} fusion(f32[4,2,128]{2,1,0:T(2,128)} %reshape.175, f32[4,136,128]{2,1,0:T(8,128)S(1)} %get-tuple-element.68, f32[192]{0:T(256)} %copy-done.39), kind=kLoop, calls=%fused_computation.65 | loop fusion | flops 196608 | bytes 676608 | tf_op jit(solution)/shard_map/concatenate | solution.py:32
  73.8 1.4 %fusion.59 = f32[4,2,256,128]{3,2,1,0:T(8,128)} fusion(bf16[4,2,256,256]{2,3,1,0:T(8,128)(2,1)S(1)} %copy-done, bf16[4,2,256,128]{3,2,1,0:T(8,128)(2,1)S(1)} %copy-done.3), kind=kOutput, calls=%fused_computation.137 | convolution fusion | flops 134217728 | bytes 2621440 | tf_op jit(solution)/shard_map/...ij,...id->...jd/dot_general | solution.py:61
  76.1 2.3 %fusion.10 = f32[4,2,256,16]{2,3,1,0:T(8,128)S(1)} fusion(f32[4,2,256,16,16]{2,4,3,1,0:T(8,128)S(1)} %bitcast.158, f32[4,2,256,16]{2,3,1,0:T(8,128)S(1)} %copy-done.26), kind=kLoop, calls=%fused_computation.16 | loop fusion | flops 1540096 | bytes 2359296 | tf_op jit(solution)/shard_map/reduce_sum | solution.py:89
  78.4 4.4 %all-to-all-start.3 = ((f32[32,24,128]{2,1,0:T(8,128)}), f32[32,24,128]{2,1,0:T(8,128)}, u32[]{:S(2)}, u32[]{:S(2)}) async-start(f32[32,24,128]{2,1,0:T(8,128)} %bitcast.32), calls=%async_computation.3 | async-start | bytes 786432 | tf_op jit(solution)/shard_map/all_to_all | solution.py:41
  82.8 0.9 rev.14
  83.7 2.1 %fusion.57 = f32[4,2,136,128]{3,2,1,0:T(8,128)} fusion(f32[4,2,136,128]{3,2,1,0:T(8,128)} %rev.14), kind=kOutput, calls=%fused_computation.135 | output fusion | flops 139264 | bytes 1114112 | tf_op jit(solution)/shard_map/jit(cumsum)/reduce_window_sum | solution.py:137
  85.8 2.1 %divide_convert_fusion = bf16[4,2,256,128]{2,3,1,0:T(8,128)(2,1)} fusion(f32[4,2,256,128]{2,3,1,0:T(8,128)} %get-tuple-element.16, f32[4,2,256]{2,1,0:T(2,128)S(1)} %get-tuple-element.17), kind=kLoop, calls=%fused_computation.59 | loop fusion | flops 524288 | bytes 1581056 | tf_op jit(solution)/shard_map/convert_element_type | solution.py:262
  87.9 0.7 slice_multiply_fusion.2
  88.6 1.8 %fusion.6 = bf16[4,2,256,256]{2,3,1,0:T(8,128)(2,1)} fusion(f32[4,2,256,256]{2,3,1,0:T(8,128)S(1)} %copy-done.28, bf16[4,2,256,128]{3,2,1,0:T(8,128)(2,1)S(1)} %copy-done.3, bf16[4,2,256,128]{3,2,1,0:T(8,128)(2,1)S(1)} %bitcast.162, f32[4,2,256]{2,1,0:T(2,128)S(1)} %get-tuple-element.19, pred[256,256]{0,1:T(8,128)(4,1)S(1)} %copy-done.35), kind=kOutput, calls=%fused_computation.10 | convolution fusion | flops 138936320 | bytes 4268032 | tf_op jit(solution)/shard_map/...id,...jd->...ij/dot_general | solution.py:61
  90.3 2.6 %all-to-all-done.3 = f32[32,24,128]{2,1,0:T(8,128)} async-done(((f32[32,24,128]{2,1,0:T(8,128)}), f32[32,24,128]{2,1,0:T(8,128)}, u32[]{:S(2)}, u32[]{:S(2)}) %all-to-all-start.3) | async-done | bytes 393248 | tf_op jit(solution)/shard_map/all_to_all | solution.py:41
  93.0 1.0 slice.118
  94.3 0.8 pad_add_fusion
  95.1 4.7 %all-to-all-start.4 = ((f32[32,24,128]{2,1,0:T(8,128)}), f32[32,24,128]{2,1,0:T(8,128)}, u32[]{:S(2)}, u32[]{:S(2)}) async-start(f32[32,24,128]{2,1,0:T(8,128)} %pad_add_fusion), calls=%async_computation.4 | async-start | bytes 786432 | tf_op jit(solution)/shard_map/all_to_all | solution.py:47
  99.8 3.0 %fusion.28 = f32[4,2,256,128]{3,2,1,0:T(8,128)} fusion(f32[4,2,256,16]{2,3,1,0:T(8,128)} %get-tuple-element.53, f32[4,2,256,16]{2,3,1,0:T(8,128)} %get-tuple-element.52, bf16[128,16]{0,1:T(8,128)(2,1)S(1)} %get-tuple-element.58, bf16[128,16]{0,1:T(8,128)(2,1)S(1)} %get-tuple-element.57), kind=kOutput, calls=%fused_computation.81 | convolution fusion | flops 100810752 | bytes 1318912 | tf_op jit(solution)/shard_map/...r,dr->...d/dot_general | solution.py:65
  103.1 1.0 copy.117
  104.1 1.2 copy.118
  105.4 1.0 copy.131
  106.4 3.0 %convolution_add_fusion.4 = f32[4,2,256,128]{3,2,1,0:T(8,128)} fusion(f32[4,2,256,128]{3,2,1,0:T(8,128)} %fusion.28, bf16[4,2,256,256]{2,3,1,0:T(8,128)(2,1)} %fusion.6, bf16[4,2,256,128]{3,2,1,0:T(8,128)(2,1)S(1)} %bitcast.169), kind=kOutput, calls=%fused_computation.33 | convolution fusion | flops 134479872 | bytes 3670016 | tf_op jit(solution)/shard_map/...ij,...jd->...id/dot_general | solution.py:61
  109.4 0.7 all-to-all-done.4
  110.1 0.7 slice_bitcast_fusion
  110.9 1.0 slice.124
  111.8 1.1 subtract_convert_fusion.2
  113.9 2.3 %fusion.8 = f32[4,2,256,16]{2,3,1,0:T(8,128)S(1)} fusion(f32[4,2,256,16,16]{2,4,3,1,0:T(8,128)S(1)} %bitcast.159, f32[4,2,256,16]{2,3,1,0:T(8,128)S(1)} %copy-done.30), kind=kLoop, calls=%fused_computation.13 | loop fusion | flops 1540096 | bytes 2359296 | tf_op jit(solution)/shard_map/reduce_sum | solution.py:89
  116.3 1.0 fusion.31
  118.9 2.7 %bitcast_multiply_fusion = (f32[512,512]{1,0:T(8,128)}, f32[512]{0:T(512)S(1)}, f32[512,512]{1,0:T(8,128)}, f32[512,512]{1,0:T(8,128)}, f32[512]{0:T(512)S(1)}, /*index=5*/f32[512,512]{1,0:T(8,128)}) fusion(f32[4,64,8,128]{3,2,1,0:T(8,128)S(1)} %bitcast.171, f32[512]{0:T(512)S(1)} %copy-done.43, f32[512]{0:T(512)S(1)} %bitcast.184, ...), kind=kLoop, calls=%fused_computation.54 | loop fusion | flops 3668992 | bytes 7356416 | tf_op jit(solution)/shard_map/mul | solution.py:202
  121.6 0.6 broadcast_in_dim.19
  122.2 5.9 %all-to-all-start.5 = ((f32[8,2,512]{2,1,0:T(2,128)}), f32[8,2,512]{2,1,0:T(2,128)S(1)}, u32[]{:S(2)}, u32[]{:S(2)}) async-start(f32[8,2,512]{2,1,0:T(2,128)} %broadcast_in_dim.19), calls=%async_computation.5 | async-start | bytes 65536 | tf_op jit(solution)/shard_map/all_to_all | solution.py:55
  128.6 0.9 copy.181
  129.5 5.4 %all-to-all-done.5 = f32[8,2,512]{2,1,0:T(2,128)S(1)} async-done(((f32[8,2,512]{2,1,0:T(2,128)}), f32[8,2,512]{2,1,0:T(2,128)S(1)}, u32[]{:S(2)}, u32[]{:S(2)}) %all-to-all-start.5) | async-done | bytes 32800 | tf_op jit(solution)/shard_map/all_to_all | solution.py:55
  134.9 2.5 %subtract_convert_fusion = bf16[512,512]{1,0:T(8,128)(2,1)} fusion(f32[512,512]{1,0:T(8,128)} %get-tuple-element.24, f32[512,512]{1,0:T(8,128)} %get-tuple-element.25, f32[512]{0:T(512)S(1)} %bitcast.196), kind=kLoop, calls=%fused_computation.57 | loop fusion | flops 1048576 | bytes 2623488 | tf_op jit(solution)/shard_map/convert_element_type | solution.py:207
  137.4 1.0 subtract_convert_fusion.1
  (151 shorter events, 10.0 us)
Async XLA Ops:
  0.6 14.1 %copy-start.31 = (bf16[512,512]{1,0:T(8,128)(2,1)S(1)}, bf16[512,512]{1,0:T(8,128)(2,1)}, u32[]{:S(2)}) copy-start(bf16[512,512]{1,0:T(8,128)(2,1)} %param.14) | copy-start | bytes 1572868
  3.8 16.0 %all-to-all-start = ((f32[8,2,512]{2,1,0:T(2,128)}), f32[8,2,512]{2,1,0:T(2,128)S(1)}, u32[]{:S(2)}, u32[]{:S(2)}) async-start(f32[8,2,512]{2,1,0:T(2,128)} %broadcast_in_dim.16), calls=%async_computation | async-start | bytes 65536 | tf_op jit(solution)/shard_map/all_to_all | solution.py:55
  14.8 8.7 %copy-start.1 = (bf16[4,512,128]{2,1,0:T(8,128)(2,1)}, bf16[4,512,128]{2,1,0:T(8,128)(2,1)S(1)}, u32[]{:S(2)}) copy-start(bf16[4,512,128]{2,1,0:T(8,128)(2,1)S(1)} %copy.112) | copy-start | bytes 1572868
  16.1 3.7 %copy-start.12 = (bf16[512,512]{1,0:T(8,128)(2,1)S(1)}, bf16[512,512]{1,0:T(8,128)(2,1)}, u32[]{:S(2)}) copy-start(bf16[512,512]{1,0:T(8,128)(2,1)} %param.12) | copy-start | bytes 1572868
  16.1 3.7 %copy-start.42 = (f32[512]{0:T(512)S(1)}, f32[512]{0:T(512)}, u32[]{:S(2)}) copy-start(f32[512]{0:T(512)} %param.16) | copy-start | bytes 6148
  19.1 6.6 %copy-start.39 = (f32[192]{0:T(256)}, f32[192]{0:T(256)S(1)}, u32[]{:S(2)}) copy-start(f32[192]{0:T(256)S(1)} %pad.69.clone) | copy-start | bytes 2308
  19.8 33.6 %copy-start.37 = (f32[1,512]{1,0:T(1,128)}, f32[1,512]{1,0:T(1,128)S(1)}, u32[]{:S(2)}) copy-start(f32[1,512]{1,0:T(1,128)S(1)} %get-tuple-element.62) | copy-start | bytes 6148
  20.0 2.2 %copy-start.32 = (bf16[256,136,1,1]{0,1,3,2:T(8,128)(2,1)S(1)}, bf16[256,136,1,1]{0,1,3,2:T(8,128)(2,1)}, u32[]{:S(2)}) copy-start(bf16[256,136,1,1]{0,1,3,2:T(8,128)(2,1)} %constant.67) | copy-start | bytes 208900
  20.2 0.8 copy-start.6
  21.1 1.2 copy-start.29
  23.4 12.4 %copy-start.10 = (bf16[512,512]{1,0:T(8,128)(2,1)S(1)}, bf16[512,512]{1,0:T(8,128)(2,1)}, u32[]{:S(2)}) copy-start(bf16[512,512]{1,0:T(8,128)(2,1)} %param.11) | copy-start | bytes 1572868
  23.4 12.4 %copy-start.40 = (f32[512]{0:T(512)S(1)}, f32[512]{0:T(512)}, u32[]{:S(2)}) copy-start(f32[512]{0:T(512)} %param.15) | copy-start | bytes 6148
  26.6 19.5 %all-to-all-start.1 = ((f32[32,24,128]{2,1,0:T(8,128)}), f32[32,24,128]{2,1,0:T(8,128)}, u32[]{:S(2)}, u32[]{:S(2)}) async-start(f32[32,24,128]{2,1,0:T(8,128)} %bitcast.23), calls=%async_computation.1 | async-start | bytes 786432 | tf_op jit(solution)/shard_map/all_to_all | solution.py:41
  38.0 3.6 %copy-start.4 = (bf16[4,512,128]{2,1,0:T(8,128)(2,1)}, bf16[4,512,128]{2,1,0:T(8,128)(2,1)S(1)}, u32[]{:S(2)}) copy-start(bf16[4,512,128]{2,1,0:T(8,128)(2,1)S(1)} %copy.106) | copy-start | bytes 1572868
  38.0 3.6 %copy-start.7 = (bf16[4,512,128]{2,1,0:T(8,128)(2,1)S(1)}, bf16[4,512,128]{2,1,0:T(8,128)(2,1)}, u32[]{:S(2)}) copy-start(bf16[4,512,128]{2,1,0:T(8,128)(2,1)} %copy-done.6) | copy-start | bytes 1572868
  38.0 3.6 %copy-start.34 = (pred[256,256]{0,1:T(8,128)(4,1)S(1)}, pred[256,256]{0,1:T(8,128)(4,1)}, u32[]{:S(2)}) copy-start(pred[256,256]{0,1:T(8,128)(4,1)} %iota_compare_fusion) | copy-start | bytes 196612
  38.3 0.7 copy-start.23
  39.0 0.6 copy-start.25
  47.3 6.7 %copy-start.36 = (f32[4,2,16,16]{3,2,1,0:T(8,128)S(1)}, f32[4,2,16,16]{3,2,1,0:T(8,128)}, u32[]{:S(2)}) copy-start(f32[4,2,16,16]{3,2,1,0:T(8,128)} %get-tuple-element.41) | copy-start | bytes 24580
  48.2 15.5 %all-to-all-start.2 = ((f32[32,24,128]{2,1,0:T(8,128)}), f32[32,24,128]{2,1,0:T(8,128)}, u32[]{:S(2)}, u32[]{:S(2)}) async-start(f32[32,24,128]{2,1,0:T(8,128)} %pad_add_fusion.4), calls=%async_computation.2 | async-start | bytes 786432 | tf_op jit(solution)/shard_map/all_to_all | solution.py:47
  56.8 9.5 %copy-start.33 = (bf16[256,136,1,1]{0,1,3,2:T(8,128)(2,1)S(1)}, bf16[256,136,1,1]{0,1,3,2:T(8,128)(2,1)}, u32[]{:S(2)}) copy-start(bf16[256,136,1,1]{0,1,3,2:T(8,128)(2,1)} %constant.68) | copy-start | bytes 208900
  63.7 2.5 %copy-start.9 = (f32[4,2,136,128]{3,2,1,0:T(8,128)S(1)}, f32[4,2,136,128]{3,2,1,0:T(8,128)}, u32[]{:S(2)}) copy-start(f32[4,2,136,128]{3,2,1,0:T(8,128)} %get-tuple-element.65) | copy-start | bytes 1671172
  64.5 2.1 %copy-start.21 = (f32[4,2,256,128]{2,3,1,0:T(8,128)S(1)}, f32[4,2,256,128]{2,3,1,0:T(8,128)}, u32[]{:S(2)}) copy-start(f32[4,2,256,128]{2,3,1,0:T(8,128)} %copy.116) | copy-start | bytes 3145732
  64.5 2.1 %copy-start.22 = (f32[4,2,256,128]{2,3,1,0:T(8,128)S(1)}, f32[4,2,256,128]{2,3,1,0:T(8,128)}, u32[]{:S(2)}) copy-start(f32[4,2,256,128]{2,3,1,0:T(8,128)} %fusion.58) | copy-start | bytes 3145732
  66.7 1.3 copy-start.14
  69.1 4.7 %copy-start = (bf16[4,2,256,256]{2,3,1,0:T(8,128)(2,1)S(1)}, bf16[4,2,256,256]{2,3,1,0:T(8,128)(2,1)}, u32[]{:S(2)}) copy-start(bf16[4,2,256,256]{2,3,1,0:T(8,128)(2,1)} %get-tuple-element.45) | copy-start | bytes 3145732
  70.0 3.8 %copy-start.3 = (bf16[4,2,256,128]{3,2,1,0:T(8,128)(2,1)S(1)}, bf16[4,2,256,128]{3,2,1,0:T(8,128)(2,1)}, u32[]{:S(2)}) copy-start(bf16[4,2,256,128]{3,2,1,0:T(8,128)(2,1)} %divide_convert_fusion.1) | copy-start | bytes 1572868
  72.2 3.0 %copy-start.15 = (bf16[4,2,256,128]{2,3,1,0:T(8,128)(2,1)S(1)}, bf16[4,2,256,128]{2,3,1,0:T(8,128)(2,1)}, u32[]{:S(2)}) copy-start(bf16[4,2,256,128]{2,3,1,0:T(8,128)(2,1)} %copy-done.14) | copy-start | bytes 1572868
  75.2 0.9 copy-start.26
  78.4 14.6 %all-to-all-start.3 = ((f32[32,24,128]{2,1,0:T(8,128)}), f32[32,24,128]{2,1,0:T(8,128)}, u32[]{:S(2)}, u32[]{:S(2)}) async-start(f32[32,24,128]{2,1,0:T(8,128)} %bitcast.32), calls=%async_computation.3 | async-start | bytes 786432 | tf_op jit(solution)/shard_map/all_to_all | solution.py:41
  82.8 5.1 %copy-start.24 = (f32[4,2,256,32]{2,3,1,0:T(8,128)S(1)}, f32[4,2,256,32]{2,3,1,0:T(8,128)}, u32[]{:S(2)}) copy-start(f32[4,2,256,32]{2,3,1,0:T(8,128)} %copy-done.23) | copy-start | bytes 786436
  82.8 5.8 %copy-start.2 = (bf16[4,512,128]{2,1,0:T(8,128)(2,1)S(1)}, bf16[4,512,128]{2,1,0:T(8,128)(2,1)}, u32[]{:S(2)}) copy-start(bf16[4,512,128]{2,1,0:T(8,128)(2,1)} %copy-done.1) | copy-start | bytes 1572868
  82.8 5.8 %copy-start.35 = (pred[256,256]{0,1:T(8,128)(4,1)S(1)}, pred[256,256]{0,1:T(8,128)(4,1)}, u32[]{:S(2)}) copy-start(pred[256,256]{0,1:T(8,128)(4,1)} %iota_compare_fusion) | copy-start | bytes 196612
  83.7 4.9 %copy-start.28 = (f32[4,2,256,256]{2,3,1,0:T(8,128)S(1)}, f32[4,2,256,256]{2,3,1,0:T(8,128)}, u32[]{:S(2)}) copy-start(f32[4,2,256,256]{2,3,1,0:T(8,128)} %get-tuple-element.63) | copy-start | bytes 6291460
  94.3 8.8 %copy-start.27 = (bf16[4,2,256,128]{2,3,1,0:T(8,128)(2,1)S(1)}, bf16[4,2,256,128]{2,3,1,0:T(8,128)(2,1)}, u32[]{:S(2)}) copy-start(bf16[4,2,256,128]{2,3,1,0:T(8,128)(2,1)} %divide_convert_fusion) | copy-start | bytes 1572868
  95.1 15.0 %all-to-all-start.4 = ((f32[32,24,128]{2,1,0:T(8,128)}), f32[32,24,128]{2,1,0:T(8,128)}, u32[]{:S(2)}, u32[]{:S(2)}) async-start(f32[32,24,128]{2,1,0:T(8,128)} %pad_add_fusion), calls=%async_computation.4 | async-start | bytes 786432 | tf_op jit(solution)/shard_map/all_to_all | solution.py:47
  99.8 6.6 %copy-start.8 = (bf16[4,512,128]{2,1,0:T(8,128)(2,1)S(1)}, bf16[4,512,128]{2,1,0:T(8,128)(2,1)}, u32[]{:S(2)}) copy-start(bf16[4,512,128]{2,1,0:T(8,128)(2,1)} %copy-done.6) | copy-start | bytes 1572868
  113.0 0.9 copy-start.30
  113.9 3.4 %copy-start.5 = (bf16[4,512,128]{2,1,0:T(8,128)(2,1)S(1)}, bf16[4,512,128]{2,1,0:T(8,128)(2,1)}, u32[]{:S(2)}) copy-start(bf16[4,512,128]{2,1,0:T(8,128)(2,1)} %copy-done.4) | copy-start | bytes 1572868
  113.9 3.4 %copy-start.16 = (bf16[4,2,256,256]{2,3,1,0:T(8,128)(2,1)S(1)}, bf16[4,2,256,256]{2,3,1,0:T(8,128)(2,1)}, u32[]{:S(2)}) copy-start(bf16[4,2,256,256]{2,3,1,0:T(8,128)(2,1)} %fusion.6) | copy-start | bytes 3145732
  117.3 1.0 copy-start.11
  117.3 1.2 copy-start.13
  117.3 1.5 %copy-start.17 = (f32[4,2,256,128]{3,2,1,0:T(8,128)S(1)}, f32[4,2,256,128]{3,2,1,0:T(8,128)}, u32[]{:S(2)}) copy-start(f32[4,2,256,128]{3,2,1,0:T(8,128)} %convolution_add_fusion.4) | copy-start | bytes 3145732
  117.3 1.5 %copy-start.38 = (f32[1,512]{1,0:T(1,128)S(1)}, f32[1,512]{1,0:T(1,128)}, u32[]{:S(2)}) copy-start(f32[1,512]{1,0:T(1,128)} %copy-done.37) | copy-start | bytes 6148
  117.3 1.5 %copy-start.41 = (f32[512]{0:T(512)S(1)}, f32[512]{0:T(512)}, u32[]{:S(2)}) copy-start(f32[512]{0:T(512)} %param.15) | copy-start | bytes 6148
  117.3 1.5 %copy-start.43 = (f32[512]{0:T(512)S(1)}, f32[512]{0:T(512)}, u32[]{:S(2)}) copy-start(f32[512]{0:T(512)} %param.16) | copy-start | bytes 6148
  117.4 1.5 %copy-start.44 = (f32[512]{0:T(512)S(1)}, f32[512]{0:T(512)}, u32[]{:S(2)}) copy-start(f32[512]{0:T(512)} %multiply_multiply_fusion.4) | copy-start | bytes 6148
  117.4 1.5 %copy-start.45 = (f32[512]{0:T(512)S(1)}, f32[512]{0:T(512)}, u32[]{:S(2)}) copy-start(f32[512]{0:T(512)} %multiply_multiply_fusion.5) | copy-start | bytes 6148
  118.9 9.2 %copy-start.18 = (f32[4,2,256,128]{3,2,1,0:T(8,128)S(1)}, f32[4,2,256,128]{3,2,1,0:T(8,128)}, u32[]{:S(2)}) copy-start(f32[4,2,256,128]{3,2,1,0:T(8,128)} %fusion.59) | copy-start | bytes 3145732
  122.2 12.7 %all-to-all-start.5 = ((f32[8,2,512]{2,1,0:T(2,128)}), f32[8,2,512]{2,1,0:T(2,128)S(1)}, u32[]{:S(2)}, u32[]{:S(2)}) async-start(f32[8,2,512]{2,1,0:T(2,128)} %broadcast_in_dim.19), calls=%async_computation.5 | async-start | bytes 65536 | tf_op jit(solution)/shard_map/all_to_all | solution.py:55
  128.6 8.9 %copy-start.19 = (f32[512,512]{1,0:T(8,128)S(1)}, f32[512,512]{1,0:T(8,128)}, u32[]{:S(2)}) copy-start(f32[512,512]{1,0:T(8,128)} %get-tuple-element.22) | copy-start | bytes 3145732
  128.6 8.9 %copy-start.20 = (f32[512,512]{1,0:T(8,128)S(1)}, f32[512,512]{1,0:T(8,128)}, u32[]{:S(2)}) copy-start(f32[512,512]{1,0:T(8,128)} %get-tuple-element.21) | copy-start | bytes 3145732

commit v13 on v8

--- a/solution.py
+++ b/solution.py
@@ -212,9 +212,9 @@
     sign_pair = jnp.concatenate([2 * signs[0] - 1, 2 * signs[1] - 1], axis=1).astype(jnp.bfloat16)
     q_float = queries.astype(jnp.float32)
     k_float = keys.astype(jnp.float32)
-    (q_total, k_total), _ = head_sum(
-        (jnp.sum(q_float * q_float, axis=-1), jnp.sum(k_float * k_float, axis=-1)), "head"
-    )
+    both = jnp.stack([q_float, k_float])
+    squares = jnp.sum(both * both, axis=-1)
+    (q_total, k_total), _ = head_sum((squares[0], squares[1]), "head")
     q_scale, q_normed = normalize(queries, q_gain, q_total)
     k_scale, k_normed = normalize(keys, k_gain, k_total)
 

time: 133 us -> 129 us (0.970)
  waiting for transfers between devices: 12.8 us -> 16.1 us
  local copies, waits for them, and re-layouts: 23.3 us -> 20.8 us
  starting transfers between devices: 39.4 us -> 37 us
  other arithmetic: 29.2 us -> 27.5 us
    reduce_sum x2 -> x1, other arithmetic: 2.49 us -> 0.22 us  [on_device(): squares = jnp.sum(both * both, axis=-1)]
    reshape x3, local copies, waits for them, and re-layouts: 2.45 us -> 0.37 us  [split_heads(): array.reshape(tok_rows, heads_here, DH).transpose(1, 0, 2)]
    all_to_all x2, waiting for transfers between devices: 3.1 us -> 4.93 us  [carried_in(): mine = lax.all_to_all(stacked, axis, 0, 0, tiled=True)]
    all_to_all x2, starting transfers between devices: 14.9 us -> 13.2 us  [head_sum(): gathered = lax.all_to_all(spread, axis, 0, 0, tiled=True)]
    all_to_all x2, waiting for transfers between devices: 4.08 us -> 5.77 us  [head_sum(): gathered = lax.all_to_all(spread, axis, 0, 0, tiled=True)]
    another operation x0 -> x1, other arithmetic: none -> 1.53 us  [on_device(): both = jnp.stack([q_float, k_float])]
    convert_element_type x1 -> x2, other arithmetic: 2.77 us -> 3.29 us  [norm_back(): return (scale * gain * normed_grad - raw_float * scale ** 3 * dot_total[:...]
    unnamed x114 -> x120, local copies, waits for them, and re-layouts: 6.07 us -> 5.57 us
  transfers between devices with their start and end apart: 6 -> 6, of which waited for: 5 -> 6; matrix products, arithmetic and copies ran while one was open for 31% -> 29% of each run, Pallas kernels for 0% -> 0%
where the time goes in v13:
time: 129 us; the launch traced here: 128 us
  starting transfers between devices  37 us (29%)
  other arithmetic  27.5 us (21%)
  matrix products  24.6 us (19%)
  local copies, waits for them, and re-layouts  20.8 us (16%)
  waiting for transfers between devices  16.1 us (12%)
  between operations  1.67 us (1%)
    dot_general x18, matrix products, product_of(): return jnp.einsum(spec, lhs, rhs, preferred_element_type=jnp.float32)  21.1 us
    all_to_all x2, starting transfers between devices, head_sum(): gathered = lax.all_to_all(spread, axis, 0, 0, tiled=True)  13.2 us
    all_to_all x2, starting transfers between devices, carried_in(): mine = lax.all_to_all(stacked, axis, 0, 0, tiled=True)  13.1 us
    all_to_all x2, starting transfers between devices, carried_in(): lax.all_to_all(shifted, axis, 0, 0, tiled=True)  10.8 us
    all_to_all x2, waiting for transfers between devices, head_sum(): gathered = lax.all_to_all(spread, axis, 0, 0, tiled=True)  5.77 us
    unnamed x120, local copies, waits for them, and re-layouts  5.57 us
    all_to_all x2, waiting for transfers between devices, carried_in(): lax.all_to_all(shifted, axis, 0, 0, tiled=True)  5.43 us
    all_to_all x2, waiting for transfers between devices, carried_in(): mine = lax.all_to_all(stacked, axis, 0, 0, tiled=True)  4.93 us
  transfers between devices with their start and end apart: 6, of which 6 were waited for; matrix products, arithmetic and copies ran while one was open for 29% of the time, Pallas kernels for 0%

profile of v13, /device:TPU:1, one launch (start us, length us, event | category | flops | bytes accessed | tf_op | source)
XLA Modules:
  0.0 127.7 jit_solution(6387308057900453091)
XLA Ops:
  0.7 1.5 %convert_bitcast_fusion = (f32[1,512,512]{2,1,0:T(8,128)S(1)}, f32[1,512,512]{2,1,0:T(8,128)S(1)}) fusion(bf16[512,512]{1,0:T(8,128)(2,1)} %param.12, bf16[512,512]{1,0:T(8,128)(2,1)} %param.11), kind=kLoop, calls=%fused_computation.26 | loop fusion | flops 524288 | bytes 3145728 | tf_op jit(solution)/shard_map/stack | solution.py:215
  2.4 0.6 broadcast_in_dim.16
  3.1 9.0 %all-to-all-start = ((f32[8,2,512]{2,1,0:T(2,128)}), f32[8,2,512]{2,1,0:T(2,128)S(1)}, u32[]{:S(2)}, u32[]{:S(2)}) async-start(f32[8,2,512]{2,1,0:T(2,128)} %broadcast_in_dim.16), calls=%async_computation | async-start | bytes 65536 | tf_op jit(solution)/shard_map/all_to_all | solution.py:55
  12.5 1.1 convert_bitcast_fusion.2
  13.7 1.6 %copy.109 = f32[4,512,128]{2,1,0:T(8,128)S(1)} copy(f32[4,512,128]{1,2,0:T(8,128)} %convert_bitcast_fusion.2) | data formatting | bytes 2097152 | tf_op jit(solution)/shard_map/convert_element_type | solution.py:156
  15.3 1.3 %copy.116 = f32[4,2,256,128]{2,3,1,0:T(8,128)} copy(f32[4,2,256,128]{3,2,1,0:T(8,128)S(1)} %bitcast.166) | data formatting | bytes 2097152 | tf_op jit(solution)/shard_map/convert_element_type | solution.py:156
  16.7 0.6 iota_compare_fusion
  17.3 1.6 %all-to-all-done = f32[8,2,512]{2,1,0:T(2,128)S(1)} async-done(((f32[8,2,512]{2,1,0:T(2,128)}), f32[8,2,512]{2,1,0:T(2,128)S(1)}, u32[]{:S(2)}, u32[]{:S(2)}) %all-to-all-start) | async-done | bytes 32800 | tf_op jit(solution)/shard_map/all_to_all | solution.py:55
  19.8 1.2 convert_reduce_fusion.1
  21.0 1.1 convolution_convert_fusion
  22.2 2.2 %fusion.62 = (f32[4,136,128]{2,1,0:T(8,128)S(1)}, f32[4,2,136,128]{3,2,1,0:T(8,128)}) fusion(bf16[4,2,256,136]{2,3,1,0:T(8,128)(2,1)} %convolution_convert_fusion, bf16[4,2,256,128]{3,2,1,0:T(8,128)(2,1)S(1)} %bitcast.170), kind=kOutput, calls=%fused_computation.138 | convolution fusion | flops 71372800 | bytes 1916928 | tf_op jit(solution)/shard_map/...jr,...jd->...rd/dot_general | solution.py:61
  24.5 0.8 maximum_maximum_fusion
  25.3 9.2 %all-to-all-start.1 = ((f32[32,24,128]{2,1,0:T(8,128)}), f32[32,24,128]{2,1,0:T(8,128)}, u32[]{:S(2)}, u32[]{:S(2)}) async-start(f32[32,24,128]{2,1,0:T(8,128)} %bitcast.23), calls=%async_computation.1 | async-start | bytes 786432 | tf_op jit(solution)/shard_map/all_to_all | solution.py:41
  35.3 0.7 copy-done.24
  36.3 1.1 convolution_convert_fusion.1
  37.4 0.6 multiply_multiply_fusion.4
  38.0 2.8 %convert_reduce_fusion.2 = (f32[4,2,256]{2,1,0:T(2,128)}, bf16[4,2,256,256]{2,3,1,0:T(8,128)(2,1)}, f32[4,2,256,256]{2,3,1,0:T(8,128)}) fusion(pred[256,256]{0,1:T(8,128)(4,1)S(1)} %copy-done.35, bf16[4,2,256,128]{3,2,1,0:T(8,128)(2,1)S(1)} %bitcast.175, bf16[4,2,256,128]{3,2,1,0:T(8,128)(2,1)S(1)} %bitcast.178), kind=kOutput, calls=%fused_computation.21 | convolution fusion | flops 137885696 | bytes 4268032 | tf_op jit(solution)/shard_map/...id,...jd->...ij/dot_general | solution.py:61
  40.8 4.1 %all-to-all-done.1 = f32[32,24,128]{2,1,0:T(8,128)} async-done(((f32[32,24,128]{2,1,0:T(8,128)}), f32[32,24,128]{2,1,0:T(8,128)}, u32[]{:S(2)}, u32[]{:S(2)}) %all-to-all-start.1) | async-done | bytes 393248 | tf_op jit(solution)/shard_map/all_to_all | solution.py:41
  44.9 1.0 slice.113
  46.2 0.8 pad_add_fusion.4
  47.0 4.4 %all-to-all-start.2 = ((f32[32,24,128]{2,1,0:T(8,128)}), f32[32,24,128]{2,1,0:T(8,128)}, u32[]{:S(2)}, u32[]{:S(2)}) async-start(f32[32,24,128]{2,1,0:T(8,128)} %pad_add_fusion.4), calls=%async_computation.2 | async-start | bytes 786432 | tf_op jit(solution)/shard_map/all_to_all | solution.py:47
  51.4 0.6 multiply_multiply_fusion.5
  52.0 0.9 reduce_sum.134
  52.9 0.6 reduce_window_sum.34
  53.6 2.7 %fusion.65 = f32[4,2,256,128]{2,3,1,0:T(8,128)} fusion(bf16[4,2,256,256]{2,3,1,0:T(8,128)(2,1)} %get-tuple-element.37, bf16[4,2,256,128]{3,2,1,0:T(8,128)(2,1)} %bitcast.171), kind=kOutput, calls=%fused_computation.141 | convolution fusion | flops 134217728 | bytes 2621440 | tf_op jit(solution)/shard_map/...ij,...jd->...id/dot_general | solution.py:61
  56.3 5.3 %all-to-all-done.2 = f32[32,24,128]{2,1,0:T(8,128)} async-done(((f32[32,24,128]{2,1,0:T(8,128)}), f32[32,24,128]{2,1,0:T(8,128)}, u32[]{:S(2)}, u32[]{:S(2)}) %all-to-all-start.2) | async-done | bytes 393248 | tf_op jit(solution)/shard_map/all_to_all | solution.py:47
  61.6 0.8 slice_bitcast_fusion.1
  62.4 1.1 slice.120
  63.5 0.7 add_subtract_fusion.1
  64.3 0.5 fusion.45
  65.3 1.3 %multiply_reduce_fusion = (f32[4,2,256]{2,1,0:T(2,128)S(1)}, f32[4,2,256,128]{2,3,1,0:T(8,128)}) fusion(f32[4,2,256,128]{2,3,1,0:T(8,128)S(1)} %copy-done.21, f32[4,2,256,128]{2,3,1,0:T(8,128)S(1)} %copy-done.23, bf16[4,2,256,128]{2,3,1,0:T(8,128)(2,1)S(1)} %fusion.15, bf16[4,2,256,256]{2,3,1,0:T(8,128)(2,1)S(1)} %bitcast.158), kind=kOutput, calls=%fused_computation.66 | convolution fusion | flops 135002112 | bytes 4726784 | tf_op jit(solution)/shard_map/...ir,...rd->...id/dot_general | solution.py:61
  66.6 1.1 divide_convert_fusion.1
  67.7 0.9 fusion.43
  68.7 1.5 %fusion.63 = (f32[4,136,128]{2,1,0:T(8,128)S(1)}, f32[4,2,136,128]{3,2,1,0:T(8,128)S(1)}) fusion(bf16[4,2,256,136]{2,3,1,0:T(8,128)(2,1)} %convolution_convert_fusion.1, bf16[4,2,256,128]{3,2,1,0:T(8,128)(2,1)} %divide_convert_fusion.1), kind=kOutput, calls=%fused_computation.139 | convolution fusion | flops 71372800 | bytes 1916928 | tf_op jit(solution)/shard_map/...ir,...id->...rd/dot_general | solution.py:61
  70.3 1.6 %maximum_maximum_fusion.1 = f32[4,192,128]{2,1,0:T(8,128)} fusion(f32[4,2,128]{2,1,0:T(2,128)S(1)} %reshape.175, f32[4,136,128]{2,1,0:T(8,128)S(1)} %get-tuple-element.54, f32[192]{0:T(256)} %copy-done.54), kind=kLoop, calls=%fused_computation.71 | loop fusion | flops 196608 | bytes 676608 | tf_op jit(solution)/shard_map/concatenate | solution.py:32
  71.9 3.8 %all-to-all-start.3 = ((f32[32,24,128]{2,1,0:T(8,128)}), f32[32,24,128]{2,1,0:T(8,128)S(1)}, u32[]{:S(2)}, u32[]{:S(2)}) async-start(f32[32,24,128]{2,1,0:T(8,128)} %bitcast.32), calls=%async_computation.3 | async-start | bytes 786432 | tf_op jit(solution)/shard_map/all_to_all | solution.py:41
  75.8 0.8 rev.14
  76.6 2.1 %fusion.64 = f32[4,2,136,128]{3,2,1,0:T(8,128)} fusion(f32[4,2,136,128]{3,2,1,0:T(8,128)} %rev.14), kind=kOutput, calls=%fused_computation.140 | output fusion | flops 139264 | bytes 1114112 | tf_op jit(solution)/shard_map/jit(cumsum)/reduce_window_sum | solution.py:137
  79.3 0.8 fusion.6
  80.1 2.3 %fusion.11 = f32[4,2,256,16]{2,3,1,0:T(8,128)S(1)} fusion(f32[4,2,256,16,16]{2,4,3,1,0:T(8,128)S(1)} %bitcast.168, f32[4,2,256,16]{2,3,1,0:T(8,128)S(1)} %multiply_multiply_fusion.3), kind=kLoop, calls=%fused_computation.18 | loop fusion | flops 1540096 | bytes 2359296 | tf_op jit(solution)/shard_map/reduce_sum | solution.py:89
  82.5 0.9 divide_convert_fusion
  83.4 1.0 fusion.35
  84.9 0.8 all-to-all-done.3
  86.1 0.8 pad_add_fusion
  86.9 6.4 %all-to-all-start.4 = ((f32[32,24,128]{2,1,0:T(8,128)}), f32[32,24,128]{2,1,0:T(8,128)}, u32[]{:S(2)}, u32[]{:S(2)}) async-start(f32[32,24,128]{2,1,0:T(8,128)} %pad_add_fusion), calls=%async_computation.4 | async-start | bytes 786432 | tf_op jit(solution)/shard_map/all_to_all | solution.py:47
  93.3 1.3 %fusion.24 = f32[512]{0:T(512)S(1)} fusion(bf16[512,512]{1,0:T(8,128)(2,1)} %param.11, f32[4,64,8,128]{3,2,1,0:T(8,128)S(1)} %bitcast.162, f32[512]{0:T(512)S(1)} %copy-done.52), kind=kLoop, calls=%fused_computation.53 | loop fusion | flops 1048064 | bytes 1576960 | tf_op jit(solution)/shard_map/reduce_sum | solution.py:283
  95.0 2.0 %copy.117 = bf16[4,2,256,128]{3,2,1,0:T(8,128)(2,1)} copy(bf16[4,2,256,128]{2,3,1,0:T(8,128)(2,1)} %divide_convert_fusion) | data formatting | bytes 1048576 | tf_op jit(solution)/shard_map/convert_element_type | solution.py:260
  97.0 2.0 %copy.118 = bf16[512,4,128]{0,2,1:T(8,128)(2,1)} copy(bf16[512,4,128]{2,0,1:T(8,128)(2,1)} %bitcast.183) | data formatting | bytes 1048576 | tf_op jit(solution)/shard_map/transpose | solution.py:231
  99.0 2.0 %copy.131 = bf16[512,512]{1,0:T(8,128)(2,1)} copy(bf16[512,512]{0,1:T(8,128)(2,1)} %bitcast.184) | data formatting | bytes 1048576
  101.1 2.4 %fusion.66 = f32[4,2,256,128]{3,2,1,0:T(8,128)} fusion(bf16[4,2,256,256]{2,3,1,0:T(8,128)(2,1)S(1)} %copy-done, bf16[4,2,256,128]{3,2,1,0:T(8,128)(2,1)} %divide_convert_fusion.1), kind=kOutput, calls=%fused_computation.142 | convolution fusion | flops 134217728 | bytes 2621440 | tf_op jit(solution)/shard_map/...ij,...id->...jd/dot_general | solution.py:61
  103.6 0.8 slice_bitcast_fusion
  104.4 1.0 slice.127
  105.4 1.3 %subtract_convert_fusion = bf16[4,2,136,128]{3,2,1,0:T(8,128)(2,1)S(1)} fusion(f32[4,2,136,128]{3,2,1,0:T(8,128)} %copy-done.14, f32[4,2,136,128]{3,2,1,0:T(8,128)} %fusion.64, f32[4,136,128]{2,1,0:T(8,128)S(1)} %slice.127), kind=kLoop, calls=%fused_computation.68 | loop fusion | flops 417792 | bytes 1671168 | tf_op jit(solution)/shard_map/convert_element_type | solution.py:116
  107.1 0.5 convolution_add_fusion
  107.9 2.3 %fusion.9 = f32[4,2,256,16]{2,3,1,0:T(8,128)S(1)} fusion(f32[4,2,256,16,16]{2,4,3,1,0:T(8,128)S(1)} %bitcast.169, f32[4,2,256,16]{2,3,1,0:T(8,128)S(1)} %copy-done.28), kind=kLoop, calls=%fused_computation.15 | loop fusion | flops 1540096 | bytes 2359296 | tf_op jit(solution)/shard_map/reduce_sum | solution.py:89
  110.2 1.0 fusion.38
  111.8 0.6 copy-done.2
  112.5 0.6 broadcast_in_dim.19
  113.2 4.2 %all-to-all-start.5 = ((f32[8,2,512]{2,1,0:T(2,128)}), f32[8,2,512]{2,1,0:T(2,128)S(1)}, u32[]{:S(2)}, u32[]{:S(2)}) async-start(f32[8,2,512]{2,1,0:T(2,128)} %broadcast_in_dim.19), calls=%async_computation.5 | async-start | bytes 65536 | tf_op jit(solution)/shard_map/all_to_all | solution.py:55
  117.3 1.9 %fusion.13 = bf16[4,2,256,128]{3,2,1,0:T(8,128)(2,1)S(1)} fusion(f32[4,2,256,128]{3,2,1,0:T(8,128)} %fusion.66, bf16[4,2,256,256]{2,3,1,0:T(8,128)(2,1)S(1)} %bitcast.161, bf16[4,2,256,128]{2,3,1,0:T(8,128)(2,1)} %copy-done.18), kind=kOutput, calls=%fused_computation.40 | convolution fusion | flops 134742016 | bytes 3145728 | tf_op jit(solution)/shard_map/...jr,...rd->...jd/dot_general | solution.py:61
  119.3 0.9 copy.181
  120.1 4.2 %all-to-all-done.5 = f32[8,2,512]{2,1,0:T(2,128)S(1)} async-done(((f32[8,2,512]{2,1,0:T(2,128)}), f32[8,2,512]{2,1,0:T(2,128)S(1)}, u32[]{:S(2)}, u32[]{:S(2)}) %all-to-all-start.5) | async-done | bytes 32800 | tf_op jit(solution)/shard_map/all_to_all | solution.py:55
  124.4 2.2 %fusion.32 = bf16[512,512]{1,0:T(8,128)(2,1)} fusion(bf16[512,512]{1,0:T(8,128)(2,1)} %param.12, f32[4,64,8,128]{3,2,1,0:T(8,128)S(1)} %bitcast.165, f32[512]{0:T(512)S(1)} %bitcast.202, f32[512]{0:T(512)S(1)} %copy-done.55, f32[512]{0:T(512)S(1)} %copy-done.50, f32[512]{0:T(512)S(1)} %bitcast.196), kind=kLoop, calls=%fused_computation.61 | loop fusion | flops 2097152 | bytes 2105344 | tf_op jit(solution)/shard_map/convert_element_type | solution.py:205
  126.5 1.1 fusion.22
  (173 shorter events, 6.5 us)
Async XLA Ops:
  0.6 11.4 %copy-start.53 = (s32[2,128,16]{1,2,0:T(8,128)S(1)}, s32[2,128,16]{1,2,0:T(8,128)}, u32[]{:S(2)}) copy-start(s32[2,128,16]{1,2,0:T(8,128)} %param.17) | copy-start | bytes 49156
  0.6 11.4 %copy-start.29 = (bf16[512,512]{1,0:T(8,128)(2,1)S(1)}, bf16[512,512]{1,0:T(8,128)(2,1)}, u32[]{:S(2)}) copy-start(bf16[512,512]{1,0:T(8,128)(2,1)} %param.13) | copy-start | bytes 1572868
  2.2 10.1 %copy-start.30 = (bf16[512,512]{1,0:T(8,128)(2,1)S(1)}, bf16[512,512]{1,0:T(8,128)(2,1)}, u32[]{:S(2)}) copy-start(bf16[512,512]{1,0:T(8,128)(2,1)} %param.14) | copy-start | bytes 1572868
  3.1 15.9 %all-to-all-start = ((f32[8,2,512]{2,1,0:T(2,128)}), f32[8,2,512]{2,1,0:T(2,128)S(1)}, u32[]{:S(2)}, u32[]{:S(2)}) async-start(f32[8,2,512]{2,1,0:T(2,128)} %broadcast_in_dim.16), calls=%async_computation | async-start | bytes 65536 | tf_op jit(solution)/shard_map/all_to_all | solution.py:55
  12.3 9.9 %copy-start.5 = (bf16[4,512,128]{2,1,0:T(8,128)(2,1)}, bf16[4,512,128]{2,1,0:T(8,128)(2,1)S(1)}, u32[]{:S(2)}) copy-start(bf16[4,512,128]{2,1,0:T(8,128)(2,1)S(1)} %copy.112) | copy-start | bytes 1572868
  13.7 5.3 %copy-start.1 = (bf16[512,512]{1,0:T(8,128)(2,1)S(1)}, bf16[512,512]{1,0:T(8,128)(2,1)}, u32[]{:S(2)}) copy-start(bf16[512,512]{1,0:T(8,128)(2,1)} %param.12) | copy-start | bytes 1572868
  13.7 5.3 %copy-start.49 = (f32[512]{0:T(512)S(1)}, f32[512]{0:T(512)}, u32[]{:S(2)}) copy-start(f32[512]{0:T(512)} %param.16) | copy-start | bytes 6148
  16.7 7.8 %copy-start.54 = (f32[192]{0:T(256)}, f32[192]{0:T(256)S(1)}, u32[]{:S(2)}) copy-start(f32[192]{0:T(256)S(1)} %pad.69.clone) | copy-start | bytes 2308
  19.0 18.4 %copy-start.47 = (f32[1,512]{1,0:T(1,128)}, f32[1,512]{1,0:T(1,128)S(1)}, u32[]{:S(2)}) copy-start(f32[1,512]{1,0:T(1,128)S(1)} %get-tuple-element.47) | copy-start | bytes 6148
  19.0 32.4 %copy-start.45 = (f32[1,512]{1,0:T(1,128)}, f32[1,512]{1,0:T(1,128)S(1)}, u32[]{:S(2)}) copy-start(f32[1,512]{1,0:T(1,128)S(1)} %get-tuple-element.48) | copy-start | bytes 6148
  19.2 1.8 %copy-start.31 = (bf16[256,136,1,1]{0,1,3,2:T(8,128)(2,1)S(1)}, bf16[256,136,1,1]{0,1,3,2:T(8,128)(2,1)}, u32[]{:S(2)}) copy-start(bf16[256,136,1,1]{0,1,3,2:T(8,128)(2,1)} %constant.67) | copy-start | bytes 208900
  19.4 1.5 %copy-start.11 = (bf16[4,512,128]{2,1,0:T(8,128)(2,1)}, bf16[4,512,128]{2,1,0:T(8,128)(2,1)S(1)}, u32[]{:S(2)}) copy-start(bf16[4,512,128]{2,1,0:T(8,128)(2,1)S(1)} %copy.110) | copy-start | bytes 1572868
  19.8 2.4 %copy-start.27 = (f32[4,2,256,16]{2,3,1,0:T(8,128)}, f32[4,2,256,16]{2,3,1,0:T(8,128)S(1)}, u32[]{:S(2)}) copy-start(f32[4,2,256,16]{2,3,1,0:T(8,128)S(1)} %multiply_multiply_fusion.2) | copy-start | bytes 393220
  22.1 12.4 %copy-start.3 = (bf16[512,512]{1,0:T(8,128)(2,1)S(1)}, bf16[512,512]{1,0:T(8,128)(2,1)}, u32[]{:S(2)}) copy-start(bf16[512,512]{1,0:T(8,128)(2,1)} %param.11) | copy-start | bytes 1572868
  22.1 12.4 %copy-start.51 = (f32[512]{0:T(512)S(1)}, f32[512]{0:T(512)}, u32[]{:S(2)}) copy-start(f32[512]{0:T(512)} %param.15) | copy-start | bytes 6148
  25.3 19.6 %all-to-all-start.1 = ((f32[32,24,128]{2,1,0:T(8,128)}), f32[32,24,128]{2,1,0:T(8,128)}, u32[]{:S(2)}, u32[]{:S(2)}) async-start(f32[32,24,128]{2,1,0:T(8,128)} %bitcast.23), calls=%async_computation.1 | async-start | bytes 786432 | tf_op jit(solution)/shard_map/all_to_all | solution.py:41
  34.9 1.4 %copy-start.32 = (bf16[256,136,1,1]{0,1,3,2:T(8,128)(2,1)S(1)}, bf16[256,136,1,1]{0,1,3,2:T(8,128)(2,1)}, u32[]{:S(2)}) copy-start(bf16[256,136,1,1]{0,1,3,2:T(8,128)(2,1)} %constant.67) | copy-start | bytes 208900
  35.0 3.0 %copy-start.9 = (bf16[4,512,128]{2,1,0:T(8,128)(2,1)}, bf16[4,512,128]{2,1,0:T(8,128)(2,1)S(1)}, u32[]{:S(2)}) copy-start(bf16[4,512,128]{2,1,0:T(8,128)(2,1)S(1)} %copy.106) | copy-start | bytes 1572868
  35.0 3.0 %copy-start.12 = (bf16[4,512,128]{2,1,0:T(8,128)(2,1)S(1)}, bf16[4,512,128]{2,1,0:T(8,128)(2,1)}, u32[]{:S(2)}) copy-start(bf16[4,512,128]{2,1,0:T(8,128)(2,1)} %copy-done.11) | copy-start | bytes 1572868
  35.0 3.0 %copy-start.35 = (pred[256,256]{0,1:T(8,128)(4,1)S(1)}, pred[256,256]{0,1:T(8,128)(4,1)}, u32[]{:S(2)}) copy-start(pred[256,256]{0,1:T(8,128)(4,1)} %iota_compare_fusion) | copy-start | bytes 196612
  35.3 0.7 copy-start.24
  47.0 14.6 %all-to-all-start.2 = ((f32[32,24,128]{2,1,0:T(8,128)}), f32[32,24,128]{2,1,0:T(8,128)}, u32[]{:S(2)}, u32[]{:S(2)}) async-start(f32[32,24,128]{2,1,0:T(8,128)} %pad_add_fusion.4), calls=%async_computation.2 | async-start | bytes 786432 | tf_op jit(solution)/shard_map/all_to_all | solution.py:47
  52.9 10.6 %copy-start.43 = (f32[4,2,256]{2,1,0:T(2,128)}, f32[4,2,256]{2,1,0:T(2,128)S(1)}, u32[]{:S(2)}) copy-start(f32[4,2,256]{2,1,0:T(2,128)S(1)} %reduce_sum.134) | copy-start | bytes 24580
  61.6 3.2 %copy-start.15 = (f32[4,2,136,128]{3,2,1,0:T(8,128)S(1)}, f32[4,2,136,128]{3,2,1,0:T(8,128)}, u32[]{:S(2)}) copy-start(f32[4,2,136,128]{3,2,1,0:T(8,128)} %get-tuple-element.51) | copy-start | bytes 1671172
  61.6 3.3 %copy-start.33 = (bf16[256,136,1,1]{0,1,3,2:T(8,128)(2,1)S(1)}, bf16[256,136,1,1]{0,1,3,2:T(8,128)(2,1)}, u32[]{:S(2)}) copy-start(bf16[256,136,1,1]{0,1,3,2:T(8,128)(2,1)} %constant.68) | copy-start | bytes 208900
  62.4 2.9 %copy-start.21 = (f32[4,2,256,128]{2,3,1,0:T(8,128)S(1)}, f32[4,2,256,128]{2,3,1,0:T(8,128)}, u32[]{:S(2)}) copy-start(f32[4,2,256,128]{2,3,1,0:T(8,128)} %copy.116) | copy-start | bytes 3145732
  62.4 2.9 %copy-start.23 = (f32[4,2,256,128]{2,3,1,0:T(8,128)S(1)}, f32[4,2,256,128]{2,3,1,0:T(8,128)}, u32[]{:S(2)}) copy-start(f32[4,2,256,128]{2,3,1,0:T(8,128)} %fusion.65) | copy-start | bytes 3145732
  64.3 2.3 %copy-start.37 = (f32[4,2,256]{2,1,0:T(2,128)}, f32[4,2,256]{2,1,0:T(2,128)S(1)}, u32[]{:S(2)}) copy-start(f32[4,2,256]{2,1,0:T(2,128)S(1)} %add_subtract_fusion.1) | copy-start | bytes 24580
  65.3 1.3 %copy-start.16 = (bf16[4,2,256,128]{2,3,1,0:T(8,128)(2,1)}, bf16[4,2,256,128]{2,3,1,0:T(8,128)(2,1)S(1)}, u32[]{:S(2)}) copy-start(bf16[4,2,256,128]{2,3,1,0:T(8,128)(2,1)S(1)} %fusion.15) | copy-start | bytes 1572868
  65.3 1.3 %copy-start.44 = (f32[4,2,256]{2,1,0:T(2,128)S(1)}, f32[4,2,256]{2,1,0:T(2,128)}, u32[]{:S(2)}) copy-start(f32[4,2,256]{2,1,0:T(2,128)} %get-tuple-element.36) | copy-start | bytes 24580
  66.6 1.2 copy-start.39
  66.6 2.1 %copy-start.41 = (f32[4,2,256]{2,1,0:T(2,128)}, f32[4,2,256]{2,1,0:T(2,128)S(1)}, u32[]{:S(2)}) copy-start(f32[4,2,256]{2,1,0:T(2,128)S(1)} %get-tuple-element.15) | copy-start | bytes 24580
  70.2 9.0 %copy-start.14 = (f32[4,2,136,128]{3,2,1,0:T(8,128)}, f32[4,2,136,128]{3,2,1,0:T(8,128)S(1)}, u32[]{:S(2)}) copy-start(f32[4,2,136,128]{3,2,1,0:T(8,128)S(1)} %get-tuple-element.55) | copy-start | bytes 1671172
  70.3 8.4 %copy-start.8 = (bf16[4,2,256,128]{3,2,1,0:T(8,128)(2,1)S(1)}, bf16[4,2,256,128]{3,2,1,0:T(8,128)(2,1)}, u32[]{:S(2)}) copy-start(bf16[4,2,256,128]{3,2,1,0:T(8,128)(2,1)} %divide_convert_fusion.1) | copy-start | bytes 1572868
  70.3 8.4 %copy-start.17 = (bf16[4,2,256,128]{2,3,1,0:T(8,128)(2,1)S(1)}, bf16[4,2,256,128]{2,3,1,0:T(8,128)(2,1)}, u32[]{:S(2)}) copy-start(bf16[4,2,256,128]{2,3,1,0:T(8,128)(2,1)} %copy-done.16) | copy-start | bytes 1572868
  70.3 8.4 %copy-start.38 = (f32[4,2,256]{2,1,0:T(2,128)S(1)}, f32[4,2,256]{2,1,0:T(2,128)}, u32[]{:S(2)}) copy-start(f32[4,2,256]{2,1,0:T(2,128)} %copy-done.37) | copy-start | bytes 24580
  70.3 8.4 %copy-start.42 = (f32[4,2,256]{2,1,0:T(2,128)S(1)}, f32[4,2,256]{2,1,0:T(2,128)}, u32[]{:S(2)}) copy-start(f32[4,2,256]{2,1,0:T(2,128)} %copy-done.41) | copy-start | bytes 24580
  71.9 13.9 %all-to-all-start.3 = ((f32[32,24,128]{2,1,0:T(8,128)}), f32[32,24,128]{2,1,0:T(8,128)S(1)}, u32[]{:S(2)}, u32[]{:S(2)}) async-start(f32[32,24,128]{2,1,0:T(8,128)} %bitcast.32), calls=%async_computation.3 | async-start | bytes 786432 | tf_op jit(solution)/shard_map/all_to_all | solution.py:41
  76.6 2.6 %copy-start.6 = (bf16[4,512,128]{2,1,0:T(8,128)(2,1)S(1)}, bf16[4,512,128]{2,1,0:T(8,128)(2,1)}, u32[]{:S(2)}) copy-start(bf16[4,512,128]{2,1,0:T(8,128)(2,1)} %copy-done.5) | copy-start | bytes 1572868
  76.6 2.6 %copy-start.26 = (f32[4,2,256,256]{2,3,1,0:T(8,128)S(1)}, f32[4,2,256,256]{2,3,1,0:T(8,128)}, u32[]{:S(2)}) copy-start(f32[4,2,256,256]{2,3,1,0:T(8,128)} %get-tuple-element.49) | copy-start | bytes 6291460
  76.6 2.6 %copy-start.36 = (pred[256,256]{0,1:T(8,128)(4,1)S(1)}, pred[256,256]{0,1:T(8,128)(4,1)}, u32[]{:S(2)}) copy-start(pred[256,256]{0,1:T(8,128)(4,1)} %iota_compare_fusion) | copy-start | bytes 196612
  80.1 4.4 %copy-start.19 = (bf16[4,2,256,256]{2,3,1,0:T(8,128)(2,1)}, bf16[4,2,256,256]{2,3,1,0:T(8,128)(2,1)S(1)}, u32[]{:S(2)}) copy-start(bf16[4,2,256,256]{2,3,1,0:T(8,128)(2,1)S(1)} %fusion.6) | copy-start | bytes 3145732
  80.1 2.4 %copy-start.25 = (f32[4,2,256,32]{2,3,1,0:T(8,128)S(1)}, f32[4,2,256,32]{2,3,1,0:T(8,128)}, u32[]{:S(2)}) copy-start(f32[4,2,256,32]{2,3,1,0:T(8,128)} %copy-done.24) | copy-start | bytes 786436
  80.1 2.4 %copy-start.22 = (f32[4,2,256,128]{2,3,1,0:T(8,128)S(1)}, f32[4,2,256,128]{2,3,1,0:T(8,128)}, u32[]{:S(2)}) copy-start(f32[4,2,256,128]{2,3,1,0:T(8,128)} %get-tuple-element.12) | copy-start | bytes 3145732
  80.1 2.4 %copy-start.40 = (f32[4,2,256]{2,1,0:T(2,128)S(1)}, f32[4,2,256]{2,1,0:T(2,128)}, u32[]{:S(2)}) copy-start(f32[4,2,256]{2,1,0:T(2,128)} %copy-done.39) | copy-start | bytes 24580
  82.4 2.0 %copy-start.13 = (bf16[4,512,128]{2,1,0:T(8,128)(2,1)S(1)}, bf16[4,512,128]{2,1,0:T(8,128)(2,1)}, u32[]{:S(2)}) copy-start(bf16[4,512,128]{2,1,0:T(8,128)(2,1)} %copy-done.11) | copy-start | bytes 1572868
  86.0 7.3 %copy-start.52 = (f32[512]{0:T(512)S(1)}, f32[512]{0:T(512)}, u32[]{:S(2)}) copy-start(f32[512]{0:T(512)} %param.15) | copy-start | bytes 6148
  86.9 16.7 %all-to-all-start.4 = ((f32[32,24,128]{2,1,0:T(8,128)}), f32[32,24,128]{2,1,0:T(8,128)}, u32[]{:S(2)}, u32[]{:S(2)}) async-start(f32[32,24,128]{2,1,0:T(8,128)} %pad_add_fusion), calls=%async_computation.4 | async-start | bytes 786432 | tf_op jit(solution)/shard_map/all_to_all | solution.py:47
  93.3 7.8 %copy-start = (bf16[4,2,256,256]{2,3,1,0:T(8,128)(2,1)S(1)}, bf16[4,2,256,256]{2,3,1,0:T(8,128)(2,1)}, u32[]{:S(2)}) copy-start(bf16[4,2,256,256]{2,3,1,0:T(8,128)(2,1)} %get-tuple-element.37) | copy-start | bytes 3145732
  101.1 5.6 %copy-start.34 = (bf16[256,136,1,1]{0,1,3,2:T(8,128)(2,1)S(1)}, bf16[256,136,1,1]{0,1,3,2:T(8,128)(2,1)}, u32[]{:S(2)}) copy-start(bf16[256,136,1,1]{0,1,3,2:T(8,128)(2,1)} %constant.68) | copy-start | bytes 208900
  103.5 3.6 %copy-start.7 = (bf16[4,512,128]{2,1,0:T(8,128)(2,1)S(1)}, bf16[4,512,128]{2,1,0:T(8,128)(2,1)}, u32[]{:S(2)}) copy-start(bf16[4,512,128]{2,1,0:T(8,128)(2,1)} %copy-done.5) | copy-start | bytes 1572868
  106.7 1.2 copy-start.28
  107.1 0.8 copy-start.18
  107.9 3.4 %copy-start.10 = (bf16[4,512,128]{2,1,0:T(8,128)(2,1)S(1)}, bf16[4,512,128]{2,1,0:T(8,128)(2,1)}, u32[]{:S(2)}) copy-start(bf16[4,512,128]{2,1,0:T(8,128)(2,1)} %copy-done.9) | copy-start | bytes 1572868
  107.9 3.4 %copy-start.20 = (bf16[4,2,256,256]{2,3,1,0:T(8,128)(2,1)S(1)}, bf16[4,2,256,256]{2,3,1,0:T(8,128)(2,1)}, u32[]{:S(2)}) copy-start(bf16[4,2,256,256]{2,3,1,0:T(8,128)(2,1)} %copy-done.19) | copy-start | bytes 3145732
  111.3 1.0 copy-start.2
  111.3 1.0 copy-start.50
  113.2 11.1 %all-to-all-start.5 = ((f32[8,2,512]{2,1,0:T(2,128)}), f32[8,2,512]{2,1,0:T(2,128)S(1)}, u32[]{:S(2)}, u32[]{:S(2)}) async-start(f32[8,2,512]{2,1,0:T(2,128)} %broadcast_in_dim.19), calls=%async_computation.5 | async-start | bytes 65536 | tf_op jit(solution)/shard_map/all_to_all | solution.py:55
  117.3 7.0 %copy-start.48 = (f32[1,512]{1,0:T(1,128)S(1)}, f32[1,512]{1,0:T(1,128)}, u32[]{:S(2)}) copy-start(f32[1,512]{1,0:T(1,128)} %copy-done.47) | copy-start | bytes 6148
  117.3 7.0 %copy-start.55 = (f32[512]{0:T(512)S(1)}, f32[512]{0:T(512)}, u32[]{:S(2)}) copy-start(f32[512]{0:T(512)} %multiply_multiply_fusion.4) | copy-start | bytes 6148
  119.2 7.3 %copy-start.4 = (bf16[512,512]{1,0:T(8,128)(2,1)S(1)}, bf16[512,512]{1,0:T(8,128)(2,1)}, u32[]{:S(2)}) copy-start(bf16[512,512]{1,0:T(8,128)(2,1)} %param.11) | copy-start | bytes 1572868
  119.2 7.3 %copy-start.46 = (f32[1,512]{1,0:T(1,128)S(1)}, f32[1,512]{1,0:T(1,128)}, u32[]{:S(2)}) copy-start(f32[1,512]{1,0:T(1,128)} %copy-done.45) | copy-start | bytes 6148
  119.3 7.3 %copy-start.56 = (f32[512]{0:T(512)S(1)}, f32[512]{0:T(512)}, u32[]{:S(2)}) copy-start(f32[512]{0:T(512)} %multiply_multiply_fusion.5) | copy-start | bytes 6148

commit v14 on v13

--- a/solution.py
+++ b/solution.py
@@ -278,11 +278,11 @@
     kn_grad = join_heads(
         k_diag + sketch_back(kf_grad, k_parts[1], k_parts[2], k_parts[3], sign_pair)
     )
+    dots = jnp.sum(
+        jnp.stack([q_float * q_gain * qn_grad, k_float * k_gain * kn_grad]), axis=-1
+    )
     (q_dot, k_dot), (v_diag, later_state) = head_sum(
-        (
-            jnp.sum(q_float * q_gain * qn_grad, axis=-1),
-            jnp.sum(k_float * k_gain * kn_grad, axis=-1),
-        ),
+        (dots[0], dots[1]),
         "head",
         (v_diag, later_state),
     )

time: 129 us -> 137 us (1.062)
  matrix products: 24.6 us -> 29.2 us
  local copies, waits for them, and re-layouts: 20.8 us -> 24 us
  starting transfers between devices: 37 us -> 39.3 us
  waiting for transfers between devices: 16.1 us -> 14.2 us
    dot_general x18, matrix products: 21.1 us -> 24.8 us  [product_of(): return jnp.einsum(spec, lhs, rhs, preferred_element_type=jnp.float32)]
    all_to_all x2, waiting for transfers between devices: 4.93 us -> 2.27 us  [carried_in(): mine = lax.all_to_all(stacked, axis, 0, 0, tiled=True)]
    all_to_all x2, starting transfers between devices: 10.8 us -> 12.3 us  [carried_in(): lax.all_to_all(shifted, axis, 0, 0, tiled=True)]
    unnamed x120 -> x116, local copies, waits for them, and re-layouts: 5.57 us -> 6.8 us
  transfers between devices with their start and end apart: 6 -> 6, of which waited for: 6 -> 5; matrix products, arithmetic and copies ran while one was open for 29% -> 31% of each run, Pallas kernels for 0% -> 0%
where the time goes in v14:
time: 137 us; the launch traced here: 136 us
  starting transfers between devices  39.3 us (29%)
  matrix products  29.2 us (21%)
  other arithmetic  27.8 us (20%)
  local copies, waits for them, and re-layouts  24 us (18%)
  waiting for transfers between devices  14.2 us (10%)
  between operations  1.54 us (1%)
    dot_general x18, matrix products, product_of(): return jnp.einsum(spec, lhs, rhs, preferred_element_type=jnp.float32)  24.8 us
    all_to_all x2, starting transfers between devices, carried_in(): mine = lax.all_to_all(stacked, axis, 0, 0, tiled=True)  13.8 us
    all_to_all x2, starting transfers between devices, head_sum(): gathered = lax.all_to_all(spread, axis, 0, 0, tiled=True)  13.2 us
    all_to_all x2, starting transfers between devices, carried_in(): lax.all_to_all(shifted, axis, 0, 0, tiled=True)  12.3 us
    unnamed x116, local copies, waits for them, and re-layouts  6.8 us
    all_to_all x2, waiting for transfers between devices, carried_in(): lax.all_to_all(shifted, axis, 0, 0, tiled=True)  6.35 us
    all_to_all x2, waiting for transfers between devices, head_sum(): gathered = lax.all_to_all(spread, axis, 0, 0, tiled=True)  5.59 us
    reduce_sum x2, other arithmetic, sketch_back(): sketch_grad = jnp.sum(symmetric * sketched[..., None, :], axis=-1)  4.64 us
  transfers between devices with their start and end apart: 6, of which 5 were waited for; matrix products, arithmetic and copies ran while one was open for 31% of the time, Pallas kernels for 0%

profile of v14, /device:TPU:1, one launch (start us, length us, event | category | flops | bytes accessed | tf_op | source)
XLA Modules:
  0.0 136.0 jit_solution(10366299682314295180)
XLA Ops:
  0.7 1.4 %convert_bitcast_fusion = (f32[1,512,512]{2,1,0:T(8,128)S(1)}, f32[1,512,512]{2,1,0:T(8,128)S(1)}) fusion(bf16[512,512]{1,0:T(8,128)(2,1)} %param.12, bf16[512,512]{1,0:T(8,128)(2,1)} %param.11), kind=kLoop, calls=%fused_computation.27 | loop fusion | flops 524288 | bytes 3145728 | tf_op jit(solution)/shard_map/stack | solution.py:215
  2.3 0.6 broadcast_in_dim.16
  2.9 9.0 %all-to-all-start = ((f32[8,2,512]{2,1,0:T(2,128)}), f32[8,2,512]{2,1,0:T(2,128)S(1)}, u32[]{:S(2)}, u32[]{:S(2)}) async-start(f32[8,2,512]{2,1,0:T(2,128)} %broadcast_in_dim.16), calls=%async_computation | async-start | bytes 65536 | tf_op jit(solution)/shard_map/all_to_all | solution.py:55
  12.4 1.1 convert_bitcast_fusion.2
  13.6 1.6 %copy.109 = f32[4,512,128]{2,1,0:T(8,128)S(1)} copy(f32[4,512,128]{1,2,0:T(8,128)} %convert_bitcast_fusion.2) | data formatting | bytes 2097152 | tf_op jit(solution)/shard_map/convert_element_type | solution.py:156
  15.2 1.3 copy.116
  16.6 0.6 iota_compare_fusion
  17.2 1.6 %all-to-all-done = f32[8,2,512]{2,1,0:T(2,128)S(1)} async-done(((f32[8,2,512]{2,1,0:T(2,128)}), f32[8,2,512]{2,1,0:T(2,128)S(1)}, u32[]{:S(2)}, u32[]{:S(2)}) %all-to-all-start) | async-done | bytes 32800 | tf_op jit(solution)/shard_map/all_to_all | solution.py:55
  20.1 1.2 convert_reduce_fusion.1
  21.3 1.2 convolution_convert_fusion
  22.6 2.2 %fusion.62 = (f32[4,136,128]{2,1,0:T(8,128)S(1)}, f32[4,2,136,128]{3,2,1,0:T(8,128)}) fusion(bf16[4,2,256,136]{2,3,1,0:T(8,128)(2,1)} %convolution_convert_fusion, bf16[4,2,256,128]{3,2,1,0:T(8,128)(2,1)S(1)} %bitcast.172), kind=kOutput, calls=%fused_computation.138 | convolution fusion | flops 71372800 | bytes 1916928 | tf_op jit(solution)/shard_map/...jr,...jd->...rd/dot_general | solution.py:61
  24.8 0.8 maximum_maximum_fusion
  25.7 9.2 %all-to-all-start.1 = ((f32[32,24,128]{2,1,0:T(8,128)}), f32[32,24,128]{2,1,0:T(8,128)}, u32[]{:S(2)}, u32[]{:S(2)}) async-start(f32[32,24,128]{2,1,0:T(8,128)} %bitcast.23), calls=%async_computation.1 | async-start | bytes 786432 | tf_op jit(solution)/shard_map/all_to_all | solution.py:41
  35.0 1.0 fusion.18
  35.9 1.2 reshape.166
  37.5 0.7 copy-done.23
  38.5 1.1 convolution_convert_fusion.1
  40.2 2.8 %convert_reduce_fusion.2 = (f32[4,2,256]{2,1,0:T(2,128)}, bf16[4,2,256,256]{2,3,1,0:T(8,128)(2,1)}, f32[4,2,256,256]{2,3,1,0:T(8,128)}) fusion(pred[256,256]{0,1:T(8,128)(4,1)S(1)} %copy-done.34, bf16[4,2,256,128]{3,2,1,0:T(8,128)(2,1)S(1)} %bitcast.177, bf16[4,2,256,128]{3,2,1,0:T(8,128)(2,1)S(1)} %bitcast.180), kind=kOutput, calls=%fused_computation.22 | convolution fusion | flops 137885696 | bytes 4268032 | tf_op jit(solution)/shard_map/...id,...jd->...ij/dot_general | solution.py:61
  43.0 2.3 %all-to-all-done.1 = f32[32,24,128]{2,1,0:T(8,128)} async-done(((f32[32,24,128]{2,1,0:T(8,128)}), f32[32,24,128]{2,1,0:T(8,128)}, u32[]{:S(2)}, u32[]{:S(2)}) %all-to-all-start.1) | async-done | bytes 393248 | tf_op jit(solution)/shard_map/all_to_all | solution.py:41
  45.3 1.0 slice.116
  46.6 0.8 pad_add_fusion.4
  47.4 5.2 %all-to-all-start.2 = ((f32[32,24,128]{2,1,0:T(8,128)}), f32[32,24,128]{2,1,0:T(8,128)}, u32[]{:S(2)}, u32[]{:S(2)}) async-start(f32[32,24,128]{2,1,0:T(8,128)} %pad_add_fusion.4), calls=%async_computation.2 | async-start | bytes 786432 | tf_op jit(solution)/shard_map/all_to_all | solution.py:47
  53.1 0.9 reduce_sum.125
  54.1 0.6 reduce_window_sum.34
  54.7 2.7 %fusion.65 = f32[4,2,256,128]{2,3,1,0:T(8,128)} fusion(bf16[4,2,256,256]{2,3,1,0:T(8,128)(2,1)} %get-tuple-element.37, bf16[4,2,256,128]{3,2,1,0:T(8,128)(2,1)} %bitcast.173), kind=kOutput, calls=%fused_computation.141 | convolution fusion | flops 134217728 | bytes 2621440 | tf_op jit(solution)/shard_map/...ij,...jd->...id/dot_general | solution.py:61
  57.4 5.5 %all-to-all-done.2 = f32[32,24,128]{2,1,0:T(8,128)} async-done(((f32[32,24,128]{2,1,0:T(8,128)}), f32[32,24,128]{2,1,0:T(8,128)}, u32[]{:S(2)}, u32[]{:S(2)}) %all-to-all-start.2) | async-done | bytes 393248 | tf_op jit(solution)/shard_map/all_to_all | solution.py:47
  62.9 0.8 slice_bitcast_fusion.1
  63.7 1.1 slice.123
  64.9 0.7 add_subtract_fusion.1
  66.6 1.3 multiply_reduce_fusion
  68.0 1.1 divide_convert_fusion.1
  69.1 0.9 fusion.43
  70.1 2.4 %fusion.63 = (f32[4,136,128]{2,1,0:T(8,128)S(1)}, f32[4,2,136,128]{3,2,1,0:T(8,128)}) fusion(bf16[4,2,256,136]{2,3,1,0:T(8,128)(2,1)} %convolution_convert_fusion.1, bf16[4,2,256,128]{3,2,1,0:T(8,128)(2,1)} %divide_convert_fusion.1), kind=kOutput, calls=%fused_computation.139 | convolution fusion | flops 71372800 | bytes 1916928 | tf_op jit(solution)/shard_map/...ir,...id->...rd/dot_general | solution.py:61
  72.5 1.5 %maximum_maximum_fusion.1 = f32[4,192,128]{2,1,0:T(8,128)} fusion(f32[4,2,128]{2,1,0:T(2,128)S(1)} %reshape.175, f32[4,136,128]{2,1,0:T(8,128)S(1)} %get-tuple-element.54, f32[192]{0:T(256)} %copy-done.52), kind=kLoop, calls=%fused_computation.72 | loop fusion | flops 196608 | bytes 676608 | tf_op jit(solution)/shard_map/concatenate | solution.py:32
  74.0 4.6 %all-to-all-start.3 = ((f32[32,24,128]{2,1,0:T(8,128)}), f32[32,24,128]{2,1,0:T(8,128)}, u32[]{:S(2)}, u32[]{:S(2)}) async-start(f32[32,24,128]{2,1,0:T(8,128)} %bitcast.32), calls=%async_computation.3 | async-start | bytes 786432 | tf_op jit(solution)/shard_map/all_to_all | solution.py:41
  78.5 1.4 %fusion.66 = f32[4,2,256,128]{3,2,1,0:T(8,128)} fusion(bf16[4,2,256,256]{2,3,1,0:T(8,128)(2,1)S(1)} %copy-done, bf16[4,2,256,128]{3,2,1,0:T(8,128)(2,1)S(1)} %copy-done.3), kind=kOutput, calls=%fused_computation.142 | convolution fusion | flops 134217728 | bytes 2621440 | tf_op jit(solution)/shard_map/...ij,...id->...jd/dot_general | solution.py:61
  80.0 1.7 %multiply_add_fusion = f32[4,2,256,256]{2,3,1,0:T(8,128)S(1)} fusion(bf16[4,2,256,128]{3,2,1,0:T(8,128)(2,1)S(1)} %copy-done.3, bf16[4,2,256,128]{2,3,1,0:T(8,128)(2,1)} %copy-done.16, f32[4,2,256]{2,1,0:T(2,128)} %copy-done.36, f32[4,2,256]{2,1,0:T(2,128)} %copy-done.39), kind=kOutput, calls=%fused_computation.20 | convolution fusion | flops 135266304 | bytes 3162112 | tf_op jit(solution)/shard_map/...id,...rd->...ir/dot_general | solution.py:61
  81.9 1.8 %fusion.6 = bf16[4,2,256,256]{2,3,1,0:T(8,128)(2,1)} fusion(f32[4,2,256,256]{2,3,1,0:T(8,128)S(1)} %copy-done.25, bf16[4,2,256,128]{3,2,1,0:T(8,128)(2,1)S(1)} %copy-done.3, bf16[4,2,256,128]{3,2,1,0:T(8,128)(2,1)S(1)} %bitcast.174, f32[4,2,256]{2,1,0:T(2,128)S(1)} %copy-done.40, pred[256,256]{0,1:T(8,128)(4,1)S(1)} %copy-done.35), kind=kOutput, calls=%fused_computation.10 | convolution fusion | flops 138936320 | bytes 4268032 | tf_op jit(solution)/shard_map/...id,...jd->...ij/dot_general | solution.py:61
  83.7 2.3 %fusion.11 = f32[4,2,256,16]{2,3,1,0:T(8,128)S(1)} fusion(f32[4,2,256,16,16]{2,4,3,1,0:T(8,128)S(1)} %bitcast.170, f32[4,2,256,16]{2,3,1,0:T(8,128)S(1)} %multiply_multiply_fusion.3), kind=kLoop, calls=%fused_computation.19 | loop fusion | flops 1540096 | bytes 2359296 | tf_op jit(solution)/shard_map/reduce_sum | solution.py:89
  86.1 0.9 divide_convert_fusion
  87.0 2.0 %fusion.35 = f32[4,2,256,128]{3,2,1,0:T(8,128)} fusion(f32[4,2,256,16]{2,3,1,0:T(8,128)S(1)} %get-tuple-element.41, f32[4,2,256,16]{2,3,1,0:T(8,128)S(1)} %get-tuple-element.40, bf16[128,16]{0,1:T(8,128)(2,1)S(1)} %get-tuple-element.44, bf16[128,16]{0,1:T(8,128)(2,1)S(1)} %get-tuple-element.43), kind=kOutput, calls=%fused_computation.88 | convolution fusion | flops 100810752 | bytes 1318912 | tf_op jit(solution)/shard_map/...r,dr->...d/dot_general | solution.py:65
  89.0 0.9 rev.14
  89.8 2.0 %convolution_add_fusion.4 = f32[4,2,256,128]{3,2,1,0:T(8,128)S(1)} fusion(f32[4,2,256,128]{3,2,1,0:T(8,128)} %fusion.35, bf16[4,2,256,256]{2,3,1,0:T(8,128)(2,1)} %fusion.6, bf16[4,2,256,128]{3,2,1,0:T(8,128)(2,1)S(1)} %bitcast.181), kind=kOutput, calls=%fused_computation.36 | convolution fusion | flops 134479872 | bytes 3670016 | tf_op jit(solution)/shard_map/...ij,...jd->...id/dot_general | solution.py:61
  91.9 1.0 slice.124
  93.2 0.8 pad_add_fusion
  94.0 7.1 %all-to-all-start.4 = ((f32[32,24,128]{2,1,0:T(8,128)}), f32[32,24,128]{2,1,0:T(8,128)}, u32[]{:S(2)}, u32[]{:S(2)}) async-start(f32[32,24,128]{2,1,0:T(8,128)} %pad_add_fusion), calls=%async_computation.4 | async-start | bytes 786432 | tf_op jit(solution)/shard_map/all_to_all | solution.py:47
  101.2 2.0 %fusion.64 = f32[4,2,136,128]{3,2,1,0:T(8,128)} fusion(f32[4,2,136,128]{3,2,1,0:T(8,128)} %rev.14), kind=kOutput, calls=%fused_computation.140 | output fusion | flops 139264 | bytes 1114112 | tf_op jit(solution)/shard_map/jit(cumsum)/reduce_window_sum | solution.py:137
  103.4 2.0 %copy.117 = bf16[4,2,256,128]{3,2,1,0:T(8,128)(2,1)} copy(bf16[4,2,256,128]{2,3,1,0:T(8,128)(2,1)} %divide_convert_fusion) | data formatting | bytes 1048576 | tf_op jit(solution)/shard_map/convert_element_type | solution.py:260
  105.4 2.0 %copy.118 = bf16[512,4,128]{0,2,1:T(8,128)(2,1)} copy(bf16[512,4,128]{2,0,1:T(8,128)(2,1)} %bitcast.185) | data formatting | bytes 1048576 | tf_op jit(solution)/shard_map/transpose | solution.py:231
  107.4 2.0 %copy.131 = bf16[512,512]{1,0:T(8,128)(2,1)} copy(bf16[512,512]{0,1:T(8,128)(2,1)} %bitcast.186) | data formatting | bytes 1048576
  109.5 1.1 fusion.24
  110.6 0.9 all-to-all-done.4
  111.5 0.7 slice_bitcast_fusion
  112.2 1.0 slice.130
  113.2 1.3 subtract_convert_fusion
  115.7 2.3 %fusion.9 = f32[4,2,256,16]{2,3,1,0:T(8,128)S(1)} fusion(f32[4,2,256,16,16]{2,4,3,1,0:T(8,128)S(1)} %bitcast.171, f32[4,2,256,16]{2,3,1,0:T(8,128)S(1)} %copy-done.27), kind=kLoop, calls=%fused_computation.16 | loop fusion | flops 1540096 | bytes 2359296 | tf_op jit(solution)/shard_map/reduce_sum | solution.py:89
  118.0 1.0 fusion.38
  121.0 0.6 broadcast_in_dim.19
  121.7 4.2 %all-to-all-start.5 = ((f32[8,2,512]{2,1,0:T(2,128)}), f32[8,2,512]{2,1,0:T(2,128)S(1)}, u32[]{:S(2)}, u32[]{:S(2)}) async-start(f32[8,2,512]{2,1,0:T(2,128)} %broadcast_in_dim.19), calls=%async_computation.5 | async-start | bytes 65536 | tf_op jit(solution)/shard_map/all_to_all | solution.py:55
  125.9 1.9 %fusion.13 = bf16[4,2,256,128]{3,2,1,0:T(8,128)(2,1)S(1)} fusion(f32[4,2,256,128]{3,2,1,0:T(8,128)} %fusion.66, bf16[4,2,256,256]{2,3,1,0:T(8,128)(2,1)S(1)} %bitcast.163, bf16[4,2,256,128]{2,3,1,0:T(8,128)(2,1)} %copy-done.17), kind=kOutput, calls=%fused_computation.41 | convolution fusion | flops 134742016 | bytes 3145728 | tf_op jit(solution)/shard_map/...jr,...rd->...jd/dot_general | solution.py:61
  127.8 0.9 copy.181
  128.7 4.0 %all-to-all-done.5 = f32[8,2,512]{2,1,0:T(2,128)S(1)} async-done(((f32[8,2,512]{2,1,0:T(2,128)}), f32[8,2,512]{2,1,0:T(2,128)S(1)}, u32[]{:S(2)}, u32[]{:S(2)}) %all-to-all-start.5) | async-done | bytes 32800 | tf_op jit(solution)/shard_map/all_to_all | solution.py:55
  132.7 2.2 %fusion.32 = bf16[512,512]{1,0:T(8,128)(2,1)} fusion(bf16[512,512]{1,0:T(8,128)(2,1)} %param.12, f32[4,64,8,128]{3,2,1,0:T(8,128)S(1)} %bitcast.167, f32[512]{0:T(512)S(1)} %bitcast.202, f32[512]{0:T(512)S(1)} %copy-done.53, f32[512]{0:T(512)S(1)} %copy-done.48, f32[512]{0:T(512)S(1)} %bitcast.198), kind=kLoop, calls=%fused_computation.62 | loop fusion | flops 2097152 | bytes 2105344 | tf_op jit(solution)/shard_map/convert_element_type | solution.py:205
  134.9 1.1 fusion.22
  (169 shorter events, 9.1 us)
Async XLA Ops:
  0.6 11.3 %copy-start.51 = (s32[2,128,16]{1,2,0:T(8,128)S(1)}, s32[2,128,16]{1,2,0:T(8,128)}, u32[]{:S(2)}) copy-start(s32[2,128,16]{1,2,0:T(8,128)} %param.17) | copy-start | bytes 49156
  0.6 11.3 %copy-start.28 = (bf16[512,512]{1,0:T(8,128)(2,1)S(1)}, bf16[512,512]{1,0:T(8,128)(2,1)}, u32[]{:S(2)}) copy-start(bf16[512,512]{1,0:T(8,128)(2,1)} %param.13) | copy-start | bytes 1572868
  2.1 10.1 %copy-start.29 = (bf16[512,512]{1,0:T(8,128)(2,1)S(1)}, bf16[512,512]{1,0:T(8,128)(2,1)}, u32[]{:S(2)}) copy-start(bf16[512,512]{1,0:T(8,128)(2,1)} %param.14) | copy-start | bytes 1572868
  2.9 15.9 %all-to-all-start = ((f32[8,2,512]{2,1,0:T(2,128)}), f32[8,2,512]{2,1,0:T(2,128)S(1)}, u32[]{:S(2)}, u32[]{:S(2)}) async-start(f32[8,2,512]{2,1,0:T(2,128)} %broadcast_in_dim.16), calls=%async_computation | async-start | bytes 65536 | tf_op jit(solution)/shard_map/all_to_all | solution.py:55
  12.2 10.4 %copy-start.1 = (bf16[4,512,128]{2,1,0:T(8,128)(2,1)}, bf16[4,512,128]{2,1,0:T(8,128)(2,1)S(1)}, u32[]{:S(2)}) copy-start(bf16[4,512,128]{2,1,0:T(8,128)(2,1)S(1)} %copy.112) | copy-start | bytes 1572868
  13.6 5.3 %copy-start.9 = (bf16[512,512]{1,0:T(8,128)(2,1)S(1)}, bf16[512,512]{1,0:T(8,128)(2,1)}, u32[]{:S(2)}) copy-start(bf16[512,512]{1,0:T(8,128)(2,1)} %param.12) | copy-start | bytes 1572868
  13.6 5.3 %copy-start.47 = (f32[512]{0:T(512)S(1)}, f32[512]{0:T(512)}, u32[]{:S(2)}) copy-start(f32[512]{0:T(512)} %param.16) | copy-start | bytes 6148
  16.6 8.3 %copy-start.52 = (f32[192]{0:T(256)}, f32[192]{0:T(256)S(1)}, u32[]{:S(2)}) copy-start(f32[192]{0:T(256)S(1)} %pad.69.clone) | copy-start | bytes 2308
  18.9 20.7 %copy-start.45 = (f32[1,512]{1,0:T(1,128)}, f32[1,512]{1,0:T(1,128)S(1)}, u32[]{:S(2)}) copy-start(f32[1,512]{1,0:T(1,128)S(1)} %get-tuple-element.47) | copy-start | bytes 6148
  18.9 33.7 %copy-start.43 = (f32[1,512]{1,0:T(1,128)}, f32[1,512]{1,0:T(1,128)S(1)}, u32[]{:S(2)}) copy-start(f32[1,512]{1,0:T(1,128)S(1)} %get-tuple-element.48) | copy-start | bytes 6148
  19.1 2.2 %copy-start.30 = (bf16[256,136,1,1]{0,1,3,2:T(8,128)(2,1)S(1)}, bf16[256,136,1,1]{0,1,3,2:T(8,128)(2,1)}, u32[]{:S(2)}) copy-start(bf16[256,136,1,1]{0,1,3,2:T(8,128)(2,1)} %constant.67) | copy-start | bytes 208900
  19.3 0.8 copy-start.6
  20.1 1.2 copy-start.26
  22.5 12.4 %copy-start.11 = (bf16[512,512]{1,0:T(8,128)(2,1)S(1)}, bf16[512,512]{1,0:T(8,128)(2,1)}, u32[]{:S(2)}) copy-start(bf16[512,512]{1,0:T(8,128)(2,1)} %param.11) | copy-start | bytes 1572868
  22.5 12.4 %copy-start.49 = (f32[512]{0:T(512)S(1)}, f32[512]{0:T(512)}, u32[]{:S(2)}) copy-start(f32[512]{0:T(512)} %param.15) | copy-start | bytes 6148
  25.7 19.6 %all-to-all-start.1 = ((f32[32,24,128]{2,1,0:T(8,128)}), f32[32,24,128]{2,1,0:T(8,128)}, u32[]{:S(2)}, u32[]{:S(2)}) async-start(f32[32,24,128]{2,1,0:T(8,128)} %bitcast.23), calls=%async_computation.1 | async-start | bytes 786432 | tf_op jit(solution)/shard_map/all_to_all | solution.py:41
  37.1 1.4 %copy-start.31 = (bf16[256,136,1,1]{0,1,3,2:T(8,128)(2,1)S(1)}, bf16[256,136,1,1]{0,1,3,2:T(8,128)(2,1)}, u32[]{:S(2)}) copy-start(bf16[256,136,1,1]{0,1,3,2:T(8,128)(2,1)} %constant.67) | copy-start | bytes 208900
  37.2 3.0 %copy-start.4 = (bf16[4,512,128]{2,1,0:T(8,128)(2,1)}, bf16[4,512,128]{2,1,0:T(8,128)(2,1)S(1)}, u32[]{:S(2)}) copy-start(bf16[4,512,128]{2,1,0:T(8,128)(2,1)S(1)} %copy.106) | copy-start | bytes 1572868
  37.2 3.0 %copy-start.7 = (bf16[4,512,128]{2,1,0:T(8,128)(2,1)S(1)}, bf16[4,512,128]{2,1,0:T(8,128)(2,1)}, u32[]{:S(2)}) copy-start(bf16[4,512,128]{2,1,0:T(8,128)(2,1)} %copy-done.6) | copy-start | bytes 1572868
  37.2 3.0 %copy-start.34 = (pred[256,256]{0,1:T(8,128)(4,1)S(1)}, pred[256,256]{0,1:T(8,128)(4,1)}, u32[]{:S(2)}) copy-start(pred[256,256]{0,1:T(8,128)(4,1)} %iota_compare_fusion) | copy-start | bytes 196612
  37.5 0.7 copy-start.23
  47.4 15.5 %all-to-all-start.2 = ((f32[32,24,128]{2,1,0:T(8,128)}), f32[32,24,128]{2,1,0:T(8,128)}, u32[]{:S(2)}, u32[]{:S(2)}) async-start(f32[32,24,128]{2,1,0:T(8,128)} %pad_add_fusion.4), calls=%async_computation.2 | async-start | bytes 786432 | tf_op jit(solution)/shard_map/all_to_all | solution.py:47
  54.1 10.8 %copy-start.41 = (f32[4,2,256]{2,1,0:T(2,128)}, f32[4,2,256]{2,1,0:T(2,128)S(1)}, u32[]{:S(2)}) copy-start(f32[4,2,256]{2,1,0:T(2,128)S(1)} %reduce_sum.125) | copy-start | bytes 24580
  62.9 3.2 %copy-start.15 = (f32[4,2,136,128]{3,2,1,0:T(8,128)S(1)}, f32[4,2,136,128]{3,2,1,0:T(8,128)}, u32[]{:S(2)}) copy-start(f32[4,2,136,128]{3,2,1,0:T(8,128)} %get-tuple-element.51) | copy-start | bytes 1671172
  62.9 3.3 %copy-start.32 = (bf16[256,136,1,1]{0,1,3,2:T(8,128)(2,1)S(1)}, bf16[256,136,1,1]{0,1,3,2:T(8,128)(2,1)}, u32[]{:S(2)}) copy-start(bf16[256,136,1,1]{0,1,3,2:T(8,128)(2,1)} %constant.68) | copy-start | bytes 208900
  63.7 2.9 %copy-start.20 = (f32[4,2,256,128]{2,3,1,0:T(8,128)S(1)}, f32[4,2,256,128]{2,3,1,0:T(8,128)}, u32[]{:S(2)}) copy-start(f32[4,2,256,128]{2,3,1,0:T(8,128)} %copy.116) | copy-start | bytes 3145732
  63.7 2.9 %copy-start.22 = (f32[4,2,256,128]{2,3,1,0:T(8,128)S(1)}, f32[4,2,256,128]{2,3,1,0:T(8,128)}, u32[]{:S(2)}) copy-start(f32[4,2,256,128]{2,3,1,0:T(8,128)} %fusion.65) | copy-start | bytes 3145732
  65.6 2.4 %copy-start.36 = (f32[4,2,256]{2,1,0:T(2,128)}, f32[4,2,256]{2,1,0:T(2,128)S(1)}, u32[]{:S(2)}) copy-start(f32[4,2,256]{2,1,0:T(2,128)S(1)} %add_subtract_fusion.1) | copy-start | bytes 24580
  66.6 1.4 %copy-start.16 = (bf16[4,2,256,128]{2,3,1,0:T(8,128)(2,1)}, bf16[4,2,256,128]{2,3,1,0:T(8,128)(2,1)S(1)}, u32[]{:S(2)}) copy-start(bf16[4,2,256,128]{2,3,1,0:T(8,128)(2,1)S(1)} %fusion.15) | copy-start | bytes 1572868
  66.6 1.4 copy-start.42
  68.0 1.2 copy-start.37
  68.0 2.1 %copy-start.39 = (f32[4,2,256]{2,1,0:T(2,128)}, f32[4,2,256]{2,1,0:T(2,128)S(1)}, u32[]{:S(2)}) copy-start(f32[4,2,256]{2,1,0:T(2,128)S(1)} %get-tuple-element.15) | copy-start | bytes 24580
  69.1 9.4 %copy-start = (bf16[4,2,256,256]{2,3,1,0:T(8,128)(2,1)S(1)}, bf16[4,2,256,256]{2,3,1,0:T(8,128)(2,1)}, u32[]{:S(2)}) copy-start(bf16[4,2,256,256]{2,3,1,0:T(8,128)(2,1)} %get-tuple-element.37) | copy-start | bytes 3145732
  70.1 8.5 %copy-start.3 = (bf16[4,2,256,128]{3,2,1,0:T(8,128)(2,1)S(1)}, bf16[4,2,256,128]{3,2,1,0:T(8,128)(2,1)}, u32[]{:S(2)}) copy-start(bf16[4,2,256,128]{3,2,1,0:T(8,128)(2,1)} %divide_convert_fusion.1) | copy-start | bytes 1572868
  74.0 17.9 %all-to-all-start.3 = ((f32[32,24,128]{2,1,0:T(8,128)}), f32[32,24,128]{2,1,0:T(8,128)}, u32[]{:S(2)}, u32[]{:S(2)}) async-start(f32[32,24,128]{2,1,0:T(8,128)} %bitcast.32), calls=%async_computation.3 | async-start | bytes 786432 | tf_op jit(solution)/shard_map/all_to_all | solution.py:41
  80.0 1.7 %copy-start.2 = (bf16[4,512,128]{2,1,0:T(8,128)(2,1)S(1)}, bf16[4,512,128]{2,1,0:T(8,128)(2,1)}, u32[]{:S(2)}) copy-start(bf16[4,512,128]{2,1,0:T(8,128)(2,1)} %copy-done.1) | copy-start | bytes 1572868
  80.0 2.0 %copy-start.25 = (f32[4,2,256,256]{2,3,1,0:T(8,128)S(1)}, f32[4,2,256,256]{2,3,1,0:T(8,128)}, u32[]{:S(2)}) copy-start(f32[4,2,256,256]{2,3,1,0:T(8,128)} %get-tuple-element.49) | copy-start | bytes 6291460
  80.0 2.0 %copy-start.35 = (pred[256,256]{0,1:T(8,128)(4,1)S(1)}, pred[256,256]{0,1:T(8,128)(4,1)}, u32[]{:S(2)}) copy-start(pred[256,256]{0,1:T(8,128)(4,1)} %iota_compare_fusion) | copy-start | bytes 196612
  80.0 2.0 %copy-start.40 = (f32[4,2,256]{2,1,0:T(2,128)S(1)}, f32[4,2,256]{2,1,0:T(2,128)}, u32[]{:S(2)}) copy-start(f32[4,2,256]{2,1,0:T(2,128)} %copy-done.39) | copy-start | bytes 24580
  83.7 2.3 %copy-start.24 = (f32[4,2,256,32]{2,3,1,0:T(8,128)S(1)}, f32[4,2,256,32]{2,3,1,0:T(8,128)}, u32[]{:S(2)}) copy-start(f32[4,2,256,32]{2,3,1,0:T(8,128)} %copy-done.23) | copy-start | bytes 786436
  83.7 2.4 %copy-start.21 = (f32[4,2,256,128]{2,3,1,0:T(8,128)S(1)}, f32[4,2,256,128]{2,3,1,0:T(8,128)}, u32[]{:S(2)}) copy-start(f32[4,2,256,128]{2,3,1,0:T(8,128)} %get-tuple-element.12) | copy-start | bytes 3145732
  83.7 2.4 %copy-start.38 = (f32[4,2,256]{2,1,0:T(2,128)S(1)}, f32[4,2,256]{2,1,0:T(2,128)}, u32[]{:S(2)}) copy-start(f32[4,2,256]{2,1,0:T(2,128)} %copy-done.37) | copy-start | bytes 24580
  86.0 2.9 %copy-start.14 = (f32[4,2,136,128]{3,2,1,0:T(8,128)S(1)}, f32[4,2,136,128]{3,2,1,0:T(8,128)}, u32[]{:S(2)}) copy-start(f32[4,2,136,128]{3,2,1,0:T(8,128)} %get-tuple-element.55) | copy-start | bytes 1671172
  86.1 3.7 %copy-start.8 = (bf16[4,512,128]{2,1,0:T(8,128)(2,1)S(1)}, bf16[4,512,128]{2,1,0:T(8,128)(2,1)}, u32[]{:S(2)}) copy-start(bf16[4,512,128]{2,1,0:T(8,128)(2,1)} %copy-done.6) | copy-start | bytes 1572868
  94.0 17.5 %all-to-all-start.4 = ((f32[32,24,128]{2,1,0:T(8,128)}), f32[32,24,128]{2,1,0:T(8,128)}, u32[]{:S(2)}, u32[]{:S(2)}) async-start(f32[32,24,128]{2,1,0:T(8,128)} %pad_add_fusion), calls=%async_computation.4 | async-start | bytes 786432 | tf_op jit(solution)/shard_map/all_to_all | solution.py:47
  101.2 8.3 %copy-start.12 = (bf16[512,512]{1,0:T(8,128)(2,1)S(1)}, bf16[512,512]{1,0:T(8,128)(2,1)}, u32[]{:S(2)}) copy-start(bf16[512,512]{1,0:T(8,128)(2,1)} %param.11) | copy-start | bytes 1572868
  101.2 8.3 %copy-start.50 = (f32[512]{0:T(512)S(1)}, f32[512]{0:T(512)}, u32[]{:S(2)}) copy-start(f32[512]{0:T(512)} %param.15) | copy-start | bytes 6148
  109.5 5.0 %copy-start.33 = (bf16[256,136,1,1]{0,1,3,2:T(8,128)(2,1)S(1)}, bf16[256,136,1,1]{0,1,3,2:T(8,128)(2,1)}, u32[]{:S(2)}) copy-start(bf16[256,136,1,1]{0,1,3,2:T(8,128)(2,1)} %constant.68) | copy-start | bytes 208900
  114.5 1.2 copy-start.27
  114.9 0.8 copy-start.17
  115.7 3.4 %copy-start.5 = (bf16[4,512,128]{2,1,0:T(8,128)(2,1)S(1)}, bf16[4,512,128]{2,1,0:T(8,128)(2,1)}, u32[]{:S(2)}) copy-start(bf16[4,512,128]{2,1,0:T(8,128)(2,1)} %copy-done.4) | copy-start | bytes 1572868
  115.7 3.4 %copy-start.18 = (bf16[4,2,256,256]{2,3,1,0:T(8,128)(2,1)S(1)}, bf16[4,2,256,256]{2,3,1,0:T(8,128)(2,1)}, u32[]{:S(2)}) copy-start(bf16[4,2,256,256]{2,3,1,0:T(8,128)(2,1)} %fusion.6) | copy-start | bytes 3145732
  119.1 1.0 copy-start.10
  119.1 1.0 copy-start.48
  119.5 1.3 copy-start.19
  121.7 11.0 %all-to-all-start.5 = ((f32[8,2,512]{2,1,0:T(2,128)}), f32[8,2,512]{2,1,0:T(2,128)S(1)}, u32[]{:S(2)}, u32[]{:S(2)}) async-start(f32[8,2,512]{2,1,0:T(2,128)} %broadcast_in_dim.19), calls=%async_computation.5 | async-start | bytes 65536 | tf_op jit(solution)/shard_map/all_to_all | solution.py:55
  125.8 6.9 %copy-start.46 = (f32[1,512]{1,0:T(1,128)S(1)}, f32[1,512]{1,0:T(1,128)}, u32[]{:S(2)}) copy-start(f32[1,512]{1,0:T(1,128)} %copy-done.45) | copy-start | bytes 6148
  125.9 6.9 %copy-start.53 = (f32[512]{0:T(512)S(1)}, f32[512]{0:T(512)}, u32[]{:S(2)}) copy-start(f32[512]{0:T(512)} %multiply_multiply_fusion.4) | copy-start | bytes 6148
  127.8 7.2 %copy-start.13 = (bf16[512,512]{1,0:T(8,128)(2,1)S(1)}, bf16[512,512]{1,0:T(8,128)(2,1)}, u32[]{:S(2)}) copy-start(bf16[512,512]{1,0:T(8,128)(2,1)} %param.11) | copy-start | bytes 1572868
  127.8 7.1 %copy-start.44 = (f32[1,512]{1,0:T(1,128)S(1)}, f32[1,512]{1,0:T(1,128)}, u32[]{:S(2)}) copy-start(f32[1,512]{1,0:T(1,128)} %copy-done.43) | copy-start | bytes 6148
  127.8 7.1 %copy-start.54 = (f32[512]{0:T(512)S(1)}, f32[512]{0:T(512)}, u32[]{:S(2)}) copy-start(f32[512]{0:T(512)} %multiply_multiply_fusion.5) | copy-start | bytes 6148

commit v15 on v13

--- a/solution.py
+++ b/solution.py
@@ -210,9 +210,9 @@
     heads_here = queries.shape[1] // DH
     block_count = tok_rows // BLOCK
     sign_pair = jnp.concatenate([2 * signs[0] - 1, 2 * signs[1] - 1], axis=1).astype(jnp.bfloat16)
-    q_float = queries.astype(jnp.float32)
-    k_float = keys.astype(jnp.float32)
-    both = jnp.stack([q_float, k_float])
+    both = jnp.stack([queries, keys]).astype(jnp.float32)
+    q_float = both[0]
+    k_float = both[1]
     squares = jnp.sum(both * both, axis=-1)
     (q_total, k_total), _ = head_sum((squares[0], squares[1]), "head")
     q_scale, q_normed = normalize(queries, q_gain, q_total)

time: 129 us -> 138 us (1.070)
  local copies, waits for them, and re-layouts: 20.8 us -> 29.4 us
  starting transfers between devices: 37 us -> 39.4 us
  waiting for transfers between devices: 16.1 us -> 13.9 us
    squeeze x0 -> x2, local copies, waits for them, and re-layouts: none -> 5.13 us  [the longest x1 2.61 us: on_device(): k_float = both[1]]
    slice x0 -> x1, local copies, waits for them, and re-layouts: none -> 3.01 us  [on_device(): q_float = both[0]]
    all_to_all x2, starting transfers between devices: 13.2 us -> 15.9 us  [head_sum(): gathered = lax.all_to_all(spread, axis, 0, 0, tiled=True)]
    convert_element_type x0 -> x1, other arithmetic: none -> 2.74 us  [on_device(): both = jnp.stack([queries, keys]).astype(jnp.float32)]
    all_to_all x2, waiting for transfers between devices: 4.93 us -> 3.08 us  [carried_in(): mine = lax.all_to_all(stacked, axis, 0, 0, tiled=True)]
    all_to_all x2, waiting for transfers between devices: 5.77 us -> 4.03 us  [head_sum(): gathered = lax.all_to_all(spread, axis, 0, 0, tiled=True)]
    another operation x1 -> x0, other arithmetic: 1.53 us -> none  [on_device(): both = jnp.stack([q_float, k_float])]
    convert_element_type x2 -> x1, other arithmetic: 3.29 us -> 2.77 us  [norm_back(): return (scale * gain * normed_grad - raw_float * scale ** 3 * dot_total[:...]
  transfers between devices with their start and end apart: 6 -> 6, of which waited for: 6 -> 5; matrix products, arithmetic and copies ran while one was open for 29% -> 34% of each run, Pallas kernels for 0% -> 0%
where the time goes in v15:
time: 138 us; the launch traced here: 137 us
  starting transfers between devices  39.4 us (29%)
  local copies, waits for them, and re-layouts  29.4 us (21%)
  other arithmetic  28.1 us (20%)
  matrix products  24.7 us (18%)
  waiting for transfers between devices  13.9 us (10%)
  between operations  1.66 us (1%)
    dot_general x18, matrix products, product_of(): return jnp.einsum(spec, lhs, rhs, preferred_element_type=jnp.float32)  21.2 us
    all_to_all x2, starting transfers between devices, head_sum(): gathered = lax.all_to_all(spread, axis, 0, 0, tiled=True)  15.9 us
    all_to_all x2, starting transfers between devices, carried_in(): mine = lax.all_to_all(stacked, axis, 0, 0, tiled=True)  11.9 us
    all_to_all x2, starting transfers between devices, carried_in(): lax.all_to_all(shifted, axis, 0, 0, tiled=True)  11.5 us
    all_to_all x2, waiting for transfers between devices, carried_in(): lax.all_to_all(shifted, axis, 0, 0, tiled=True)  6.76 us
    unnamed x120, local copies, waits for them, and re-layouts  6.23 us
    reduce_sum x2, other arithmetic, sketch_back(): sketch_grad = jnp.sum(symmetric * sketched[..., None, :], axis=-1)  4.65 us
    all_to_all x2, waiting for transfers between devices, head_sum(): gathered = lax.all_to_all(spread, axis, 0, 0, tiled=True)  4.03 us
  transfers between devices with their start and end apart: 6, of which 5 were waited for; matrix products, arithmetic and copies ran while one was open for 34% of the time, Pallas kernels for 0%

profile of v15, /device:TPU:1, one launch (start us, length us, event | category | flops | bytes accessed | tf_op | source)
XLA Modules:
  0.0 137.1 jit_solution(2142871942418979896)
XLA Ops:
  0.7 1.5 %multiply_reduce_fusion = f32[2,512]{1,0:T(2,128)S(1)} fusion(bf16[1,512,512]{2,1,0:T(8,128)(2,1)} %bitcast.184, bf16[1,512,512]{2,1,0:T(8,128)(2,1)} %bitcast.182), kind=kLoop, calls=%fused_computation.21 | loop fusion | flops 2096128 | bytes 1052672 | tf_op jit(solution)/shard_map/reduce_sum | solution.py:216
  2.2 0.6 broadcast_in_dim.16
  2.8 9.0 %all-to-all-start = ((f32[8,2,512]{2,1,0:T(2,128)}), f32[8,2,512]{2,1,0:T(2,128)S(1)}, u32[]{:S(2)}, u32[]{:S(2)}) async-start(f32[8,2,512]{2,1,0:T(2,128)} %broadcast_in_dim.16), calls=%async_computation | async-start | bytes 65536 | tf_op jit(solution)/shard_map/all_to_all | solution.py:55
  11.8 2.7 %maximum_convert_fusion = f32[2,512,512]{2,1,0:T(8,128)} fusion(bf16[1,512,512]{2,1,0:T(8,128)(2,1)} %bitcast.185, bf16[1,512,512]{2,1,0:T(8,128)(2,1)} %bitcast.183), kind=kLoop, calls=%fused_computation.55 | loop fusion | flops 1048576 | bytes 3145728 | tf_op jit(solution)/shard_map/convert_element_type | solution.py:213
  15.5 1.4 copy.124
  16.9 3.0 %fusion.58 = (f32[1,512,512]{2,1,0:T(8,128)}, f32[1,512,512]{2,1,0:T(8,128)}) fusion(f32[2,512,512]{2,1,0:T(8,128)} %maximum_convert_fusion), kind=kLoop, calls=%fused_computation.135 | loop fusion | bytes 4194304 | tf_op jit(solution)/shard_map/slice | solution.py:214
  19.9 2.6 %squeeze.5 = f32[512,4,128]{2,1,0:T(4,128)} reshape(f32[1,512,512]{2,1,0:T(8,128)} %get-tuple-element.39) | data formatting | bytes 2097152 | tf_op jit(solution)/shard_map/squeeze | solution.py:215
  22.5 2.5 %squeeze.4 = f32[512,4,128]{2,1,0:T(4,128)} reshape(f32[1,512,512]{2,1,0:T(8,128)} %get-tuple-element.38) | data formatting | bytes 2097152 | tf_op jit(solution)/shard_map/squeeze | solution.py:214
  25.1 0.6 iota_compare_fusion
  27.1 1.2 convert_reduce_fusion.1
  28.3 1.2 convolution_convert_fusion
  29.5 2.3 %fusion.60 = (f32[4,136,128]{2,1,0:T(8,128)S(1)}, f32[4,2,136,128]{3,2,1,0:T(8,128)}) fusion(bf16[4,2,256,136]{2,3,1,0:T(8,128)(2,1)} %convolution_convert_fusion, bf16[4,2,256,128]{3,2,1,0:T(8,128)(2,1)S(1)} %bitcast.172), kind=kOutput, calls=%fused_computation.137 | convolution fusion | flops 71372800 | bytes 1916928 | tf_op jit(solution)/shard_map/...jr,...jd->...rd/dot_general | solution.py:61
  31.8 0.8 maximum_maximum_fusion
  32.6 8.1 %all-to-all-start.1 = ((f32[32,24,128]{2,1,0:T(8,128)}), f32[32,24,128]{2,1,0:T(8,128)}, u32[]{:S(2)}, u32[]{:S(2)}) async-start(f32[32,24,128]{2,1,0:T(8,128)} %bitcast.23), calls=%async_computation.1 | async-start | bytes 786432 | tf_op jit(solution)/shard_map/all_to_all | solution.py:41
  40.8 1.0 fusion.17
  41.7 1.2 reshape.176
  43.3 0.7 copy-done.24
  44.3 1.1 convolution_convert_fusion.1
  45.4 0.6 multiply_multiply_fusion.4
  46.0 2.7 %convert_reduce_fusion.2 = (f32[4,2,256]{2,1,0:T(2,128)}, bf16[4,2,256,256]{2,3,1,0:T(8,128)(2,1)}, f32[4,2,256,256]{2,3,1,0:T(8,128)}) fusion(pred[256,256]{0,1:T(8,128)(4,1)S(1)} %copy-done.35, bf16[4,2,256,128]{3,2,1,0:T(8,128)(2,1)S(1)} %bitcast.177, bf16[4,2,256,128]{3,2,1,0:T(8,128)(2,1)S(1)} %bitcast.180), kind=kOutput, calls=%fused_computation.19 | convolution fusion | flops 137885696 | bytes 4268032 | tf_op jit(solution)/shard_map/...id,...jd->...ij/dot_general | solution.py:61
  48.8 2.3 %all-to-all-done.1 = f32[32,24,128]{2,1,0:T(8,128)} async-done(((f32[32,24,128]{2,1,0:T(8,128)}), f32[32,24,128]{2,1,0:T(8,128)}, u32[]{:S(2)}, u32[]{:S(2)}) %all-to-all-start.1) | async-done | bytes 393248 | tf_op jit(solution)/shard_map/all_to_all | solution.py:41
  51.1 1.0 slice.121
  52.4 0.8 pad_add_fusion.4
  53.2 5.1 %all-to-all-start.2 = ((f32[32,24,128]{2,1,0:T(8,128)}), f32[32,24,128]{2,1,0:T(8,128)}, u32[]{:S(2)}, u32[]{:S(2)}) async-start(f32[32,24,128]{2,1,0:T(8,128)} %pad_add_fusion.4), calls=%async_computation.2 | async-start | bytes 786432 | tf_op jit(solution)/shard_map/all_to_all | solution.py:47
  58.4 0.5 multiply_multiply_fusion.5
  58.9 0.9 reduce_sum.134
  59.8 0.6 reduce_window_sum.34
  60.5 2.7 %fusion.63 = f32[4,2,256,128]{2,3,1,0:T(8,128)} fusion(bf16[4,2,256,256]{2,3,1,0:T(8,128)(2,1)} %get-tuple-element.37, bf16[4,2,256,128]{3,2,1,0:T(8,128)(2,1)} %bitcast.173), kind=kOutput, calls=%fused_computation.140 | convolution fusion | flops 134217728 | bytes 2621440 | tf_op jit(solution)/shard_map/...ij,...jd->...id/dot_general | solution.py:61
  63.1 5.5 %all-to-all-done.2 = f32[32,24,128]{2,1,0:T(8,128)} async-done(((f32[32,24,128]{2,1,0:T(8,128)}), f32[32,24,128]{2,1,0:T(8,128)}, u32[]{:S(2)}, u32[]{:S(2)}) %all-to-all-start.2) | async-done | bytes 393248 | tf_op jit(solution)/shard_map/all_to_all | solution.py:47
  68.7 0.8 slice_bitcast_fusion.1
  69.5 1.1 slice.128
  70.6 0.7 add_subtract_fusion.1
  72.4 1.3 multiply_reduce_fusion.1
  73.8 1.1 divide_convert_fusion.1
  74.9 0.9 fusion.40
  75.9 1.5 %fusion.61 = (f32[4,136,128]{2,1,0:T(8,128)S(1)}, f32[4,2,136,128]{3,2,1,0:T(8,128)S(1)}) fusion(bf16[4,2,256,136]{2,3,1,0:T(8,128)(2,1)} %convolution_convert_fusion.1, bf16[4,2,256,128]{3,2,1,0:T(8,128)(2,1)} %divide_convert_fusion.1), kind=kOutput, calls=%fused_computation.138 | convolution fusion | flops 71372800 | bytes 1916928 | tf_op jit(solution)/shard_map/...ir,...id->...rd/dot_general | solution.py:61
  77.5 1.7 %maximum_maximum_fusion.1 = f32[4,192,128]{2,1,0:T(8,128)} fusion(f32[4,2,128]{2,1,0:T(2,128)S(1)} %reshape.185, f32[4,136,128]{2,1,0:T(8,128)S(1)} %get-tuple-element.56, f32[192]{0:T(256)} %copy-done.54), kind=kLoop, calls=%fused_computation.69 | loop fusion | flops 196608 | bytes 676608 | tf_op jit(solution)/shard_map/concatenate | solution.py:32
  79.1 3.8 %all-to-all-start.3 = ((f32[32,24,128]{2,1,0:T(8,128)}), f32[32,24,128]{2,1,0:T(8,128)S(1)}, u32[]{:S(2)}, u32[]{:S(2)}) async-start(f32[32,24,128]{2,1,0:T(8,128)} %bitcast.32), calls=%async_computation.3 | async-start | bytes 786432 | tf_op jit(solution)/shard_map/all_to_all | solution.py:41
  83.0 0.9 rev.14
  83.9 2.1 %fusion.62 = f32[4,2,136,128]{3,2,1,0:T(8,128)} fusion(f32[4,2,136,128]{3,2,1,0:T(8,128)} %rev.14), kind=kOutput, calls=%fused_computation.139 | output fusion | flops 139264 | bytes 1114112 | tf_op jit(solution)/shard_map/jit(cumsum)/reduce_window_sum | solution.py:137
  86.5 0.8 fusion.6
  87.4 2.3 %fusion.10 = f32[4,2,256,16]{2,3,1,0:T(8,128)S(1)} fusion(f32[4,2,256,16,16]{2,4,3,1,0:T(8,128)S(1)} %bitcast.170, f32[4,2,256,16]{2,3,1,0:T(8,128)S(1)} %multiply_multiply_fusion.3), kind=kLoop, calls=%fused_computation.16 | loop fusion | flops 1540096 | bytes 2359296 | tf_op jit(solution)/shard_map/reduce_sum | solution.py:89
  89.8 0.9 divide_convert_fusion
  90.7 1.0 fusion.32
  92.2 0.8 all-to-all-done.3
  93.4 0.8 pad_add_fusion
  94.2 6.4 %all-to-all-start.4 = ((f32[32,24,128]{2,1,0:T(8,128)}), f32[32,24,128]{2,1,0:T(8,128)}, u32[]{:S(2)}, u32[]{:S(2)}) async-start(f32[32,24,128]{2,1,0:T(8,128)} %pad_add_fusion), calls=%async_computation.4 | async-start | bytes 786432 | tf_op jit(solution)/shard_map/all_to_all | solution.py:47
  101.1 2.1 %copy.125 = bf16[4,2,256,128]{3,2,1,0:T(8,128)(2,1)} copy(bf16[4,2,256,128]{2,3,1,0:T(8,128)(2,1)} %divide_convert_fusion) | data formatting | bytes 1048576 | tf_op jit(solution)/shard_map/convert_element_type | solution.py:260
  103.1 2.0 %copy.126 = bf16[512,4,128]{0,2,1:T(8,128)(2,1)} copy(bf16[512,4,128]{2,0,1:T(8,128)(2,1)} %bitcast.189) | data formatting | bytes 1048576 | tf_op jit(solution)/shard_map/transpose | solution.py:231
  105.2 2.0 %copy.141 = bf16[512,512]{1,0:T(8,128)(2,1)} copy(bf16[512,512]{0,1:T(8,128)(2,1)} %bitcast.190) | data formatting | bytes 1048576
  107.2 2.5 %fusion.64 = f32[4,2,256,128]{3,2,1,0:T(8,128)} fusion(bf16[4,2,256,256]{2,3,1,0:T(8,128)(2,1)S(1)} %copy-done, bf16[4,2,256,128]{3,2,1,0:T(8,128)(2,1)} %divide_convert_fusion.1), kind=kOutput, calls=%fused_computation.141 | convolution fusion | flops 134217728 | bytes 2621440 | tf_op jit(solution)/shard_map/...ij,...id->...jd/dot_general | solution.py:61
  109.7 1.2 all-to-all-done.4
  110.9 0.7 slice_bitcast_fusion
  111.6 1.0 slice.137
  112.6 1.3 subtract_convert_fusion
  115.1 2.3 %fusion.8 = f32[4,2,256,16]{2,3,1,0:T(8,128)S(1)} fusion(f32[4,2,256,16,16]{2,4,3,1,0:T(8,128)S(1)} %bitcast.171, f32[4,2,256,16]{2,3,1,0:T(8,128)S(1)} %copy-done.28), kind=kLoop, calls=%fused_computation.13 | loop fusion | flops 1540096 | bytes 2359296 | tf_op jit(solution)/shard_map/reduce_sum | solution.py:89
  117.4 1.0 fusion.35
  119.0 0.7 copy-done.19
  119.9 0.6 broadcast_in_dim.19
  120.5 6.9 %all-to-all-start.5 = ((f32[8,2,512]{2,1,0:T(2,128)}), f32[8,2,512]{2,1,0:T(2,128)S(1)}, u32[]{:S(2)}, u32[]{:S(2)}) async-start(f32[8,2,512]{2,1,0:T(2,128)} %broadcast_in_dim.19), calls=%async_computation.5 | async-start | bytes 65536 | tf_op jit(solution)/shard_map/all_to_all | solution.py:55
  127.5 1.9 %fusion.12 = bf16[4,2,256,128]{3,2,1,0:T(8,128)(2,1)S(1)} fusion(f32[4,2,256,128]{3,2,1,0:T(8,128)} %fusion.64, bf16[4,2,256,256]{2,3,1,0:T(8,128)(2,1)S(1)} %bitcast.165, bf16[4,2,256,128]{2,3,1,0:T(8,128)(2,1)} %copy-done.16), kind=kOutput, calls=%fused_computation.35 | convolution fusion | flops 134742016 | bytes 3145728 | tf_op jit(solution)/shard_map/...jr,...rd->...jd/dot_general | solution.py:61
  129.4 0.9 copy.195
  130.3 4.0 %all-to-all-done.5 = f32[8,2,512]{2,1,0:T(2,128)S(1)} async-done(((f32[8,2,512]{2,1,0:T(2,128)}), f32[8,2,512]{2,1,0:T(2,128)S(1)}, u32[]{:S(2)}, u32[]{:S(2)}) %all-to-all-start.5) | async-done | bytes 32800 | tf_op jit(solution)/shard_map/all_to_all | solution.py:55
  134.4 2.8 %fusion.21 = (bf16[512,512]{1,0:T(8,128)(2,1)}, bf16[512,512]{1,0:T(8,128)(2,1)}) fusion(bf16[512,512]{1,0:T(8,128)(2,1)} %param.11, f32[4,64,8,128]{3,2,1,0:T(8,128)S(1)} %bitcast.168, f32[512]{0:T(512)S(1)} %bitcast.208, f32[512]{0:T(512)S(1)} %copy-done.56, f32[512]{0:T(512)S(1)} %copy-done.50, f32[512]{0:T(512)S(1)} %bitcast.201, f32[512]{0:T(512)S(1)} %bitcast.207, ...), kind=kLoop, calls=%fused_computation.46 | loop fusion | flops 4194304 | bytes 4210688 | tf_op jit(solution)/shard_map/convert_element_type | solution.py:205
  (175 shorter events, 8.0 us)
Async XLA Ops:
  0.6 13.9 %copy-start.53 = (s32[2,128,16]{1,2,0:T(8,128)S(1)}, s32[2,128,16]{1,2,0:T(8,128)}, u32[]{:S(2)}) copy-start(s32[2,128,16]{1,2,0:T(8,128)} %param.17) | copy-start | bytes 49156
  0.6 13.9 %copy-start.29 = (bf16[512,512]{1,0:T(8,128)(2,1)S(1)}, bf16[512,512]{1,0:T(8,128)(2,1)}, u32[]{:S(2)}) copy-start(bf16[512,512]{1,0:T(8,128)(2,1)} %param.13) | copy-start | bytes 1572868
  2.8 22.9 %all-to-all-start = ((f32[8,2,512]{2,1,0:T(2,128)}), f32[8,2,512]{2,1,0:T(2,128)S(1)}, u32[]{:S(2)}, u32[]{:S(2)}) async-start(f32[8,2,512]{2,1,0:T(2,128)} %broadcast_in_dim.16), calls=%async_computation | async-start | bytes 65536 | tf_op jit(solution)/shard_map/all_to_all | solution.py:55
  11.8 3.0 %copy-start.30 = (bf16[512,512]{1,0:T(8,128)(2,1)S(1)}, bf16[512,512]{1,0:T(8,128)(2,1)}, u32[]{:S(2)}) copy-start(bf16[512,512]{1,0:T(8,128)(2,1)} %param.14) | copy-start | bytes 1572868
  14.8 14.7 %copy-start.1 = (bf16[4,512,128]{2,1,0:T(8,128)(2,1)}, bf16[4,512,128]{2,1,0:T(8,128)(2,1)S(1)}, u32[]{:S(2)}) copy-start(bf16[4,512,128]{2,1,0:T(8,128)(2,1)S(1)} %copy.120) | copy-start | bytes 1572868
  19.9 5.9 %copy-start.11 = (bf16[512,512]{1,0:T(8,128)(2,1)S(1)}, bf16[512,512]{1,0:T(8,128)(2,1)}, u32[]{:S(2)}) copy-start(bf16[512,512]{1,0:T(8,128)(2,1)} %param.12) | copy-start | bytes 1572868
  19.9 5.9 %copy-start.51 = (f32[512]{0:T(512)S(1)}, f32[512]{0:T(512)}, u32[]{:S(2)}) copy-start(f32[512]{0:T(512)} %param.16) | copy-start | bytes 6148
  25.1 6.7 %copy-start.54 = (f32[192]{0:T(256)}, f32[192]{0:T(256)S(1)}, u32[]{:S(2)}) copy-start(f32[192]{0:T(256)S(1)} %pad.69.clone) | copy-start | bytes 2308
  25.8 19.7 %copy-start.45 = (f32[1,512]{1,0:T(1,128)}, f32[1,512]{1,0:T(1,128)S(1)}, u32[]{:S(2)}) copy-start(f32[1,512]{1,0:T(1,128)S(1)} %get-tuple-element.49) | copy-start | bytes 6148
  25.8 32.6 %copy-start.47 = (f32[1,512]{1,0:T(1,128)}, f32[1,512]{1,0:T(1,128)S(1)}, u32[]{:S(2)}) copy-start(f32[1,512]{1,0:T(1,128)S(1)} %get-tuple-element.50) | copy-start | bytes 6148
  26.0 2.3 %copy-start.31 = (bf16[256,136,1,1]{0,1,3,2:T(8,128)(2,1)S(1)}, bf16[256,136,1,1]{0,1,3,2:T(8,128)(2,1)}, u32[]{:S(2)}) copy-start(bf16[256,136,1,1]{0,1,3,2:T(8,128)(2,1)} %constant.67) | copy-start | bytes 208900
  26.2 0.8 copy-start.7
  27.0 1.2 copy-start.27
  29.4 11.3 %copy-start.10 = (bf16[512,512]{1,0:T(8,128)(2,1)S(1)}, bf16[512,512]{1,0:T(8,128)(2,1)}, u32[]{:S(2)}) copy-start(bf16[512,512]{1,0:T(8,128)(2,1)} %param.11) | copy-start | bytes 1572868
  29.4 11.3 %copy-start.49 = (f32[512]{0:T(512)S(1)}, f32[512]{0:T(512)}, u32[]{:S(2)}) copy-start(f32[512]{0:T(512)} %param.15) | copy-start | bytes 6148
  32.6 18.4 %all-to-all-start.1 = ((f32[32,24,128]{2,1,0:T(8,128)}), f32[32,24,128]{2,1,0:T(8,128)}, u32[]{:S(2)}, u32[]{:S(2)}) async-start(f32[32,24,128]{2,1,0:T(8,128)} %bitcast.23), calls=%async_computation.1 | async-start | bytes 786432 | tf_op jit(solution)/shard_map/all_to_all | solution.py:41
  42.9 1.4 %copy-start.32 = (bf16[256,136,1,1]{0,1,3,2:T(8,128)(2,1)S(1)}, bf16[256,136,1,1]{0,1,3,2:T(8,128)(2,1)}, u32[]{:S(2)}) copy-start(bf16[256,136,1,1]{0,1,3,2:T(8,128)(2,1)} %constant.67) | copy-start | bytes 208900
  43.0 3.0 %copy-start.5 = (bf16[4,512,128]{2,1,0:T(8,128)(2,1)}, bf16[4,512,128]{2,1,0:T(8,128)(2,1)S(1)}, u32[]{:S(2)}) copy-start(bf16[4,512,128]{2,1,0:T(8,128)(2,1)S(1)} %copy.114) | copy-start | bytes 1572868
  43.0 3.0 %copy-start.8 = (bf16[4,512,128]{2,1,0:T(8,128)(2,1)S(1)}, bf16[4,512,128]{2,1,0:T(8,128)(2,1)}, u32[]{:S(2)}) copy-start(bf16[4,512,128]{2,1,0:T(8,128)(2,1)} %copy-done.7) | copy-start | bytes 1572868
  43.0 3.0 %copy-start.35 = (pred[256,256]{0,1:T(8,128)(4,1)S(1)}, pred[256,256]{0,1:T(8,128)(4,1)}, u32[]{:S(2)}) copy-start(pred[256,256]{0,1:T(8,128)(4,1)} %iota_compare_fusion) | copy-start | bytes 196612
  43.3 0.7 copy-start.24
  53.2 15.5 %all-to-all-start.2 = ((f32[32,24,128]{2,1,0:T(8,128)}), f32[32,24,128]{2,1,0:T(8,128)}, u32[]{:S(2)}, u32[]{:S(2)}) async-start(f32[32,24,128]{2,1,0:T(8,128)} %pad_add_fusion.4), calls=%async_computation.2 | async-start | bytes 786432 | tf_op jit(solution)/shard_map/all_to_all | solution.py:47
  59.8 10.8 %copy-start.43 = (f32[4,2,256]{2,1,0:T(2,128)}, f32[4,2,256]{2,1,0:T(2,128)S(1)}, u32[]{:S(2)}) copy-start(f32[4,2,256]{2,1,0:T(2,128)S(1)} %reduce_sum.134) | copy-start | bytes 24580
  68.7 3.2 %copy-start.13 = (f32[4,2,136,128]{3,2,1,0:T(8,128)S(1)}, f32[4,2,136,128]{3,2,1,0:T(8,128)}, u32[]{:S(2)}) copy-start(f32[4,2,136,128]{3,2,1,0:T(8,128)} %get-tuple-element.53) | copy-start | bytes 1671172
  68.7 3.3 %copy-start.33 = (bf16[256,136,1,1]{0,1,3,2:T(8,128)(2,1)S(1)}, bf16[256,136,1,1]{0,1,3,2:T(8,128)(2,1)}, u32[]{:S(2)}) copy-start(bf16[256,136,1,1]{0,1,3,2:T(8,128)(2,1)} %constant.68) | copy-start | bytes 208900
  69.5 2.9 %copy-start.21 = (f32[4,2,256,128]{2,3,1,0:T(8,128)S(1)}, f32[4,2,256,128]{2,3,1,0:T(8,128)}, u32[]{:S(2)}) copy-start(f32[4,2,256,128]{2,3,1,0:T(8,128)} %copy.124) | copy-start | bytes 3145732
  69.5 2.9 %copy-start.23 = (f32[4,2,256,128]{2,3,1,0:T(8,128)S(1)}, f32[4,2,256,128]{2,3,1,0:T(8,128)}, u32[]{:S(2)}) copy-start(f32[4,2,256,128]{2,3,1,0:T(8,128)} %fusion.63) | copy-start | bytes 3145732
  71.4 2.4 %copy-start.37 = (f32[4,2,256]{2,1,0:T(2,128)}, f32[4,2,256]{2,1,0:T(2,128)S(1)}, u32[]{:S(2)}) copy-start(f32[4,2,256]{2,1,0:T(2,128)S(1)} %add_subtract_fusion.1) | copy-start | bytes 24580
  72.4 1.4 copy-start.14
  72.4 1.4 copy-start.44
  73.8 1.2 copy-start.39
  73.8 2.1 %copy-start.41 = (f32[4,2,256]{2,1,0:T(2,128)}, f32[4,2,256]{2,1,0:T(2,128)S(1)}, u32[]{:S(2)}) copy-start(f32[4,2,256]{2,1,0:T(2,128)S(1)} %get-tuple-element.15) | copy-start | bytes 24580
  77.4 9.0 %copy-start.12 = (f32[4,2,136,128]{3,2,1,0:T(8,128)}, f32[4,2,136,128]{3,2,1,0:T(8,128)S(1)}, u32[]{:S(2)}) copy-start(f32[4,2,136,128]{3,2,1,0:T(8,128)S(1)} %get-tuple-element.57) | copy-start | bytes 1671172
  77.4 8.5 %copy-start.4 = (bf16[4,2,256,128]{3,2,1,0:T(8,128)(2,1)S(1)}, bf16[4,2,256,128]{3,2,1,0:T(8,128)(2,1)}, u32[]{:S(2)}) copy-start(bf16[4,2,256,128]{3,2,1,0:T(8,128)(2,1)} %divide_convert_fusion.1) | copy-start | bytes 1572868
  77.4 8.5 %copy-start.15 = (bf16[4,2,256,128]{2,3,1,0:T(8,128)(2,1)S(1)}, bf16[4,2,256,128]{2,3,1,0:T(8,128)(2,1)}, u32[]{:S(2)}) copy-start(bf16[4,2,256,128]{2,3,1,0:T(8,128)(2,1)} %copy-done.14) | copy-start | bytes 1572868
  77.5 8.5 %copy-start.38 = (f32[4,2,256]{2,1,0:T(2,128)S(1)}, f32[4,2,256]{2,1,0:T(2,128)}, u32[]{:S(2)}) copy-start(f32[4,2,256]{2,1,0:T(2,128)} %copy-done.37) | copy-start | bytes 24580
  77.5 8.5 %copy-start.42 = (f32[4,2,256]{2,1,0:T(2,128)S(1)}, f32[4,2,256]{2,1,0:T(2,128)}, u32[]{:S(2)}) copy-start(f32[4,2,256]{2,1,0:T(2,128)} %copy-done.41) | copy-start | bytes 24580
  79.1 13.9 %all-to-all-start.3 = ((f32[32,24,128]{2,1,0:T(8,128)}), f32[32,24,128]{2,1,0:T(8,128)S(1)}, u32[]{:S(2)}, u32[]{:S(2)}) async-start(f32[32,24,128]{2,1,0:T(8,128)} %bitcast.32), calls=%async_computation.3 | async-start | bytes 786432 | tf_op jit(solution)/shard_map/all_to_all | solution.py:41
  83.9 2.6 %copy-start.2 = (bf16[4,512,128]{2,1,0:T(8,128)(2,1)S(1)}, bf16[4,512,128]{2,1,0:T(8,128)(2,1)}, u32[]{:S(2)}) copy-start(bf16[4,512,128]{2,1,0:T(8,128)(2,1)} %copy-done.1) | copy-start | bytes 1572868
  83.9 2.6 %copy-start.26 = (f32[4,2,256,256]{2,3,1,0:T(8,128)S(1)}, f32[4,2,256,256]{2,3,1,0:T(8,128)}, u32[]{:S(2)}) copy-start(f32[4,2,256,256]{2,3,1,0:T(8,128)} %get-tuple-element.51) | copy-start | bytes 6291460
  83.9 2.6 %copy-start.36 = (pred[256,256]{0,1:T(8,128)(4,1)S(1)}, pred[256,256]{0,1:T(8,128)(4,1)}, u32[]{:S(2)}) copy-start(pred[256,256]{0,1:T(8,128)(4,1)} %iota_compare_fusion) | copy-start | bytes 196612
  87.3 4.4 %copy-start.17 = (bf16[4,2,256,256]{2,3,1,0:T(8,128)(2,1)}, bf16[4,2,256,256]{2,3,1,0:T(8,128)(2,1)S(1)}, u32[]{:S(2)}) copy-start(bf16[4,2,256,256]{2,3,1,0:T(8,128)(2,1)S(1)} %fusion.6) | copy-start | bytes 3145732
  87.3 2.4 %copy-start.25 = (f32[4,2,256,32]{2,3,1,0:T(8,128)S(1)}, f32[4,2,256,32]{2,3,1,0:T(8,128)}, u32[]{:S(2)}) copy-start(f32[4,2,256,32]{2,3,1,0:T(8,128)} %copy-done.24) | copy-start | bytes 786436
  87.3 2.4 %copy-start.22 = (f32[4,2,256,128]{2,3,1,0:T(8,128)S(1)}, f32[4,2,256,128]{2,3,1,0:T(8,128)}, u32[]{:S(2)}) copy-start(f32[4,2,256,128]{2,3,1,0:T(8,128)} %get-tuple-element.12) | copy-start | bytes 3145732
  87.4 2.4 %copy-start.40 = (f32[4,2,256]{2,1,0:T(2,128)S(1)}, f32[4,2,256]{2,1,0:T(2,128)}, u32[]{:S(2)}) copy-start(f32[4,2,256]{2,1,0:T(2,128)} %copy-done.39) | copy-start | bytes 24580
  89.7 2.0 %copy-start.9 = (bf16[4,512,128]{2,1,0:T(8,128)(2,1)S(1)}, bf16[4,512,128]{2,1,0:T(8,128)(2,1)}, u32[]{:S(2)}) copy-start(bf16[4,512,128]{2,1,0:T(8,128)(2,1)} %copy-done.7) | copy-start | bytes 1572868
  93.3 7.3 %copy-start.20 = (f32[512,4,128]{2,1,0:T(4,128)S(1)}, f32[512,4,128]{2,1,0:T(4,128)}, u32[]{:S(2)}) copy-start(f32[512,4,128]{2,1,0:T(4,128)} %squeeze.4) | copy-start | bytes 3145732
  93.3 7.3 %copy-start.50 = (f32[512]{0:T(512)S(1)}, f32[512]{0:T(512)}, u32[]{:S(2)}) copy-start(f32[512]{0:T(512)} %param.15) | copy-start | bytes 6148
  94.2 16.7 %all-to-all-start.4 = ((f32[32,24,128]{2,1,0:T(8,128)}), f32[32,24,128]{2,1,0:T(8,128)}, u32[]{:S(2)}, u32[]{:S(2)}) async-start(f32[32,24,128]{2,1,0:T(8,128)} %pad_add_fusion), calls=%async_computation.4 | async-start | bytes 786432 | tf_op jit(solution)/shard_map/all_to_all | solution.py:47
  100.8 6.4 %copy-start = (bf16[4,2,256,256]{2,3,1,0:T(8,128)(2,1)S(1)}, bf16[4,2,256,256]{2,3,1,0:T(8,128)(2,1)}, u32[]{:S(2)}) copy-start(bf16[4,2,256,256]{2,3,1,0:T(8,128)(2,1)} %get-tuple-element.37) | copy-start | bytes 3145732
  107.2 6.7 %copy-start.34 = (bf16[256,136,1,1]{0,1,3,2:T(8,128)(2,1)S(1)}, bf16[256,136,1,1]{0,1,3,2:T(8,128)(2,1)}, u32[]{:S(2)}) copy-start(bf16[256,136,1,1]{0,1,3,2:T(8,128)(2,1)} %constant.68) | copy-start | bytes 208900
  109.7 4.6 %copy-start.3 = (bf16[4,512,128]{2,1,0:T(8,128)(2,1)S(1)}, bf16[4,512,128]{2,1,0:T(8,128)(2,1)}, u32[]{:S(2)}) copy-start(bf16[4,512,128]{2,1,0:T(8,128)(2,1)} %copy-done.1) | copy-start | bytes 1572868
  113.9 1.2 copy-start.28
  114.3 0.8 copy-start.16
  115.1 3.4 %copy-start.6 = (bf16[4,512,128]{2,1,0:T(8,128)(2,1)S(1)}, bf16[4,512,128]{2,1,0:T(8,128)(2,1)}, u32[]{:S(2)}) copy-start(bf16[4,512,128]{2,1,0:T(8,128)(2,1)} %copy-done.5) | copy-start | bytes 1572868
  115.1 3.4 %copy-start.18 = (bf16[4,2,256,256]{2,3,1,0:T(8,128)(2,1)S(1)}, bf16[4,2,256,256]{2,3,1,0:T(8,128)(2,1)}, u32[]{:S(2)}) copy-start(bf16[4,2,256,256]{2,3,1,0:T(8,128)(2,1)} %copy-done.17) | copy-start | bytes 3145732
  118.5 1.2 copy-start.19
  118.5 1.2 copy-start.52
  120.5 13.8 %all-to-all-start.5 = ((f32[8,2,512]{2,1,0:T(2,128)}), f32[8,2,512]{2,1,0:T(2,128)S(1)}, u32[]{:S(2)}, u32[]{:S(2)}) async-start(f32[8,2,512]{2,1,0:T(2,128)} %broadcast_in_dim.19), calls=%async_computation.5 | async-start | bytes 65536 | tf_op jit(solution)/shard_map/all_to_all | solution.py:55
  127.5 6.9 %copy-start.46 = (f32[1,512]{1,0:T(1,128)S(1)}, f32[1,512]{1,0:T(1,128)}, u32[]{:S(2)}) copy-start(f32[1,512]{1,0:T(1,128)} %copy-done.45) | copy-start | bytes 6148
  127.5 6.9 %copy-start.48 = (f32[1,512]{1,0:T(1,128)S(1)}, f32[1,512]{1,0:T(1,128)}, u32[]{:S(2)}) copy-start(f32[1,512]{1,0:T(1,128)} %copy-done.47) | copy-start | bytes 6148
  127.5 6.9 %copy-start.55 = (f32[512]{0:T(512)S(1)}, f32[512]{0:T(512)}, u32[]{:S(2)}) copy-start(f32[512]{0:T(512)} %multiply_multiply_fusion.4) | copy-start | bytes 6148
  127.5 6.9 %copy-start.56 = (f32[512]{0:T(512)S(1)}, f32[512]{0:T(512)}, u32[]{:S(2)}) copy-start(f32[512]{0:T(512)} %multiply_multiply_fusion.5) | copy-start | bytes 6148
